TPU v7x, 32 devices: a whole 2x2x4 slice. The times are simulated.
32 devices in a mesh: groups: 2 (over x), seq: 16 (over z, y, core).
Axes of the slice: x: 2, y: 2, z: 4, core: 2. Of those that a mesh axis runs over, the one named last changes fastest.
Arguments:
- fine_qkv: bfloat16 [16384, 3, 1024], P(('groups', 'seq')), parts along dimension 0, may hold values from -64 to 64
- clip_ids: int32 [4096], P('groups'), parts along dimension 0, may hold values from 0 to 1, never falling along the last dimension, each value on 1 to 1792 neighbouring positions
- w_coarse: bfloat16 [1024, 3, 1024], replicated, may hold values from -16 to 16
- w_out: bfloat16 [1024, 1024], replicated, may hold values from -0.25 to 0.25
Outputs:
- mixed: bfloat16 [16384, 1024], P(('groups', 'seq')), parts along dimension 0
There are 2 independent parts, one for each index of `groups`. A program takes and returns all parts, laid end to end along the dimension named above; an argument that names none is the same for every part. Nothing has to cross between parts.
Inputs may be any that keep to these rules, and one draw needn't show every extreme that they name: clip_ids never falls along the positions; each clip covers 1 to 1792 positions, one exactly 1792.
All inputs are finite; a program needn't handle non-finite values.
Results may differ from a plain program's by a relative error of at most 0.018.
The roundings to bfloat16 on the way count: a program that leaves them out, or rounds other values in their place, can miss the bound.
Values may be sent and summed in bfloat16 or wider, within the bound.
No kernel may reach another device: no remote copies, remote signals or barrier semaphores. Data moves between devices by JAX's collectives and lax.ppermute only.
A program may use at most 128 MiB of HBM per device.

v0:
```python
import math

import jax
import jax.numpy as jnp
from jax import lax
from jax.sharding import PartitionSpec as P

FHEADS = 16
CHEADS = 8
POOL = 4
QUARTERS = 4
FREACH = 2
CREACH = 3


def passed_along(value, axis, steps):
    count = lax.axis_size(axis)
    first, last = (max(0, -steps), min(count, count - steps))
    return lax.ppermute(value, axis, [(source, source + steps) for source in range(first, last)])


def from_partner(value, axis, bit):
    mask = 2**bit
    pairs = [(source, source ^ mask) for source in range(lax.axis_size(axis))]
    return lax.ppermute(value, axis, pairs)


def attend(queries, key_rows, value_rows, allowed, heads, head_groups):
    row_count = queries.shape[0]
    feat_width = queries.shape[1]
    head_dim = feat_width // heads
    per_group = heads // head_groups
    score_scale = 1.0 / math.sqrt(head_dim)

    def split_heads(source_rows):
        return source_rows.reshape(
            source_rows.shape[0], head_groups, per_group, head_dim
        ).transpose(1, 0, 2, 3)

    def one_group(operands):
        group_queries, group_keys, group_values = operands
        scores = (
            jnp.einsum(
                "rhd,khd->hrk", group_queries, group_keys, preferred_element_type=jnp.float32
            )
            * score_scale
        )
        masked = jnp.where(allowed[None], scores, -1e30)
        row_top = jnp.max(masked, axis=2, keepdims=True)
        weights = jnp.where(allowed[None], jnp.exp(masked - row_top), 0.0)
        row_total = jnp.sum(weights, axis=2)
        summed = jnp.einsum(
            "hrk,khd->rhd",
            weights.astype(jnp.bfloat16),
            group_values,
            preferred_element_type=jnp.float32,
        )
        return summed / jnp.transpose(row_total)[:, :, None]

    results = lax.map(
        one_group, (split_heads(queries), split_heads(key_rows), split_heads(value_rows))
    )
    return results.transpose(1, 0, 2, 3).reshape(row_count, feat_width).astype(jnp.bfloat16)


def body(fine_qkv, clip_ids, w_coarse, w_out):
    tok_count = fine_qkv.shape[0]
    feat_width = fine_qkv.shape[2]
    coarse_rows = tok_count // POOL
    group_rows = QUARTERS * coarse_rows
    position = lax.axis_index("seq")
    quarter = position % QUARTERS
    cycle_place = position // QUARTERS
    queries = fine_qkv[:, 0]
    own_pairs = fine_qkv[:, 1:3]
    arrived = []
    current = own_pairs
    for hop_index in range(FREACH):
        current = passed_along(current, "seq", 1)
        arrived.insert(0, current)
    window_pairs = jnp.concatenate(arrived + [own_pairs], axis=0)
    clip_front = jnp.concatenate([jnp.full((FREACH * coarse_rows,), -1, jnp.int32), clip_ids])
    key_clip = jnp.repeat(
        lax.dynamic_slice_in_dim(clip_front, position * coarse_rows, (FREACH + 1) * coarse_rows, 0),
        POOL,
    )
    own_clip = lax.dynamic_slice_in_dim(clip_ids, position * coarse_rows, coarse_rows, 0)
    query_clip = jnp.repeat(own_clip, POOL)
    query_pos = jnp.arange(tok_count, dtype=jnp.int32) + FREACH * tok_count
    key_pos = jnp.arange((FREACH + 1) * tok_count, dtype=jnp.int32)
    allowed = (key_pos[None, :] <= query_pos[:, None]) & (key_clip[None, :] == query_clip[:, None])
    fine_out = attend(queries, window_pairs[:, 0], window_pairs[:, 1], allowed, FHEADS, 4)
    pooled = jnp.mean(
        fine_out.astype(jnp.float32).reshape(coarse_rows, POOL, feat_width), axis=1
    ).astype(jnp.bfloat16)
    gathered = pooled
    for bit_index in range(2):
        partner = from_partner(gathered, "seq", bit_index)
        low_side = position // (1 << bit_index) % 2 == 0
        gathered = jnp.where(
            low_side,
            jnp.concatenate([gathered, partner], 0),
            jnp.concatenate([partner, gathered], 0),
        )
    quarter_width = w_coarse.shape[2] // QUARTERS
    quarter_weight = lax.dynamic_slice_in_dim(w_coarse, quarter * quarter_width, quarter_width, 2)
    projected = jnp.dot(
        gathered,
        quarter_weight.reshape(feat_width, 3 * quarter_width),
        preferred_element_type=jnp.float32,
    )
    projected = projected.astype(jnp.bfloat16).reshape(group_rows, 3, quarter_width)
    coarse_queries = projected[:, 0]
    coarse_pairs = projected[:, 1:3]
    earlier = []
    current = coarse_pairs
    for hop_index in range(CREACH):
        current = passed_along(current, "seq", QUARTERS)
        earlier.insert(0, current)
    coarse_window = jnp.concatenate(earlier + [coarse_pairs], axis=0)
    clip_back = jnp.concatenate([jnp.full((CREACH * group_rows,), -1, jnp.int32), clip_ids])
    coarse_key_clip = lax.dynamic_slice_in_dim(
        clip_back, cycle_place * group_rows, (CREACH + 1) * group_rows, 0
    )
    coarse_query_clip = lax.dynamic_slice_in_dim(clip_ids, cycle_place * group_rows, group_rows, 0)
    coarse_qpos = jnp.arange(group_rows, dtype=jnp.int32) + CREACH * group_rows
    coarse_kpos = jnp.arange((CREACH + 1) * group_rows, dtype=jnp.int32)
    coarse_allowed = (coarse_kpos[None, :] <= coarse_qpos[:, None]) & (
        coarse_key_clip[None, :] == coarse_query_clip[:, None]
    )
    coarse_att = attend(
        coarse_queries,
        coarse_window[:, 0],
        coarse_window[:, 1],
        coarse_allowed,
        CHEADS // QUARTERS,
        1,
    )
    row_weight = lax.dynamic_slice_in_dim(w_out, quarter * quarter_width, quarter_width, 0)
    stacked = jnp.dot(coarse_att, row_weight, preferred_element_type=jnp.float32).reshape(
        QUARTERS, coarse_rows, feat_width
    )
    for bit_index in range(2):
        paired = stacked.reshape(-1, 2, coarse_rows, feat_width)
        own_bit = quarter // (1 << bit_index) % 2
        retained = lax.dynamic_index_in_dim(paired, own_bit, 1, False)
        outgoing = lax.dynamic_index_in_dim(paired, 1 - own_bit, 1, False)
        stacked = retained + from_partner(outgoing, "seq", bit_index)
    coarse_up = stacked.reshape(coarse_rows, feat_width).astype(jnp.bfloat16)
    carried = passed_along(coarse_up[-1:], "seq", 1)
    previous = jnp.concatenate([carried, coarse_up[:-1]], axis=0)
    clip_before = jnp.concatenate([jnp.full((1,), -1, jnp.int32), clip_ids])
    prev_clip = lax.dynamic_slice_in_dim(clip_before, position * coarse_rows, coarse_rows, 0)
    joined = prev_clip == own_clip
    lifted = jnp.where(joined[:, None], previous.astype(jnp.float32), 0.0)
    mixed_rows = (
        fine_out.astype(jnp.float32).reshape(coarse_rows, POOL, feat_width) + lifted[:, None, :]
    )
    return mixed_rows.reshape(tok_count, feat_width).astype(jnp.bfloat16)


def solution(mesh):
    return jax.shard_map(
        body,
        mesh=mesh,
        in_specs=(P(("groups", "seq"), None, None), P("groups"), P(), P()),
        out_specs=P(("groups", "seq"), None),
        check_vma=False,
    )
```

profile of v0, /device:TPU:7, one launch (start us, length us, event | category | flops | bytes accessed | tf_op | source)
XLA Modules:
  0.0 273.6 jit_solution(15961018222022780202)
XLA Ops:
  3.3 3.7 %collective-permute-start = (bf16[512,2,1024]{2,0,1:T(8,128)(2,1)S(1)}, bf16[512,2,1024]{2,0,1:T(8,128)(2,1)}, u32[]{:S(2)}, u32[]{:S(2)}) collective-permute-start(bf16[512,2,1024]{2,0,1:T(8,128)(2,1)S(1)} %slice.36), channel_id=1, source_target_pairs={{0,1},{1,2},{2,3},{3,4},{4,5},{5,6},{6,7},{7,8},{8,9},{9,10},{10,1... | collective-permute-start | bytes 6291464 | tf_op jit(solution)/shard_map/ppermute | solution.py:19
  7.0 23.0 %collective-permute-done = bf16[512,2,1024]{2,0,1:T(8,128)(2,1)} collective-permute-done((bf16[512,2,1024]{2,0,1:T(8,128)(2,1)S(1)}, bf16[512,2,1024]{2,0,1:T(8,128)(2,1)}, u32[]{:S(2)}, u32[]{:S(2)}) %collective-permute-start) | collective-permute-done | bytes 2097184 | tf_op jit(solution)/shard_map/ppermute | solution.py:19
  29.9 5.4 %collective-permute-start.1 = (bf16[512,2,1024]{2,0,1:T(8,128)(2,1)}, bf16[512,2,1024]{2,0,1:T(8,128)(2,1)}, u32[]{:S(2)}, u32[]{:S(2)}) collective-permute-start(bf16[512,2,1024]{2,0,1:T(8,128)(2,1)} %collective-permute-done), channel_id=1, source_target_pairs={{0,1},{1,2},{2,3},{3,4},{4,5},{5,6},{6,7},{7,8},{8,9},{9,10},{10,1... | collective-permute-start | bytes 6291464 | tf_op jit(solution)/shard_map/ppermute | solution.py:19
  37.4 21.2 %collective-permute-done.1 = bf16[512,2,1024]{2,0,1:T(8,128)(2,1)} collective-permute-done((bf16[512,2,1024]{2,0,1:T(8,128)(2,1)}, bf16[512,2,1024]{2,0,1:T(8,128)(2,1)}, u32[]{:S(2)}, u32[]{:S(2)}) %collective-permute-start.1) | collective-permute-done | bytes 2097184 | tf_op jit(solution)/shard_map/ppermute | solution.py:19
  58.6 3.8 %pad_maximum_fusion = bf16[1536,2,1024]{2,0,1:T(8,128)(2,1)S(1)} fusion(bf16[512,2,1024]{2,0,1:T(8,128)(2,1)} %copy-done.2, bf16[512,2,1024]{2,0,1:T(8,128)(2,1)} %collective-permute-done, bf16[512,2,1024]{2,0,1:T(8,128)(2,1)} %collective-permute-done.1), kind=kLoop, calls=%fused_computation.37 | loop fusion | flops 18874368 | bytes 12582912 | tf_op jit(solution)/shard_map/concatenate | solution.py:81
  62.4 3.4 %fusion.98 = (bf16[1536,1,1024]{2,0,1:T(8,128)(2,1)}, bf16[1536,1,1024]{2,0,1:T(8,128)(2,1)}) fusion(bf16[1536,2,1024]{2,0,1:T(8,128)(2,1)S(1)} %pad_maximum_fusion), kind=kLoop, calls=%fused_computation.88 | loop fusion | bytes 12582912 | tf_op jit(solution)/shard_map/slice | solution.py:92
  65.8 4.8 %copy.22 = bf16[1536,1,1024]{0,2,1:T(8,128)(2,1)} copy(bf16[1536,1,1024]{2,0,1:T(8,128)(2,1)} %get-tuple-element.98) | data formatting | bytes 6291456 | tf_op jit(solution)/shard_map/slice | solution.py:92
  70.5 4.7 %copy.24 = bf16[1536,1,1024]{0,2,1:T(8,128)(2,1)} copy(bf16[1536,1,1024]{2,0,1:T(8,128)(2,1)} %get-tuple-element.97) | data formatting | bytes 6291456 | tf_op jit(solution)/shard_map/slice | solution.py:92
  75.2 62.0 %while.3 = (s32[]{:T(128)}, bf16[4,512,4,64]{1,3,2,0:T(8,128)(2,1)}, bf16[4,1536,4,64]{1,3,2,0:T(8,128)(2,1)}, bf16[4,512,4,64]{1,3,2,0:T(8,128)(2,1)}, bf16[4,1...) while((s32[]{:T(128)}, ...), condition=%wide.region_3.4_spmd.clone, body=%wide.region_0.3_spmd.clone.sunk | while | flops 826672640 | bytes 17330268 | solution.py:60
  76.0 9.0 %fusion.122 = (f32[4,512]{1,0:T(4,128)S(1)}, bf16[4,512,1536]{2,1,0:T(8,128)(2,1)}) fusion(pred[512,1536]{1,0:T(8,128)(4,1)S(1)} %fusion.121, bf16[4,1536,4,64]{1,3,2,0:T(8,128)(2,1)} %get-tuple-element.184, s32[]{:T(128)} %get-tuple-element.171, bf16[4,512,4,64]{1,3,2,0:T(8,128)(2,1)} %get-tuple-element.183), kind=kOutput, calls=%fused_computation.87.clone.1 | convolution fusion | flops 421529088 | bytes 8922112 | tf_op jit(solution)/shard_map/while/body/eval_jaxpr/sub | solution.py:50
  84.9 5.8 %fusion.123 = bf16[4,512,4,64]{1,3,2,0:T(8,128)(2,1)} fusion(bf16[4,512,4,64]{1,3,2,0:T(8,128)(2,1)} %get-tuple-element.172, s32[]{:T(128)} %get-tuple-element.171, bf16[4,512,1536]{2,1,0:T(8,128)(2,1)} %get-tuple-element.160, bf16[4,1536,4,64]{1,3,2,0:T(8,128)(2,1)} %get-tuple-element.182, f32[512,4]{0,1:T(4,128)S(1)} %bitcast.114), kind=kOutput, calls=%fused_computation.16.clone.1 | convolution fusion | flops 402784256 | bytes 7611392 | tf_op jit(solution)/shard_map/while/body/eval_jaxpr/hrk,khd->rhd/dot_general | solution.py:52
  91.5 9.0 %fusion.122 = (f32[4,512]{1,0:T(4,128)S(1)}, bf16[4,512,1536]{2,1,0:T(8,128)(2,1)}) fusion(pred[512,1536]{1,0:T(8,128)(4,1)S(1)} %fusion.121, bf16[4,1536,4,64]{1,3,2,0:T(8,128)(2,1)} %get-tuple-element.184, s32[]{:T(128)} %get-tuple-element.171, bf16[4,512,4,64]{1,3,2,0:T(8,128)(2,1)} %get-tuple-element.183), kind=kOutput, calls=%fused_computation.87.clone.1 | convolution fusion | flops 421529088 | bytes 8922112 | tf_op jit(solution)/shard_map/while/body/eval_jaxpr/sub | solution.py:50
  100.4 5.8 %fusion.123 = bf16[4,512,4,64]{1,3,2,0:T(8,128)(2,1)} fusion(bf16[4,512,4,64]{1,3,2,0:T(8,128)(2,1)} %get-tuple-element.172, s32[]{:T(128)} %get-tuple-element.171, bf16[4,512,1536]{2,1,0:T(8,128)(2,1)} %get-tuple-element.160, bf16[4,1536,4,64]{1,3,2,0:T(8,128)(2,1)} %get-tuple-element.182, f32[512,4]{0,1:T(4,128)S(1)} %bitcast.114), kind=kOutput, calls=%fused_computation.16.clone.1 | convolution fusion | flops 402784256 | bytes 7611392 | tf_op jit(solution)/shard_map/while/body/eval_jaxpr/hrk,khd->rhd/dot_general | solution.py:52
  107.0 9.0 %fusion.122 = (f32[4,512]{1,0:T(4,128)S(1)}, bf16[4,512,1536]{2,1,0:T(8,128)(2,1)}) fusion(pred[512,1536]{1,0:T(8,128)(4,1)S(1)} %fusion.121, bf16[4,1536,4,64]{1,3,2,0:T(8,128)(2,1)} %get-tuple-element.184, s32[]{:T(128)} %get-tuple-element.171, bf16[4,512,4,64]{1,3,2,0:T(8,128)(2,1)} %get-tuple-element.183), kind=kOutput, calls=%fused_computation.87.clone.1 | convolution fusion | flops 421529088 | bytes 8922112 | tf_op jit(solution)/shard_map/while/body/eval_jaxpr/sub | solution.py:50
  115.9 5.8 %fusion.123 = bf16[4,512,4,64]{1,3,2,0:T(8,128)(2,1)} fusion(bf16[4,512,4,64]{1,3,2,0:T(8,128)(2,1)} %get-tuple-element.172, s32[]{:T(128)} %get-tuple-element.171, bf16[4,512,1536]{2,1,0:T(8,128)(2,1)} %get-tuple-element.160, bf16[4,1536,4,64]{1,3,2,0:T(8,128)(2,1)} %get-tuple-element.182, f32[512,4]{0,1:T(4,128)S(1)} %bitcast.114), kind=kOutput, calls=%fused_computation.16.clone.1 | convolution fusion | flops 402784256 | bytes 7611392 | tf_op jit(solution)/shard_map/while/body/eval_jaxpr/hrk,khd->rhd/dot_general | solution.py:52
  122.5 9.0 %fusion.122 = (f32[4,512]{1,0:T(4,128)S(1)}, bf16[4,512,1536]{2,1,0:T(8,128)(2,1)}) fusion(pred[512,1536]{1,0:T(8,128)(4,1)S(1)} %fusion.121, bf16[4,1536,4,64]{1,3,2,0:T(8,128)(2,1)} %get-tuple-element.184, s32[]{:T(128)} %get-tuple-element.171, bf16[4,512,4,64]{1,3,2,0:T(8,128)(2,1)} %get-tuple-element.183), kind=kOutput, calls=%fused_computation.87.clone.1 | convolution fusion | flops 421529088 | bytes 8922112 | tf_op jit(solution)/shard_map/while/body/eval_jaxpr/sub | solution.py:50
  131.4 5.8 %fusion.123 = bf16[4,512,4,64]{1,3,2,0:T(8,128)(2,1)} fusion(bf16[4,512,4,64]{1,3,2,0:T(8,128)(2,1)} %get-tuple-element.172, s32[]{:T(128)} %get-tuple-element.171, bf16[4,512,1536]{2,1,0:T(8,128)(2,1)} %get-tuple-element.160, bf16[4,1536,4,64]{1,3,2,0:T(8,128)(2,1)} %get-tuple-element.182, f32[512,4]{0,1:T(4,128)S(1)} %bitcast.114), kind=kOutput, calls=%fused_computation.16.clone.1 | convolution fusion | flops 402784256 | bytes 7611392 | tf_op jit(solution)/shard_map/while/body/eval_jaxpr/hrk,khd->rhd/dot_general | solution.py:52
  137.2 3.8 %fusion.100 = (f32[4,512,4,64]{1,3,2,0:T(8,128)}, f32[512,4,4,64]{0,3,2,1:T(8,128)}) fusion(bf16[4,512,4,64]{1,3,2,0:T(8,128)(2,1)} %get-tuple-element.55), kind=kLoop, calls=%fused_computation.90 | loop fusion | flops 524288 | bytes 5242880 | tf_op jit(solution)/shard_map/convert_element_type | solution.py:157
  140.9 4.9 %copy.25 = f32[512,4,4,64]{3,2,1,0:T(4,128)} copy(f32[512,4,4,64]{0,3,2,1:T(8,128)} %get-tuple-element.102) | data formatting | bytes 4194304 | tf_op jit(solution)/shard_map/convert_element_type | solution.py:157
  145.8 5.9 %reshape.127 = f32[128,4,1024]{2,1,0:T(4,128)} reshape(f32[512,4,4,64]{3,2,1,0:T(4,128)} %copy.25) | data formatting | bytes 4194304 | tf_op jit(solution)/shard_map/convert_element_type | solution.py:157
  161.9 7.8 %collective-permute-done.3 = bf16[256,1024]{1,0:T(8,128)(2,1)S(1)} collective-permute-done((bf16[256,1024]{1,0:T(8,128)(2,1)S(1)}, bf16[256,1024]{1,0:T(8,128)(2,1)S(1)}, u32[]{:S(2)}, u32[]{:S(2)}) %collective-permute-start.3) | collective-permute-done | bytes 524320 | tf_op jit(solution)/shard_map/ppermute | solution.py:25
  174.4 4.9 %collective-permute-start.4 = (bf16[512,2,256]{0,2,1:T(8,128)(2,1)S(1)}, bf16[512,2,256]{0,2,1:T(8,128)(2,1)}, u32[]{:S(2)}, u32[]{:S(2)}) collective-permute-start(bf16[512,2,256]{0,2,1:T(8,128)(2,1)S(1)} %slice.50), channel_id=1, source_target_pairs={{0,4},{1,5},{2,6},{3,7},{4,8},{5,9},{6,10},{7,11},{8,12},{9,13},{1... | collective-permute-start | bytes 1572872 | tf_op jit(solution)/shard_map/ppermute | solution.py:19
  179.4 9.5 %collective-permute-done.4 = bf16[512,2,256]{0,2,1:T(8,128)(2,1)} collective-permute-done((bf16[512,2,256]{0,2,1:T(8,128)(2,1)S(1)}, bf16[512,2,256]{0,2,1:T(8,128)(2,1)}, u32[]{:S(2)}, u32[]{:S(2)}) %collective-permute-start.4) | collective-permute-done | bytes 524320 | tf_op jit(solution)/shard_map/ppermute | solution.py:19
  188.9 5.0 %collective-permute-start.5 = (bf16[512,2,256]{0,2,1:T(8,128)(2,1)}, bf16[512,2,256]{0,2,1:T(8,128)(2,1)}, u32[]{:S(2)}, u32[]{:S(2)}) collective-permute-start(bf16[512,2,256]{0,2,1:T(8,128)(2,1)} %collective-permute-done.4), channel_id=1, source_target_pairs={{0,4},{1,5},{2,6},{3,7},{4,8},{5,9},{6,10},{7,11},{8,12},{9,13},{1... | collective-permute-start | bytes 1572872 | tf_op jit(solution)/shard_map/ppermute | solution.py:19
  194.0 8.8 %collective-permute-done.5 = bf16[512,2,256]{0,2,1:T(8,128)(2,1)} collective-permute-done((bf16[512,2,256]{0,2,1:T(8,128)(2,1)}, bf16[512,2,256]{0,2,1:T(8,128)(2,1)}, u32[]{:S(2)}, u32[]{:S(2)}) %collective-permute-start.5) | collective-permute-done | bytes 524320 | tf_op jit(solution)/shard_map/ppermute | solution.py:19
  202.8 4.9 %collective-permute-start.6 = (bf16[512,2,256]{0,2,1:T(8,128)(2,1)}, bf16[512,2,256]{0,2,1:T(8,128)(2,1)}, u32[]{:S(2)}, u32[]{:S(2)}) collective-permute-start(bf16[512,2,256]{0,2,1:T(8,128)(2,1)} %collective-permute-done.5), channel_id=1, source_target_pairs={{0,4},{1,5},{2,6},{3,7},{4,8},{5,9},{6,10},{7,11},{8,12},{9,13},{1... | collective-permute-start | bytes 1572872 | tf_op jit(solution)/shard_map/ppermute | solution.py:19
  210.5 5.2 %collective-permute-done.6 = bf16[512,2,256]{0,2,1:T(8,128)(2,1)} collective-permute-done((bf16[512,2,256]{0,2,1:T(8,128)(2,1)}, bf16[512,2,256]{0,2,1:T(8,128)(2,1)}, u32[]{:S(2)}, u32[]{:S(2)}) %collective-permute-start.6) | collective-permute-done | bytes 524320 | tf_op jit(solution)/shard_map/ppermute | solution.py:19
  219.0 7.5 %fusion.101 = (f32[2,512]{1,0:T(2,128)S(1)}, bf16[2,512,2048]{2,1,0:T(8,128)(2,1)}) fusion(pred[512,2048]{1,0:T(8,128)(4,1)S(1)} %copy-done.3, bf16[512,2,128]{0,2,1:T(8,128)(2,1)S(1)} %bitcast.113, bf16[2048,2,128]{0,2,1:T(8,128)(2,1)} %bitcast.112), kind=kOutput, calls=%fused_computation.91 | convolution fusion | flops 549455872 | bytes 6557696 | tf_op jit(solution)/shard_map/while/body/eval_jaxpr/sub | solution.py:50
  226.4 4.0 %fusion.67 = bf16[512,2,128]{0,2,1:T(8,128)(2,1)S(1)} fusion(bf16[2048,2,128]{0,2,1:T(8,128)(2,1)} %bitcast.111, bf16[2,512,2048]{2,1,0:T(8,128)(2,1)} %get-tuple-element.104, f32[512,2]{0,1:T(2,128)S(1)} %bitcast.115), kind=kOutput, calls=%fused_computation.51 | convolution fusion | flops 537133056 | bytes 5509120 | tf_op jit(solution)/shard_map/while/body/eval_jaxpr/hrk,khd->rhd/dot_general | solution.py:52
  232.4 3.7 %collective-permute-start.7 = (f32[2,128,1024]{2,1,0:T(8,128)S(1)}, f32[2,128,1024]{2,1,0:T(8,128)}, u32[]{:S(2)}, u32[]{:S(2)}) collective-permute-start(f32[2,128,1024]{2,1,0:T(8,128)S(1)} %dynamic-slice_bitcast_fusion), channel_id=1, source_target_pairs={{0,1},{1,0},{2,3},{3,2},{4,5},{5,4},{6,7},{7,6},{8,9},{9,8},{10,11... | collective-permute-start | bytes 3145736 | tf_op jit(solution)/shard_map/ppermute | solution.py:25
  241.5 13.0 %collective-permute-done.8 = f32[1,128,1024]{2,1,0:T(8,128)} collective-permute-done((f32[1,128,1024]{2,1,0:T(8,128)}, f32[1,128,1024]{2,1,0:T(8,128)}, u32[]{:S(2)}, u32[]{:S(2)}) %collective-permute-start.8) | collective-permute-done | bytes 524320 | tf_op jit(solution)/shard_map/ppermute | solution.py:25
  255.6 5.4 %collective-permute-start.9 = (bf16[1,1024]{1,0:T(2,128)(2,1)S(1)}, bf16[1,1024]{1,0:T(2,128)(2,1)S(1)}, u32[]{:S(2)}, u32[]{:S(2)}) collective-permute-start(bf16[1,1024]{1,0:T(2,128)(2,1)S(1)} %slice_bitcast_fusion.1), channel_id=1, source_target_pairs={{0,1},{1,2},{2,3},{3,4},{4,5},{5,6},{6,7},{7,8},{8,9},{9,10},{10,1... | collective-permute-start | bytes 6152 | tf_op jit(solution)/shard_map/ppermute | solution.py:19
  (63 shorter events, 50.2 us)
Async XLA Ops:
  0.0 230.5 %copy-start = (bf16[1024,1024]{1,0:T(8,128)(2,1)S(1)}, bf16[1024,1024]{1,0:T(8,128)(2,1)}, u32[]{:S(2)}) copy-start(bf16[1024,1024]{1,0:T(8,128)(2,1)} %param.9) | copy-start | bytes 6291460
  0.0 36.0 %slice-start = ((bf16[512,3,1024]{2,0,1:T(8,128)(2,1)}), bf16[512,1,1024]{2,0,1:T(8,128)(2,1)S(1)}, s32[]{:S(2)}) async-start(bf16[512,3,1024]{2,0,1:T(8,128)(2,1)} %param.6), calls=%async_computation | async-start | bytes 2097152 | tf_op jit(solution)/shard_map/slice | solution.py:74
  0.0 35.3 %copy-start.5 = (s32[2048]{0:T(1024)S(1)}, s32[2048]{0:T(1024)}, u32[]{:S(2)}) copy-start(s32[2048]{0:T(1024)} %param.7) | copy-start | bytes 24580
  1.9 1.3 copy-start.2
  3.3 26.7 %collective-permute-start = (bf16[512,2,1024]{2,0,1:T(8,128)(2,1)S(1)}, bf16[512,2,1024]{2,0,1:T(8,128)(2,1)}, u32[]{:S(2)}, u32[]{:S(2)}) collective-permute-start(bf16[512,2,1024]{2,0,1:T(8,128)(2,1)S(1)} %slice.36), channel_id=1, source_target_pairs={{0,1},{1,2},{2,3},{3,4},{4,5},{5,6},{6,7},{7,8},{8,9},{9,10},{10,1... | collective-permute-start | bytes 6291464 | tf_op jit(solution)/shard_map/ppermute | solution.py:19
  29.9 28.7 %collective-permute-start.1 = (bf16[512,2,1024]{2,0,1:T(8,128)(2,1)}, bf16[512,2,1024]{2,0,1:T(8,128)(2,1)}, u32[]{:S(2)}, u32[]{:S(2)}) collective-permute-start(bf16[512,2,1024]{2,0,1:T(8,128)(2,1)} %collective-permute-done), channel_id=1, source_target_pairs={{0,1},{1,2},{2,3},{3,4},{4,5},{5,6},{6,7},{7,8},{8,9},{9,10},{10,1... | collective-permute-start | bytes 6291464 | tf_op jit(solution)/shard_map/ppermute | solution.py:19
  154.7 1.7 collective-permute-start.2
  156.5 13.2 %collective-permute-start.3 = (bf16[256,1024]{1,0:T(8,128)(2,1)S(1)}, bf16[256,1024]{1,0:T(8,128)(2,1)S(1)}, u32[]{:S(2)}, u32[]{:S(2)}) collective-permute-start(bf16[256,1024]{1,0:T(8,128)(2,1)S(1)} %maximum_select_fusion.2), channel_id=1, source_target_pairs={{0,2},{1,3},{2,0},{3,1},{4,6},{5,7},{6,4},{7,5},{8,10},{9,11},{10,... | collective-permute-start | bytes 1572872 | tf_op jit(solution)/shard_map/ppermute | solution.py:25
  174.4 14.4 %collective-permute-start.4 = (bf16[512,2,256]{0,2,1:T(8,128)(2,1)S(1)}, bf16[512,2,256]{0,2,1:T(8,128)(2,1)}, u32[]{:S(2)}, u32[]{:S(2)}) collective-permute-start(bf16[512,2,256]{0,2,1:T(8,128)(2,1)S(1)} %slice.50), channel_id=1, source_target_pairs={{0,4},{1,5},{2,6},{3,7},{4,8},{5,9},{6,10},{7,11},{8,12},{9,13},{1... | collective-permute-start | bytes 1572872 | tf_op jit(solution)/shard_map/ppermute | solution.py:19
  188.9 13.9 %collective-permute-start.5 = (bf16[512,2,256]{0,2,1:T(8,128)(2,1)}, bf16[512,2,256]{0,2,1:T(8,128)(2,1)}, u32[]{:S(2)}, u32[]{:S(2)}) collective-permute-start(bf16[512,2,256]{0,2,1:T(8,128)(2,1)} %collective-permute-done.4), channel_id=1, source_target_pairs={{0,4},{1,5},{2,6},{3,7},{4,8},{5,9},{6,10},{7,11},{8,12},{9,13},{1... | collective-permute-start | bytes 1572872 | tf_op jit(solution)/shard_map/ppermute | solution.py:19
  202.8 12.9 %collective-permute-start.6 = (bf16[512,2,256]{0,2,1:T(8,128)(2,1)}, bf16[512,2,256]{0,2,1:T(8,128)(2,1)}, u32[]{:S(2)}, u32[]{:S(2)}) collective-permute-start(bf16[512,2,256]{0,2,1:T(8,128)(2,1)} %collective-permute-done.5), channel_id=1, source_target_pairs={{0,4},{1,5},{2,6},{3,7},{4,8},{5,9},{6,10},{7,11},{8,12},{9,13},{1... | collective-permute-start | bytes 1572872 | tf_op jit(solution)/shard_map/ppermute | solution.py:19
  217.3 1.6 copy-start.3
  217.4 1.6 copy-start.4
  231.0 1.3 copy-start.1
  232.4 6.1 %collective-permute-start.7 = (f32[2,128,1024]{2,1,0:T(8,128)S(1)}, f32[2,128,1024]{2,1,0:T(8,128)}, u32[]{:S(2)}, u32[]{:S(2)}) collective-permute-start(f32[2,128,1024]{2,1,0:T(8,128)S(1)} %dynamic-slice_bitcast_fusion), channel_id=1, source_target_pairs={{0,1},{1,0},{2,3},{3,2},{4,5},{5,4},{6,7},{7,6},{8,9},{9,8},{10,11... | collective-permute-start | bytes 3145736 | tf_op jit(solution)/shard_map/ppermute | solution.py:25
  241.1 13.5 %collective-permute-start.8 = (f32[1,128,1024]{2,1,0:T(8,128)}, f32[1,128,1024]{2,1,0:T(8,128)}, u32[]{:S(2)}, u32[]{:S(2)}) collective-permute-start(f32[1,128,1024]{2,1,0:T(8,128)} %constant_dynamic-slice_fusion), channel_id=1, source_target_pairs={{0,2},{1,3},{2,0},{3,1},{4,6},{5,7},{6,4},{7,5},{8,10},{9,11},{10,... | collective-permute-start | bytes 1572872 | tf_op jit(solution)/shard_map/ppermute | solution.py:25
  255.6 6.1 %collective-permute-start.9 = (bf16[1,1024]{1,0:T(2,128)(2,1)S(1)}, bf16[1,1024]{1,0:T(2,128)(2,1)S(1)}, u32[]{:S(2)}, u32[]{:S(2)}) collective-permute-start(bf16[1,1024]{1,0:T(2,128)(2,1)S(1)} %slice_bitcast_fusion.1), channel_id=1, source_target_pairs={{0,1},{1,2},{2,3},{3,4},{4,5},{5,6},{6,7},{7,8},{8,9},{9,10},{10,1... | collective-permute-start | bytes 6152 | tf_op jit(solution)/shard_map/ppermute | solution.py:19
where the time goes:
time: 276 us; the launch traced here: 274 us
  waiting for transfers between devices  92.8 us (34%)
  matrix products  74.1 us (27%)
  local copies, waits for them, and re-layouts  49.4 us (18%)
  starting transfers between devices  34.1 us (12%)
  other arithmetic  22.8 us (8%)
    ppermute x6, waiting for transfers between devices, passed_along(): lax.ppermute(value, axis, [(source, source + steps) for source in range(f...  68.5 us
    sub x5, matrix products, one_group(): weights = jnp.where(allowed[None], jnp.exp(masked - row_top), 0.0)  43.3 us
    ppermute x6, starting transfers between devices, passed_along(): lax.ppermute(value, axis, [(source, source + steps) for source in range(f...  29.3 us
    dot_general x5, matrix products, one_group(): jnp.einsum('hrk,khd->rhd', weights.astype(jnp.bfloat16), group_values, pr...  27.1 us
    ppermute x4, waiting for transfers between devices, from_partner(): return lax.ppermute(value, axis, pairs)  24.4 us
    convert_element_type x2, local copies, waits for them, and re-layouts, body(): fine_out.astype(jnp.float32).reshape(coarse_rows, POOL, feat_width)  10.8 us
    slice x2, local copies, waits for them, and re-layouts, body(): window_pairs[:, 0]  8.04 us
    add x3, local copies, waits for them, and re-layouts, body(): fine_out.astype(jnp.float32).reshape(coarse_rows, POOL, feat_width)  7.8 us
  transfers between devices with their start and end apart: 10, of which 10 were waited for; matrix products, arithmetic and copies ran while one was open for 4% of the time, Pallas kernels for 0%

commit v1 on v0

--- a/solution.py
+++ b/solution.py
@@ -1,8 +1,11 @@
+import functools
 import math
 
 import jax
 import jax.numpy as jnp
 from jax import lax
+from jax.experimental import pallas as pl
+from jax.experimental.pallas import tpu as pltpu
 from jax.sharding import PartitionSpec as P
 
 FHEADS = 16
@@ -11,6 +14,7 @@
 QUARTERS = 4
 FREACH = 2
 CREACH = 3
+FINE_TILE = 256
 
 
 def passed_along(value, axis, steps):
@@ -19,10 +23,87 @@
     return lax.ppermute(value, axis, [(source, source + steps) for source in range(first, last)])
 
 
-def from_partner(value, axis, bit):
-    mask = 2**bit
-    pairs = [(source, source ^ mask) for source in range(lax.axis_size(axis))]
+def within_group(value, axis, shift):
+    count = lax.axis_size(axis)
+    pairs = []
+    for source in range(count):
+        base = source - source % QUARTERS
+        pairs.append((source, base + (source % QUARTERS + shift) % QUARTERS))
     return lax.ppermute(value, axis, pairs)
+
+
+def fine_kernel(qclip_ref, kclip0_ref, kclip1_ref, kclip2_ref, q_ref,
+                k0_ref, v0_ref, k1_ref, v1_ref, k2_ref, v2_ref, out_ref, *, scale):
+    tile = q_ref.shape[0]
+    width = q_ref.shape[1]
+    half = width // 2
+    q = q_ref[...]
+    lane = lax.broadcasted_iota(jnp.int32, (1, width), 1)
+    low = lane < half
+    zero = jnp.zeros_like(q)
+    head_q = (jnp.where(low, q, zero), jnp.where(low, zero, q))
+    qclip = qclip_ref[...]
+    keys = (k0_ref, k1_ref, k2_ref)
+    values = (v0_ref, v1_ref, v2_ref)
+    clips = (kclip0_ref, kclip1_ref, kclip2_ref)
+    seg = k0_ref.shape[0]
+    qpos = pl.program_id(1) * tile + lax.broadcasted_iota(jnp.int32, (tile, seg), 0)
+    kpos = lax.broadcasted_iota(jnp.int32, (tile, seg), 1)
+    masks = []
+    for j in range(3):
+        allowed = clips[j][...] == qclip
+        if j == 2:
+            allowed = allowed & (kpos <= qpos)
+        masks.append(allowed)
+    results = []
+    for h in range(2):
+        scores = []
+        for j in range(3):
+            s = lax.dot_general(head_q[h], keys[j][...], (((1,), (1,)), ((), ())),
+                                preferred_element_type=jnp.float32) * scale
+            scores.append(jnp.where(masks[j], s, -1e30))
+        top = jnp.max(scores[0], axis=1, keepdims=True)
+        for j in range(1, 3):
+            top = jnp.maximum(top, jnp.max(scores[j], axis=1, keepdims=True))
+        total = None
+        summed = None
+        for j in range(3):
+            w = jnp.where(masks[j], jnp.exp(scores[j] - top), 0.0)
+            part = jnp.sum(w, axis=1, keepdims=True)
+            pv = jnp.dot(w.astype(jnp.bfloat16), values[j][...], preferred_element_type=jnp.float32)
+            total = part if total is None else total + part
+            summed = pv if summed is None else summed + pv
+        results.append(summed / total)
+    out_ref[...] = jnp.where(low, results[0], results[1]).astype(out_ref.dtype)
+
+
+def fine_attention(qkv_flat, prev0, prev1, qclip, kclip, heads):
+    tok, width3 = qkv_flat.shape
+    width = width3 // 3
+    head_dim = width // heads
+    pair = 2 * head_dim
+    pairs = width // pair
+    tile = min(FINE_TILE, tok)
+    nq = tok // tile
+    kernel = functools.partial(fine_kernel, scale=1.0 / math.sqrt(head_dim))
+    qspec = pl.BlockSpec((tile, pair), lambda h, i: (i, h))
+    own_k = pl.BlockSpec((tok, pair), lambda h, i: (0, pairs + h))
+    own_v = pl.BlockSpec((tok, pair), lambda h, i: (0, 2 * pairs + h))
+    prev_k = pl.BlockSpec((tok, pair), lambda h, i: (0, h))
+    prev_v = pl.BlockSpec((tok, pair), lambda h, i: (0, pairs + h))
+    return pl.pallas_call(
+        kernel,
+        grid=(pairs, nq),
+        in_specs=[
+            pl.BlockSpec((tile, 1), lambda h, i: (i, 0)),
+            pl.BlockSpec((1, tok), lambda h, i: (0, 0)),
+            pl.BlockSpec((1, tok), lambda h, i: (0, 1)),
+            pl.BlockSpec((1, tok), lambda h, i: (0, 2)),
+            qspec, prev_k, prev_v, prev_k, prev_v, own_k, own_v,
+        ],
+        out_specs=pl.BlockSpec((tile, pair), lambda h, i: (i, h)),
+        out_shape=jax.ShapeDtypeStruct((tok, width), jnp.bfloat16),
+    )(qclip, kclip, kclip, kclip, qkv_flat, prev0, prev0, prev1, prev1, qkv_flat, qkv_flat)
 
 
 def attend(queries, key_rows, value_rows, allowed, heads, head_groups):
@@ -71,14 +152,10 @@
     position = lax.axis_index("seq")
     quarter = position % QUARTERS
     cycle_place = position // QUARTERS
-    queries = fine_qkv[:, 0]
-    own_pairs = fine_qkv[:, 1:3]
-    arrived = []
-    current = own_pairs
-    for hop_index in range(FREACH):
-        current = passed_along(current, "seq", 1)
-        arrived.insert(0, current)
-    window_pairs = jnp.concatenate(arrived + [own_pairs], axis=0)
+    qkv_flat = fine_qkv.reshape(tok_count, 3 * feat_width)
+    own_pairs = qkv_flat[:, feat_width:]
+    prev1 = passed_along(own_pairs, "seq", 1)
+    prev0 = passed_along(own_pairs, "seq", 2)
     clip_front = jnp.concatenate([jnp.full((FREACH * coarse_rows,), -1, jnp.int32), clip_ids])
     key_clip = jnp.repeat(
         lax.dynamic_slice_in_dim(clip_front, position * coarse_rows, (FREACH + 1) * coarse_rows, 0),
@@ -86,22 +163,16 @@
     )
     own_clip = lax.dynamic_slice_in_dim(clip_ids, position * coarse_rows, coarse_rows, 0)
     query_clip = jnp.repeat(own_clip, POOL)
-    query_pos = jnp.arange(tok_count, dtype=jnp.int32) + FREACH * tok_count
-    key_pos = jnp.arange((FREACH + 1) * tok_count, dtype=jnp.int32)
-    allowed = (key_pos[None, :] <= query_pos[:, None]) & (key_clip[None, :] == query_clip[:, None])
-    fine_out = attend(queries, window_pairs[:, 0], window_pairs[:, 1], allowed, FHEADS, 4)
+    fine_out = fine_attention(
+        qkv_flat, prev0, prev1, query_clip.reshape(tok_count, 1),
+        key_clip.reshape(1, (FREACH + 1) * tok_count), FHEADS,
+    )
     pooled = jnp.mean(
         fine_out.astype(jnp.float32).reshape(coarse_rows, POOL, feat_width), axis=1
     ).astype(jnp.bfloat16)
-    gathered = pooled
-    for bit_index in range(2):
-        partner = from_partner(gathered, "seq", bit_index)
-        low_side = position // (1 << bit_index) % 2 == 0
-        gathered = jnp.where(
-            low_side,
-            jnp.concatenate([gathered, partner], 0),
-            jnp.concatenate([partner, gathered], 0),
-        )
+    received = [pooled] + [within_group(pooled, "seq", shift) for shift in range(1, QUARTERS)]
+    from_next = jnp.stack([received[0]] + received[:0:-1], axis=0)
+    gathered = jnp.roll(from_next, quarter, axis=0).reshape(group_rows, feat_width)
     quarter_width = w_coarse.shape[2] // QUARTERS
     quarter_weight = lax.dynamic_slice_in_dim(w_coarse, quarter * quarter_width, quarter_width, 2)
     projected = jnp.dot(
@@ -112,11 +183,7 @@
     projected = projected.astype(jnp.bfloat16).reshape(group_rows, 3, quarter_width)
     coarse_queries = projected[:, 0]
     coarse_pairs = projected[:, 1:3]
-    earlier = []
-    current = coarse_pairs
-    for hop_index in range(CREACH):
-        current = passed_along(current, "seq", QUARTERS)
-        earlier.insert(0, current)
+    earlier = [passed_along(coarse_pairs, "seq", QUARTERS * hop) for hop in range(CREACH, 0, -1)]
     coarse_window = jnp.concatenate(earlier + [coarse_pairs], axis=0)
     clip_back = jnp.concatenate([jnp.full((CREACH * group_rows,), -1, jnp.int32), clip_ids])
     coarse_key_clip = lax.dynamic_slice_in_dim(
@@ -140,13 +207,11 @@
     stacked = jnp.dot(coarse_att, row_weight, preferred_element_type=jnp.float32).reshape(
         QUARTERS, coarse_rows, feat_width
     )
-    for bit_index in range(2):
-        paired = stacked.reshape(-1, 2, coarse_rows, feat_width)
-        own_bit = quarter // (1 << bit_index) % 2
-        retained = lax.dynamic_index_in_dim(paired, own_bit, 1, False)
-        outgoing = lax.dynamic_index_in_dim(paired, 1 - own_bit, 1, False)
-        stacked = retained + from_partner(outgoing, "seq", bit_index)
-    coarse_up = stacked.reshape(coarse_rows, feat_width).astype(jnp.bfloat16)
+    summed_up = lax.dynamic_index_in_dim(stacked, quarter, 0, False)
+    for shift in range(1, QUARTERS):
+        outgoing = lax.dynamic_index_in_dim(stacked, (quarter + shift) % QUARTERS, 0, False)
+        summed_up = summed_up + within_group(outgoing, "seq", shift)
+    coarse_up = summed_up.astype(jnp.bfloat16)
     carried = passed_along(coarse_up[-1:], "seq", 1)
     previous = jnp.concatenate([carried, coarse_up[:-1]], axis=0)
     clip_before = jnp.concatenate([jnp.full((1,), -1, jnp.int32), clip_ids])

time: 276 us -> 256 us (0.928)
  matrix products: 74.1 us -> 13.9 us
  Pallas kernels: 0 us -> 32.6 us
  waiting for transfers between devices: 92.8 us -> 114 us
  other arithmetic: 22.8 us -> 11.8 us
  local copies, waits for them, and re-layouts: 49.4 us -> 40.5 us
  starting transfers between devices: 34.1 us -> 40.2 us
    sub x5 -> x1, matrix products: 43.3 us -> 7.46 us  [one_group(): weights = jnp.where(allowed[None], jnp.exp(masked - row_top), 0.0)]
    pallas_call x0 -> x1, Pallas kernels: none -> 32.6 us  [fine_attention(): pl.pallas_call(kernel, grid=(pairs, nq), in_specs=[pl.BlockSpec((tile, 1)...]
    dot_general x5 -> x1, matrix products: 27.1 us -> 4.04 us  [one_group(): jnp.einsum('hrk,khd->rhd', weights.astype(jnp.bfloat16), group_values, pr...]
    ppermute x6, waiting for transfers between devices: 68.5 us -> 87.3 us  [passed_along(): lax.ppermute(value, axis, [(source, source + steps) for source in range(f...]
    slice x8 -> x1, local copies, waits for them, and re-layouts: 16.1 us -> 3.25 us  [body(): own_pairs = qkv_flat[:, feat_width:]]
    convert_element_type x3 -> x0, local copies, waits for them, and re-layouts: 12.1 us -> none  [the longest x2 10.8 us: body(): fine_out.astype(jnp.float32).reshape(coarse_rows, POOL, feat_width)]
    unnamed x13 -> x22, local copies, waits for them, and re-layouts: 5.26 us -> 13.2 us
    reshape x0 -> x2, local copies, waits for them, and re-layouts: none -> 7.38 us  [the longest x1 4.67 us: body(): qkv_flat = fine_qkv.reshape(tok_count, 3 * feat_width)]
  transfers between devices with their start and end apart: 10 -> 12, of which waited for: 10 -> 10; matrix products, arithmetic and copies ran while one was open for 4% -> 5% of each run, Pallas kernels for 0% -> 0%
where the time goes in v1:
time: 256 us; the launch traced here: 253 us
  waiting for transfers between devices  114 us (45%)
  local copies, waits for them, and re-layouts  40.5 us (16%)
  starting transfers between devices  40.2 us (16%)
  Pallas kernels  32.6 us (13%)
  matrix products  13.9 us (5%)
  other arithmetic  11.8 us (5%)
    ppermute x6, waiting for transfers between devices, passed_along(): lax.ppermute(value, axis, [(source, source + steps) for source in range(f...  87.3 us
    ppermute x6, starting transfers between devices, passed_along(): lax.ppermute(value, axis, [(source, source + steps) for source in range(f...  33.5 us
    pallas_call x1, Pallas kernels, fine_attention(): pl.pallas_call(kernel, grid=(pairs, nq), in_specs=[pl.BlockSpec((tile, 1)...  32.6 us
    ppermute x6, waiting for transfers between devices, within_group(): return lax.ppermute(value, axis, pairs)  26.4 us
    unnamed x22, local copies, waits for them, and re-layouts  13.2 us
    sub x1, matrix products, one_group(): weights = jnp.where(allowed[None], jnp.exp(masked - row_top), 0.0)  7.46 us
    ppermute x6, starting transfers between devices, within_group(): return lax.ppermute(value, axis, pairs)  6.74 us
  transfers between devices with their start and end apart: 12, of which 10 were waited for; matrix products, arithmetic and copies ran while one was open for 5% of the time, Pallas kernels for 0%

profile of v1, /device:TPU:7, one launch (start us, length us, event | category | flops | bytes accessed | tf_op | source)
XLA Modules:
  0.0 252.9 jit_solution(10794694520936407406)
XLA Ops:
  0.0 4.8 %copy.8 = bf16[512,3,1024]{0,2,1:T(8,128)(2,1)} copy(bf16[512,3,1024]{2,0,1:T(8,128)(2,1)} %param.4) | data formatting | bytes 6291456 | tf_op args[0]
  4.8 4.7 %copy.11.q_ref.k2_ref.v2_ref = bf16[512,3072]{1,0:T(8,128)(2,1)} copy(bf16[512,3072]{0,1:T(8,128)(2,1)} %bitcast.54) | data formatting | bytes 6291456 | tf_op jit(solution)/shard_map/reshape | solution.py:155
  9.5 3.3 %slice.28 = bf16[512,2048]{1,0:T(8,128)(2,1)} slice(bf16[512,3072]{1,0:T(8,128)(2,1)} %copy.11.q_ref.k2_ref.v2_ref), slice={[0:512], [1024:3072]} | slice | bytes 4194304 | tf_op jit(solution)/shard_map/slice | solution.py:156
  12.8 3.1 %collective-permute-start = (bf16[512,2048]{1,0:T(8,128)(2,1)}, bf16[512,2048]{1,0:T(8,128)(2,1)}, u32[]{:S(2)}, u32[]{:S(2)}) collective-permute-start(bf16[512,2048]{1,0:T(8,128)(2,1)} %slice.28), channel_id=1, source_target_pairs={{0,2},{1,3},{2,4},{3,5},{4,6},{5,7},{6,8},{7,9},{8,10},{9,11},{10,... | collective-permute-start | bytes 6291464 | tf_op jit(solution)/shard_map/ppermute | solution.py:23
  15.9 4.0 %collective-permute-start.1 = (bf16[512,2048]{1,0:T(8,128)(2,1)}, bf16[512,2048]{1,0:T(8,128)(2,1)}, u32[]{:S(2)}, u32[]{:S(2)}) collective-permute-start(bf16[512,2048]{1,0:T(8,128)(2,1)} %slice.28), channel_id=1, source_target_pairs={{0,1},{1,2},{2,3},{3,4},{4,5},{5,6},{6,7},{7,8},{8,9},{9,10},{10,1... | collective-permute-start | bytes 6291464 | tf_op jit(solution)/shard_map/ppermute | solution.py:23
  21.9 39.6 %collective-permute-done.k0_ref.v0_ref = bf16[512,2048]{1,0:T(8,128)(2,1)} collective-permute-done((bf16[512,2048]{1,0:T(8,128)(2,1)}, bf16[512,2048]{1,0:T(8,128)(2,1)}, u32[]{:S(2)}, u32[]{:S(2)}) %collective-permute-start) | collective-permute-done | bytes 2097184 | tf_op jit(solution)/shard_map/ppermute | solution.py:23
  61.5 22.7 %collective-permute-done.1.k1_ref.v1_ref = bf16[512,2048]{1,0:T(8,128)(2,1)} collective-permute-done((bf16[512,2048]{1,0:T(8,128)(2,1)}, bf16[512,2048]{1,0:T(8,128)(2,1)}, u32[]{:S(2)}, u32[]{:S(2)}) %collective-permute-start.1) | collective-permute-done | bytes 2097184 | tf_op jit(solution)/shard_map/ppermute | solution.py:23
  84.1 32.6 %shard_map.46 = bf16[512,1024]{1,0:T(8,128)(2,1)} custom-call(s32[512,1]{1,0:T(8,128)} %reshape_reshape.8.qclip_ref, s32[1,1536]{1,0:T(1,128)} %reshape_reshape.7.kclip0_ref.kclip1_ref.kclip2_ref, s32[1,1536]{1,0:T(1,128)} %reshape_reshape.7.kclip0_ref.kclip1_ref.kclip2_ref, s32[1,1536]{1,0:T(1,128)} %reshape_reshape.7.kclip0_ref.kclip1_ref.kclip2_ref, ...), custom_call_target="tpu_custom_call" | custom-call | tf_op jit(solution)/shard_map/pallas_call | solution.py:94
  116.7 2.7 %reshape.120 = f32[128,4,1024]{2,1,0:T(4,128)} reshape(bf16[512,1024]{1,0:T(8,128)(2,1)} %shard_map.46) | data formatting | bytes 3145728 | tf_op jit(solution)/shard_map/reshape | solution.py:222
  119.4 2.9 %reduce_sum.19 = f32[128,1024]{1,0:T(8,128)S(1)} reduce(f32[128,4,1024]{2,1,0:T(4,128)} %reshape.120, f32[]{:T(128)} %constant.107.clone.1), dimensions={1}, to_apply=%region_0.1 | reduce | flops 393216 | bytes 2621444 | tf_op jit(solution)/shard_map/reduce_sum | solution.py:170
  124.4 2.7 %constant_dynamic-slice_fusion = bf16[1024,3,256]{2,0,1:T(8,128)(2,1)} fusion(bf16[1024,3,1024]{2,0,1:T(8,128)(2,1)} %param.6, s32[]{:T(128)S(6)} %select_n.90), kind=kLoop, calls=%fused_computation.44 | loop fusion | bytes 3145732 | tf_op jit(solution)/shard_map/dynamic_slice | solution.py:177
  127.2 2.6 %copy.21 = bf16[1024,3,256]{0,2,1:T(8,128)(2,1)} copy(bf16[1024,3,256]{2,0,1:T(8,128)(2,1)} %constant_dynamic-slice_fusion) | data formatting | bytes 3145728
  129.8 1.6 collective-permute-start.4
  132.1 2.9 %collective-permute-done.3 = bf16[128,1024]{1,0:T(8,128)(2,1)S(1)} collective-permute-done((bf16[128,1024]{1,0:T(8,128)(2,1)S(1)}, bf16[128,1024]{1,0:T(8,128)(2,1)S(1)}, u32[]{:S(2)}, u32[]{:S(2)}) %collective-permute-start.3) | collective-permute-done | bytes 262176 | tf_op jit(solution)/shard_map/ppermute | solution.py:32
  141.3 1.9 convolution_convert_fusion
  144.7 6.9 %collective-permute-start.5 = (bf16[512,2,256]{0,2,1:T(8,128)(2,1)S(1)}, bf16[512,2,256]{0,2,1:T(8,128)(2,1)}, u32[]{:S(2)}, u32[]{:S(2)}) collective-permute-start(bf16[512,2,256]{0,2,1:T(8,128)(2,1)S(1)} %slice.29), channel_id=1, source_target_pairs={{0,12},{1,13},{2,14},{3,15},{16,28},{17,29},{18,30},{19,31}} | collective-permute-start | bytes 1572872 | tf_op jit(solution)/shard_map/ppermute | solution.py:23
  151.6 2.1 collective-permute-start.6
  153.7 2.2 collective-permute-start.7
  156.0 2.0 fusion.6
  158.8 1.9 collective-permute-done.5
  160.7 11.2 %collective-permute-done.6 = bf16[512,2,256]{0,2,1:T(8,128)(2,1)} collective-permute-done((bf16[512,2,256]{0,2,1:T(8,128)(2,1)S(1)}, bf16[512,2,256]{0,2,1:T(8,128)(2,1)}, u32[]{:S(2)}, u32[]{:S(2)}) %collective-permute-start.6) | collective-permute-done | bytes 524320 | tf_op jit(solution)/shard_map/ppermute | solution.py:23
  171.9 11.2 %collective-permute-done.7 = bf16[512,2,256]{0,2,1:T(8,128)(2,1)} collective-permute-done((bf16[512,2,256]{0,2,1:T(8,128)(2,1)S(1)}, bf16[512,2,256]{0,2,1:T(8,128)(2,1)}, u32[]{:S(2)}, u32[]{:S(2)}) %collective-permute-start.7) | collective-permute-done | bytes 524320 | tf_op jit(solution)/shard_map/ppermute | solution.py:23
  183.1 1.6 pad_maximum_fusion
  186.4 7.5 %fusion.32 = (f32[2,512]{1,0:T(2,128)S(1)}, bf16[2,512,2048]{2,1,0:T(8,128)(2,1)}) fusion(pred[512,2048]{1,0:T(8,128)(4,1)S(1)} %copy-done.4, bf16[512,2,128]{0,2,1:T(8,128)(2,1)S(1)} %bitcast.62, bf16[2048,2,128]{0,2,1:T(8,128)(2,1)} %bitcast.61), kind=kOutput, calls=%fused_computation.51 | convolution fusion | flops 549455872 | bytes 6557696 | tf_op jit(solution)/shard_map/while/body/eval_jaxpr/sub | solution.py:131
  193.8 4.0 %fusion.14 = bf16[512,2,128]{0,2,1:T(8,128)(2,1)S(1)} fusion(bf16[2048,2,128]{0,2,1:T(8,128)(2,1)} %bitcast.60, bf16[2,512,2048]{2,1,0:T(8,128)(2,1)} %get-tuple-element.33, f32[512,2]{0,1:T(2,128)S(1)} %bitcast.63), kind=kOutput, calls=%fused_computation.16 | convolution fusion | flops 537133056 | bytes 5509120 | tf_op jit(solution)/shard_map/while/body/eval_jaxpr/hrk,khd->rhd/dot_general | solution.py:133
  200.9 2.4 collective-permute-start.10
  204.6 11.1 %collective-permute-done.10 = f32[128,1024]{1,0:T(8,128)S(1)} collective-permute-done((f32[128,1024]{1,0:T(8,128)}, f32[128,1024]{1,0:T(8,128)S(1)}, u32[]{:S(2)}, u32[]{:S(2)}) %collective-permute-start.10) | collective-permute-done | bytes 524320 | tf_op jit(solution)/shard_map/ppermute | solution.py:32
  215.7 11.8 %collective-permute-done.9 = f32[128,1024]{1,0:T(8,128)} collective-permute-done((f32[128,1024]{1,0:T(8,128)S(1)}, f32[128,1024]{1,0:T(8,128)}, u32[]{:S(2)}, u32[]{:S(2)}) %collective-permute-start.9) | collective-permute-done | bytes 524320 | tf_op jit(solution)/shard_map/ppermute | solution.py:32
  229.0 15.1 %collective-permute-start.11 = (bf16[1,1024]{1,0:T(2,128)(2,1)S(1)}, bf16[1,1024]{1,0:T(2,128)(2,1)S(1)}, u32[]{:S(2)}, u32[]{:S(2)}) collective-permute-start(bf16[1,1024]{1,0:T(2,128)(2,1)S(1)} %slice.33), channel_id=1, source_target_pairs={{0,1},{1,2},{2,3},{3,4},{4,5},{5,6},{6,7},{7,8},{8,9},{9,10},{10,1... | collective-permute-start | bytes 6152 | tf_op jit(solution)/shard_map/ppermute | solution.py:23
  245.0 1.9 add.125
  246.9 3.0 %add.126 = f32[512,1024]{1,0:T(8,128)} reshape(f32[128,4,1024]{2,1,0:T(4,128)} %add.125) | data formatting | bytes 4194304 | tf_op jit(solution)/shard_map/add | solution.py:222
  250.0 2.9 %add_convert_fusion = bf16[512,1024]{1,0:T(8,128)(2,1)} fusion(f32[512,1024]{1,0:T(8,128)} %add.126, bf16[512,1024]{1,0:T(8,128)(2,1)S(1)} %copy-done.1), kind=kLoop, calls=%fused_computation.12 | loop fusion | flops 1572864 | bytes 4194304 | tf_op jit(solution)/shard_map/convert_element_type | solution.py:224
  (50 shorter events, 21.8 us)
Async XLA Ops:
  0.0 198.0 %copy-start = (bf16[1024,1024]{1,0:T(8,128)(2,1)S(1)}, bf16[1024,1024]{1,0:T(8,128)(2,1)}, u32[]{:S(2)}) copy-start(bf16[1024,1024]{1,0:T(8,128)(2,1)} %param.7) | copy-start | bytes 6291460
  9.5 10.4 %copy-start.6 = (s32[2048]{0:T(1024)S(1)}, s32[2048]{0:T(1024)}, u32[]{:S(2)}) copy-start(s32[2048]{0:T(1024)} %param.5) | copy-start | bytes 24580
  12.8 48.7 %collective-permute-start = (bf16[512,2048]{1,0:T(8,128)(2,1)}, bf16[512,2048]{1,0:T(8,128)(2,1)}, u32[]{:S(2)}, u32[]{:S(2)}) collective-permute-start(bf16[512,2048]{1,0:T(8,128)(2,1)} %slice.28), channel_id=1, source_target_pairs={{0,2},{1,3},{2,4},{3,5},{4,6},{5,7},{6,8},{7,9},{8,10},{9,11},{10,... | collective-permute-start | bytes 6291464 | tf_op jit(solution)/shard_map/ppermute | solution.py:23
  15.9 68.2 %collective-permute-start.1 = (bf16[512,2048]{1,0:T(8,128)(2,1)}, bf16[512,2048]{1,0:T(8,128)(2,1)}, u32[]{:S(2)}, u32[]{:S(2)}) collective-permute-start(bf16[512,2048]{1,0:T(8,128)(2,1)} %slice.28), channel_id=1, source_target_pairs={{0,1},{1,2},{2,3},{3,4},{4,5},{5,6},{6,7},{7,8},{8,9},{9,10},{10,1... | collective-permute-start | bytes 6291464 | tf_op jit(solution)/shard_map/ppermute | solution.py:23
  123.0 8.4 %collective-permute-start.2 = (bf16[128,1024]{1,0:T(8,128)(2,1)S(1)}, bf16[128,1024]{1,0:T(8,128)(2,1)S(1)}, u32[]{:S(2)}, u32[]{:S(2)}) collective-permute-start(bf16[128,1024]{1,0:T(8,128)(2,1)S(1)} %get-tuple-element.24), channel_id=1, source_target_pairs={{0,3},{1,0},{2,1},{3,2},{4,7},{5,4},{6,5},{7,6},{8,11},{9,8},{10,9... | collective-permute-start | bytes 786440 | tf_op jit(solution)/shard_map/ppermute | solution.py:32
  127.1 7.9 %collective-permute-start.3 = (bf16[128,1024]{1,0:T(8,128)(2,1)S(1)}, bf16[128,1024]{1,0:T(8,128)(2,1)S(1)}, u32[]{:S(2)}, u32[]{:S(2)}) collective-permute-start(bf16[128,1024]{1,0:T(8,128)(2,1)S(1)} %get-tuple-element.24), channel_id=1, source_target_pairs={{0,2},{1,3},{2,0},{3,1},{4,6},{5,7},{6,4},{7,5},{8,10},{9,11},{10,... | collective-permute-start | bytes 786440 | tf_op jit(solution)/shard_map/ppermute | solution.py:32
  129.8 6.6 %collective-permute-start.4 = (bf16[128,1024]{1,0:T(8,128)(2,1)S(1)}, bf16[128,1024]{1,0:T(8,128)(2,1)S(1)}, u32[]{:S(2)}, u32[]{:S(2)}) collective-permute-start(bf16[128,1024]{1,0:T(8,128)(2,1)S(1)} %get-tuple-element.24), channel_id=1, source_target_pairs={{0,1},{1,2},{2,3},{3,0},{4,5},{5,6},{6,7},{7,4},{8,9},{9,10},{10,1... | collective-permute-start | bytes 786440 | tf_op jit(solution)/shard_map/ppermute | solution.py:32
  137.1 4.3 %copy-start.3 = (bf16[1024,3,256]{0,2,1:T(8,128)(2,1)S(1)}, bf16[1024,3,256]{0,2,1:T(8,128)(2,1)}, u32[]{:S(2)}) copy-start(bf16[1024,3,256]{0,2,1:T(8,128)(2,1)} %copy.21) | copy-start | bytes 4718596
  144.7 15.9 %collective-permute-start.5 = (bf16[512,2,256]{0,2,1:T(8,128)(2,1)S(1)}, bf16[512,2,256]{0,2,1:T(8,128)(2,1)}, u32[]{:S(2)}, u32[]{:S(2)}) collective-permute-start(bf16[512,2,256]{0,2,1:T(8,128)(2,1)S(1)} %slice.29), channel_id=1, source_target_pairs={{0,12},{1,13},{2,14},{3,15},{16,28},{17,29},{18,30},{19,31}} | collective-permute-start | bytes 1572872 | tf_op jit(solution)/shard_map/ppermute | solution.py:23
  151.6 20.3 %collective-permute-start.6 = (bf16[512,2,256]{0,2,1:T(8,128)(2,1)S(1)}, bf16[512,2,256]{0,2,1:T(8,128)(2,1)}, u32[]{:S(2)}, u32[]{:S(2)}) collective-permute-start(bf16[512,2,256]{0,2,1:T(8,128)(2,1)S(1)} %slice.29), channel_id=1, source_target_pairs={{0,8},{1,9},{2,10},{3,11},{4,12},{5,13},{6,14},{7,15},{16,24},{17,... | collective-permute-start | bytes 1572872 | tf_op jit(solution)/shard_map/ppermute | solution.py:23
  153.7 29.4 %collective-permute-start.7 = (bf16[512,2,256]{0,2,1:T(8,128)(2,1)S(1)}, bf16[512,2,256]{0,2,1:T(8,128)(2,1)}, u32[]{:S(2)}, u32[]{:S(2)}) collective-permute-start(bf16[512,2,256]{0,2,1:T(8,128)(2,1)S(1)} %slice.29), channel_id=1, source_target_pairs={{0,4},{1,5},{2,6},{3,7},{4,8},{5,9},{6,10},{7,11},{8,12},{9,13},{1... | collective-permute-start | bytes 1572872 | tf_op jit(solution)/shard_map/ppermute | solution.py:23
  184.8 1.6 copy-start.4
  184.8 1.6 copy-start.5
  198.4 1.3 copy-start.2
  200.9 14.8 %collective-permute-start.10 = (f32[128,1024]{1,0:T(8,128)}, f32[128,1024]{1,0:T(8,128)S(1)}, u32[]{:S(2)}, u32[]{:S(2)}) collective-permute-start(f32[128,1024]{1,0:T(8,128)} %get-tuple-element.28), channel_id=1, source_target_pairs={{0,3},{1,0},{2,1},{3,2},{4,7},{5,4},{6,5},{7,6},{8,11},{9,8},{10,9... | collective-permute-start | bytes 1572872 | tf_op jit(solution)/shard_map/ppermute | solution.py:32
  203.3 12.5 %collective-permute-start.8 = (f32[128,1024]{1,0:T(8,128)}, f32[128,1024]{1,0:T(8,128)}, u32[]{:S(2)}, u32[]{:S(2)}) collective-permute-start(f32[128,1024]{1,0:T(8,128)} %get-tuple-element.26), channel_id=1, source_target_pairs={{0,1},{1,2},{2,3},{3,0},{4,5},{5,6},{6,7},{7,4},{8,9},{9,10},{10,1... | collective-permute-start | bytes 1572872 | tf_op jit(solution)/shard_map/ppermute | solution.py:32
  203.5 24.0 %collective-permute-start.9 = (f32[128,1024]{1,0:T(8,128)S(1)}, f32[128,1024]{1,0:T(8,128)}, u32[]{:S(2)}, u32[]{:S(2)}) collective-permute-start(f32[128,1024]{1,0:T(8,128)S(1)} %get-tuple-element.29), channel_id=1, source_target_pairs={{0,2},{1,3},{2,0},{3,1},{4,6},{5,7},{6,4},{7,5},{8,10},{9,11},{10,... | collective-permute-start | bytes 1572872 | tf_op jit(solution)/shard_map/ppermute | solution.py:32
  229.0 15.8 %collective-permute-start.11 = (bf16[1,1024]{1,0:T(2,128)(2,1)S(1)}, bf16[1,1024]{1,0:T(2,128)(2,1)S(1)}, u32[]{:S(2)}, u32[]{:S(2)}) collective-permute-start(bf16[1,1024]{1,0:T(2,128)(2,1)S(1)} %slice.33), channel_id=1, source_target_pairs={{0,1},{1,2},{2,3},{3,4},{4,5},{5,6},{6,7},{7,8},{8,9},{9,10},{10,1... | collective-permute-start | bytes 6152 | tf_op jit(solution)/shard_map/ppermute | solution.py:23
  246.9 3.1 %copy-start.1 = (bf16[512,1024]{1,0:T(8,128)(2,1)S(1)}, bf16[512,1024]{1,0:T(8,128)(2,1)}, u32[]{:S(2)}) copy-start(bf16[512,1024]{1,0:T(8,128)(2,1)} %shard_map.46) | copy-start | bytes 3145732

commit v2 on v1

--- a/solution.py
+++ b/solution.py
@@ -33,18 +33,19 @@
 
 
 def fine_kernel(qclip_ref, kclip0_ref, kclip1_ref, kclip2_ref, q_ref,
-                k0_ref, v0_ref, k1_ref, v1_ref, k2_ref, v2_ref, out_ref, *, scale):
+                k0_ref, v0_ref, k1_ref, v1_ref, k1b_ref, v1b_ref, k2_ref, v2_ref,
+                out_ref, pool_ref, *, scale):
     tile = q_ref.shape[0]
     width = q_ref.shape[1]
     half = width // 2
-    q = q_ref[...]
+    q = q_ref[...] * jnp.asarray(scale, q_ref.dtype)
     lane = lax.broadcasted_iota(jnp.int32, (1, width), 1)
     low = lane < half
     zero = jnp.zeros_like(q)
     head_q = (jnp.where(low, q, zero), jnp.where(low, zero, q))
     qclip = qclip_ref[...]
-    keys = (k0_ref, k1_ref, k2_ref)
-    values = (v0_ref, v1_ref, v2_ref)
+    keys = (k0_ref[...], k1_ref[...] + k1b_ref[...], k2_ref[...])
+    values = (v0_ref[...], v1_ref[...] + v1b_ref[...], v2_ref[...])
     clips = (kclip0_ref, kclip1_ref, kclip2_ref)
     seg = k0_ref.shape[0]
     qpos = pl.program_id(1) * tile + lax.broadcasted_iota(jnp.int32, (tile, seg), 0)
@@ -59,8 +60,8 @@
     for h in range(2):
         scores = []
         for j in range(3):
-            s = lax.dot_general(head_q[h], keys[j][...], (((1,), (1,)), ((), ())),
-                                preferred_element_type=jnp.float32) * scale
+            s = lax.dot_general(head_q[h], keys[j], (((1,), (1,)), ((), ())),
+                                preferred_element_type=jnp.float32)
             scores.append(jnp.where(masks[j], s, -1e30))
         top = jnp.max(scores[0], axis=1, keepdims=True)
         for j in range(1, 3):
@@ -68,29 +69,33 @@
         total = None
         summed = None
         for j in range(3):
-            w = jnp.where(masks[j], jnp.exp(scores[j] - top), 0.0)
+            w = jnp.exp(scores[j] - top)
             part = jnp.sum(w, axis=1, keepdims=True)
-            pv = jnp.dot(w.astype(jnp.bfloat16), values[j][...], preferred_element_type=jnp.float32)
+            pv = jnp.dot(w.astype(jnp.bfloat16), values[j], preferred_element_type=jnp.float32)
             total = part if total is None else total + part
             summed = pv if summed is None else summed + pv
         results.append(summed / total)
-    out_ref[...] = jnp.where(low, results[0], results[1]).astype(out_ref.dtype)
-
-
-def fine_attention(qkv_flat, prev0, prev1, qclip, kclip, heads):
-    tok, width3 = qkv_flat.shape
-    width = width3 // 3
+    out = jnp.where(low, results[0], results[1]).astype(out_ref.dtype)
+    out_ref[...] = out
+    rows = tile // POOL
+    pool_row = lax.broadcasted_iota(jnp.int32, (rows, tile), 0)
+    pool_col = lax.broadcasted_iota(jnp.int32, (rows, tile), 1)
+    pool_mat = jnp.where(pool_col // POOL == pool_row, 1.0 / POOL, 0.0).astype(jnp.bfloat16)
+    pool_ref[...] = jnp.dot(pool_mat, out, preferred_element_type=jnp.float32).astype(pool_ref.dtype)
+
+
+def fine_attention(planes, prev0, prev1a, prev1b, qclip, kclip, heads):
+    _, tok, width = planes.shape
     head_dim = width // heads
     pair = 2 * head_dim
     pairs = width // pair
     tile = min(FINE_TILE, tok)
     nq = tok // tile
     kernel = functools.partial(fine_kernel, scale=1.0 / math.sqrt(head_dim))
-    qspec = pl.BlockSpec((tile, pair), lambda h, i: (i, h))
-    own_k = pl.BlockSpec((tok, pair), lambda h, i: (0, pairs + h))
-    own_v = pl.BlockSpec((tok, pair), lambda h, i: (0, 2 * pairs + h))
-    prev_k = pl.BlockSpec((tok, pair), lambda h, i: (0, h))
-    prev_v = pl.BlockSpec((tok, pair), lambda h, i: (0, pairs + h))
+
+    def plane_spec(plane):
+        return pl.BlockSpec((None, tok, pair), lambda h, i: (plane, 0, h))
+
     return pl.pallas_call(
         kernel,
         grid=(pairs, nq),
@@ -99,11 +104,54 @@
             pl.BlockSpec((1, tok), lambda h, i: (0, 0)),
             pl.BlockSpec((1, tok), lambda h, i: (0, 1)),
             pl.BlockSpec((1, tok), lambda h, i: (0, 2)),
-            qspec, prev_k, prev_v, prev_k, prev_v, own_k, own_v,
-        ],
-        out_specs=pl.BlockSpec((tile, pair), lambda h, i: (i, h)),
-        out_shape=jax.ShapeDtypeStruct((tok, width), jnp.bfloat16),
-    )(qclip, kclip, kclip, kclip, qkv_flat, prev0, prev0, prev1, prev1, qkv_flat, qkv_flat)
+            pl.BlockSpec((None, tile, pair), lambda h, i: (0, i, h)),
+            plane_spec(0), plane_spec(1),
+            plane_spec(0), plane_spec(1),
+            plane_spec(0), plane_spec(1),
+            plane_spec(1), plane_spec(2),
+        ],
+        out_specs=[
+            pl.BlockSpec((tile, pair), lambda h, i: (i, h)),
+            pl.BlockSpec((tile // POOL, pair), lambda h, i: (i, h)),
+        ],
+        out_shape=[
+            jax.ShapeDtypeStruct((tok, width), jnp.bfloat16),
+            jax.ShapeDtypeStruct((tok // POOL, width), jnp.bfloat16),
+        ],
+    )(qclip, kclip, kclip, kclip, planes, prev0, prev0, prev1a, prev1a, prev1b, prev1b,
+      planes, planes)
+
+
+def mix_kernel(fine_ref, lift_ref, out_ref):
+    tile = fine_ref.shape[0]
+    rows = lift_ref.shape[0]
+    spread_row = lax.broadcasted_iota(jnp.int32, (tile, rows), 0)
+    spread_col = lax.broadcasted_iota(jnp.int32, (tile, rows), 1)
+    spread = jnp.where(spread_row // POOL == spread_col, 1.0, 0.0).astype(jnp.bfloat16)
+    lifted = jnp.dot(spread, lift_ref[...], preferred_element_type=jnp.float32)
+    out_ref[...] = (fine_ref[...].astype(jnp.float32) + lifted).astype(out_ref.dtype)
+
+
+def mix(fine_out, lifted):
+    tok, width = fine_out.shape
+    tile = min(FINE_TILE, tok)
+    return pl.pallas_call(
+        mix_kernel,
+        grid=(tok // tile,),
+        in_specs=[
+            pl.BlockSpec((tile, width), lambda i: (i, 0)),
+            pl.BlockSpec((tile // POOL, width), lambda i: (i, 0)),
+        ],
+        out_specs=pl.BlockSpec((tile, width), lambda i: (i, 0)),
+        out_shape=jax.ShapeDtypeStruct((tok, width), fine_out.dtype),
+    )(fine_out, lifted)
+
+
+def pair_swap(value, axis, from_odd):
+    count = lax.axis_size(axis)
+    start = 1 if from_odd else 0
+    step = -1 if from_odd else 1
+    return lax.ppermute(value, axis, [(source, source + step) for source in range(start, count, 2)])
 
 
 def attend(queries, key_rows, value_rows, allowed, heads, head_groups):
@@ -152,10 +200,11 @@
     position = lax.axis_index("seq")
     quarter = position % QUARTERS
     cycle_place = position // QUARTERS
-    qkv_flat = fine_qkv.reshape(tok_count, 3 * feat_width)
-    own_pairs = qkv_flat[:, feat_width:]
-    prev1 = passed_along(own_pairs, "seq", 1)
+    planes = jnp.transpose(fine_qkv, (1, 0, 2))
+    own_pairs = planes[1:]
     prev0 = passed_along(own_pairs, "seq", 2)
+    prev1a = pair_swap(own_pairs, "seq", False)
+    prev1b = pair_swap(prev0, "seq", True)
     clip_front = jnp.concatenate([jnp.full((FREACH * coarse_rows,), -1, jnp.int32), clip_ids])
     key_clip = jnp.repeat(
         lax.dynamic_slice_in_dim(clip_front, position * coarse_rows, (FREACH + 1) * coarse_rows, 0),
@@ -163,13 +212,10 @@
     )
     own_clip = lax.dynamic_slice_in_dim(clip_ids, position * coarse_rows, coarse_rows, 0)
     query_clip = jnp.repeat(own_clip, POOL)
-    fine_out = fine_attention(
-        qkv_flat, prev0, prev1, query_clip.reshape(tok_count, 1),
+    fine_out, pooled = fine_attention(
+        planes, prev0, prev1a, prev1b, query_clip.reshape(tok_count, 1),
         key_clip.reshape(1, (FREACH + 1) * tok_count), FHEADS,
     )
-    pooled = jnp.mean(
-        fine_out.astype(jnp.float32).reshape(coarse_rows, POOL, feat_width), axis=1
-    ).astype(jnp.bfloat16)
     received = [pooled] + [within_group(pooled, "seq", shift) for shift in range(1, QUARTERS)]
     from_next = jnp.stack([received[0]] + received[:0:-1], axis=0)
     gathered = jnp.roll(from_next, quarter, axis=0).reshape(group_rows, feat_width)
@@ -217,11 +263,8 @@
     clip_before = jnp.concatenate([jnp.full((1,), -1, jnp.int32), clip_ids])
     prev_clip = lax.dynamic_slice_in_dim(clip_before, position * coarse_rows, coarse_rows, 0)
     joined = prev_clip == own_clip
-    lifted = jnp.where(joined[:, None], previous.astype(jnp.float32), 0.0)
-    mixed_rows = (
-        fine_out.astype(jnp.float32).reshape(coarse_rows, POOL, feat_width) + lifted[:, None, :]
-    )
-    return mixed_rows.reshape(tok_count, feat_width).astype(jnp.bfloat16)
+    lifted = jnp.where(joined[:, None], previous, jnp.zeros_like(previous))
+    return mix(fine_out, lifted)
 
 
 def solution(mesh):

time: 256 us -> 214 us (0.84)
  local copies, waits for them, and re-layouts: 40.5 us -> 18.3 us
  waiting for transfers between devices: 114 us -> 96.3 us
  other arithmetic: 11.8 us -> 5.98 us
  starting transfers between devices: 40.2 us -> 44 us
    ppermute x6 -> x5, waiting for transfers between devices: 87.3 us -> 67.3 us  [passed_along(): lax.ppermute(value, axis, [(source, source + steps) for source in range(f...]
    unnamed x22, local copies, waits for them, and re-layouts: 13.2 us -> 5.28 us
    reshape x2 -> x0, local copies, waits for them, and re-layouts: 7.38 us -> none  [the longest x1 4.67 us: body(): qkv_flat = fine_qkv.reshape(tok_count, 3 * feat_width)]
    ppermute x0 -> x2, starting transfers between devices: none -> 6.1 us  [pair_swap(): lax.ppermute(value, axis, [(source, source + step) for source in range(st...]
    add x2 -> x0, local copies, waits for them, and re-layouts: 4.98 us -> none  [body(): fine_out.astype(jnp.float32).reshape(coarse_rows, POOL, feat_width)]
    convert_element_type x1 -> x0, other arithmetic: 2.91 us -> none  [body(): return mixed_rows.reshape(tok_count, feat_width).astype(jnp.bfloat16)]
    reduce_sum x1 -> x0, other arithmetic: 2.86 us -> none  [body(): jnp.mean(fine_out.astype(jnp.float32).reshape(coarse_rows, POOL, feat_wid...]
    ppermute x6, waiting for transfers between devices: 26.4 us -> 29 us  [within_group(): return lax.ppermute(value, axis, pairs)]
  transfers between devices with their start and end apart: 12 -> 13, of which waited for: 10 -> 10; matrix products, arithmetic and copies ran while one was open for 5% -> 5% of each run, Pallas kernels for 0% -> 0%
where the time goes in v2:
time: 214 us; the launch traced here: 211 us
  waiting for transfers between devices  96.3 us (45%)
  starting transfers between devices  44 us (21%)
  Pallas kernels  32.3 us (15%)
  local copies, waits for them, and re-layouts  18.3 us (9%)
  matrix products  13.9 us (6%)
  other arithmetic  5.98 us (3%)
    ppermute x5, waiting for transfers between devices, passed_along(): lax.ppermute(value, axis, [(source, source + steps) for source in range(f...  67.3 us
    ppermute x5, starting transfers between devices, passed_along(): lax.ppermute(value, axis, [(source, source + steps) for source in range(f...  32 us
    pallas_call x1, Pallas kernels, fine_attention(): pl.pallas_call(kernel, grid=(pairs, nq), in_specs=[pl.BlockSpec((tile, 1)...  29.9 us
    ppermute x6, waiting for transfers between devices, within_group(): return lax.ppermute(value, axis, pairs)  29 us
    sub x1, matrix products, one_group(): weights = jnp.where(allowed[None], jnp.exp(masked - row_top), 0.0)  7.46 us
    ppermute x2, starting transfers between devices, pair_swap(): lax.ppermute(value, axis, [(source, source + step) for source in range(st...  6.1 us
    ppermute x6, starting transfers between devices, within_group(): return lax.ppermute(value, axis, pairs)  5.86 us
    unnamed x22, local copies, waits for them, and re-layouts  5.28 us
  transfers between devices with their start and end apart: 13, of which 10 were waited for; matrix products, arithmetic and copies ran while one was open for 5% of the time, Pallas kernels for 0%

profile of v2, /device:TPU:7, one launch (start us, length us, event | category | flops | bytes accessed | tf_op | source)
XLA Modules:
  0.0 211.0 jit_solution(15660896553569695404)
XLA Ops:
  0.0 3.3 %slice.28 = bf16[2,512,1024]{2,1,0:T(8,128)(2,1)} slice(bf16[3,512,1024]{2,1,0:T(8,128)(2,1)} %bitcast.54), slice={[1:3], [0:512], [0:1024]} | slice | bytes 4194304 | tf_op jit(solution)/shard_map/slice | solution.py:204
  3.3 3.1 %collective-permute-start = (bf16[2,512,1024]{2,1,0:T(8,128)(2,1)}, bf16[2,512,1024]{2,1,0:T(8,128)(2,1)}, u32[]{:S(2)}, u32[]{:S(2)}) collective-permute-start(bf16[2,512,1024]{2,1,0:T(8,128)(2,1)} %slice.28), channel_id=1, source_target_pairs={{0,2},{1,3},{2,4},{3,5},{4,6},{5,7},{6,8},{7,9},{8,10},{9,11},{10,... | collective-permute-start | bytes 6291464 | tf_op jit(solution)/shard_map/ppermute | solution.py:23
  6.4 1.3 collective-permute-start.1
  7.7 44.3 %collective-permute-done.k0_ref.v0_ref = bf16[2,512,1024]{2,1,0:T(8,128)(2,1)} collective-permute-done((bf16[2,512,1024]{2,1,0:T(8,128)(2,1)}, bf16[2,512,1024]{2,1,0:T(8,128)(2,1)}, u32[]{:S(2)}, u32[]{:S(2)}) %collective-permute-start) | collective-permute-done | bytes 2097184 | tf_op jit(solution)/shard_map/ppermute | solution.py:23
  52.0 4.8 %collective-permute-start.2 = (bf16[2,512,1024]{2,1,0:T(8,128)(2,1)}, bf16[2,512,1024]{2,1,0:T(8,128)(2,1)}, u32[]{:S(2)}, u32[]{:S(2)}) collective-permute-start(bf16[2,512,1024]{2,1,0:T(8,128)(2,1)} %collective-permute-done.k0_ref.v0_ref), channel_id=1, source_target_pairs={{1,0},{3,2},{5,4},{7,6},{9,8},{11,10},{13,12},{15,14},{17,16},{19,... | collective-permute-start | bytes 6291464 | tf_op jit(solution)/shard_map/ppermute | solution.py:154
  58.7 2.7 %constant_dynamic-slice_fusion = bf16[1024,3,256]{2,0,1:T(8,128)(2,1)} fusion(bf16[1024,3,1024]{2,0,1:T(8,128)(2,1)} %param.6, s32[]{:T(128)S(6)} %select_n.86), kind=kLoop, calls=%fused_computation.42 | loop fusion | bytes 3145732 | tf_op jit(solution)/shard_map/dynamic_slice | solution.py:223
  61.5 29.9 %shard_map.46 = (bf16[512,1024]{1,0:T(8,128)(2,1)}, bf16[128,1024]{1,0:T(8,128)(2,1)}) custom-call(s32[512,1]{1,0:T(8,128)} %reshape_reshape.8.qclip_ref, s32[1,1536]{1,0:T(1,128)} %reshape_reshape.7.kclip0_ref.kclip1_ref.kclip2_ref, s32[1,1536]{1,0:T(1,128)} %reshape_reshape.7.kclip0_ref.kclip1_ref.kclip2_ref, ...), custom_call_target="tpu_custom_call" | custom-call | tf_op jit(solution)/shard_map/pallas_call | solution.py:99
  91.6 2.6 %copy.15 = bf16[1024,3,256]{0,2,1:T(8,128)(2,1)} copy(bf16[1024,3,256]{2,0,1:T(8,128)(2,1)} %constant_dynamic-slice_fusion) | data formatting | bytes 3145728
  94.2 1.8 collective-permute-start.5
  95.9 2.3 %collective-permute-done.3 = bf16[128,1024]{1,0:T(8,128)(2,1)S(1)} collective-permute-done((bf16[128,1024]{1,0:T(8,128)(2,1)}, bf16[128,1024]{1,0:T(8,128)(2,1)S(1)}, u32[]{:S(2)}, u32[]{:S(2)}) %collective-permute-start.3) | collective-permute-done | bytes 262176 | tf_op jit(solution)/shard_map/ppermute | solution.py:32
  98.3 4.2 %collective-permute-done.4 = bf16[128,1024]{1,0:T(8,128)(2,1)S(1)} collective-permute-done((bf16[128,1024]{1,0:T(8,128)(2,1)S(1)}, bf16[128,1024]{1,0:T(8,128)(2,1)S(1)}, u32[]{:S(2)}, u32[]{:S(2)}) %collective-permute-start.4) | collective-permute-done | bytes 262176 | tf_op jit(solution)/shard_map/ppermute | solution.py:32
  104.7 1.9 convolution_convert_fusion
  106.6 1.4 copy.9
  108.0 5.9 %collective-permute-start.8 = (bf16[512,2,256]{0,2,1:T(8,128)(2,1)S(1)}, bf16[512,2,256]{0,2,1:T(8,128)(2,1)}, u32[]{:S(2)}, u32[]{:S(2)}) collective-permute-start(bf16[512,2,256]{0,2,1:T(8,128)(2,1)S(1)} %slice.29), channel_id=1, source_target_pairs={{0,4},{1,5},{2,6},{3,7},{4,8},{5,9},{6,10},{7,11},{8,12},{9,13},{1... | collective-permute-start | bytes 1572872 | tf_op jit(solution)/shard_map/ppermute | solution.py:23
  113.9 4.2 %collective-permute-start.7 = (bf16[512,2,256]{0,2,1:T(8,128)(2,1)S(1)}, bf16[512,2,256]{0,2,1:T(8,128)(2,1)}, u32[]{:S(2)}, u32[]{:S(2)}) collective-permute-start(bf16[512,2,256]{0,2,1:T(8,128)(2,1)S(1)} %slice.29), channel_id=1, source_target_pairs={{0,8},{1,9},{2,10},{3,11},{4,12},{5,13},{6,14},{7,15},{16,24},{17,... | collective-permute-start | bytes 1572872 | tf_op jit(solution)/shard_map/ppermute | solution.py:23
  118.2 2.1 collective-permute-start.6
  120.3 2.0 fusion.6
  123.1 11.0 %collective-permute-done.7 = bf16[512,2,256]{0,2,1:T(8,128)(2,1)} collective-permute-done((bf16[512,2,256]{0,2,1:T(8,128)(2,1)S(1)}, bf16[512,2,256]{0,2,1:T(8,128)(2,1)}, u32[]{:S(2)}, u32[]{:S(2)}) %collective-permute-start.7) | collective-permute-done | bytes 524320 | tf_op jit(solution)/shard_map/ppermute | solution.py:23
  134.1 11.2 %collective-permute-done.6 = bf16[512,2,256]{0,2,1:T(8,128)(2,1)} collective-permute-done((bf16[512,2,256]{0,2,1:T(8,128)(2,1)S(1)}, bf16[512,2,256]{0,2,1:T(8,128)(2,1)}, u32[]{:S(2)}, u32[]{:S(2)}) %collective-permute-start.6) | collective-permute-done | bytes 524320 | tf_op jit(solution)/shard_map/ppermute | solution.py:23
  145.3 1.6 pad_maximum_fusion
  147.0 1.6 fusion.31
  148.6 7.5 %fusion.32 = (f32[2,512]{1,0:T(2,128)S(1)}, bf16[2,512,2048]{2,1,0:T(8,128)(2,1)}) fusion(pred[512,2048]{1,0:T(8,128)(4,1)S(1)} %copy-done.3, bf16[512,2,128]{0,2,1:T(8,128)(2,1)S(1)} %bitcast.65, bf16[2048,2,128]{0,2,1:T(8,128)(2,1)} %bitcast.64), kind=kOutput, calls=%fused_computation.49 | convolution fusion | flops 549455872 | bytes 6557696 | tf_op jit(solution)/shard_map/while/body/eval_jaxpr/sub | solution.py:179
  156.0 4.0 %fusion.14 = bf16[512,2,128]{0,2,1:T(8,128)(2,1)S(1)} fusion(bf16[2048,2,128]{0,2,1:T(8,128)(2,1)} %bitcast.63, bf16[2,512,2048]{2,1,0:T(8,128)(2,1)} %get-tuple-element.35, f32[512,2]{0,1:T(2,128)S(1)} %bitcast.66), kind=kOutput, calls=%fused_computation.15 | convolution fusion | flops 537133056 | bytes 5509120 | tf_op jit(solution)/shard_map/while/body/eval_jaxpr/hrk,khd->rhd/dot_general | solution.py:181
  160.6 1.3 copy-done.1
  163.1 2.4 %collective-permute-start.11 = (f32[128,1024]{1,0:T(8,128)}, f32[128,1024]{1,0:T(8,128)S(1)}, u32[]{:S(2)}, u32[]{:S(2)}) collective-permute-start(f32[128,1024]{1,0:T(8,128)} %get-tuple-element.30), channel_id=1, source_target_pairs={{0,3},{1,0},{2,1},{3,2},{4,7},{5,4},{6,5},{7,6},{8,11},{9,8},{10,9... | collective-permute-start | bytes 1572872 | tf_op jit(solution)/shard_map/ppermute | solution.py:32
  165.8 1.3 collective-permute-start.9
  167.1 10.4 %collective-permute-done.11 = f32[128,1024]{1,0:T(8,128)S(1)} collective-permute-done((f32[128,1024]{1,0:T(8,128)}, f32[128,1024]{1,0:T(8,128)S(1)}, u32[]{:S(2)}, u32[]{:S(2)}) %collective-permute-start.11) | collective-permute-done | bytes 524320 | tf_op jit(solution)/shard_map/ppermute | solution.py:32
  177.4 2.3 %collective-permute-done.10 = f32[128,1024]{1,0:T(8,128)} collective-permute-done((f32[128,1024]{1,0:T(8,128)}, f32[128,1024]{1,0:T(8,128)}, u32[]{:S(2)}, u32[]{:S(2)}) %collective-permute-start.10) | collective-permute-done | bytes 524320 | tf_op jit(solution)/shard_map/ppermute | solution.py:32
  179.7 9.2 %collective-permute-done.9 = f32[128,1024]{1,0:T(8,128)} collective-permute-done((f32[128,1024]{1,0:T(8,128)S(1)}, f32[128,1024]{1,0:T(8,128)}, u32[]{:S(2)}, u32[]{:S(2)}) %collective-permute-start.9) | collective-permute-done | bytes 524320 | tf_op jit(solution)/shard_map/ppermute | solution.py:32
  188.9 1.5 fusion.21
  190.4 16.7 %collective-permute-start.12 = (bf16[1,1024]{1,0:T(2,128)(2,1)S(1)}, bf16[1,1024]{1,0:T(2,128)(2,1)S(1)}, u32[]{:S(2)}, u32[]{:S(2)}) collective-permute-start(bf16[1,1024]{1,0:T(2,128)(2,1)S(1)} %slice.33), channel_id=1, source_target_pairs={{0,1},{1,2},{2,3},{3,4},{4,5},{5,6},{6,7},{7,8},{8,9},{9,10},{10,1... | collective-permute-start | bytes 6152 | tf_op jit(solution)/shard_map/ppermute | solution.py:23
  208.6 2.4 %shard_map.47 = bf16[512,1024]{1,0:T(8,128)(2,1)} custom-call(bf16[512,1024]{1,0:T(8,128)(2,1)} %get-tuple-element.17.fine_ref, bf16[128,1024]{1,0:T(8,128)(2,1)} %maximum_select_fusion.lift_ref), custom_call_target="tpu_custom_call" | custom-call | tf_op jit(solution)/shard_map/pallas_call | solution.py:138
  (46 shorter events, 8.6 us)
Async XLA Ops:
  0.0 160.1 %copy-start = (bf16[1024,1024]{1,0:T(8,128)(2,1)S(1)}, bf16[1024,1024]{1,0:T(8,128)(2,1)}, u32[]{:S(2)}) copy-start(bf16[1024,1024]{1,0:T(8,128)(2,1)} %param.7) | copy-start | bytes 6291460
  0.0 56.8 %copy-start.6 = (s32[2048]{0:T(1024)S(1)}, s32[2048]{0:T(1024)}, u32[]{:S(2)}) copy-start(s32[2048]{0:T(1024)} %param.5) | copy-start | bytes 24580
  3.3 48.7 %collective-permute-start = (bf16[2,512,1024]{2,1,0:T(8,128)(2,1)}, bf16[2,512,1024]{2,1,0:T(8,128)(2,1)}, u32[]{:S(2)}, u32[]{:S(2)}) collective-permute-start(bf16[2,512,1024]{2,1,0:T(8,128)(2,1)} %slice.28), channel_id=1, source_target_pairs={{0,2},{1,3},{2,4},{3,5},{4,6},{5,7},{6,8},{7,9},{8,10},{9,11},{10,... | collective-permute-start | bytes 6291464 | tf_op jit(solution)/shard_map/ppermute | solution.py:23
  6.4 55.0 %collective-permute-start.1 = (bf16[2,512,1024]{2,1,0:T(8,128)(2,1)}, bf16[2,512,1024]{2,1,0:T(8,128)(2,1)}, u32[]{:S(2)}, u32[]{:S(2)}) collective-permute-start(bf16[2,512,1024]{2,1,0:T(8,128)(2,1)} %slice.28), channel_id=1, source_target_pairs={{0,1},{2,3},{4,5},{6,7},{8,9},{10,11},{12,13},{14,15},{16,17},{18,... | collective-permute-start | bytes 6291464 | tf_op jit(solution)/shard_map/ppermute | solution.py:154
  52.0 9.5 %collective-permute-start.2 = (bf16[2,512,1024]{2,1,0:T(8,128)(2,1)}, bf16[2,512,1024]{2,1,0:T(8,128)(2,1)}, u32[]{:S(2)}, u32[]{:S(2)}) collective-permute-start(bf16[2,512,1024]{2,1,0:T(8,128)(2,1)} %collective-permute-done.k0_ref.v0_ref), channel_id=1, source_target_pairs={{1,0},{3,2},{5,4},{7,6},{9,8},{11,10},{13,12},{15,14},{17,16},{19,... | collective-permute-start | bytes 6291464 | tf_op jit(solution)/shard_map/ppermute | solution.py:154
  91.4 2.8 %copy-start.4 = (bf16[128,1024]{1,0:T(8,128)(2,1)S(1)}, bf16[128,1024]{1,0:T(8,128)(2,1)}, u32[]{:S(2)}) copy-start(bf16[128,1024]{1,0:T(8,128)(2,1)} %get-tuple-element.24) | copy-start | bytes 786436
  91.4 6.9 %collective-permute-start.3 = (bf16[128,1024]{1,0:T(8,128)(2,1)}, bf16[128,1024]{1,0:T(8,128)(2,1)S(1)}, u32[]{:S(2)}, u32[]{:S(2)}) collective-permute-start(bf16[128,1024]{1,0:T(8,128)(2,1)} %get-tuple-element.24), channel_id=1, source_target_pairs={{0,3},{1,0},{2,1},{3,2},{4,7},{5,4},{6,5},{7,6},{8,11},{9,8},{10,9... | collective-permute-start | bytes 786440 | tf_op jit(solution)/shard_map/ppermute | solution.py:32
  94.1 8.4 %collective-permute-start.4 = (bf16[128,1024]{1,0:T(8,128)(2,1)S(1)}, bf16[128,1024]{1,0:T(8,128)(2,1)S(1)}, u32[]{:S(2)}, u32[]{:S(2)}) collective-permute-start(bf16[128,1024]{1,0:T(8,128)(2,1)S(1)} %copy-done.4), channel_id=1, source_target_pairs={{0,2},{1,3},{2,0},{3,1},{4,6},{5,7},{6,4},{7,5},{8,10},{9,11},{10,... | collective-permute-start | bytes 786440 | tf_op jit(solution)/shard_map/ppermute | solution.py:32
  94.2 9.1 %collective-permute-start.5 = (bf16[128,1024]{1,0:T(8,128)(2,1)S(1)}, bf16[128,1024]{1,0:T(8,128)(2,1)S(1)}, u32[]{:S(2)}, u32[]{:S(2)}) collective-permute-start(bf16[128,1024]{1,0:T(8,128)(2,1)S(1)} %copy-done.4), channel_id=1, source_target_pairs={{0,1},{1,2},{2,3},{3,0},{4,5},{5,6},{6,7},{7,4},{8,9},{9,10},{10,1... | collective-permute-start | bytes 786440 | tf_op jit(solution)/shard_map/ppermute | solution.py:32
  103.3 1.4 copy-start.2
  108.0 15.0 %collective-permute-start.8 = (bf16[512,2,256]{0,2,1:T(8,128)(2,1)S(1)}, bf16[512,2,256]{0,2,1:T(8,128)(2,1)}, u32[]{:S(2)}, u32[]{:S(2)}) collective-permute-start(bf16[512,2,256]{0,2,1:T(8,128)(2,1)S(1)} %slice.29), channel_id=1, source_target_pairs={{0,4},{1,5},{2,6},{3,7},{4,8},{5,9},{6,10},{7,11},{8,12},{9,13},{1... | collective-permute-start | bytes 1572872 | tf_op jit(solution)/shard_map/ppermute | solution.py:23
  113.9 20.2 %collective-permute-start.7 = (bf16[512,2,256]{0,2,1:T(8,128)(2,1)S(1)}, bf16[512,2,256]{0,2,1:T(8,128)(2,1)}, u32[]{:S(2)}, u32[]{:S(2)}) collective-permute-start(bf16[512,2,256]{0,2,1:T(8,128)(2,1)S(1)} %slice.29), channel_id=1, source_target_pairs={{0,8},{1,9},{2,10},{3,11},{4,12},{5,13},{6,14},{7,15},{16,24},{17,... | collective-permute-start | bytes 1572872 | tf_op jit(solution)/shard_map/ppermute | solution.py:23
  118.2 27.2 %collective-permute-start.6 = (bf16[512,2,256]{0,2,1:T(8,128)(2,1)S(1)}, bf16[512,2,256]{0,2,1:T(8,128)(2,1)}, u32[]{:S(2)}, u32[]{:S(2)}) collective-permute-start(bf16[512,2,256]{0,2,1:T(8,128)(2,1)S(1)} %slice.29), channel_id=1, source_target_pairs={{0,12},{1,13},{2,14},{3,15},{16,28},{17,29},{18,30},{19,31}} | collective-permute-start | bytes 1572872 | tf_op jit(solution)/shard_map/ppermute | solution.py:23
  147.0 1.6 copy-start.3
  147.0 1.6 copy-start.5
  160.6 1.3 copy-start.1
  163.1 14.4 %collective-permute-start.11 = (f32[128,1024]{1,0:T(8,128)}, f32[128,1024]{1,0:T(8,128)S(1)}, u32[]{:S(2)}, u32[]{:S(2)}) collective-permute-start(f32[128,1024]{1,0:T(8,128)} %get-tuple-element.30), channel_id=1, source_target_pairs={{0,3},{1,0},{2,1},{3,2},{4,7},{5,4},{6,5},{7,6},{8,11},{9,8},{10,9... | collective-permute-start | bytes 1572872 | tf_op jit(solution)/shard_map/ppermute | solution.py:32
  165.4 14.2 %collective-permute-start.10 = (f32[128,1024]{1,0:T(8,128)}, f32[128,1024]{1,0:T(8,128)}, u32[]{:S(2)}, u32[]{:S(2)}) collective-permute-start(f32[128,1024]{1,0:T(8,128)} %get-tuple-element.31), channel_id=1, source_target_pairs={{0,2},{1,3},{2,0},{3,1},{4,6},{5,7},{6,4},{7,5},{8,10},{9,11},{10,... | collective-permute-start | bytes 1572872 | tf_op jit(solution)/shard_map/ppermute | solution.py:32
  165.8 23.1 %collective-permute-start.9 = (f32[128,1024]{1,0:T(8,128)S(1)}, f32[128,1024]{1,0:T(8,128)}, u32[]{:S(2)}, u32[]{:S(2)}) collective-permute-start(f32[128,1024]{1,0:T(8,128)S(1)} %get-tuple-element.29), channel_id=1, source_target_pairs={{0,1},{1,2},{2,3},{3,0},{4,5},{5,6},{6,7},{7,4},{8,9},{9,10},{10,1... | collective-permute-start | bytes 1572872 | tf_op jit(solution)/shard_map/ppermute | solution.py:32
  190.4 17.4 %collective-permute-start.12 = (bf16[1,1024]{1,0:T(2,128)(2,1)S(1)}, bf16[1,1024]{1,0:T(2,128)(2,1)S(1)}, u32[]{:S(2)}, u32[]{:S(2)}) collective-permute-start(bf16[1,1024]{1,0:T(2,128)(2,1)S(1)} %slice.33), channel_id=1, source_target_pairs={{0,1},{1,2},{2,3},{3,4},{4,5},{5,6},{6,7},{7,8},{8,9},{9,10},{10,1... | collective-permute-start | bytes 6152 | tf_op jit(solution)/shard_map/ppermute | solution.py:23

commit v3 on v2

--- a/solution.py
+++ b/solution.py
@@ -154,6 +154,71 @@
     return lax.ppermute(value, axis, [(source, source + step) for source in range(start, count, 2)])
 
 
+def coarse_kernel(qclip_ref, kc0_ref, kc1_ref, kc2_ref, kc3_ref, q_ref,
+                  k0_ref, v0_ref, k1_ref, v1_ref, k2_ref, v2_ref, k3_ref, v3_ref,
+                  out_ref, *, scale):
+    tile = q_ref.shape[0]
+    seg = k0_ref.shape[0]
+    q = q_ref[...]
+    qclip = qclip_ref[...]
+    keys = (k0_ref, k1_ref, k2_ref, k3_ref)
+    values = (v0_ref, v1_ref, v2_ref, v3_ref)
+    clips = (kc0_ref, kc1_ref, kc2_ref, kc3_ref)
+    qpos = pl.program_id(1) * tile + lax.broadcasted_iota(jnp.int32, (tile, seg), 0)
+    kpos = lax.broadcasted_iota(jnp.int32, (tile, seg), 1)
+    last = len(keys) - 1
+    scores = []
+    masks = []
+    for j in range(len(keys)):
+        allowed = clips[j][...] == qclip
+        if j == last:
+            allowed = allowed & (kpos <= qpos)
+        s = lax.dot_general(q, keys[j][...], (((1,), (1,)), ((), ())),
+                            preferred_element_type=jnp.float32) * scale
+        scores.append(jnp.where(allowed, s, -1e30))
+    top = jnp.max(scores[0], axis=1, keepdims=True)
+    for j in range(1, len(keys)):
+        top = jnp.maximum(top, jnp.max(scores[j], axis=1, keepdims=True))
+    total = None
+    summed = None
+    for j in range(len(keys)):
+        w = jnp.exp(scores[j] - top)
+        part = jnp.sum(w, axis=1, keepdims=True)
+        pv = jnp.dot(w.astype(jnp.bfloat16), values[j][...], preferred_element_type=jnp.float32)
+        total = part if total is None else total + part
+        summed = pv if summed is None else summed + pv
+    out_ref[...] = (summed / total).astype(out_ref.dtype)
+
+
+def coarse_attention(queries, windows, qclip, kclip, heads):
+    rows, width = queries.shape
+    head_dim = width // heads
+    tile = min(FINE_TILE, rows)
+    seg = windows[0].shape[1]
+    kernel = functools.partial(coarse_kernel, scale=1.0 / math.sqrt(head_dim))
+    clip_specs = [pl.BlockSpec((1, seg), functools.partial(lambda j, h, i: (0, j), j))
+                  for j in range(len(windows))]
+    kv_specs = []
+    kv_args = []
+    for window in windows:
+        kv_specs.append(pl.BlockSpec((None, seg, head_dim), lambda h, i: (0, 0, h)))
+        kv_specs.append(pl.BlockSpec((None, seg, head_dim), lambda h, i: (1, 0, h)))
+        kv_args += [window, window]
+    return pl.pallas_call(
+        kernel,
+        grid=(heads, rows // tile),
+        in_specs=[pl.BlockSpec((tile, 1), lambda h, i: (i, 0))] + clip_specs
+        + [pl.BlockSpec((tile, head_dim), lambda h, i: (i, h))] + kv_specs,
+        out_specs=pl.BlockSpec((tile, head_dim), lambda h, i: (i, h)),
+        out_shape=jax.ShapeDtypeStruct((rows, width), jnp.bfloat16),
+    )(qclip, *([kclip] * len(windows)), queries, *kv_args)
+
+
+def group_order(parts, quarter):
+    ordered = jnp.stack([parts[0]] + parts[:0:-1], axis=0)
+    return jnp.roll(ordered, quarter, axis=0)
+
+
 def attend(queries, key_rows, value_rows, allowed, heads, head_groups):
     row_count = queries.shape[0]
     feat_width = queries.shape[1]
@@ -216,48 +281,41 @@
         planes, prev0, prev1a, prev1b, query_clip.reshape(tok_count, 1),
         key_clip.reshape(1, (FREACH + 1) * tok_count), FHEADS,
     )
-    received = [pooled] + [within_group(pooled, "seq", shift) for shift in range(1, QUARTERS)]
-    from_next = jnp.stack([received[0]] + received[:0:-1], axis=0)
-    gathered = jnp.roll(from_next, quarter, axis=0).reshape(group_rows, feat_width)
     quarter_width = w_coarse.shape[2] // QUARTERS
-    quarter_weight = lax.dynamic_slice_in_dim(w_coarse, quarter * quarter_width, quarter_width, 2)
-    projected = jnp.dot(
-        gathered,
-        quarter_weight.reshape(feat_width, 3 * quarter_width),
-        preferred_element_type=jnp.float32,
-    )
-    projected = projected.astype(jnp.bfloat16).reshape(group_rows, 3, quarter_width)
-    coarse_queries = projected[:, 0]
-    coarse_pairs = projected[:, 1:3]
+    wplanes = jnp.transpose(w_coarse, (1, 0, 2))
+    projected = jnp.einsum(
+        "rd,mdc->mrc", pooled, wplanes, preferred_element_type=jnp.float32
+    ).astype(jnp.bfloat16)
+    pieces = []
+    for shift in range(QUARTERS):
+        piece = lax.dynamic_slice_in_dim(
+            projected, ((quarter + shift) % QUARTERS) * quarter_width, quarter_width, 2
+        )
+        pieces.append(piece if shift == 0 else within_group(piece, "seq", shift))
+    grouped = group_order(pieces, quarter)
+    grouped = jnp.transpose(grouped, (1, 0, 2, 3)).reshape(3, group_rows, quarter_width)
+    coarse_queries = grouped[0]
+    coarse_pairs = grouped[1:]
     earlier = [passed_along(coarse_pairs, "seq", QUARTERS * hop) for hop in range(CREACH, 0, -1)]
-    coarse_window = jnp.concatenate(earlier + [coarse_pairs], axis=0)
     clip_back = jnp.concatenate([jnp.full((CREACH * group_rows,), -1, jnp.int32), clip_ids])
     coarse_key_clip = lax.dynamic_slice_in_dim(
         clip_back, cycle_place * group_rows, (CREACH + 1) * group_rows, 0
     )
     coarse_query_clip = lax.dynamic_slice_in_dim(clip_ids, cycle_place * group_rows, group_rows, 0)
-    coarse_qpos = jnp.arange(group_rows, dtype=jnp.int32) + CREACH * group_rows
-    coarse_kpos = jnp.arange((CREACH + 1) * group_rows, dtype=jnp.int32)
-    coarse_allowed = (coarse_kpos[None, :] <= coarse_qpos[:, None]) & (
-        coarse_key_clip[None, :] == coarse_query_clip[:, None]
-    )
-    coarse_att = attend(
-        coarse_queries,
-        coarse_window[:, 0],
-        coarse_window[:, 1],
-        coarse_allowed,
-        CHEADS // QUARTERS,
-        1,
-    )
-    row_weight = lax.dynamic_slice_in_dim(w_out, quarter * quarter_width, quarter_width, 0)
-    stacked = jnp.dot(coarse_att, row_weight, preferred_element_type=jnp.float32).reshape(
-        QUARTERS, coarse_rows, feat_width
-    )
-    summed_up = lax.dynamic_index_in_dim(stacked, quarter, 0, False)
-    for shift in range(1, QUARTERS):
-        outgoing = lax.dynamic_index_in_dim(stacked, (quarter + shift) % QUARTERS, 0, False)
-        summed_up = summed_up + within_group(outgoing, "seq", shift)
-    coarse_up = summed_up.astype(jnp.bfloat16)
+    coarse_att = coarse_attention(
+        coarse_queries, earlier + [coarse_pairs], coarse_query_clip.reshape(group_rows, 1),
+        coarse_key_clip.reshape(1, (CREACH + 1) * group_rows), CHEADS // QUARTERS,
+    )
+    shares = []
+    for shift in range(QUARTERS):
+        share = lax.dynamic_slice_in_dim(
+            coarse_att, ((quarter + shift) % QUARTERS) * coarse_rows, coarse_rows, 0
+        )
+        shares.append(share if shift == 0 else within_group(share, "seq", shift))
+    att_rows = jnp.transpose(group_order(shares, quarter), (1, 0, 2)).reshape(
+        coarse_rows, QUARTERS * quarter_width
+    )
+    coarse_up = jnp.dot(att_rows, w_out, preferred_element_type=jnp.float32).astype(jnp.bfloat16)
     carried = passed_along(coarse_up[-1:], "seq", 1)
     previous = jnp.concatenate([carried, coarse_up[:-1]], axis=0)
     clip_before = jnp.concatenate([jnp.full((1,), -1, jnp.int32), clip_ids])

time: 214 us -> 181 us (0.85)
  waiting for transfers between devices: 96.3 us -> 78.3 us
  matrix products: 13.9 us -> 4.35 us
  local copies, waits for them, and re-layouts: 18.3 us -> 11.4 us
  Pallas kernels: 32.3 us -> 39.1 us
  other arithmetic: 5.98 us -> 0.88 us
    ppermute x6, waiting for transfers between devices: 29 us -> 8.03 us  [within_group(): return lax.ppermute(value, axis, pairs)]
    sub x1 -> x0, matrix products: 7.46 us -> none  [one_group(): weights = jnp.where(allowed[None], jnp.exp(masked - row_top), 0.0)]
    pallas_call x0 -> x1, Pallas kernels: none -> 6.81 us  [coarse_attention(): pl.pallas_call(kernel, grid=(heads, rows // tile), in_specs=[pl.BlockSpec...]
    unnamed x22 -> x20, local copies, waits for them, and re-layouts: 5.28 us -> 1.87 us
    ppermute x5, waiting for transfers between devices: 67.3 us -> 69.5 us  [passed_along(): lax.ppermute(value, axis, [(source, source + steps) for source in range(f...]
    dot_general x3 -> x2, matrix products: 6.41 us -> 4.35 us  [the longest x1 3.88 us: body(): jnp.einsum('rd,mdc->mrc', pooled, wplanes, preferred_element_type=jnp.flo...]
  transfers between devices with their start and end apart: 13 -> 13, of which waited for: 10 -> 9; matrix products, arithmetic and copies ran while one was open for 5% -> 3% of each run, Pallas kernels for 0% -> 0%
where the time goes in v3:
time: 181 us; the launch traced here: 178 us
  waiting for transfers between devices  78.3 us (43%)
  starting transfers between devices  43.7 us (24%)
  Pallas kernels  39.1 us (22%)
  local copies, waits for them, and re-layouts  11.4 us (6%)
  matrix products  4.35 us (2%)
    ppermute x5, waiting for transfers between devices, passed_along(): lax.ppermute(value, axis, [(source, source + steps) for source in range(f...  69.5 us
    ppermute x5, starting transfers between devices, passed_along(): lax.ppermute(value, axis, [(source, source + steps) for source in range(f...  31.1 us
    pallas_call x1, Pallas kernels, fine_attention(): pl.pallas_call(kernel, grid=(pairs, nq), in_specs=[pl.BlockSpec((tile, 1)...  29.9 us
    ppermute x6, waiting for transfers between devices, within_group(): return lax.ppermute(value, axis, pairs)  8.03 us
    pallas_call x1, Pallas kernels, coarse_attention(): pl.pallas_call(kernel, grid=(heads, rows // tile), in_specs=[pl.BlockSpec...  6.81 us
    ppermute x6, starting transfers between devices, within_group(): return lax.ppermute(value, axis, pairs)  6.49 us
    ppermute x2, starting transfers between devices, pair_swap(): lax.ppermute(value, axis, [(source, source + step) for source in range(st...  6.1 us
    dot_general x1, matrix products, body(): jnp.einsum('rd,mdc->mrc', pooled, wplanes, preferred_element_type=jnp.flo...  3.88 us
  transfers between devices with their start and end apart: 13, of which 9 were waited for; matrix products, arithmetic and copies ran while one was open for 3% of the time, Pallas kernels for 0%

profile of v3, /device:TPU:7, one launch (start us, length us, event | category | flops | bytes accessed | tf_op | source)
XLA Modules:
  0.0 178.0 jit_solution(5809671860909391814)
XLA Ops:
  0.0 3.3 %slice.25 = bf16[2,512,1024]{2,1,0:T(8,128)(2,1)} slice(bf16[3,512,1024]{2,1,0:T(8,128)(2,1)} %bitcast.53), slice={[1:3], [0:512], [0:1024]} | slice | bytes 4194304 | tf_op jit(solution)/shard_map/slice | solution.py:269
  3.3 3.1 %collective-permute-start = (bf16[2,512,1024]{2,1,0:T(8,128)(2,1)}, bf16[2,512,1024]{2,1,0:T(8,128)(2,1)}, u32[]{:S(2)}, u32[]{:S(2)}) collective-permute-start(bf16[2,512,1024]{2,1,0:T(8,128)(2,1)} %slice.25), channel_id=1, source_target_pairs={{0,2},{1,3},{2,4},{3,5},{4,6},{5,7},{6,8},{7,9},{8,10},{9,11},{10,... | collective-permute-start | bytes 6291464 | tf_op jit(solution)/shard_map/ppermute | solution.py:23
  6.4 1.3 collective-permute-start.1
  7.7 44.3 %collective-permute-done.k0_ref.v0_ref = bf16[2,512,1024]{2,1,0:T(8,128)(2,1)} collective-permute-done((bf16[2,512,1024]{2,1,0:T(8,128)(2,1)}, bf16[2,512,1024]{2,1,0:T(8,128)(2,1)}, u32[]{:S(2)}, u32[]{:S(2)}) %collective-permute-start) | collective-permute-done | bytes 2097184 | tf_op jit(solution)/shard_map/ppermute | solution.py:23
  52.0 4.8 %collective-permute-start.2 = (bf16[2,512,1024]{2,1,0:T(8,128)(2,1)}, bf16[2,512,1024]{2,1,0:T(8,128)(2,1)}, u32[]{:S(2)}, u32[]{:S(2)}) collective-permute-start(bf16[2,512,1024]{2,1,0:T(8,128)(2,1)} %collective-permute-done.k0_ref.v0_ref), channel_id=1, source_target_pairs={{1,0},{3,2},{5,4},{7,6},{9,8},{11,10},{13,12},{15,14},{17,16},{19,... | collective-permute-start | bytes 6291464 | tf_op jit(solution)/shard_map/ppermute | solution.py:154
  56.9 0.8 reshape_reshape.8.qclip_ref
  58.0 0.8 reshape_reshape.7.kclip0_ref.kclip1_ref.kclip2_ref
  58.7 0.8 collective-permute-done.2.k1b_ref.v1b_ref
  59.5 29.9 %shard_map.46 = (bf16[512,1024]{1,0:T(8,128)(2,1)}, bf16[128,1024]{1,0:T(8,128)(2,1)}) custom-call(s32[512,1]{1,0:T(8,128)} %reshape_reshape.8.qclip_ref, s32[1,1536]{1,0:T(1,128)} %reshape_reshape.7.kclip0_ref.kclip1_ref.kclip2_ref, s32[1,1536]{1,0:T(1,128)} %reshape_reshape.7.kclip0_ref.kclip1_ref.kclip2_ref, ...), custom_call_target="tpu_custom_call" | custom-call | tf_op jit(solution)/shard_map/pallas_call | solution.py:99
  89.4 3.9 %fusion.2 = bf16[128,3,1024]{2,0,1:T(8,128)(2,1)S(1)} fusion(bf16[1024,3,1024]{2,0,1:T(8,128)(2,1)} %param.6, bf16[128,1024]{1,0:T(8,128)(2,1)} %get-tuple-element.8), kind=kOutput, calls=%fused_computation.2 | convolution fusion | flops 805699584 | bytes 7340032 | tf_op jit(solution)/shard_map/rd,mdc->mrc/dot_general | solution.py:286
  93.3 0.8 dynamic-slice_bitcast_fusion.2
  94.5 1.6 collective-permute-start.5
  96.1 5.6 %collective-permute-done.3 = bf16[3,128,256]{2,1,0:T(8,128)(2,1)S(1)} collective-permute-done((bf16[3,128,256]{2,1,0:T(8,128)(2,1)}, bf16[3,128,256]{2,1,0:T(8,128)(2,1)S(1)}, u32[]{:S(2)}, u32[]{:S(2)}) %collective-permute-start.3) | collective-permute-done | bytes 196640 | tf_op jit(solution)/shard_map/ppermute | solution.py:32
  101.8 1.3 collective-permute-done.5
  103.4 7.1 %collective-permute-start.6 = (bf16[2,512,256]{2,1,0:T(8,128)(2,1)S(1)}, bf16[2,512,256]{2,1,0:T(8,128)(2,1)}, u32[]{:S(2)}, u32[]{:S(2)}) collective-permute-start(bf16[2,512,256]{2,1,0:T(8,128)(2,1)S(1)} %bitcast.57), channel_id=1, source_target_pairs={{0,12},{1,13},{2,14},{3,15},{16,28},{17,29},{18,30},{19,31}} | collective-permute-start | bytes 1572872 | tf_op jit(solution)/shard_map/ppermute | solution.py:23
  110.5 2.1 %collective-permute-start.7 = (bf16[2,512,256]{2,1,0:T(8,128)(2,1)S(1)}, bf16[2,512,256]{2,1,0:T(8,128)(2,1)}, u32[]{:S(2)}, u32[]{:S(2)}) collective-permute-start(bf16[2,512,256]{2,1,0:T(8,128)(2,1)S(1)} %bitcast.58), channel_id=1, source_target_pairs={{0,8},{1,9},{2,10},{3,11},{4,12},{5,13},{6,14},{7,15},{16,24},{17,... | collective-permute-start | bytes 1572872 | tf_op jit(solution)/shard_map/ppermute | solution.py:23
  112.6 2.2 %collective-permute-start.8 = (bf16[2,512,256]{2,1,0:T(8,128)(2,1)S(1)}, bf16[2,512,256]{2,1,0:T(8,128)(2,1)}, u32[]{:S(2)}, u32[]{:S(2)}) collective-permute-start(bf16[2,512,256]{2,1,0:T(8,128)(2,1)S(1)} %bitcast.59), channel_id=1, source_target_pairs={{0,4},{1,5},{2,6},{3,7},{4,8},{5,9},{6,10},{7,11},{8,12},{9,13},{1... | collective-permute-start | bytes 1572872 | tf_op jit(solution)/shard_map/ppermute | solution.py:23
  114.9 0.9 copy.8.qclip_ref
  116.4 0.7 slice.26
  117.2 2.0 %collective-permute-done.6.k0_ref.v0_ref = bf16[2,512,256]{2,1,0:T(8,128)(2,1)} collective-permute-done((bf16[2,512,256]{2,1,0:T(8,128)(2,1)S(1)}, bf16[2,512,256]{2,1,0:T(8,128)(2,1)}, u32[]{:S(2)}, u32[]{:S(2)}) %collective-permute-start.6) | collective-permute-done | bytes 524320 | tf_op jit(solution)/shard_map/ppermute | solution.py:23
  119.2 11.2 %collective-permute-done.7.k1_ref.v1_ref = bf16[2,512,256]{2,1,0:T(8,128)(2,1)} collective-permute-done((bf16[2,512,256]{2,1,0:T(8,128)(2,1)S(1)}, bf16[2,512,256]{2,1,0:T(8,128)(2,1)}, u32[]{:S(2)}, u32[]{:S(2)}) %collective-permute-start.7) | collective-permute-done | bytes 524320 | tf_op jit(solution)/shard_map/ppermute | solution.py:23
  130.5 11.2 %collective-permute-done.8.k2_ref.v2_ref = bf16[2,512,256]{2,1,0:T(8,128)(2,1)} collective-permute-done((bf16[2,512,256]{2,1,0:T(8,128)(2,1)S(1)}, bf16[2,512,256]{2,1,0:T(8,128)(2,1)}, u32[]{:S(2)}, u32[]{:S(2)}) %collective-permute-start.8) | collective-permute-done | bytes 524320 | tf_op jit(solution)/shard_map/ppermute | solution.py:23
  141.7 6.8 %shard_map.47 = bf16[512,256]{1,0:T(8,128)(2,1)} custom-call(s32[512,1]{1,0:T(8,128)} %copy.8.qclip_ref, s32[1,2048]{1,0:T(1,128)} %bitcast.65, s32[1,2048]{1,0:T(1,128)} %bitcast.66, s32[1,2048]{1,0:T(1,128)} %bitcast.67, s32[1,2048]{1,0:T(1,128)} %bitcast.68, bf16[512,256]{1,0:T(8,128)(2,1)} %bitcast.63, ...), custom_call_target="tpu_custom_call" | custom-call | tf_op jit(solution)/shard_map/pallas_call | solution.py:207
  148.5 0.9 constant_dynamic-slice_fusion
  149.4 2.8 %collective-permute-start.9 = (bf16[128,256]{1,0:T(8,128)(2,1)S(1)}, bf16[128,256]{1,0:T(8,128)(2,1)S(1)}, u32[]{:S(2)}, u32[]{:S(2)}) collective-permute-start(bf16[128,256]{1,0:T(8,128)(2,1)S(1)} %get-tuple-element.16), channel_id=1, source_target_pairs={{0,3},{1,0},{2,1},{3,2},{4,7},{5,4},{6,5},{7,6},{8,11},{9,8},{10,9... | collective-permute-start | bytes 196616 | tf_op jit(solution)/shard_map/ppermute | solution.py:32
  152.5 1.4 collective-permute-start.11
  153.9 0.8 bitcast_dynamic-update-slice_fusion.14
  154.8 1.1 collective-permute-done.10
  155.9 0.9 bitcast_dynamic-update-slice_fusion.15
  157.5 16.5 %collective-permute-start.12 = (bf16[1,1024]{1,0:T(2,128)(2,1)S(1)}, bf16[1,1024]{1,0:T(2,128)(2,1)S(1)}, u32[]{:S(2)}, u32[]{:S(2)}) collective-permute-start(bf16[1,1024]{1,0:T(2,128)(2,1)S(1)} %slice.28), channel_id=1, source_target_pairs={{0,1},{1,2},{2,3},{3,4},{4,5},{5,6},{6,7},{7,8},{8,9},{9,10},{10,1... | collective-permute-start | bytes 6152 | tf_op jit(solution)/shard_map/ppermute | solution.py:23
  174.8 0.8 maximum_select_fusion.lift_ref
  175.6 2.4 %shard_map.48 = bf16[512,1024]{1,0:T(8,128)(2,1)} custom-call(bf16[512,1024]{1,0:T(8,128)(2,1)} %get-tuple-element.7.fine_ref, bf16[128,1024]{1,0:T(8,128)(2,1)} %maximum_select_fusion.lift_ref), custom_call_target="tpu_custom_call" | custom-call | tf_op jit(solution)/shard_map/pallas_call | solution.py:138
  (41 shorter events, 3.5 us)
Async XLA Ops:
  0.0 157.0 %copy-start = (bf16[1024,1024]{1,0:T(8,128)(2,1)S(1)}, bf16[1024,1024]{1,0:T(8,128)(2,1)}, u32[]{:S(2)}) copy-start(bf16[1024,1024]{1,0:T(8,128)(2,1)} %param.7) | copy-start | bytes 6291460
  0.0 56.8 %copy-start.2 = (s32[2048]{0:T(1024)S(1)}, s32[2048]{0:T(1024)}, u32[]{:S(2)}) copy-start(s32[2048]{0:T(1024)} %param.5) | copy-start | bytes 24580
  3.3 48.7 %collective-permute-start = (bf16[2,512,1024]{2,1,0:T(8,128)(2,1)}, bf16[2,512,1024]{2,1,0:T(8,128)(2,1)}, u32[]{:S(2)}, u32[]{:S(2)}) collective-permute-start(bf16[2,512,1024]{2,1,0:T(8,128)(2,1)} %slice.25), channel_id=1, source_target_pairs={{0,2},{1,3},{2,4},{3,5},{4,6},{5,7},{6,8},{7,9},{8,10},{9,11},{10,... | collective-permute-start | bytes 6291464 | tf_op jit(solution)/shard_map/ppermute | solution.py:23
  6.4 52.3 %collective-permute-start.1 = (bf16[2,512,1024]{2,1,0:T(8,128)(2,1)}, bf16[2,512,1024]{2,1,0:T(8,128)(2,1)}, u32[]{:S(2)}, u32[]{:S(2)}) collective-permute-start(bf16[2,512,1024]{2,1,0:T(8,128)(2,1)} %slice.25), channel_id=1, source_target_pairs={{0,1},{2,3},{4,5},{6,7},{8,9},{10,11},{12,13},{14,15},{16,17},{18,... | collective-permute-start | bytes 6291464 | tf_op jit(solution)/shard_map/ppermute | solution.py:154
  52.0 7.6 %collective-permute-start.2 = (bf16[2,512,1024]{2,1,0:T(8,128)(2,1)}, bf16[2,512,1024]{2,1,0:T(8,128)(2,1)}, u32[]{:S(2)}, u32[]{:S(2)}) collective-permute-start(bf16[2,512,1024]{2,1,0:T(8,128)(2,1)} %collective-permute-done.k0_ref.v0_ref), channel_id=1, source_target_pairs={{1,0},{3,2},{5,4},{7,6},{9,8},{11,10},{13,12},{15,14},{17,16},{19,... | collective-permute-start | bytes 6291464 | tf_op jit(solution)/shard_map/ppermute | solution.py:154
  94.1 7.6 %collective-permute-start.3 = (bf16[3,128,256]{2,1,0:T(8,128)(2,1)}, bf16[3,128,256]{2,1,0:T(8,128)(2,1)S(1)}, u32[]{:S(2)}, u32[]{:S(2)}) collective-permute-start(bf16[3,128,256]{2,1,0:T(8,128)(2,1)} %get-tuple-element.13), channel_id=1, source_target_pairs={{0,3},{1,0},{2,1},{3,2},{4,7},{5,4},{6,5},{7,6},{8,11},{9,8},{10,9... | collective-permute-start | bytes 589832 | tf_op jit(solution)/shard_map/ppermute | solution.py:32
  94.5 7.3 %collective-permute-start.4 = (bf16[3,128,256]{2,1,0:T(8,128)(2,1)S(1)}, bf16[3,128,256]{2,1,0:T(8,128)(2,1)S(1)}, u32[]{:S(2)}, u32[]{:S(2)}) collective-permute-start(bf16[3,128,256]{2,1,0:T(8,128)(2,1)S(1)} %get-tuple-element.12), channel_id=1, source_target_pairs={{0,2},{1,3},{2,0},{3,1},{4,6},{5,7},{6,4},{7,5},{8,10},{9,11},{10,... | collective-permute-start | bytes 589832 | tf_op jit(solution)/shard_map/ppermute | solution.py:32
  94.5 8.6 %collective-permute-start.5 = (bf16[3,128,256]{2,1,0:T(8,128)(2,1)S(1)}, bf16[3,128,256]{2,1,0:T(8,128)(2,1)S(1)}, u32[]{:S(2)}, u32[]{:S(2)}) collective-permute-start(bf16[3,128,256]{2,1,0:T(8,128)(2,1)S(1)} %get-tuple-element.11), channel_id=1, source_target_pairs={{0,1},{1,2},{2,3},{3,0},{4,5},{5,6},{6,7},{7,4},{8,9},{9,10},{10,1... | collective-permute-start | bytes 589832 | tf_op jit(solution)/shard_map/ppermute | solution.py:32
  103.4 38.3 %copy-start.1 = (bf16[2,4,128,256]{3,2,1,0:T(8,128)(2,1)}, bf16[2,4,128,256]{3,2,1,0:T(8,128)(2,1)S(1)}, u32[]{:S(2)}) copy-start(bf16[2,4,128,256]{3,2,1,0:T(8,128)(2,1)S(1)} %copy.7) | copy-start | bytes 1572868
  103.4 15.8 %collective-permute-start.6 = (bf16[2,512,256]{2,1,0:T(8,128)(2,1)S(1)}, bf16[2,512,256]{2,1,0:T(8,128)(2,1)}, u32[]{:S(2)}, u32[]{:S(2)}) collective-permute-start(bf16[2,512,256]{2,1,0:T(8,128)(2,1)S(1)} %bitcast.57), channel_id=1, source_target_pairs={{0,12},{1,13},{2,14},{3,15},{16,28},{17,29},{18,30},{19,31}} | collective-permute-start | bytes 1572872 | tf_op jit(solution)/shard_map/ppermute | solution.py:23
  110.5 19.9 %collective-permute-start.7 = (bf16[2,512,256]{2,1,0:T(8,128)(2,1)S(1)}, bf16[2,512,256]{2,1,0:T(8,128)(2,1)}, u32[]{:S(2)}, u32[]{:S(2)}) collective-permute-start(bf16[2,512,256]{2,1,0:T(8,128)(2,1)S(1)} %bitcast.58), channel_id=1, source_target_pairs={{0,8},{1,9},{2,10},{3,11},{4,12},{5,13},{6,14},{7,15},{16,24},{17,... | collective-permute-start | bytes 1572872 | tf_op jit(solution)/shard_map/ppermute | solution.py:23
  112.6 29.1 %collective-permute-start.8 = (bf16[2,512,256]{2,1,0:T(8,128)(2,1)S(1)}, bf16[2,512,256]{2,1,0:T(8,128)(2,1)}, u32[]{:S(2)}, u32[]{:S(2)}) collective-permute-start(bf16[2,512,256]{2,1,0:T(8,128)(2,1)S(1)} %bitcast.59), channel_id=1, source_target_pairs={{0,4},{1,5},{2,6},{3,7},{4,8},{5,9},{6,10},{7,11},{8,12},{9,13},{1... | collective-permute-start | bytes 1572872 | tf_op jit(solution)/shard_map/ppermute | solution.py:23
  149.4 5.3 %collective-permute-start.9 = (bf16[128,256]{1,0:T(8,128)(2,1)S(1)}, bf16[128,256]{1,0:T(8,128)(2,1)S(1)}, u32[]{:S(2)}, u32[]{:S(2)}) collective-permute-start(bf16[128,256]{1,0:T(8,128)(2,1)S(1)} %get-tuple-element.16), channel_id=1, source_target_pairs={{0,3},{1,0},{2,1},{3,2},{4,7},{5,4},{6,5},{7,6},{8,11},{9,8},{10,9... | collective-permute-start | bytes 196616 | tf_op jit(solution)/shard_map/ppermute | solution.py:32
  152.2 3.7 %collective-permute-start.10 = (bf16[128,256]{1,0:T(8,128)(2,1)S(1)}, bf16[128,256]{1,0:T(8,128)(2,1)S(1)}, u32[]{:S(2)}, u32[]{:S(2)}) collective-permute-start(bf16[128,256]{1,0:T(8,128)(2,1)S(1)} %get-tuple-element.15), channel_id=1, source_target_pairs={{0,2},{1,3},{2,0},{3,1},{4,6},{5,7},{6,4},{7,5},{8,10},{9,11},{10,... | collective-permute-start | bytes 196616 | tf_op jit(solution)/shard_map/ppermute | solution.py:32
  152.5 3.4 %collective-permute-start.11 = (bf16[128,256]{1,0:T(8,128)(2,1)S(1)}, bf16[128,256]{1,0:T(8,128)(2,1)S(1)}, u32[]{:S(2)}, u32[]{:S(2)}) collective-permute-start(bf16[128,256]{1,0:T(8,128)(2,1)S(1)} %get-tuple-element.14), channel_id=1, source_target_pairs={{0,1},{1,2},{2,3},{3,0},{4,5},{5,6},{6,7},{7,4},{8,9},{9,10},{10,1... | collective-permute-start | bytes 196616 | tf_op jit(solution)/shard_map/ppermute | solution.py:32
  157.5 17.3 %collective-permute-start.12 = (bf16[1,1024]{1,0:T(2,128)(2,1)S(1)}, bf16[1,1024]{1,0:T(2,128)(2,1)S(1)}, u32[]{:S(2)}, u32[]{:S(2)}) collective-permute-start(bf16[1,1024]{1,0:T(2,128)(2,1)S(1)} %slice.28), channel_id=1, source_target_pairs={{0,1},{1,2},{2,3},{3,4},{4,5},{5,6},{6,7},{7,8},{8,9},{9,10},{10,1... | collective-permute-start | bytes 6152 | tf_op jit(solution)/shard_map/ppermute | solution.py:23

commit v4 on v3

--- a/solution.py
+++ b/solution.py
@@ -296,7 +296,10 @@
     grouped = jnp.transpose(grouped, (1, 0, 2, 3)).reshape(3, group_rows, quarter_width)
     coarse_queries = grouped[0]
     coarse_pairs = grouped[1:]
-    earlier = [passed_along(coarse_pairs, "seq", QUARTERS * hop) for hop in range(CREACH, 0, -1)]
+    one_back = passed_along(coarse_pairs, "seq", QUARTERS)
+    two_back = passed_along(coarse_pairs, "seq", 2 * QUARTERS)
+    three_back = passed_along(two_back, "seq", QUARTERS)
+    earlier = [three_back, two_back, one_back]
     clip_back = jnp.concatenate([jnp.full((CREACH * group_rows,), -1, jnp.int32), clip_ids])
     coarse_key_clip = lax.dynamic_slice_in_dim(
         clip_back, cycle_place * group_rows, (CREACH + 1) * group_rows, 0

time: 181 us -> 180 us (level)
  waiting for transfers between devices: 78.3 us -> 66.3 us
  starting transfers between devices: 43.7 us -> 54.8 us
    ppermute x5, starting transfers between devices: 31.1 us -> 43.5 us  [passed_along(): lax.ppermute(value, axis, [(source, source + steps) for source in range(f...]
    ppermute x5, waiting for transfers between devices: 69.5 us -> 57.5 us  [passed_along(): lax.ppermute(value, axis, [(source, source + steps) for source in range(f...]
  transfers between devices with their start and end apart: 13 -> 13, of which waited for: 9 -> 8; matrix products, arithmetic and copies ran while one was open for 3% -> 3% of each run, Pallas kernels for 0% -> 0%
where the time goes in v4:
time: 180 us; the launch traced here: 177 us
  waiting for transfers between devices  66.3 us (37%)
  starting transfers between devices  54.8 us (30%)
  Pallas kernels  39.1 us (22%)
  local copies, waits for them, and re-layouts  11.4 us (6%)
  matrix products  4.35 us (2%)
    ppermute x5, waiting for transfers between devices, passed_along(): lax.ppermute(value, axis, [(source, source + steps) for source in range(f...  57.5 us
    ppermute x5, starting transfers between devices, passed_along(): lax.ppermute(value, axis, [(source, source + steps) for source in range(f...  43.5 us
    pallas_call x1, Pallas kernels, fine_attention(): pl.pallas_call(kernel, grid=(pairs, nq), in_specs=[pl.BlockSpec((tile, 1)...  29.9 us
    ppermute x6, waiting for transfers between devices, within_group(): return lax.ppermute(value, axis, pairs)  8.03 us
    pallas_call x1, Pallas kernels, coarse_attention(): pl.pallas_call(kernel, grid=(heads, rows // tile), in_specs=[pl.BlockSpec...  6.81 us
    ppermute x2, starting transfers between devices, pair_swap(): lax.ppermute(value, axis, [(source, source + step) for source in range(st...  6.1 us
    ppermute x6, starting transfers between devices, within_group(): return lax.ppermute(value, axis, pairs)  5.22 us
    dot_general x1, matrix products, body(): jnp.einsum('rd,mdc->mrc', pooled, wplanes, preferred_element_type=jnp.flo...  3.88 us
  transfers between devices with their start and end apart: 13, of which 8 were waited for; matrix products, arithmetic and copies ran while one was open for 3% of the time, Pallas kernels for 0%

profile of v4, /device:TPU:7, one launch (start us, length us, event | category | flops | bytes accessed | tf_op | source)
XLA Modules:
  0.0 177.1 jit_solution(3995358176180691665)
XLA Ops:
  0.0 3.3 %slice.25 = bf16[2,512,1024]{2,1,0:T(8,128)(2,1)} slice(bf16[3,512,1024]{2,1,0:T(8,128)(2,1)} %bitcast.53), slice={[1:3], [0:512], [0:1024]} | slice | bytes 4194304 | tf_op jit(solution)/shard_map/slice | solution.py:269
  3.3 3.1 %collective-permute-start = (bf16[2,512,1024]{2,1,0:T(8,128)(2,1)}, bf16[2,512,1024]{2,1,0:T(8,128)(2,1)}, u32[]{:S(2)}, u32[]{:S(2)}) collective-permute-start(bf16[2,512,1024]{2,1,0:T(8,128)(2,1)} %slice.25), channel_id=1, source_target_pairs={{0,2},{1,3},{2,4},{3,5},{4,6},{5,7},{6,8},{7,9},{8,10},{9,11},{10,... | collective-permute-start | bytes 6291464 | tf_op jit(solution)/shard_map/ppermute | solution.py:23
  6.4 1.3 collective-permute-start.1
  7.7 44.3 %collective-permute-done.k0_ref.v0_ref = bf16[2,512,1024]{2,1,0:T(8,128)(2,1)} collective-permute-done((bf16[2,512,1024]{2,1,0:T(8,128)(2,1)}, bf16[2,512,1024]{2,1,0:T(8,128)(2,1)}, u32[]{:S(2)}, u32[]{:S(2)}) %collective-permute-start) | collective-permute-done | bytes 2097184 | tf_op jit(solution)/shard_map/ppermute | solution.py:23
  52.0 4.8 %collective-permute-start.2 = (bf16[2,512,1024]{2,1,0:T(8,128)(2,1)}, bf16[2,512,1024]{2,1,0:T(8,128)(2,1)}, u32[]{:S(2)}, u32[]{:S(2)}) collective-permute-start(bf16[2,512,1024]{2,1,0:T(8,128)(2,1)} %collective-permute-done.k0_ref.v0_ref), channel_id=1, source_target_pairs={{1,0},{3,2},{5,4},{7,6},{9,8},{11,10},{13,12},{15,14},{17,16},{19,... | collective-permute-start | bytes 6291464 | tf_op jit(solution)/shard_map/ppermute | solution.py:154
  56.9 0.8 reshape_reshape.8.qclip_ref
  58.0 0.8 reshape_reshape.7.kclip0_ref.kclip1_ref.kclip2_ref
  58.7 0.8 collective-permute-done.2.k1b_ref.v1b_ref
  59.5 29.9 %shard_map.46 = (bf16[512,1024]{1,0:T(8,128)(2,1)}, bf16[128,1024]{1,0:T(8,128)(2,1)}) custom-call(s32[512,1]{1,0:T(8,128)} %reshape_reshape.8.qclip_ref, s32[1,1536]{1,0:T(1,128)} %reshape_reshape.7.kclip0_ref.kclip1_ref.kclip2_ref, s32[1,1536]{1,0:T(1,128)} %reshape_reshape.7.kclip0_ref.kclip1_ref.kclip2_ref, ...), custom_call_target="tpu_custom_call" | custom-call | tf_op jit(solution)/shard_map/pallas_call | solution.py:99
  89.4 3.9 %fusion.2 = bf16[128,3,1024]{2,0,1:T(8,128)(2,1)S(1)} fusion(bf16[1024,3,1024]{2,0,1:T(8,128)(2,1)} %param.6, bf16[128,1024]{1,0:T(8,128)(2,1)} %get-tuple-element.8), kind=kOutput, calls=%fused_computation.2 | convolution fusion | flops 805699584 | bytes 7340032 | tf_op jit(solution)/shard_map/rd,mdc->mrc/dot_general | solution.py:286
  93.3 0.8 dynamic-slice_bitcast_fusion.2
  94.5 1.6 collective-permute-start.5
  96.1 5.6 %collective-permute-done.3 = bf16[3,128,256]{2,1,0:T(8,128)(2,1)S(1)} collective-permute-done((bf16[3,128,256]{2,1,0:T(8,128)(2,1)}, bf16[3,128,256]{2,1,0:T(8,128)(2,1)S(1)}, u32[]{:S(2)}, u32[]{:S(2)}) %collective-permute-start.3) | collective-permute-done | bytes 196640 | tf_op jit(solution)/shard_map/ppermute | solution.py:32
  101.8 1.3 collective-permute-done.5
  103.4 6.1 %collective-permute-start.6 = (bf16[2,512,256]{2,1,0:T(8,128)(2,1)S(1)}, bf16[2,512,256]{2,1,0:T(8,128)(2,1)}, u32[]{:S(2)}, u32[]{:S(2)}) collective-permute-start(bf16[2,512,256]{2,1,0:T(8,128)(2,1)S(1)} %bitcast.57), channel_id=1, source_target_pairs={{0,8},{1,9},{2,10},{3,11},{4,12},{5,13},{6,14},{7,15},{16,24},{17,... | collective-permute-start | bytes 1572872 | tf_op jit(solution)/shard_map/ppermute | solution.py:23
  109.5 4.0 %collective-permute-start.8 = (bf16[2,512,256]{2,1,0:T(8,128)(2,1)S(1)}, bf16[2,512,256]{2,1,0:T(8,128)(2,1)}, u32[]{:S(2)}, u32[]{:S(2)}) collective-permute-start(bf16[2,512,256]{2,1,0:T(8,128)(2,1)S(1)} %bitcast.58), channel_id=1, source_target_pairs={{0,4},{1,5},{2,6},{3,7},{4,8},{5,9},{6,10},{7,11},{8,12},{9,13},{1... | collective-permute-start | bytes 1572872 | tf_op jit(solution)/shard_map/ppermute | solution.py:23
  113.5 4.6 %collective-permute-done.6.k1_ref.v1_ref = bf16[2,512,256]{2,1,0:T(8,128)(2,1)} collective-permute-done((bf16[2,512,256]{2,1,0:T(8,128)(2,1)S(1)}, bf16[2,512,256]{2,1,0:T(8,128)(2,1)}, u32[]{:S(2)}, u32[]{:S(2)}) %collective-permute-start.6) | collective-permute-done | bytes 524320 | tf_op jit(solution)/shard_map/ppermute | solution.py:23
  118.2 17.3 %collective-permute-start.7 = (bf16[2,512,256]{2,1,0:T(8,128)(2,1)}, bf16[2,512,256]{2,1,0:T(8,128)(2,1)}, u32[]{:S(2)}, u32[]{:S(2)}) collective-permute-start(bf16[2,512,256]{2,1,0:T(8,128)(2,1)} %collective-permute-done.6.k1_ref.v1_ref), channel_id=1, source_target_pairs={{0,4},{1,5},{2,6},{3,7},{4,8},{5,9},{6,10},{7,11},{8,12},{9,13},{1... | collective-permute-start | bytes 1572872 | tf_op jit(solution)/shard_map/ppermute | solution.py:23
  135.6 0.9 copy.8.qclip_ref
  137.1 0.7 slice.26
  137.9 7.8 %collective-permute-done.7.k0_ref.v0_ref = bf16[2,512,256]{2,1,0:T(8,128)(2,1)} collective-permute-done((bf16[2,512,256]{2,1,0:T(8,128)(2,1)}, bf16[2,512,256]{2,1,0:T(8,128)(2,1)}, u32[]{:S(2)}, u32[]{:S(2)}) %collective-permute-start.7) | collective-permute-done | bytes 524320 | tf_op jit(solution)/shard_map/ppermute | solution.py:23
  145.7 6.8 %shard_map.47 = bf16[512,256]{1,0:T(8,128)(2,1)} custom-call(s32[512,1]{1,0:T(8,128)} %copy.8.qclip_ref, s32[1,2048]{1,0:T(1,128)} %bitcast.64, s32[1,2048]{1,0:T(1,128)} %bitcast.65, s32[1,2048]{1,0:T(1,128)} %bitcast.66, s32[1,2048]{1,0:T(1,128)} %bitcast.67, bf16[512,256]{1,0:T(8,128)(2,1)} %bitcast.62, ...), custom_call_target="tpu_custom_call" | custom-call | tf_op jit(solution)/shard_map/pallas_call | solution.py:207
  152.5 0.9 constant_dynamic-slice_fusion
  153.4 1.5 collective-permute-start.9
  155.3 1.4 collective-permute-start.11
  156.7 0.8 bitcast_dynamic-update-slice_fusion.14
  157.5 1.1 collective-permute-done.10
  158.6 0.9 bitcast_dynamic-update-slice_fusion.15
  160.2 12.9 %collective-permute-start.12 = (bf16[1,1024]{1,0:T(2,128)(2,1)S(1)}, bf16[1,1024]{1,0:T(2,128)(2,1)S(1)}, u32[]{:S(2)}, u32[]{:S(2)}) collective-permute-start(bf16[1,1024]{1,0:T(2,128)(2,1)S(1)} %slice.28), channel_id=1, source_target_pairs={{0,1},{1,2},{2,3},{3,4},{4,5},{5,6},{6,7},{7,8},{8,9},{9,10},{10,1... | collective-permute-start | bytes 6152 | tf_op jit(solution)/shard_map/ppermute | solution.py:23
  173.1 0.7 collective-permute-done.12
  173.9 0.8 maximum_select_fusion.lift_ref
  174.7 2.4 %shard_map.48 = bf16[512,1024]{1,0:T(8,128)(2,1)} custom-call(bf16[512,1024]{1,0:T(8,128)(2,1)} %get-tuple-element.7.fine_ref, bf16[128,1024]{1,0:T(8,128)(2,1)} %maximum_select_fusion.lift_ref), custom_call_target="tpu_custom_call" | custom-call | tf_op jit(solution)/shard_map/pallas_call | solution.py:138
  (41 shorter events, 2.8 us)
Async XLA Ops:
  0.0 159.7 %copy-start = (bf16[1024,1024]{1,0:T(8,128)(2,1)S(1)}, bf16[1024,1024]{1,0:T(8,128)(2,1)}, u32[]{:S(2)}) copy-start(bf16[1024,1024]{1,0:T(8,128)(2,1)} %param.7) | copy-start | bytes 6291460
  0.0 56.8 %copy-start.2 = (s32[2048]{0:T(1024)S(1)}, s32[2048]{0:T(1024)}, u32[]{:S(2)}) copy-start(s32[2048]{0:T(1024)} %param.5) | copy-start | bytes 24580
  3.3 48.7 %collective-permute-start = (bf16[2,512,1024]{2,1,0:T(8,128)(2,1)}, bf16[2,512,1024]{2,1,0:T(8,128)(2,1)}, u32[]{:S(2)}, u32[]{:S(2)}) collective-permute-start(bf16[2,512,1024]{2,1,0:T(8,128)(2,1)} %slice.25), channel_id=1, source_target_pairs={{0,2},{1,3},{2,4},{3,5},{4,6},{5,7},{6,8},{7,9},{8,10},{9,11},{10,... | collective-permute-start | bytes 6291464 | tf_op jit(solution)/shard_map/ppermute | solution.py:23
  6.4 52.3 %collective-permute-start.1 = (bf16[2,512,1024]{2,1,0:T(8,128)(2,1)}, bf16[2,512,1024]{2,1,0:T(8,128)(2,1)}, u32[]{:S(2)}, u32[]{:S(2)}) collective-permute-start(bf16[2,512,1024]{2,1,0:T(8,128)(2,1)} %slice.25), channel_id=1, source_target_pairs={{0,1},{2,3},{4,5},{6,7},{8,9},{10,11},{12,13},{14,15},{16,17},{18,... | collective-permute-start | bytes 6291464 | tf_op jit(solution)/shard_map/ppermute | solution.py:154
  52.0 7.6 %collective-permute-start.2 = (bf16[2,512,1024]{2,1,0:T(8,128)(2,1)}, bf16[2,512,1024]{2,1,0:T(8,128)(2,1)}, u32[]{:S(2)}, u32[]{:S(2)}) collective-permute-start(bf16[2,512,1024]{2,1,0:T(8,128)(2,1)} %collective-permute-done.k0_ref.v0_ref), channel_id=1, source_target_pairs={{1,0},{3,2},{5,4},{7,6},{9,8},{11,10},{13,12},{15,14},{17,16},{19,... | collective-permute-start | bytes 6291464 | tf_op jit(solution)/shard_map/ppermute | solution.py:154
  94.1 7.6 %collective-permute-start.3 = (bf16[3,128,256]{2,1,0:T(8,128)(2,1)}, bf16[3,128,256]{2,1,0:T(8,128)(2,1)S(1)}, u32[]{:S(2)}, u32[]{:S(2)}) collective-permute-start(bf16[3,128,256]{2,1,0:T(8,128)(2,1)} %get-tuple-element.13), channel_id=1, source_target_pairs={{0,3},{1,0},{2,1},{3,2},{4,7},{5,4},{6,5},{7,6},{8,11},{9,8},{10,9... | collective-permute-start | bytes 589832 | tf_op jit(solution)/shard_map/ppermute | solution.py:32
  94.5 7.3 %collective-permute-start.4 = (bf16[3,128,256]{2,1,0:T(8,128)(2,1)S(1)}, bf16[3,128,256]{2,1,0:T(8,128)(2,1)S(1)}, u32[]{:S(2)}, u32[]{:S(2)}) collective-permute-start(bf16[3,128,256]{2,1,0:T(8,128)(2,1)S(1)} %get-tuple-element.12), channel_id=1, source_target_pairs={{0,2},{1,3},{2,0},{3,1},{4,6},{5,7},{6,4},{7,5},{8,10},{9,11},{10,... | collective-permute-start | bytes 589832 | tf_op jit(solution)/shard_map/ppermute | solution.py:32
  94.5 8.6 %collective-permute-start.5 = (bf16[3,128,256]{2,1,0:T(8,128)(2,1)S(1)}, bf16[3,128,256]{2,1,0:T(8,128)(2,1)S(1)}, u32[]{:S(2)}, u32[]{:S(2)}) collective-permute-start(bf16[3,128,256]{2,1,0:T(8,128)(2,1)S(1)} %get-tuple-element.11), channel_id=1, source_target_pairs={{0,1},{1,2},{2,3},{3,0},{4,5},{5,6},{6,7},{7,4},{8,9},{9,10},{10,1... | collective-permute-start | bytes 589832 | tf_op jit(solution)/shard_map/ppermute | solution.py:32
  103.4 42.3 %copy-start.1 = (bf16[2,4,128,256]{3,2,1,0:T(8,128)(2,1)}, bf16[2,4,128,256]{3,2,1,0:T(8,128)(2,1)S(1)}, u32[]{:S(2)}) copy-start(bf16[2,4,128,256]{3,2,1,0:T(8,128)(2,1)S(1)} %copy.7) | copy-start | bytes 1572868
  103.4 14.8 %collective-permute-start.6 = (bf16[2,512,256]{2,1,0:T(8,128)(2,1)S(1)}, bf16[2,512,256]{2,1,0:T(8,128)(2,1)}, u32[]{:S(2)}, u32[]{:S(2)}) collective-permute-start(bf16[2,512,256]{2,1,0:T(8,128)(2,1)S(1)} %bitcast.57), channel_id=1, source_target_pairs={{0,8},{1,9},{2,10},{3,11},{4,12},{5,13},{6,14},{7,15},{16,24},{17,... | collective-permute-start | bytes 1572872 | tf_op jit(solution)/shard_map/ppermute | solution.py:23
  109.5 28.3 %collective-permute-start.8 = (bf16[2,512,256]{2,1,0:T(8,128)(2,1)S(1)}, bf16[2,512,256]{2,1,0:T(8,128)(2,1)}, u32[]{:S(2)}, u32[]{:S(2)}) collective-permute-start(bf16[2,512,256]{2,1,0:T(8,128)(2,1)S(1)} %bitcast.58), channel_id=1, source_target_pairs={{0,4},{1,5},{2,6},{3,7},{4,8},{5,9},{6,10},{7,11},{8,12},{9,13},{1... | collective-permute-start | bytes 1572872 | tf_op jit(solution)/shard_map/ppermute | solution.py:23
  118.2 27.5 %collective-permute-start.7 = (bf16[2,512,256]{2,1,0:T(8,128)(2,1)}, bf16[2,512,256]{2,1,0:T(8,128)(2,1)}, u32[]{:S(2)}, u32[]{:S(2)}) collective-permute-start(bf16[2,512,256]{2,1,0:T(8,128)(2,1)} %collective-permute-done.6.k1_ref.v1_ref), channel_id=1, source_target_pairs={{0,4},{1,5},{2,6},{3,7},{4,8},{5,9},{6,10},{7,11},{8,12},{9,13},{1... | collective-permute-start | bytes 1572872 | tf_op jit(solution)/shard_map/ppermute | solution.py:23
  153.4 4.1 %collective-permute-start.9 = (bf16[128,256]{1,0:T(8,128)(2,1)S(1)}, bf16[128,256]{1,0:T(8,128)(2,1)S(1)}, u32[]{:S(2)}, u32[]{:S(2)}) collective-permute-start(bf16[128,256]{1,0:T(8,128)(2,1)S(1)} %get-tuple-element.16), channel_id=1, source_target_pairs={{0,3},{1,0},{2,1},{3,2},{4,7},{5,4},{6,5},{7,6},{8,11},{9,8},{10,9... | collective-permute-start | bytes 196616 | tf_op jit(solution)/shard_map/ppermute | solution.py:32
  154.9 3.7 %collective-permute-start.10 = (bf16[128,256]{1,0:T(8,128)(2,1)S(1)}, bf16[128,256]{1,0:T(8,128)(2,1)S(1)}, u32[]{:S(2)}, u32[]{:S(2)}) collective-permute-start(bf16[128,256]{1,0:T(8,128)(2,1)S(1)} %get-tuple-element.15), channel_id=1, source_target_pairs={{0,2},{1,3},{2,0},{3,1},{4,6},{5,7},{6,4},{7,5},{8,10},{9,11},{10,... | collective-permute-start | bytes 196616 | tf_op jit(solution)/shard_map/ppermute | solution.py:32
  155.3 3.3 %collective-permute-start.11 = (bf16[128,256]{1,0:T(8,128)(2,1)S(1)}, bf16[128,256]{1,0:T(8,128)(2,1)S(1)}, u32[]{:S(2)}, u32[]{:S(2)}) collective-permute-start(bf16[128,256]{1,0:T(8,128)(2,1)S(1)} %get-tuple-element.14), channel_id=1, source_target_pairs={{0,1},{1,2},{2,3},{3,0},{4,5},{5,6},{6,7},{7,4},{8,9},{9,10},{10,1... | collective-permute-start | bytes 196616 | tf_op jit(solution)/shard_map/ppermute | solution.py:32
  160.2 13.6 %collective-permute-start.12 = (bf16[1,1024]{1,0:T(2,128)(2,1)S(1)}, bf16[1,1024]{1,0:T(2,128)(2,1)S(1)}, u32[]{:S(2)}, u32[]{:S(2)}) collective-permute-start(bf16[1,1024]{1,0:T(2,128)(2,1)S(1)} %slice.28), channel_id=1, source_target_pairs={{0,1},{1,2},{2,3},{3,4},{4,5},{5,6},{6,7},{7,8},{8,9},{9,10},{10,1... | collective-permute-start | bytes 6152 | tf_op jit(solution)/shard_map/ppermute | solution.py:23

commit v5 on v4

--- a/solution.py
+++ b/solution.py
@@ -309,18 +309,29 @@
         coarse_queries, earlier + [coarse_pairs], coarse_query_clip.reshape(group_rows, 1),
         coarse_key_clip.reshape(1, (CREACH + 1) * group_rows), CHEADS // QUARTERS,
     )
+    att_pad = jnp.concatenate([jnp.zeros_like(coarse_att[:1]), coarse_att], axis=0)
     shares = []
     for shift in range(QUARTERS):
         share = lax.dynamic_slice_in_dim(
-            coarse_att, ((quarter + shift) % QUARTERS) * coarse_rows, coarse_rows, 0
+            att_pad, ((quarter + shift) % QUARTERS) * coarse_rows, coarse_rows, 0
         )
         shares.append(share if shift == 0 else within_group(share, "seq", shift))
     att_rows = jnp.transpose(group_order(shares, quarter), (1, 0, 2)).reshape(
         coarse_rows, QUARTERS * quarter_width
     )
-    coarse_up = jnp.dot(att_rows, w_out, preferred_element_type=jnp.float32).astype(jnp.bfloat16)
-    carried = passed_along(coarse_up[-1:], "seq", 1)
-    previous = jnp.concatenate([carried, coarse_up[:-1]], axis=0)
+    count = lax.axis_size("seq")
+    group_last = coarse_att[-1:]
+    cross = []
+    for source_quarter in range(QUARTERS):
+        pairs = [
+            (source, source + QUARTERS - source_quarter)
+            for source in range(source_quarter, count - QUARTERS + source_quarter, QUARTERS)
+        ]
+        cross.append(lax.ppermute(group_last, "seq", pairs))
+    cross_row = jnp.concatenate(cross, axis=1)
+    first_row = jnp.where(quarter == 0, cross_row, att_rows[:1])
+    att_rows = jnp.concatenate([first_row, att_rows[1:]], axis=0)
+    previous = jnp.dot(att_rows, w_out, preferred_element_type=jnp.float32).astype(jnp.bfloat16)
     clip_before = jnp.concatenate([jnp.full((1,), -1, jnp.int32), clip_ids])
     prev_clip = lax.dynamic_slice_in_dim(clip_before, position * coarse_rows, coarse_rows, 0)
     joined = prev_clip == own_clip

time: 180 us -> 188 us (1.044)
  waiting for transfers between devices: 66.3 us -> 71.4 us
    ppermute x0 -> x4, starting transfers between devices: none -> 14 us  [body(): cross.append(lax.ppermute(group_last, 'seq', pairs))]
    ppermute x5 -> x4, starting transfers between devices: 43.5 us -> 30.6 us  [passed_along(): lax.ppermute(value, axis, [(source, source + steps) for source in range(f...]
    ppermute x6, waiting for transfers between devices: 8.03 us -> 13.8 us  [within_group(): return lax.ppermute(value, axis, pairs)]
    ppermute x5 -> x4, waiting for transfers between devices: 57.5 us -> 56.8 us  [passed_along(): lax.ppermute(value, axis, [(source, source + steps) for source in range(f...]
  transfers between devices with their start and end apart: 13 -> 16, of which waited for: 8 -> 9; matrix products, arithmetic and copies ran while one was open for 3% -> 4% of each run, Pallas kernels for 0% -> 0%
where the time goes in v5:
time: 188 us; the launch traced here: 184 us
  waiting for transfers between devices  71.4 us (38%)
  starting transfers between devices  55.3 us (29%)
  Pallas kernels  39.1 us (21%)
  local copies, waits for them, and re-layouts  12.6 us (7%)
  matrix products  5.22 us (3%)
    ppermute x4, waiting for transfers between devices, passed_along(): lax.ppermute(value, axis, [(source, source + steps) for source in range(f...  56.8 us
    ppermute x4, starting transfers between devices, passed_along(): lax.ppermute(value, axis, [(source, source + steps) for source in range(f...  30.6 us
    pallas_call x1, Pallas kernels, fine_attention(): pl.pallas_call(kernel, grid=(pairs, nq), in_specs=[pl.BlockSpec((tile, 1)...  29.9 us
    ppermute x4, starting transfers between devices, body(): cross.append(lax.ppermute(group_last, 'seq', pairs))  14 us
    ppermute x6, waiting for transfers between devices, within_group(): return lax.ppermute(value, axis, pairs)  13.8 us
    pallas_call x1, Pallas kernels, coarse_attention(): pl.pallas_call(kernel, grid=(heads, rows // tile), in_specs=[pl.BlockSpec...  6.82 us
    ppermute x2, starting transfers between devices, pair_swap(): lax.ppermute(value, axis, [(source, source + step) for source in range(st...  6.09 us
    ppermute x6, starting transfers between devices, within_group(): return lax.ppermute(value, axis, pairs)  4.65 us
  transfers between devices with their start and end apart: 16, of which 9 were waited for; matrix products, arithmetic and copies ran while one was open for 4% of the time, Pallas kernels for 0%

profile of v5, /device:TPU:7, one launch (start us, length us, event | category | flops | bytes accessed | tf_op | source)
XLA Modules:
  0.0 184.0 jit_solution(10039936214737770547)
XLA Ops:
  0.0 3.3 %slice.37 = bf16[2,512,1024]{2,1,0:T(8,128)(2,1)} slice(bf16[3,512,1024]{2,1,0:T(8,128)(2,1)} %bitcast.55), slice={[1:3], [0:512], [0:1024]} | slice | bytes 4194304 | tf_op jit(solution)/shard_map/slice | solution.py:269
  3.3 3.1 %collective-permute-start = (bf16[2,512,1024]{2,1,0:T(8,128)(2,1)}, bf16[2,512,1024]{2,1,0:T(8,128)(2,1)}, u32[]{:S(2)}, u32[]{:S(2)}) collective-permute-start(bf16[2,512,1024]{2,1,0:T(8,128)(2,1)} %slice.37), channel_id=1, source_target_pairs={{0,2},{1,3},{2,4},{3,5},{4,6},{5,7},{6,8},{7,9},{8,10},{9,11},{10,... | collective-permute-start | bytes 6291464 | tf_op jit(solution)/shard_map/ppermute | solution.py:23
  6.4 1.3 collective-permute-start.1
  7.7 44.3 %collective-permute-done.k0_ref.v0_ref = bf16[2,512,1024]{2,1,0:T(8,128)(2,1)} collective-permute-done((bf16[2,512,1024]{2,1,0:T(8,128)(2,1)}, bf16[2,512,1024]{2,1,0:T(8,128)(2,1)}, u32[]{:S(2)}, u32[]{:S(2)}) %collective-permute-start) | collective-permute-done | bytes 2097184 | tf_op jit(solution)/shard_map/ppermute | solution.py:23
  52.0 4.8 %collective-permute-start.2 = (bf16[2,512,1024]{2,1,0:T(8,128)(2,1)}, bf16[2,512,1024]{2,1,0:T(8,128)(2,1)}, u32[]{:S(2)}, u32[]{:S(2)}) collective-permute-start(bf16[2,512,1024]{2,1,0:T(8,128)(2,1)} %collective-permute-done.k0_ref.v0_ref), channel_id=1, source_target_pairs={{1,0},{3,2},{5,4},{7,6},{9,8},{11,10},{13,12},{15,14},{17,16},{19,... | collective-permute-start | bytes 6291464 | tf_op jit(solution)/shard_map/ppermute | solution.py:154
  56.9 0.8 reshape_reshape.8.qclip_ref
  58.0 0.8 reshape_reshape.7.kclip0_ref.kclip1_ref.kclip2_ref
  58.7 0.8 collective-permute-done.2.k1b_ref.v1b_ref
  59.5 29.9 %shard_map.46 = (bf16[512,1024]{1,0:T(8,128)(2,1)}, bf16[128,1024]{1,0:T(8,128)(2,1)}) custom-call(s32[512,1]{1,0:T(8,128)} %reshape_reshape.8.qclip_ref, s32[1,1536]{1,0:T(1,128)} %reshape_reshape.7.kclip0_ref.kclip1_ref.kclip2_ref, s32[1,1536]{1,0:T(1,128)} %reshape_reshape.7.kclip0_ref.kclip1_ref.kclip2_ref, ...), custom_call_target="tpu_custom_call" | custom-call | tf_op jit(solution)/shard_map/pallas_call | solution.py:99
  89.5 3.9 %fusion.2 = bf16[128,3,1024]{2,0,1:T(8,128)(2,1)S(1)} fusion(bf16[1024,3,1024]{2,0,1:T(8,128)(2,1)} %param.6, bf16[128,1024]{1,0:T(8,128)(2,1)} %get-tuple-element.8), kind=kOutput, calls=%fused_computation.2 | convolution fusion | flops 805699584 | bytes 7340032 | tf_op jit(solution)/shard_map/rd,mdc->mrc/dot_general | solution.py:286
  93.3 0.8 dynamic-slice_bitcast_fusion.2
  94.5 1.6 collective-permute-start.5
  96.1 5.6 %collective-permute-done.3 = bf16[3,128,256]{2,1,0:T(8,128)(2,1)S(1)} collective-permute-done((bf16[3,128,256]{2,1,0:T(8,128)(2,1)}, bf16[3,128,256]{2,1,0:T(8,128)(2,1)S(1)}, u32[]{:S(2)}, u32[]{:S(2)}) %collective-permute-start.3) | collective-permute-done | bytes 196640 | tf_op jit(solution)/shard_map/ppermute | solution.py:32
  101.8 1.3 collective-permute-done.5
  103.4 6.2 %collective-permute-start.6 = (bf16[2,512,256]{2,1,0:T(8,128)(2,1)S(1)}, bf16[2,512,256]{2,1,0:T(8,128)(2,1)}, u32[]{:S(2)}, u32[]{:S(2)}) collective-permute-start(bf16[2,512,256]{2,1,0:T(8,128)(2,1)S(1)} %bitcast.59), channel_id=1, source_target_pairs={{0,8},{1,9},{2,10},{3,11},{4,12},{5,13},{6,14},{7,15},{16,24},{17,... | collective-permute-start | bytes 1572872 | tf_op jit(solution)/shard_map/ppermute | solution.py:23
  109.6 4.0 %collective-permute-start.8 = (bf16[2,512,256]{2,1,0:T(8,128)(2,1)S(1)}, bf16[2,512,256]{2,1,0:T(8,128)(2,1)}, u32[]{:S(2)}, u32[]{:S(2)}) collective-permute-start(bf16[2,512,256]{2,1,0:T(8,128)(2,1)S(1)} %bitcast.60), channel_id=1, source_target_pairs={{0,4},{1,5},{2,6},{3,7},{4,8},{5,9},{6,10},{7,11},{8,12},{9,13},{1... | collective-permute-start | bytes 1572872 | tf_op jit(solution)/shard_map/ppermute | solution.py:23
  113.5 4.7 %collective-permute-done.6.k1_ref.v1_ref = bf16[2,512,256]{2,1,0:T(8,128)(2,1)} collective-permute-done((bf16[2,512,256]{2,1,0:T(8,128)(2,1)S(1)}, bf16[2,512,256]{2,1,0:T(8,128)(2,1)}, u32[]{:S(2)}, u32[]{:S(2)}) %collective-permute-start.6) | collective-permute-done | bytes 524320 | tf_op jit(solution)/shard_map/ppermute | solution.py:23
  118.2 17.3 %collective-permute-start.7 = (bf16[2,512,256]{2,1,0:T(8,128)(2,1)}, bf16[2,512,256]{2,1,0:T(8,128)(2,1)}, u32[]{:S(2)}, u32[]{:S(2)}) collective-permute-start(bf16[2,512,256]{2,1,0:T(8,128)(2,1)} %collective-permute-done.6.k1_ref.v1_ref), channel_id=1, source_target_pairs={{0,4},{1,5},{2,6},{3,7},{4,8},{5,9},{6,10},{7,11},{8,12},{9,13},{1... | collective-permute-start | bytes 1572872 | tf_op jit(solution)/shard_map/ppermute | solution.py:23
  135.6 0.9 copy.8.qclip_ref
  137.9 7.9 %collective-permute-done.7.k0_ref.v0_ref = bf16[2,512,256]{2,1,0:T(8,128)(2,1)} collective-permute-done((bf16[2,512,256]{2,1,0:T(8,128)(2,1)}, bf16[2,512,256]{2,1,0:T(8,128)(2,1)}, u32[]{:S(2)}, u32[]{:S(2)}) %collective-permute-start.7) | collective-permute-done | bytes 524320 | tf_op jit(solution)/shard_map/ppermute | solution.py:23
  145.7 6.8 %shard_map.47 = bf16[512,256]{1,0:T(8,128)(2,1)} custom-call(s32[512,1]{1,0:T(8,128)} %copy.8.qclip_ref, s32[1,2048]{1,0:T(1,128)} %bitcast.65, s32[1,2048]{1,0:T(1,128)} %bitcast.66, s32[1,2048]{1,0:T(1,128)} %bitcast.67, s32[1,2048]{1,0:T(1,128)} %bitcast.68, bf16[512,256]{1,0:T(8,128)(2,1)} %bitcast.64, ...), custom_call_target="tpu_custom_call" | custom-call | tf_op jit(solution)/shard_map/pallas_call | solution.py:207
  153.2 12.0 %collective-permute-start.12 = (bf16[1,256]{1,0:T(2,128)(2,1)S(1)}, bf16[1,256]{1,0:T(2,128)(2,1)S(1)}, u32[]{:S(2)}, u32[]{:S(2)}) collective-permute-start(bf16[1,256]{1,0:T(2,128)(2,1)S(1)} %slice.40), channel_id=1, source_target_pairs={{3,4},{7,8},{11,12},{19,20},{23,24},{27,28}} | collective-permute-start | bytes 1544 | tf_op jit(solution)/shard_map/ppermute | solution.py:330
  167.2 1.0 pad_dynamic-slice_fusion
  168.3 1.1 collective-permute-start.13
  169.4 0.9 fusion.11
  170.3 2.5 %collective-permute-done.13 = bf16[128,256]{1,0:T(8,128)(2,1)S(1)} collective-permute-done((bf16[128,256]{1,0:T(8,128)(2,1)S(1)}, bf16[128,256]{1,0:T(8,128)(2,1)S(1)}, u32[]{:S(2)}, u32[]{:S(2)}) %collective-permute-start.13) | collective-permute-done | bytes 65568 | tf_op jit(solution)/shard_map/ppermute | solution.py:32
  172.7 0.8 collective-permute-start.14
  173.6 3.1 %collective-permute-done.14 = bf16[128,256]{1,0:T(8,128)(2,1)S(1)} collective-permute-done((bf16[128,256]{1,0:T(8,128)(2,1)S(1)}, bf16[128,256]{1,0:T(8,128)(2,1)S(1)}, u32[]{:S(2)}, u32[]{:S(2)}) %collective-permute-start.14) | collective-permute-done | bytes 65568 | tf_op jit(solution)/shard_map/ppermute | solution.py:32
  177.4 1.3 collective-permute-done.15
  178.7 0.9 fusion.12
  180.3 1.3 fusion.5.lift_ref
  181.6 2.4 %shard_map.48 = bf16[512,1024]{1,0:T(8,128)(2,1)} custom-call(bf16[512,1024]{1,0:T(8,128)(2,1)} %get-tuple-element.7.fine_ref, bf16[128,1024]{1,0:T(8,128)(2,1)} %fusion.5.lift_ref), custom_call_target="tpu_custom_call" | custom-call | tf_op jit(solution)/shard_map/pallas_call | solution.py:138
  (50 shorter events, 6.4 us)
Async XLA Ops:
  0.0 180.3 %copy-start = (bf16[1024,1024]{1,0:T(8,128)(2,1)S(1)}, bf16[1024,1024]{1,0:T(8,128)(2,1)}, u32[]{:S(2)}) copy-start(bf16[1024,1024]{1,0:T(8,128)(2,1)} %param.7) | copy-start | bytes 6291460
  0.0 56.8 %copy-start.2 = (s32[2048]{0:T(1024)S(1)}, s32[2048]{0:T(1024)}, u32[]{:S(2)}) copy-start(s32[2048]{0:T(1024)} %param.5) | copy-start | bytes 24580
  3.3 48.7 %collective-permute-start = (bf16[2,512,1024]{2,1,0:T(8,128)(2,1)}, bf16[2,512,1024]{2,1,0:T(8,128)(2,1)}, u32[]{:S(2)}, u32[]{:S(2)}) collective-permute-start(bf16[2,512,1024]{2,1,0:T(8,128)(2,1)} %slice.37), channel_id=1, source_target_pairs={{0,2},{1,3},{2,4},{3,5},{4,6},{5,7},{6,8},{7,9},{8,10},{9,11},{10,... | collective-permute-start | bytes 6291464 | tf_op jit(solution)/shard_map/ppermute | solution.py:23
  6.4 52.3 %collective-permute-start.1 = (bf16[2,512,1024]{2,1,0:T(8,128)(2,1)}, bf16[2,512,1024]{2,1,0:T(8,128)(2,1)}, u32[]{:S(2)}, u32[]{:S(2)}) collective-permute-start(bf16[2,512,1024]{2,1,0:T(8,128)(2,1)} %slice.37), channel_id=1, source_target_pairs={{0,1},{2,3},{4,5},{6,7},{8,9},{10,11},{12,13},{14,15},{16,17},{18,... | collective-permute-start | bytes 6291464 | tf_op jit(solution)/shard_map/ppermute | solution.py:154
  52.0 7.6 %collective-permute-start.2 = (bf16[2,512,1024]{2,1,0:T(8,128)(2,1)}, bf16[2,512,1024]{2,1,0:T(8,128)(2,1)}, u32[]{:S(2)}, u32[]{:S(2)}) collective-permute-start(bf16[2,512,1024]{2,1,0:T(8,128)(2,1)} %collective-permute-done.k0_ref.v0_ref), channel_id=1, source_target_pairs={{1,0},{3,2},{5,4},{7,6},{9,8},{11,10},{13,12},{15,14},{17,16},{19,... | collective-permute-start | bytes 6291464 | tf_op jit(solution)/shard_map/ppermute | solution.py:154
  94.1 7.6 %collective-permute-start.3 = (bf16[3,128,256]{2,1,0:T(8,128)(2,1)}, bf16[3,128,256]{2,1,0:T(8,128)(2,1)S(1)}, u32[]{:S(2)}, u32[]{:S(2)}) collective-permute-start(bf16[3,128,256]{2,1,0:T(8,128)(2,1)} %get-tuple-element.13), channel_id=1, source_target_pairs={{0,3},{1,0},{2,1},{3,2},{4,7},{5,4},{6,5},{7,6},{8,11},{9,8},{10,9... | collective-permute-start | bytes 589832 | tf_op jit(solution)/shard_map/ppermute | solution.py:32
  94.5 7.3 %collective-permute-start.4 = (bf16[3,128,256]{2,1,0:T(8,128)(2,1)S(1)}, bf16[3,128,256]{2,1,0:T(8,128)(2,1)S(1)}, u32[]{:S(2)}, u32[]{:S(2)}) collective-permute-start(bf16[3,128,256]{2,1,0:T(8,128)(2,1)S(1)} %get-tuple-element.12), channel_id=1, source_target_pairs={{0,2},{1,3},{2,0},{3,1},{4,6},{5,7},{6,4},{7,5},{8,10},{9,11},{10,... | collective-permute-start | bytes 589832 | tf_op jit(solution)/shard_map/ppermute | solution.py:32
  94.5 8.6 %collective-permute-start.5 = (bf16[3,128,256]{2,1,0:T(8,128)(2,1)S(1)}, bf16[3,128,256]{2,1,0:T(8,128)(2,1)S(1)}, u32[]{:S(2)}, u32[]{:S(2)}) collective-permute-start(bf16[3,128,256]{2,1,0:T(8,128)(2,1)S(1)} %get-tuple-element.11), channel_id=1, source_target_pairs={{0,1},{1,2},{2,3},{3,0},{4,5},{5,6},{6,7},{7,4},{8,9},{9,10},{10,1... | collective-permute-start | bytes 589832 | tf_op jit(solution)/shard_map/ppermute | solution.py:32
  103.4 42.4 %copy-start.1 = (bf16[2,4,128,256]{3,2,1,0:T(8,128)(2,1)}, bf16[2,4,128,256]{3,2,1,0:T(8,128)(2,1)S(1)}, u32[]{:S(2)}) copy-start(bf16[2,4,128,256]{3,2,1,0:T(8,128)(2,1)S(1)} %copy.7) | copy-start | bytes 1572868
  103.4 14.8 %collective-permute-start.6 = (bf16[2,512,256]{2,1,0:T(8,128)(2,1)S(1)}, bf16[2,512,256]{2,1,0:T(8,128)(2,1)}, u32[]{:S(2)}, u32[]{:S(2)}) collective-permute-start(bf16[2,512,256]{2,1,0:T(8,128)(2,1)S(1)} %bitcast.59), channel_id=1, source_target_pairs={{0,8},{1,9},{2,10},{3,11},{4,12},{5,13},{6,14},{7,15},{16,24},{17,... | collective-permute-start | bytes 1572872 | tf_op jit(solution)/shard_map/ppermute | solution.py:23
  109.6 28.3 %collective-permute-start.8 = (bf16[2,512,256]{2,1,0:T(8,128)(2,1)S(1)}, bf16[2,512,256]{2,1,0:T(8,128)(2,1)}, u32[]{:S(2)}, u32[]{:S(2)}) collective-permute-start(bf16[2,512,256]{2,1,0:T(8,128)(2,1)S(1)} %bitcast.60), channel_id=1, source_target_pairs={{0,4},{1,5},{2,6},{3,7},{4,8},{5,9},{6,10},{7,11},{8,12},{9,13},{1... | collective-permute-start | bytes 1572872 | tf_op jit(solution)/shard_map/ppermute | solution.py:23
  118.2 27.5 %collective-permute-start.7 = (bf16[2,512,256]{2,1,0:T(8,128)(2,1)}, bf16[2,512,256]{2,1,0:T(8,128)(2,1)}, u32[]{:S(2)}, u32[]{:S(2)}) collective-permute-start(bf16[2,512,256]{2,1,0:T(8,128)(2,1)} %collective-permute-done.6.k1_ref.v1_ref), channel_id=1, source_target_pairs={{0,4},{1,5},{2,6},{3,7},{4,8},{5,9},{6,10},{7,11},{8,12},{9,13},{1... | collective-permute-start | bytes 1572872 | tf_op jit(solution)/shard_map/ppermute | solution.py:23
  153.2 26.7 %collective-permute-start.12 = (bf16[1,256]{1,0:T(2,128)(2,1)S(1)}, bf16[1,256]{1,0:T(2,128)(2,1)S(1)}, u32[]{:S(2)}, u32[]{:S(2)}) collective-permute-start(bf16[1,256]{1,0:T(2,128)(2,1)S(1)} %slice.40), channel_id=1, source_target_pairs={{3,4},{7,8},{11,12},{19,20},{23,24},{27,28}} | collective-permute-start | bytes 1544 | tf_op jit(solution)/shard_map/ppermute | solution.py:330
  165.2 14.8 %collective-permute-start.11 = (bf16[1,256]{1,0:T(2,128)(2,1)S(1)}, bf16[1,256]{1,0:T(2,128)(2,1)S(1)}, u32[]{:S(2)}, u32[]{:S(2)}) collective-permute-start(bf16[1,256]{1,0:T(2,128)(2,1)S(1)} %slice.40), channel_id=1, source_target_pairs={{2,4},{6,8},{10,12},{18,20},{22,24},{26,28}} | collective-permute-start | bytes 1544 | tf_op jit(solution)/shard_map/ppermute | solution.py:330
  165.9 14.1 %collective-permute-start.10 = (bf16[1,256]{1,0:T(2,128)(2,1)S(1)}, bf16[1,256]{1,0:T(2,128)(2,1)S(1)}, u32[]{:S(2)}, u32[]{:S(2)}) collective-permute-start(bf16[1,256]{1,0:T(2,128)(2,1)S(1)} %slice.40), channel_id=1, source_target_pairs={{1,4},{5,8},{9,12},{17,20},{21,24},{25,28}} | collective-permute-start | bytes 1544 | tf_op jit(solution)/shard_map/ppermute | solution.py:330
  166.6 13.4 %collective-permute-start.9 = (bf16[1,256]{1,0:T(2,128)(2,1)S(1)}, bf16[1,256]{1,0:T(2,128)(2,1)S(1)}, u32[]{:S(2)}, u32[]{:S(2)}) collective-permute-start(bf16[1,256]{1,0:T(2,128)(2,1)S(1)} %slice.40), channel_id=1, source_target_pairs={{0,4},{4,8},{8,12},{16,20},{20,24},{24,28}} | collective-permute-start | bytes 1544 | tf_op jit(solution)/shard_map/ppermute | solution.py:330
  168.3 4.5 %collective-permute-start.13 = (bf16[128,256]{1,0:T(8,128)(2,1)S(1)}, bf16[128,256]{1,0:T(8,128)(2,1)S(1)}, u32[]{:S(2)}, u32[]{:S(2)}) collective-permute-start(bf16[128,256]{1,0:T(8,128)(2,1)S(1)} %get-tuple-element.15), channel_id=1, source_target_pairs={{0,3},{1,0},{2,1},{3,2},{4,7},{5,4},{6,5},{7,6},{8,11},{9,8},{10,9... | collective-permute-start | bytes 196616 | tf_op jit(solution)/shard_map/ppermute | solution.py:32
  172.7 3.9 %collective-permute-start.14 = (bf16[128,256]{1,0:T(8,128)(2,1)S(1)}, bf16[128,256]{1,0:T(8,128)(2,1)S(1)}, u32[]{:S(2)}, u32[]{:S(2)}) collective-permute-start(bf16[128,256]{1,0:T(8,128)(2,1)S(1)} %get-tuple-element.16), channel_id=1, source_target_pairs={{0,2},{1,3},{2,0},{3,1},{4,6},{5,7},{6,4},{7,5},{8,10},{9,11},{10,... | collective-permute-start | bytes 196616 | tf_op jit(solution)/shard_map/ppermute | solution.py:32
  176.6 2.1 %collective-permute-start.15 = (bf16[128,256]{1,0:T(8,128)(2,1)S(1)}, bf16[128,256]{1,0:T(8,128)(2,1)S(1)}, u32[]{:S(2)}, u32[]{:S(2)}) collective-permute-start(bf16[128,256]{1,0:T(8,128)(2,1)S(1)} %get-tuple-element.14), channel_id=1, source_target_pairs={{0,1},{1,2},{2,3},{3,0},{4,5},{5,6},{6,7},{7,4},{8,9},{9,10},{10,1... | collective-permute-start | bytes 196616 | tf_op jit(solution)/shard_map/ppermute | solution.py:32

commit v6 on v4

--- a/solution.py
+++ b/solution.py
@@ -44,44 +44,49 @@
     zero = jnp.zeros_like(q)
     head_q = (jnp.where(low, q, zero), jnp.where(low, zero, q))
     qclip = qclip_ref[...]
-    keys = (k0_ref[...], k1_ref[...] + k1b_ref[...], k2_ref[...])
-    values = (v0_ref[...], v1_ref[...] + v1b_ref[...], v2_ref[...])
-    clips = (kclip0_ref, kclip1_ref, kclip2_ref)
     seg = k0_ref.shape[0]
-    qpos = pl.program_id(1) * tile + lax.broadcasted_iota(jnp.int32, (tile, seg), 0)
-    kpos = lax.broadcasted_iota(jnp.int32, (tile, seg), 1)
-    masks = []
-    for j in range(3):
-        allowed = clips[j][...] == qclip
-        if j == 2:
-            allowed = allowed & (kpos <= qpos)
-        masks.append(allowed)
-    results = []
-    for h in range(2):
-        scores = []
-        for j in range(3):
-            s = lax.dot_general(head_q[h], keys[j], (((1,), (1,)), ((), ())),
-                                preferred_element_type=jnp.float32)
-            scores.append(jnp.where(masks[j], s, -1e30))
-        top = jnp.max(scores[0], axis=1, keepdims=True)
-        for j in range(1, 3):
-            top = jnp.maximum(top, jnp.max(scores[j], axis=1, keepdims=True))
-        total = None
-        summed = None
-        for j in range(3):
-            w = jnp.exp(scores[j] - top)
-            part = jnp.sum(w, axis=1, keepdims=True)
-            pv = jnp.dot(w.astype(jnp.bfloat16), values[j], preferred_element_type=jnp.float32)
-            total = part if total is None else total + part
-            summed = pv if summed is None else summed + pv
-        results.append(summed / total)
-    out = jnp.where(low, results[0], results[1]).astype(out_ref.dtype)
-    out_ref[...] = out
-    rows = tile // POOL
-    pool_row = lax.broadcasted_iota(jnp.int32, (rows, tile), 0)
-    pool_col = lax.broadcasted_iota(jnp.int32, (rows, tile), 1)
-    pool_mat = jnp.where(pool_col // POOL == pool_row, 1.0 / POOL, 0.0).astype(jnp.bfloat16)
-    pool_ref[...] = jnp.dot(pool_mat, out, preferred_element_type=jnp.float32).astype(pool_ref.dtype)
+
+    def run(step):
+        own = (step + 1) * tile
+        keys = (k0_ref[...], k1_ref[...] + k1b_ref[...], k2_ref[0:own, :])
+        values = (v0_ref[...], v1_ref[...] + v1b_ref[...], v2_ref[0:own, :])
+        qpos = step * tile + lax.broadcasted_iota(jnp.int32, (tile, own), 0)
+        kpos = lax.broadcasted_iota(jnp.int32, (tile, own), 1)
+        masks = (
+            kclip0_ref[...] == qclip,
+            kclip1_ref[...] == qclip,
+            (kclip2_ref[:, 0:own] == qclip) & (kpos <= qpos),
+        )
+        results = []
+        for h in range(2):
+            scores = []
+            for j in range(3):
+                s = lax.dot_general(head_q[h], keys[j], (((1,), (1,)), ((), ())),
+                                    preferred_element_type=jnp.float32)
+                scores.append(jnp.where(masks[j], s, -1e30))
+            top = jnp.max(scores[0], axis=1, keepdims=True)
+            for j in range(1, 3):
+                top = jnp.maximum(top, jnp.max(scores[j], axis=1, keepdims=True))
+            total = None
+            summed = None
+            for j in range(3):
+                w = jnp.exp(scores[j] - top)
+                part = jnp.sum(w, axis=1, keepdims=True)
+                pv = jnp.dot(w.astype(jnp.bfloat16), values[j], preferred_element_type=jnp.float32)
+                total = part if total is None else total + part
+                summed = pv if summed is None else summed + pv
+            results.append(summed / total)
+        out = jnp.where(low, results[0], results[1]).astype(out_ref.dtype)
+        out_ref[...] = out
+        rows = tile // POOL
+        pool_row = lax.broadcasted_iota(jnp.int32, (rows, tile), 0)
+        pool_col = lax.broadcasted_iota(jnp.int32, (rows, tile), 1)
+        pool_mat = jnp.where(pool_col // POOL == pool_row, 1.0 / POOL, 0.0).astype(jnp.bfloat16)
+        pool_ref[...] = jnp.dot(pool_mat, out, preferred_element_type=jnp.float32).astype(
+            pool_ref.dtype)
+
+    for step in range(seg // tile):
+        pl.when(pl.program_id(1) == step)(functools.partial(run, step))
 
 
 def fine_attention(planes, prev0, prev1a, prev1b, qclip, kclip, heads):

time: 180 us -> 178 us (0.989)
  no operation moved by 1% of the time
where the time goes in v6:
time: 178 us; the launch traced here: 175 us
  waiting for transfers between devices  66.3 us (37%)
  starting transfers between devices  54.8 us (31%)
  Pallas kernels  37.4 us (21%)
  local copies, waits for them, and re-layouts  11.4 us (6%)
  matrix products  4.34 us (2%)
    ppermute x5, waiting for transfers between devices, passed_along(): lax.ppermute(value, axis, [(source, source + steps) for source in range(f...  57.4 us
    ppermute x5, starting transfers between devices, passed_along(): lax.ppermute(value, axis, [(source, source + steps) for source in range(f...  43.5 us
    pallas_call x1, Pallas kernels, fine_attention(): pl.pallas_call(kernel, grid=(pairs, nq), in_specs=[pl.BlockSpec((tile, 1)...  28.2 us
    ppermute x6, waiting for transfers between devices, within_group(): return lax.ppermute(value, axis, pairs)  8.03 us
    pallas_call x1, Pallas kernels, coarse_attention(): pl.pallas_call(kernel, grid=(heads, rows // tile), in_specs=[pl.BlockSpec...  6.8 us
    ppermute x2, starting transfers between devices, pair_swap(): lax.ppermute(value, axis, [(source, source + step) for source in range(st...  6.1 us
    ppermute x6, starting transfers between devices, within_group(): return lax.ppermute(value, axis, pairs)  5.21 us
    dot_general x1, matrix products, body(): jnp.einsum('rd,mdc->mrc', pooled, wplanes, preferred_element_type=jnp.flo...  3.87 us
  transfers between devices with their start and end apart: 13, of which 8 were waited for; matrix products, arithmetic and copies ran while one was open for 3% of the time, Pallas kernels for 0%

profile of v6, /device:TPU:7, one launch (start us, length us, event | category | flops | bytes accessed | tf_op | source)
XLA Modules:
  0.0 175.4 jit_solution(17243590207377158690)
XLA Ops:
  0.0 3.3 %slice.25 = bf16[2,512,1024]{2,1,0:T(8,128)(2,1)} slice(bf16[3,512,1024]{2,1,0:T(8,128)(2,1)} %bitcast.53), slice={[1:3], [0:512], [0:1024]} | slice | bytes 4194304 | tf_op jit(solution)/shard_map/slice | solution.py:274
  3.3 3.1 %collective-permute-start = (bf16[2,512,1024]{2,1,0:T(8,128)(2,1)}, bf16[2,512,1024]{2,1,0:T(8,128)(2,1)}, u32[]{:S(2)}, u32[]{:S(2)}) collective-permute-start(bf16[2,512,1024]{2,1,0:T(8,128)(2,1)} %slice.25), channel_id=1, source_target_pairs={{0,2},{1,3},{2,4},{3,5},{4,6},{5,7},{6,8},{7,9},{8,10},{9,11},{10,... | collective-permute-start | bytes 6291464 | tf_op jit(solution)/shard_map/ppermute | solution.py:23
  6.4 1.3 collective-permute-start.1
  7.7 44.3 %collective-permute-done.k0_ref.v0_ref = bf16[2,512,1024]{2,1,0:T(8,128)(2,1)} collective-permute-done((bf16[2,512,1024]{2,1,0:T(8,128)(2,1)}, bf16[2,512,1024]{2,1,0:T(8,128)(2,1)}, u32[]{:S(2)}, u32[]{:S(2)}) %collective-permute-start) | collective-permute-done | bytes 2097184 | tf_op jit(solution)/shard_map/ppermute | solution.py:23
  52.0 4.8 %collective-permute-start.2 = (bf16[2,512,1024]{2,1,0:T(8,128)(2,1)}, bf16[2,512,1024]{2,1,0:T(8,128)(2,1)}, u32[]{:S(2)}, u32[]{:S(2)}) collective-permute-start(bf16[2,512,1024]{2,1,0:T(8,128)(2,1)} %collective-permute-done.k0_ref.v0_ref), channel_id=1, source_target_pairs={{1,0},{3,2},{5,4},{7,6},{9,8},{11,10},{13,12},{15,14},{17,16},{19,... | collective-permute-start | bytes 6291464 | tf_op jit(solution)/shard_map/ppermute | solution.py:159
  56.9 0.8 reshape_reshape.8.qclip_ref
  58.0 0.8 reshape_reshape.7.kclip0_ref.kclip1_ref.kclip2_ref
  58.7 0.8 collective-permute-done.2.k1b_ref.v1b_ref
  59.5 28.2 %shard_map.46 = (bf16[512,1024]{1,0:T(8,128)(2,1)}, bf16[128,1024]{1,0:T(8,128)(2,1)}) custom-call(s32[512,1]{1,0:T(8,128)} %reshape_reshape.8.qclip_ref, s32[1,1536]{1,0:T(1,128)} %reshape_reshape.7.kclip0_ref.kclip1_ref.kclip2_ref, s32[1,1536]{1,0:T(1,128)} %reshape_reshape.7.kclip0_ref.kclip1_ref.kclip2_ref, ...), custom_call_target="tpu_custom_call" | custom-call | tf_op jit(solution)/shard_map/pallas_call | solution.py:104
  87.7 3.9 %fusion.2 = bf16[128,3,1024]{2,0,1:T(8,128)(2,1)S(1)} fusion(bf16[1024,3,1024]{2,0,1:T(8,128)(2,1)} %param.6, bf16[128,1024]{1,0:T(8,128)(2,1)} %get-tuple-element.8), kind=kOutput, calls=%fused_computation.2 | convolution fusion | flops 805699584 | bytes 7340032 | tf_op jit(solution)/shard_map/rd,mdc->mrc/dot_general | solution.py:291
  91.6 0.8 dynamic-slice_bitcast_fusion.2
  92.8 1.6 collective-permute-start.5
  94.4 5.6 %collective-permute-done.3 = bf16[3,128,256]{2,1,0:T(8,128)(2,1)S(1)} collective-permute-done((bf16[3,128,256]{2,1,0:T(8,128)(2,1)}, bf16[3,128,256]{2,1,0:T(8,128)(2,1)S(1)}, u32[]{:S(2)}, u32[]{:S(2)}) %collective-permute-start.3) | collective-permute-done | bytes 196640 | tf_op jit(solution)/shard_map/ppermute | solution.py:32
  100.1 1.3 collective-permute-done.5
  101.7 6.1 %collective-permute-start.6 = (bf16[2,512,256]{2,1,0:T(8,128)(2,1)S(1)}, bf16[2,512,256]{2,1,0:T(8,128)(2,1)}, u32[]{:S(2)}, u32[]{:S(2)}) collective-permute-start(bf16[2,512,256]{2,1,0:T(8,128)(2,1)S(1)} %bitcast.57), channel_id=1, source_target_pairs={{0,8},{1,9},{2,10},{3,11},{4,12},{5,13},{6,14},{7,15},{16,24},{17,... | collective-permute-start | bytes 1572872 | tf_op jit(solution)/shard_map/ppermute | solution.py:23
  107.8 4.0 %collective-permute-start.8 = (bf16[2,512,256]{2,1,0:T(8,128)(2,1)S(1)}, bf16[2,512,256]{2,1,0:T(8,128)(2,1)}, u32[]{:S(2)}, u32[]{:S(2)}) collective-permute-start(bf16[2,512,256]{2,1,0:T(8,128)(2,1)S(1)} %bitcast.58), channel_id=1, source_target_pairs={{0,4},{1,5},{2,6},{3,7},{4,8},{5,9},{6,10},{7,11},{8,12},{9,13},{1... | collective-permute-start | bytes 1572872 | tf_op jit(solution)/shard_map/ppermute | solution.py:23
  111.8 4.6 %collective-permute-done.6.k1_ref.v1_ref = bf16[2,512,256]{2,1,0:T(8,128)(2,1)} collective-permute-done((bf16[2,512,256]{2,1,0:T(8,128)(2,1)S(1)}, bf16[2,512,256]{2,1,0:T(8,128)(2,1)}, u32[]{:S(2)}, u32[]{:S(2)}) %collective-permute-start.6) | collective-permute-done | bytes 524320 | tf_op jit(solution)/shard_map/ppermute | solution.py:23
  116.4 17.3 %collective-permute-start.7 = (bf16[2,512,256]{2,1,0:T(8,128)(2,1)}, bf16[2,512,256]{2,1,0:T(8,128)(2,1)}, u32[]{:S(2)}, u32[]{:S(2)}) collective-permute-start(bf16[2,512,256]{2,1,0:T(8,128)(2,1)} %collective-permute-done.6.k1_ref.v1_ref), channel_id=1, source_target_pairs={{0,4},{1,5},{2,6},{3,7},{4,8},{5,9},{6,10},{7,11},{8,12},{9,13},{1... | collective-permute-start | bytes 1572872 | tf_op jit(solution)/shard_map/ppermute | solution.py:23
  133.9 0.9 copy.8.qclip_ref
  135.4 0.7 slice.26
  136.1 7.8 %collective-permute-done.7.k0_ref.v0_ref = bf16[2,512,256]{2,1,0:T(8,128)(2,1)} collective-permute-done((bf16[2,512,256]{2,1,0:T(8,128)(2,1)}, bf16[2,512,256]{2,1,0:T(8,128)(2,1)}, u32[]{:S(2)}, u32[]{:S(2)}) %collective-permute-start.7) | collective-permute-done | bytes 524320 | tf_op jit(solution)/shard_map/ppermute | solution.py:23
  144.0 6.8 %shard_map.47 = bf16[512,256]{1,0:T(8,128)(2,1)} custom-call(s32[512,1]{1,0:T(8,128)} %copy.8.qclip_ref, s32[1,2048]{1,0:T(1,128)} %bitcast.64, s32[1,2048]{1,0:T(1,128)} %bitcast.65, s32[1,2048]{1,0:T(1,128)} %bitcast.66, s32[1,2048]{1,0:T(1,128)} %bitcast.67, bf16[512,256]{1,0:T(8,128)(2,1)} %bitcast.62, ...), custom_call_target="tpu_custom_call" | custom-call | tf_op jit(solution)/shard_map/pallas_call | solution.py:212
  150.8 0.9 constant_dynamic-slice_fusion
  151.7 1.5 collective-permute-start.9
  153.6 1.3 collective-permute-start.11
  154.9 0.8 bitcast_dynamic-update-slice_fusion.14
  155.8 1.1 collective-permute-done.10
  156.9 0.9 bitcast_dynamic-update-slice_fusion.15
  158.5 12.9 %collective-permute-start.12 = (bf16[1,1024]{1,0:T(2,128)(2,1)S(1)}, bf16[1,1024]{1,0:T(2,128)(2,1)S(1)}, u32[]{:S(2)}, u32[]{:S(2)}) collective-permute-start(bf16[1,1024]{1,0:T(2,128)(2,1)S(1)} %slice.28), channel_id=1, source_target_pairs={{0,1},{1,2},{2,3},{3,4},{4,5},{5,6},{6,7},{7,8},{8,9},{9,10},{10,1... | collective-permute-start | bytes 6152 | tf_op jit(solution)/shard_map/ppermute | solution.py:23
  171.4 0.7 collective-permute-done.12
  172.1 0.8 maximum_select_fusion.lift_ref
  172.9 2.4 %shard_map.48 = bf16[512,1024]{1,0:T(8,128)(2,1)} custom-call(bf16[512,1024]{1,0:T(8,128)(2,1)} %get-tuple-element.7.fine_ref, bf16[128,1024]{1,0:T(8,128)(2,1)} %maximum_select_fusion.lift_ref), custom_call_target="tpu_custom_call" | custom-call | tf_op jit(solution)/shard_map/pallas_call | solution.py:143
  (41 shorter events, 2.9 us)
Async XLA Ops:
  0.0 158.0 %copy-start = (bf16[1024,1024]{1,0:T(8,128)(2,1)S(1)}, bf16[1024,1024]{1,0:T(8,128)(2,1)}, u32[]{:S(2)}) copy-start(bf16[1024,1024]{1,0:T(8,128)(2,1)} %param.7) | copy-start | bytes 6291460
  0.0 56.8 %copy-start.2 = (s32[2048]{0:T(1024)S(1)}, s32[2048]{0:T(1024)}, u32[]{:S(2)}) copy-start(s32[2048]{0:T(1024)} %param.5) | copy-start | bytes 24580
  3.3 48.7 %collective-permute-start = (bf16[2,512,1024]{2,1,0:T(8,128)(2,1)}, bf16[2,512,1024]{2,1,0:T(8,128)(2,1)}, u32[]{:S(2)}, u32[]{:S(2)}) collective-permute-start(bf16[2,512,1024]{2,1,0:T(8,128)(2,1)} %slice.25), channel_id=1, source_target_pairs={{0,2},{1,3},{2,4},{3,5},{4,6},{5,7},{6,8},{7,9},{8,10},{9,11},{10,... | collective-permute-start | bytes 6291464 | tf_op jit(solution)/shard_map/ppermute | solution.py:23
  6.4 52.3 %collective-permute-start.1 = (bf16[2,512,1024]{2,1,0:T(8,128)(2,1)}, bf16[2,512,1024]{2,1,0:T(8,128)(2,1)}, u32[]{:S(2)}, u32[]{:S(2)}) collective-permute-start(bf16[2,512,1024]{2,1,0:T(8,128)(2,1)} %slice.25), channel_id=1, source_target_pairs={{0,1},{2,3},{4,5},{6,7},{8,9},{10,11},{12,13},{14,15},{16,17},{18,... | collective-permute-start | bytes 6291464 | tf_op jit(solution)/shard_map/ppermute | solution.py:159
  52.0 7.6 %collective-permute-start.2 = (bf16[2,512,1024]{2,1,0:T(8,128)(2,1)}, bf16[2,512,1024]{2,1,0:T(8,128)(2,1)}, u32[]{:S(2)}, u32[]{:S(2)}) collective-permute-start(bf16[2,512,1024]{2,1,0:T(8,128)(2,1)} %collective-permute-done.k0_ref.v0_ref), channel_id=1, source_target_pairs={{1,0},{3,2},{5,4},{7,6},{9,8},{11,10},{13,12},{15,14},{17,16},{19,... | collective-permute-start | bytes 6291464 | tf_op jit(solution)/shard_map/ppermute | solution.py:159
  92.4 7.6 %collective-permute-start.3 = (bf16[3,128,256]{2,1,0:T(8,128)(2,1)}, bf16[3,128,256]{2,1,0:T(8,128)(2,1)S(1)}, u32[]{:S(2)}, u32[]{:S(2)}) collective-permute-start(bf16[3,128,256]{2,1,0:T(8,128)(2,1)} %get-tuple-element.13), channel_id=1, source_target_pairs={{0,3},{1,0},{2,1},{3,2},{4,7},{5,4},{6,5},{7,6},{8,11},{9,8},{10,9... | collective-permute-start | bytes 589832 | tf_op jit(solution)/shard_map/ppermute | solution.py:32
  92.8 7.3 %collective-permute-start.4 = (bf16[3,128,256]{2,1,0:T(8,128)(2,1)S(1)}, bf16[3,128,256]{2,1,0:T(8,128)(2,1)S(1)}, u32[]{:S(2)}, u32[]{:S(2)}) collective-permute-start(bf16[3,128,256]{2,1,0:T(8,128)(2,1)S(1)} %get-tuple-element.12), channel_id=1, source_target_pairs={{0,2},{1,3},{2,0},{3,1},{4,6},{5,7},{6,4},{7,5},{8,10},{9,11},{10,... | collective-permute-start | bytes 589832 | tf_op jit(solution)/shard_map/ppermute | solution.py:32
  92.8 8.6 %collective-permute-start.5 = (bf16[3,128,256]{2,1,0:T(8,128)(2,1)S(1)}, bf16[3,128,256]{2,1,0:T(8,128)(2,1)S(1)}, u32[]{:S(2)}, u32[]{:S(2)}) collective-permute-start(bf16[3,128,256]{2,1,0:T(8,128)(2,1)S(1)} %get-tuple-element.11), channel_id=1, source_target_pairs={{0,1},{1,2},{2,3},{3,0},{4,5},{5,6},{6,7},{7,4},{8,9},{9,10},{10,1... | collective-permute-start | bytes 589832 | tf_op jit(solution)/shard_map/ppermute | solution.py:32
  101.7 42.3 %copy-start.1 = (bf16[2,4,128,256]{3,2,1,0:T(8,128)(2,1)}, bf16[2,4,128,256]{3,2,1,0:T(8,128)(2,1)S(1)}, u32[]{:S(2)}) copy-start(bf16[2,4,128,256]{3,2,1,0:T(8,128)(2,1)S(1)} %copy.7) | copy-start | bytes 1572868
  101.7 14.8 %collective-permute-start.6 = (bf16[2,512,256]{2,1,0:T(8,128)(2,1)S(1)}, bf16[2,512,256]{2,1,0:T(8,128)(2,1)}, u32[]{:S(2)}, u32[]{:S(2)}) collective-permute-start(bf16[2,512,256]{2,1,0:T(8,128)(2,1)S(1)} %bitcast.57), channel_id=1, source_target_pairs={{0,8},{1,9},{2,10},{3,11},{4,12},{5,13},{6,14},{7,15},{16,24},{17,... | collective-permute-start | bytes 1572872 | tf_op jit(solution)/shard_map/ppermute | solution.py:23
  107.8 28.3 %collective-permute-start.8 = (bf16[2,512,256]{2,1,0:T(8,128)(2,1)S(1)}, bf16[2,512,256]{2,1,0:T(8,128)(2,1)}, u32[]{:S(2)}, u32[]{:S(2)}) collective-permute-start(bf16[2,512,256]{2,1,0:T(8,128)(2,1)S(1)} %bitcast.58), channel_id=1, source_target_pairs={{0,4},{1,5},{2,6},{3,7},{4,8},{5,9},{6,10},{7,11},{8,12},{9,13},{1... | collective-permute-start | bytes 1572872 | tf_op jit(solution)/shard_map/ppermute | solution.py:23
  116.4 27.5 %collective-permute-start.7 = (bf16[2,512,256]{2,1,0:T(8,128)(2,1)}, bf16[2,512,256]{2,1,0:T(8,128)(2,1)}, u32[]{:S(2)}, u32[]{:S(2)}) collective-permute-start(bf16[2,512,256]{2,1,0:T(8,128)(2,1)} %collective-permute-done.6.k1_ref.v1_ref), channel_id=1, source_target_pairs={{0,4},{1,5},{2,6},{3,7},{4,8},{5,9},{6,10},{7,11},{8,12},{9,13},{1... | collective-permute-start | bytes 1572872 | tf_op jit(solution)/shard_map/ppermute | solution.py:23
  151.7 4.1 %collective-permute-start.9 = (bf16[128,256]{1,0:T(8,128)(2,1)S(1)}, bf16[128,256]{1,0:T(8,128)(2,1)S(1)}, u32[]{:S(2)}, u32[]{:S(2)}) collective-permute-start(bf16[128,256]{1,0:T(8,128)(2,1)S(1)} %get-tuple-element.16), channel_id=1, source_target_pairs={{0,3},{1,0},{2,1},{3,2},{4,7},{5,4},{6,5},{7,6},{8,11},{9,8},{10,9... | collective-permute-start | bytes 196616 | tf_op jit(solution)/shard_map/ppermute | solution.py:32
  153.2 3.7 %collective-permute-start.10 = (bf16[128,256]{1,0:T(8,128)(2,1)S(1)}, bf16[128,256]{1,0:T(8,128)(2,1)S(1)}, u32[]{:S(2)}, u32[]{:S(2)}) collective-permute-start(bf16[128,256]{1,0:T(8,128)(2,1)S(1)} %get-tuple-element.15), channel_id=1, source_target_pairs={{0,2},{1,3},{2,0},{3,1},{4,6},{5,7},{6,4},{7,5},{8,10},{9,11},{10,... | collective-permute-start | bytes 196616 | tf_op jit(solution)/shard_map/ppermute | solution.py:32
  153.6 3.3 %collective-permute-start.11 = (bf16[128,256]{1,0:T(8,128)(2,1)S(1)}, bf16[128,256]{1,0:T(8,128)(2,1)S(1)}, u32[]{:S(2)}, u32[]{:S(2)}) collective-permute-start(bf16[128,256]{1,0:T(8,128)(2,1)S(1)} %get-tuple-element.14), channel_id=1, source_target_pairs={{0,1},{1,2},{2,3},{3,0},{4,5},{5,6},{6,7},{7,4},{8,9},{9,10},{10,1... | collective-permute-start | bytes 196616 | tf_op jit(solution)/shard_map/ppermute | solution.py:32
  158.5 13.6 %collective-permute-start.12 = (bf16[1,1024]{1,0:T(2,128)(2,1)S(1)}, bf16[1,1024]{1,0:T(2,128)(2,1)S(1)}, u32[]{:S(2)}, u32[]{:S(2)}) collective-permute-start(bf16[1,1024]{1,0:T(2,128)(2,1)S(1)} %slice.28), channel_id=1, source_target_pairs={{0,1},{1,2},{2,3},{3,4},{4,5},{5,6},{6,7},{7,8},{8,9},{9,10},{10,1... | collective-permute-start | bytes 6152 | tf_op jit(solution)/shard_map/ppermute | solution.py:23

commit v7 on v4

--- a/solution.py
+++ b/solution.py
@@ -32,48 +32,77 @@
     return lax.ppermute(value, axis, pairs)
 
 
-def fine_kernel(qclip_ref, kclip0_ref, kclip1_ref, kclip2_ref, q_ref,
-                k0_ref, v0_ref, k1_ref, v1_ref, k1b_ref, v1b_ref, k2_ref, v2_ref,
-                out_ref, pool_ref, *, scale):
-    tile = q_ref.shape[0]
+def head_queries(q_ref, scale):
     width = q_ref.shape[1]
-    half = width // 2
     q = q_ref[...] * jnp.asarray(scale, q_ref.dtype)
     lane = lax.broadcasted_iota(jnp.int32, (1, width), 1)
-    low = lane < half
+    low = lane < width // 2
     zero = jnp.zeros_like(q)
-    head_q = (jnp.where(low, q, zero), jnp.where(low, zero, q))
+    return (jnp.where(low, q, zero), jnp.where(low, zero, q)), lane, low
+
+
+def scores_of(query, keys, allowed):
+    s = lax.dot_general(query, keys, (((1,), (1,)), ((), ())), preferred_element_type=jnp.float32)
+    return jnp.where(allowed, s, -1e30)
+
+
+def own_kernel(qclip_ref, kclip_ref, q_ref, k_ref, v_ref, o_ref, st_ref, *, scale):
+    tile, width = q_ref.shape
+    head_q, lane, low = head_queries(q_ref, scale)
     qclip = qclip_ref[...]
-    keys = (k0_ref[...], k1_ref[...] + k1b_ref[...], k2_ref[...])
-    values = (v0_ref[...], v1_ref[...] + v1b_ref[...], v2_ref[...])
-    clips = (kclip0_ref, kclip1_ref, kclip2_ref)
-    seg = k0_ref.shape[0]
-    qpos = pl.program_id(1) * tile + lax.broadcasted_iota(jnp.int32, (tile, seg), 0)
-    kpos = lax.broadcasted_iota(jnp.int32, (tile, seg), 1)
-    masks = []
-    for j in range(3):
-        allowed = clips[j][...] == qclip
-        if j == 2:
-            allowed = allowed & (kpos <= qpos)
-        masks.append(allowed)
+    slot = lane // (width // 4)
+
+    def run(step):
+        own = (step + 1) * tile
+        keys = k_ref[0:own, :]
+        values = v_ref[0:own, :]
+        qpos = step * tile + lax.broadcasted_iota(jnp.int32, (tile, own), 0)
+        kpos = lax.broadcasted_iota(jnp.int32, (tile, own), 1)
+        allowed = (kclip_ref[:, 0:own] == qclip) & (kpos <= qpos)
+        outs, tops, totals = [], [], []
+        for h in range(2):
+            s = scores_of(head_q[h], keys, allowed)
+            top = jnp.max(s, axis=1, keepdims=True)
+            w = jnp.exp(s - top)
+            totals.append(jnp.sum(w, axis=1, keepdims=True))
+            tops.append(top)
+            outs.append(jnp.dot(w.astype(jnp.bfloat16), values, preferred_element_type=jnp.float32))
+        o_ref[...] = jnp.where(low, outs[0], outs[1])
+        st_ref[...] = jnp.where(
+            slot == 0, tops[0], jnp.where(slot == 1, totals[0], jnp.where(slot == 2, tops[1], totals[1]))
+        )
+
+    for step in range(k_ref.shape[0] // tile):
+        pl.when(pl.program_id(1) == step)(functools.partial(run, step))
+
+
+def remote_kernel(qclip_ref, kclip0_ref, kclip1_ref, q_ref, k0_ref, v0_ref, k1_ref, v1_ref,
+                  k1b_ref, v1b_ref, o_ref, st_ref, out_ref, pool_ref, *, scale):
+    tile, width = q_ref.shape
+    quarter = width // 4
+    head_q, lane, low = head_queries(q_ref, scale)
+    qclip = qclip_ref[...]
+    keys = (k0_ref[...], k1_ref[...] + k1b_ref[...])
+    values = (v0_ref[...], v1_ref[...] + v1b_ref[...])
+    masks = (kclip0_ref[...] == qclip, kclip1_ref[...] == qclip)
+    st = st_ref[...]
+    own_out = o_ref[...]
     results = []
     for h in range(2):
-        scores = []
-        for j in range(3):
-            s = lax.dot_general(head_q[h], keys[j], (((1,), (1,)), ((), ())),
-                                preferred_element_type=jnp.float32)
-            scores.append(jnp.where(masks[j], s, -1e30))
-        top = jnp.max(scores[0], axis=1, keepdims=True)
-        for j in range(1, 3):
+        own_top = st[:, 2 * h * quarter:2 * h * quarter + 1]
+        own_total = st[:, (2 * h + 1) * quarter:(2 * h + 1) * quarter + 1]
+        scores = [scores_of(head_q[h], keys[j], masks[j]) for j in range(2)]
+        top = own_top
+        for j in range(2):
             top = jnp.maximum(top, jnp.max(scores[j], axis=1, keepdims=True))
-        total = None
-        summed = None
-        for j in range(3):
+        rescale = jnp.exp(own_top - top)
+        total = own_total * rescale
+        summed = own_out * rescale
+        for j in range(2):
             w = jnp.exp(scores[j] - top)
-            part = jnp.sum(w, axis=1, keepdims=True)
-            pv = jnp.dot(w.astype(jnp.bfloat16), values[j], preferred_element_type=jnp.float32)
-            total = part if total is None else total + part
-            summed = pv if summed is None else summed + pv
+            total = total + jnp.sum(w, axis=1, keepdims=True)
+            summed = summed + jnp.dot(w.astype(jnp.bfloat16), values[j],
+                                      preferred_element_type=jnp.float32)
         results.append(summed / total)
     out = jnp.where(low, results[0], results[1]).astype(out_ref.dtype)
     out_ref[...] = out
@@ -84,42 +113,51 @@
     pool_ref[...] = jnp.dot(pool_mat, out, preferred_element_type=jnp.float32).astype(pool_ref.dtype)
 
 
-def fine_attention(planes, prev0, prev1a, prev1b, qclip, kclip, heads):
+def fine_attention(planes, prev0, prev1a, qclip, kclip, heads):
     _, tok, width = planes.shape
     head_dim = width // heads
     pair = 2 * head_dim
     pairs = width // pair
     tile = min(FINE_TILE, tok)
     nq = tok // tile
-    kernel = functools.partial(fine_kernel, scale=1.0 / math.sqrt(head_dim))
+    scale = 1.0 / math.sqrt(head_dim)
 
     def plane_spec(plane):
         return pl.BlockSpec((None, tok, pair), lambda h, i: (plane, 0, h))
 
+    qclip_spec = pl.BlockSpec((tile, 1), lambda h, i: (i, 0))
+    q_spec = pl.BlockSpec((None, tile, pair), lambda h, i: (0, i, h))
+    tile_spec = pl.BlockSpec((tile, pair), lambda h, i: (i, h))
+    own_out, own_stats = pl.pallas_call(
+        functools.partial(own_kernel, scale=scale),
+        grid=(pairs, nq),
+        in_specs=[qclip_spec, pl.BlockSpec((1, tok), lambda h, i: (0, 2)), q_spec,
+                  plane_spec(1), plane_spec(2)],
+        out_specs=[tile_spec, tile_spec],
+        out_shape=[jax.ShapeDtypeStruct((tok, width), jnp.float32)] * 2,
+    )(qclip, kclip, planes, planes, planes)
+    prev0, own_stats = lax.optimization_barrier((prev0, own_stats))
+    prev1b = pair_swap(prev0, "seq", True)
     return pl.pallas_call(
-        kernel,
+        functools.partial(remote_kernel, scale=scale),
         grid=(pairs, nq),
         in_specs=[
-            pl.BlockSpec((tile, 1), lambda h, i: (i, 0)),
+            qclip_spec,
             pl.BlockSpec((1, tok), lambda h, i: (0, 0)),
             pl.BlockSpec((1, tok), lambda h, i: (0, 1)),
-            pl.BlockSpec((1, tok), lambda h, i: (0, 2)),
-            pl.BlockSpec((None, tile, pair), lambda h, i: (0, i, h)),
+            q_spec,
             plane_spec(0), plane_spec(1),
             plane_spec(0), plane_spec(1),
             plane_spec(0), plane_spec(1),
-            plane_spec(1), plane_spec(2),
+            tile_spec, tile_spec,
         ],
-        out_specs=[
-            pl.BlockSpec((tile, pair), lambda h, i: (i, h)),
-            pl.BlockSpec((tile // POOL, pair), lambda h, i: (i, h)),
-        ],
+        out_specs=[tile_spec, pl.BlockSpec((tile // POOL, pair), lambda h, i: (i, h))],
         out_shape=[
             jax.ShapeDtypeStruct((tok, width), jnp.bfloat16),
             jax.ShapeDtypeStruct((tok // POOL, width), jnp.bfloat16),
         ],
-    )(qclip, kclip, kclip, kclip, planes, prev0, prev0, prev1a, prev1a, prev1b, prev1b,
-      planes, planes)
+    )(qclip, kclip, kclip, planes, prev0, prev0, prev1a, prev1a, prev1b, prev1b,
+      own_out, own_stats)
 
 
 def mix_kernel(fine_ref, lift_ref, out_ref):
@@ -269,7 +307,6 @@
     own_pairs = planes[1:]
     prev0 = passed_along(own_pairs, "seq", 2)
     prev1a = pair_swap(own_pairs, "seq", False)
-    prev1b = pair_swap(prev0, "seq", True)
     clip_front = jnp.concatenate([jnp.full((FREACH * coarse_rows,), -1, jnp.int32), clip_ids])
     key_clip = jnp.repeat(
         lax.dynamic_slice_in_dim(clip_front, position * coarse_rows, (FREACH + 1) * coarse_rows, 0),
@@ -278,7 +315,7 @@
     own_clip = lax.dynamic_slice_in_dim(clip_ids, position * coarse_rows, coarse_rows, 0)
     query_clip = jnp.repeat(own_clip, POOL)
     fine_out, pooled = fine_attention(
-        planes, prev0, prev1a, prev1b, query_clip.reshape(tok_count, 1),
+        planes, prev0, prev1a, query_clip.reshape(tok_count, 1),
         key_clip.reshape(1, (FREACH + 1) * tok_count), FHEADS,
     )
     quarter_width = w_coarse.shape[2] // QUARTERS

time: 180 us -> 188 us (1.044)
  Pallas kernels: 39.1 us -> 64.5 us
  waiting for transfers between devices: 66.3 us -> 49 us
    pallas_call x1 -> x2, Pallas kernels: 29.9 us -> 55.3 us  [the longest x1 38 us: fine_attention(): pl.pallas_call(functools.partial(remote_kernel, scale=scale), grid=(pairs...]
    ppermute x5, waiting for transfers between devices: 57.5 us -> 38.2 us  [passed_along(): lax.ppermute(value, axis, [(source, source + steps) for source in range(f...]
    ppermute x2, waiting for transfers between devices: 0.81 us -> 2.76 us  [pair_swap(): lax.ppermute(value, axis, [(source, source + step) for source in range(st...]
  transfers between devices with their start and end apart: 13 -> 13, of which waited for: 8 -> 8; matrix products, arithmetic and copies ran while one was open for 3% -> 3% of each run, Pallas kernels for 0% -> 9%
where the time goes in v7:
time: 188 us; the launch traced here: 185 us
  Pallas kernels  64.5 us (34%)
  starting transfers between devices  54.8 us (29%)
  waiting for transfers between devices  49 us (26%)
  local copies, waits for them, and re-layouts  11.4 us (6%)
  matrix products  4.34 us (2%)
    ppermute x5, starting transfers between devices, passed_along(): lax.ppermute(value, axis, [(source, source + steps) for source in range(f...  43.5 us
    ppermute x5, waiting for transfers between devices, passed_along(): lax.ppermute(value, axis, [(source, source + steps) for source in range(f...  38.2 us
    pallas_call x1, Pallas kernels, fine_attention(): pl.pallas_call(functools.partial(remote_kernel, scale=scale), grid=(pairs...  38 us
    pallas_call x1, Pallas kernels, fine_attention(): pl.pallas_call(functools.partial(own_kernel, scale=scale), grid=(pairs, n...  17.3 us
    ppermute x6, waiting for transfers between devices, within_group(): return lax.ppermute(value, axis, pairs)  8.03 us
    pallas_call x1, Pallas kernels, coarse_attention(): pl.pallas_call(kernel, grid=(heads, rows // tile), in_specs=[pl.BlockSpec...  6.8 us
    ppermute x2, starting transfers between devices, pair_swap(): lax.ppermute(value, axis, [(source, source + step) for source in range(st...  6.09 us
    ppermute x6, starting transfers between devices, within_group(): return lax.ppermute(value, axis, pairs)  5.21 us
  transfers between devices with their start and end apart: 13, of which 8 were waited for; matrix products, arithmetic and copies ran while one was open for 3% of the time, Pallas kernels for 9%

profile of v7, /device:TPU:7, one launch (start us, length us, event | category | flops | bytes accessed | tf_op | source)
XLA Modules:
  0.0 185.2 jit_solution(1365106932303507570)
XLA Ops:
  0.0 3.3 %slice.25 = bf16[2,512,1024]{2,1,0:T(8,128)(2,1)} slice(bf16[3,512,1024]{2,1,0:T(8,128)(2,1)} %bitcast.53), slice={[1:3], [0:512], [0:1024]} | slice | bytes 4194304 | tf_op jit(solution)/shard_map/slice | solution.py:307
  3.3 3.1 %collective-permute-start = (bf16[2,512,1024]{2,1,0:T(8,128)(2,1)}, bf16[2,512,1024]{2,1,0:T(8,128)(2,1)}, u32[]{:S(2)}, u32[]{:S(2)}) collective-permute-start(bf16[2,512,1024]{2,1,0:T(8,128)(2,1)} %slice.25), channel_id=1, source_target_pairs={{0,2},{1,3},{2,4},{3,5},{4,6},{5,7},{6,8},{7,9},{8,10},{9,11},{10,... | collective-permute-start | bytes 6291464 | tf_op jit(solution)/shard_map/ppermute | solution.py:23
  6.4 1.3 collective-permute-start.1
  7.9 0.8 reshape_reshape.8.qclip_ref
  8.9 0.8 reshape_reshape.7.kclip_ref.kclip0_ref.kclip1_ref
  9.7 17.3 %shard_map.46 = (f32[512,1024]{1,0:T(8,128)}, f32[512,1024]{1,0:T(8,128)}) custom-call(s32[512,1]{1,0:T(8,128)} %reshape_reshape.8.qclip_ref, s32[1,1536]{1,0:T(1,128)} %reshape_reshape.7.kclip_ref.kclip0_ref.kclip1_ref, bf16[3,512,1024]{2,1,0:T(8,128)(2,1)} %bitcast.54, bf16[3,512,1024]{2,1,0:T(8,128)(2,1)} %bitcast.55, bf16[3,512,1024]{2,1,0:T(8,128)(2,1)} %bitcast.56), custom_call_target="tpu_custom_call" | custom-call | tf_op jit(solution)/shard_map/pallas_call | solution.py:131
  27.0 25.0 %collective-permute-done.k0_ref.v0_ref = bf16[2,512,1024]{2,1,0:T(8,128)(2,1)} collective-permute-done((bf16[2,512,1024]{2,1,0:T(8,128)(2,1)}, bf16[2,512,1024]{2,1,0:T(8,128)(2,1)}, u32[]{:S(2)}, u32[]{:S(2)}) %collective-permute-start) | collective-permute-done | bytes 2097184 | tf_op jit(solution)/shard_map/ppermute | solution.py:23
  52.0 4.8 %collective-permute-start.2 = (bf16[2,512,1024]{2,1,0:T(8,128)(2,1)}, bf16[2,512,1024]{2,1,0:T(8,128)(2,1)}, u32[]{:S(2)}, u32[]{:S(2)}) collective-permute-start(bf16[2,512,1024]{2,1,0:T(8,128)(2,1)} %collective-permute-done.k0_ref.v0_ref), channel_id=1, source_target_pairs={{1,0},{3,2},{5,4},{7,6},{9,8},{11,10},{13,12},{15,14},{17,16},{19,... | collective-permute-start | bytes 6291464 | tf_op jit(solution)/shard_map/ppermute | solution.py:192
  56.8 2.8 %collective-permute-done.2.k1b_ref.v1b_ref = bf16[2,512,1024]{2,1,0:T(8,128)(2,1)} collective-permute-done((bf16[2,512,1024]{2,1,0:T(8,128)(2,1)}, bf16[2,512,1024]{2,1,0:T(8,128)(2,1)}, u32[]{:S(2)}, u32[]{:S(2)}) %collective-permute-start.2) | collective-permute-done | bytes 2097184 | tf_op jit(solution)/shard_map/ppermute | solution.py:192
  59.5 38.0 %shard_map.47 = (bf16[512,1024]{1,0:T(8,128)(2,1)}, bf16[128,1024]{1,0:T(8,128)(2,1)}) custom-call(s32[512,1]{1,0:T(8,128)} %reshape_reshape.8.qclip_ref, s32[1,1536]{1,0:T(1,128)} %reshape_reshape.7.kclip_ref.kclip0_ref.kclip1_ref, s32[1,1536]{1,0:T(1,128)} %reshape_reshape.7.kclip_ref.kclip0_ref.kclip1_ref, bf16[3,512,1024]{2,1,0:T(8,128)(2,1)} %bitcast.57, ...), custom_call_target="tpu_custom_call" | custom-call | tf_op jit(solution)/shard_map/pallas_call | solution.py:141
  97.5 3.9 %fusion.2 = bf16[128,3,1024]{2,0,1:T(8,128)(2,1)S(1)} fusion(bf16[1024,3,1024]{2,0,1:T(8,128)(2,1)} %param.6, bf16[128,1024]{1,0:T(8,128)(2,1)} %get-tuple-element.16), kind=kOutput, calls=%fused_computation.2 | convolution fusion | flops 805699584 | bytes 7340032 | tf_op jit(solution)/shard_map/rd,mdc->mrc/dot_general | solution.py:323
  101.4 0.8 dynamic-slice_bitcast_fusion.2
  102.5 1.6 collective-permute-start.5
  104.2 5.6 %collective-permute-done.3 = bf16[3,128,256]{2,1,0:T(8,128)(2,1)S(1)} collective-permute-done((bf16[3,128,256]{2,1,0:T(8,128)(2,1)}, bf16[3,128,256]{2,1,0:T(8,128)(2,1)S(1)}, u32[]{:S(2)}, u32[]{:S(2)}) %collective-permute-start.3) | collective-permute-done | bytes 196640 | tf_op jit(solution)/shard_map/ppermute | solution.py:32
  109.8 1.3 collective-permute-done.5
  111.5 6.1 %collective-permute-start.6 = (bf16[2,512,256]{2,1,0:T(8,128)(2,1)S(1)}, bf16[2,512,256]{2,1,0:T(8,128)(2,1)}, u32[]{:S(2)}, u32[]{:S(2)}) collective-permute-start(bf16[2,512,256]{2,1,0:T(8,128)(2,1)S(1)} %bitcast.58), channel_id=1, source_target_pairs={{0,8},{1,9},{2,10},{3,11},{4,12},{5,13},{6,14},{7,15},{16,24},{17,... | collective-permute-start | bytes 1572872 | tf_op jit(solution)/shard_map/ppermute | solution.py:23
  117.6 4.0 %collective-permute-start.8 = (bf16[2,512,256]{2,1,0:T(8,128)(2,1)S(1)}, bf16[2,512,256]{2,1,0:T(8,128)(2,1)}, u32[]{:S(2)}, u32[]{:S(2)}) collective-permute-start(bf16[2,512,256]{2,1,0:T(8,128)(2,1)S(1)} %bitcast.59), channel_id=1, source_target_pairs={{0,4},{1,5},{2,6},{3,7},{4,8},{5,9},{6,10},{7,11},{8,12},{9,13},{1... | collective-permute-start | bytes 1572872 | tf_op jit(solution)/shard_map/ppermute | solution.py:23
  121.6 4.6 %collective-permute-done.6.k1_ref.v1_ref = bf16[2,512,256]{2,1,0:T(8,128)(2,1)} collective-permute-done((bf16[2,512,256]{2,1,0:T(8,128)(2,1)S(1)}, bf16[2,512,256]{2,1,0:T(8,128)(2,1)}, u32[]{:S(2)}, u32[]{:S(2)}) %collective-permute-start.6) | collective-permute-done | bytes 524320 | tf_op jit(solution)/shard_map/ppermute | solution.py:23
  126.2 17.3 %collective-permute-start.7 = (bf16[2,512,256]{2,1,0:T(8,128)(2,1)}, bf16[2,512,256]{2,1,0:T(8,128)(2,1)}, u32[]{:S(2)}, u32[]{:S(2)}) collective-permute-start(bf16[2,512,256]{2,1,0:T(8,128)(2,1)} %collective-permute-done.6.k1_ref.v1_ref), channel_id=1, source_target_pairs={{0,4},{1,5},{2,6},{3,7},{4,8},{5,9},{6,10},{7,11},{8,12},{9,13},{1... | collective-permute-start | bytes 1572872 | tf_op jit(solution)/shard_map/ppermute | solution.py:23
  143.6 0.9 copy.9.qclip_ref
  145.9 7.9 %collective-permute-done.7.k0_ref.v0_ref = bf16[2,512,256]{2,1,0:T(8,128)(2,1)} collective-permute-done((bf16[2,512,256]{2,1,0:T(8,128)(2,1)}, bf16[2,512,256]{2,1,0:T(8,128)(2,1)}, u32[]{:S(2)}, u32[]{:S(2)}) %collective-permute-start.7) | collective-permute-done | bytes 524320 | tf_op jit(solution)/shard_map/ppermute | solution.py:23
  153.8 6.8 %shard_map.48 = bf16[512,256]{1,0:T(8,128)(2,1)} custom-call(s32[512,1]{1,0:T(8,128)} %copy.9.qclip_ref, s32[1,2048]{1,0:T(1,128)} %bitcast.65, s32[1,2048]{1,0:T(1,128)} %bitcast.66, s32[1,2048]{1,0:T(1,128)} %bitcast.67, s32[1,2048]{1,0:T(1,128)} %bitcast.68, bf16[512,256]{1,0:T(8,128)(2,1)} %bitcast.63, ...), custom_call_target="tpu_custom_call" | custom-call | tf_op jit(solution)/shard_map/pallas_call | solution.py:245
  160.6 0.9 constant_dynamic-slice_fusion
  161.5 1.5 collective-permute-start.9
  163.4 1.3 collective-permute-start.11
  164.7 0.8 bitcast_dynamic-update-slice_fusion.14
  165.6 1.1 collective-permute-done.10
  166.7 0.9 bitcast_dynamic-update-slice_fusion.15
  168.3 12.9 %collective-permute-start.12 = (bf16[1,1024]{1,0:T(2,128)(2,1)S(1)}, bf16[1,1024]{1,0:T(2,128)(2,1)S(1)}, u32[]{:S(2)}, u32[]{:S(2)}) collective-permute-start(bf16[1,1024]{1,0:T(2,128)(2,1)S(1)} %slice.28), channel_id=1, source_target_pairs={{0,1},{1,2},{2,3},{3,4},{4,5},{5,6},{6,7},{7,8},{8,9},{9,10},{10,1... | collective-permute-start | bytes 6152 | tf_op jit(solution)/shard_map/ppermute | solution.py:23
  181.2 0.7 collective-permute-done.12
  181.9 0.8 maximum_select_fusion.lift_ref
  182.7 2.4 %shard_map.49 = bf16[512,1024]{1,0:T(8,128)(2,1)} custom-call(bf16[512,1024]{1,0:T(8,128)(2,1)} %get-tuple-element.15.fine_ref, bf16[128,1024]{1,0:T(8,128)(2,1)} %maximum_select_fusion.lift_ref), custom_call_target="tpu_custom_call" | custom-call | tf_op jit(solution)/shard_map/pallas_call | solution.py:176
  (42 shorter events, 3.6 us)
Async XLA Ops:
  0.0 167.8 %copy-start = (bf16[1024,1024]{1,0:T(8,128)(2,1)S(1)}, bf16[1024,1024]{1,0:T(8,128)(2,1)}, u32[]{:S(2)}) copy-start(bf16[1024,1024]{1,0:T(8,128)(2,1)} %param.7) | copy-start | bytes 6291460
  0.0 7.7 %copy-start.2 = (s32[2048]{0:T(1024)S(1)}, s32[2048]{0:T(1024)}, u32[]{:S(2)}) copy-start(s32[2048]{0:T(1024)} %param.5) | copy-start | bytes 24580
  3.3 48.7 %collective-permute-start = (bf16[2,512,1024]{2,1,0:T(8,128)(2,1)}, bf16[2,512,1024]{2,1,0:T(8,128)(2,1)}, u32[]{:S(2)}, u32[]{:S(2)}) collective-permute-start(bf16[2,512,1024]{2,1,0:T(8,128)(2,1)} %slice.25), channel_id=1, source_target_pairs={{0,2},{1,3},{2,4},{3,5},{4,6},{5,7},{6,8},{7,9},{8,10},{9,11},{10,... | collective-permute-start | bytes 6291464 | tf_op jit(solution)/shard_map/ppermute | solution.py:23
  6.4 50.4 %collective-permute-start.1 = (bf16[2,512,1024]{2,1,0:T(8,128)(2,1)}, bf16[2,512,1024]{2,1,0:T(8,128)(2,1)}, u32[]{:S(2)}, u32[]{:S(2)}) collective-permute-start(bf16[2,512,1024]{2,1,0:T(8,128)(2,1)} %slice.25), channel_id=1, source_target_pairs={{0,1},{2,3},{4,5},{6,7},{8,9},{10,11},{12,13},{14,15},{16,17},{18,... | collective-permute-start | bytes 6291464 | tf_op jit(solution)/shard_map/ppermute | solution.py:192
  52.0 7.6 %collective-permute-start.2 = (bf16[2,512,1024]{2,1,0:T(8,128)(2,1)}, bf16[2,512,1024]{2,1,0:T(8,128)(2,1)}, u32[]{:S(2)}, u32[]{:S(2)}) collective-permute-start(bf16[2,512,1024]{2,1,0:T(8,128)(2,1)} %collective-permute-done.k0_ref.v0_ref), channel_id=1, source_target_pairs={{1,0},{3,2},{5,4},{7,6},{9,8},{11,10},{13,12},{15,14},{17,16},{19,... | collective-permute-start | bytes 6291464 | tf_op jit(solution)/shard_map/ppermute | solution.py:192
  102.2 7.6 %collective-permute-start.3 = (bf16[3,128,256]{2,1,0:T(8,128)(2,1)}, bf16[3,128,256]{2,1,0:T(8,128)(2,1)S(1)}, u32[]{:S(2)}, u32[]{:S(2)}) collective-permute-start(bf16[3,128,256]{2,1,0:T(8,128)(2,1)} %get-tuple-element.21), channel_id=1, source_target_pairs={{0,3},{1,0},{2,1},{3,2},{4,7},{5,4},{6,5},{7,6},{8,11},{9,8},{10,9... | collective-permute-start | bytes 589832 | tf_op jit(solution)/shard_map/ppermute | solution.py:32
  102.5 7.3 %collective-permute-start.4 = (bf16[3,128,256]{2,1,0:T(8,128)(2,1)S(1)}, bf16[3,128,256]{2,1,0:T(8,128)(2,1)S(1)}, u32[]{:S(2)}, u32[]{:S(2)}) collective-permute-start(bf16[3,128,256]{2,1,0:T(8,128)(2,1)S(1)} %get-tuple-element.20), channel_id=1, source_target_pairs={{0,2},{1,3},{2,0},{3,1},{4,6},{5,7},{6,4},{7,5},{8,10},{9,11},{10,... | collective-permute-start | bytes 589832 | tf_op jit(solution)/shard_map/ppermute | solution.py:32
  102.5 8.6 %collective-permute-start.5 = (bf16[3,128,256]{2,1,0:T(8,128)(2,1)S(1)}, bf16[3,128,256]{2,1,0:T(8,128)(2,1)S(1)}, u32[]{:S(2)}, u32[]{:S(2)}) collective-permute-start(bf16[3,128,256]{2,1,0:T(8,128)(2,1)S(1)} %get-tuple-element.19), channel_id=1, source_target_pairs={{0,1},{1,2},{2,3},{3,0},{4,5},{5,6},{6,7},{7,4},{8,9},{9,10},{10,1... | collective-permute-start | bytes 589832 | tf_op jit(solution)/shard_map/ppermute | solution.py:32
  111.4 42.3 %copy-start.1 = (bf16[2,4,128,256]{3,2,1,0:T(8,128)(2,1)}, bf16[2,4,128,256]{3,2,1,0:T(8,128)(2,1)S(1)}, u32[]{:S(2)}) copy-start(bf16[2,4,128,256]{3,2,1,0:T(8,128)(2,1)S(1)} %copy.8) | copy-start | bytes 1572868
  111.5 14.8 %collective-permute-start.6 = (bf16[2,512,256]{2,1,0:T(8,128)(2,1)S(1)}, bf16[2,512,256]{2,1,0:T(8,128)(2,1)}, u32[]{:S(2)}, u32[]{:S(2)}) collective-permute-start(bf16[2,512,256]{2,1,0:T(8,128)(2,1)S(1)} %bitcast.58), channel_id=1, source_target_pairs={{0,8},{1,9},{2,10},{3,11},{4,12},{5,13},{6,14},{7,15},{16,24},{17,... | collective-permute-start | bytes 1572872 | tf_op jit(solution)/shard_map/ppermute | solution.py:23
  117.6 28.3 %collective-permute-start.8 = (bf16[2,512,256]{2,1,0:T(8,128)(2,1)S(1)}, bf16[2,512,256]{2,1,0:T(8,128)(2,1)}, u32[]{:S(2)}, u32[]{:S(2)}) collective-permute-start(bf16[2,512,256]{2,1,0:T(8,128)(2,1)S(1)} %bitcast.59), channel_id=1, source_target_pairs={{0,4},{1,5},{2,6},{3,7},{4,8},{5,9},{6,10},{7,11},{8,12},{9,13},{1... | collective-permute-start | bytes 1572872 | tf_op jit(solution)/shard_map/ppermute | solution.py:23
  126.2 27.5 %collective-permute-start.7 = (bf16[2,512,256]{2,1,0:T(8,128)(2,1)}, bf16[2,512,256]{2,1,0:T(8,128)(2,1)}, u32[]{:S(2)}, u32[]{:S(2)}) collective-permute-start(bf16[2,512,256]{2,1,0:T(8,128)(2,1)} %collective-permute-done.6.k1_ref.v1_ref), channel_id=1, source_target_pairs={{0,4},{1,5},{2,6},{3,7},{4,8},{5,9},{6,10},{7,11},{8,12},{9,13},{1... | collective-permute-start | bytes 1572872 | tf_op jit(solution)/shard_map/ppermute | solution.py:23
  161.5 4.1 %collective-permute-start.9 = (bf16[128,256]{1,0:T(8,128)(2,1)S(1)}, bf16[128,256]{1,0:T(8,128)(2,1)S(1)}, u32[]{:S(2)}, u32[]{:S(2)}) collective-permute-start(bf16[128,256]{1,0:T(8,128)(2,1)S(1)} %get-tuple-element.24), channel_id=1, source_target_pairs={{0,3},{1,0},{2,1},{3,2},{4,7},{5,4},{6,5},{7,6},{8,11},{9,8},{10,9... | collective-permute-start | bytes 196616 | tf_op jit(solution)/shard_map/ppermute | solution.py:32
  163.0 3.7 %collective-permute-start.10 = (bf16[128,256]{1,0:T(8,128)(2,1)S(1)}, bf16[128,256]{1,0:T(8,128)(2,1)S(1)}, u32[]{:S(2)}, u32[]{:S(2)}) collective-permute-start(bf16[128,256]{1,0:T(8,128)(2,1)S(1)} %get-tuple-element.23), channel_id=1, source_target_pairs={{0,2},{1,3},{2,0},{3,1},{4,6},{5,7},{6,4},{7,5},{8,10},{9,11},{10,... | collective-permute-start | bytes 196616 | tf_op jit(solution)/shard_map/ppermute | solution.py:32
  163.4 3.3 %collective-permute-start.11 = (bf16[128,256]{1,0:T(8,128)(2,1)S(1)}, bf16[128,256]{1,0:T(8,128)(2,1)S(1)}, u32[]{:S(2)}, u32[]{:S(2)}) collective-permute-start(bf16[128,256]{1,0:T(8,128)(2,1)S(1)} %get-tuple-element.22), channel_id=1, source_target_pairs={{0,1},{1,2},{2,3},{3,0},{4,5},{5,6},{6,7},{7,4},{8,9},{9,10},{10,1... | collective-permute-start | bytes 196616 | tf_op jit(solution)/shard_map/ppermute | solution.py:32
  168.3 13.6 %collective-permute-start.12 = (bf16[1,1024]{1,0:T(2,128)(2,1)S(1)}, bf16[1,1024]{1,0:T(2,128)(2,1)S(1)}, u32[]{:S(2)}, u32[]{:S(2)}) collective-permute-start(bf16[1,1024]{1,0:T(2,128)(2,1)S(1)} %slice.28), channel_id=1, source_target_pairs={{0,1},{1,2},{2,3},{3,4},{4,5},{5,6},{6,7},{7,8},{8,9},{9,10},{10,1... | collective-permute-start | bytes 6152 | tf_op jit(solution)/shard_map/ppermute | solution.py:23

commit v8 on v6

--- a/solution.py
+++ b/solution.py
@@ -303,7 +303,7 @@
     coarse_pairs = grouped[1:]
     one_back = passed_along(coarse_pairs, "seq", QUARTERS)
     two_back = passed_along(coarse_pairs, "seq", 2 * QUARTERS)
-    three_back = passed_along(two_back, "seq", QUARTERS)
+    three_back = passed_along(one_back, "seq", 2 * QUARTERS)
     earlier = [three_back, two_back, one_back]
     clip_back = jnp.concatenate([jnp.full((CREACH * group_rows,), -1, jnp.int32), clip_ids])
     coarse_key_clip = lax.dynamic_slice_in_dim(

time: 178 us -> 188 us (1.056)
  starting transfers between devices: 54.8 us -> 61.7 us
  waiting for transfers between devices: 66.3 us -> 69.5 us
    ppermute x6, starting transfers between devices: 5.21 us -> 18.9 us  [within_group(): return lax.ppermute(value, axis, pairs)]
    ppermute x5, starting transfers between devices: 43.5 us -> 36.6 us  [passed_along(): lax.ppermute(value, axis, [(source, source + steps) for source in range(f...]
    ppermute x5, waiting for transfers between devices: 57.4 us -> 60.2 us  [passed_along(): lax.ppermute(value, axis, [(source, source + steps) for source in range(f...]
  transfers between devices with their start and end apart: 13 -> 13, of which waited for: 8 -> 10; matrix products, arithmetic and copies ran while one was open for 3% -> 3% of each run, Pallas kernels for 0% -> 0%
where the time goes in v8:
time: 188 us; the launch traced here: 185 us
  waiting for transfers between devices  69.5 us (37%)
  starting transfers between devices  61.7 us (33%)
  Pallas kernels  37.4 us (20%)
  local copies, waits for them, and re-layouts  11.4 us (6%)
  matrix products  4.35 us (2%)
    ppermute x5, waiting for transfers between devices, passed_along(): lax.ppermute(value, axis, [(source, source + steps) for source in range(f...  60.2 us
    ppermute x5, starting transfers between devices, passed_along(): lax.ppermute(value, axis, [(source, source + steps) for source in range(f...  36.6 us
    pallas_call x1, Pallas kernels, fine_attention(): pl.pallas_call(kernel, grid=(pairs, nq), in_specs=[pl.BlockSpec((tile, 1)...  28.2 us
    ppermute x6, starting transfers between devices, within_group(): return lax.ppermute(value, axis, pairs)  18.9 us
    ppermute x6, waiting for transfers between devices, within_group(): return lax.ppermute(value, axis, pairs)  8.48 us
    pallas_call x1, Pallas kernels, coarse_attention(): pl.pallas_call(kernel, grid=(heads, rows // tile), in_specs=[pl.BlockSpec...  6.8 us
    ppermute x2, starting transfers between devices, pair_swap(): lax.ppermute(value, axis, [(source, source + step) for source in range(st...  6.1 us
    dot_general x1, matrix products, body(): jnp.einsum('rd,mdc->mrc', pooled, wplanes, preferred_element_type=jnp.flo...  3.87 us
  transfers between devices with their start and end apart: 13, of which 10 were waited for; matrix products, arithmetic and copies ran while one was open for 3% of the time, Pallas kernels for 0%

profile of v8, /device:TPU:7, one launch (start us, length us, event | category | flops | bytes accessed | tf_op | source)
XLA Modules:
  0.0 185.4 jit_solution(13136534888623894549)
XLA Ops:
  0.0 3.3 %slice.25 = bf16[2,512,1024]{2,1,0:T(8,128)(2,1)} slice(bf16[3,512,1024]{2,1,0:T(8,128)(2,1)} %bitcast.53), slice={[1:3], [0:512], [0:1024]} | slice | bytes 4194304 | tf_op jit(solution)/shard_map/slice | solution.py:274
  3.3 3.1 %collective-permute-start = (bf16[2,512,1024]{2,1,0:T(8,128)(2,1)}, bf16[2,512,1024]{2,1,0:T(8,128)(2,1)}, u32[]{:S(2)}, u32[]{:S(2)}) collective-permute-start(bf16[2,512,1024]{2,1,0:T(8,128)(2,1)} %slice.25), channel_id=1, source_target_pairs={{0,2},{1,3},{2,4},{3,5},{4,6},{5,7},{6,8},{7,9},{8,10},{9,11},{10,... | collective-permute-start | bytes 6291464 | tf_op jit(solution)/shard_map/ppermute | solution.py:23
  6.4 1.3 collective-permute-start.1
  7.7 44.3 %collective-permute-done.k0_ref.v0_ref = bf16[2,512,1024]{2,1,0:T(8,128)(2,1)} collective-permute-done((bf16[2,512,1024]{2,1,0:T(8,128)(2,1)}, bf16[2,512,1024]{2,1,0:T(8,128)(2,1)}, u32[]{:S(2)}, u32[]{:S(2)}) %collective-permute-start) | collective-permute-done | bytes 2097184 | tf_op jit(solution)/shard_map/ppermute | solution.py:23
  52.0 4.8 %collective-permute-start.2 = (bf16[2,512,1024]{2,1,0:T(8,128)(2,1)}, bf16[2,512,1024]{2,1,0:T(8,128)(2,1)}, u32[]{:S(2)}, u32[]{:S(2)}) collective-permute-start(bf16[2,512,1024]{2,1,0:T(8,128)(2,1)} %collective-permute-done.k0_ref.v0_ref), channel_id=1, source_target_pairs={{1,0},{3,2},{5,4},{7,6},{9,8},{11,10},{13,12},{15,14},{17,16},{19,... | collective-permute-start | bytes 6291464 | tf_op jit(solution)/shard_map/ppermute | solution.py:159
  56.9 0.8 reshape_reshape.8.qclip_ref
  58.0 0.8 reshape_reshape.7.kclip0_ref.kclip1_ref.kclip2_ref
  58.7 0.8 collective-permute-done.2.k1b_ref.v1b_ref
  59.5 28.2 %shard_map.46 = (bf16[512,1024]{1,0:T(8,128)(2,1)}, bf16[128,1024]{1,0:T(8,128)(2,1)}) custom-call(s32[512,1]{1,0:T(8,128)} %reshape_reshape.8.qclip_ref, s32[1,1536]{1,0:T(1,128)} %reshape_reshape.7.kclip0_ref.kclip1_ref.kclip2_ref, s32[1,1536]{1,0:T(1,128)} %reshape_reshape.7.kclip0_ref.kclip1_ref.kclip2_ref, ...), custom_call_target="tpu_custom_call" | custom-call | tf_op jit(solution)/shard_map/pallas_call | solution.py:104
  87.7 3.9 %fusion.2 = bf16[128,3,1024]{2,0,1:T(8,128)(2,1)S(1)} fusion(bf16[1024,3,1024]{2,0,1:T(8,128)(2,1)} %param.6, bf16[128,1024]{1,0:T(8,128)(2,1)} %get-tuple-element.8), kind=kOutput, calls=%fused_computation.2 | convolution fusion | flops 805699584 | bytes 7340032 | tf_op jit(solution)/shard_map/rd,mdc->mrc/dot_general | solution.py:291
  91.6 0.8 dynamic-slice_bitcast_fusion.2
  92.8 1.6 collective-permute-start.5
  94.4 5.6 %collective-permute-done.3 = bf16[3,128,256]{2,1,0:T(8,128)(2,1)S(1)} collective-permute-done((bf16[3,128,256]{2,1,0:T(8,128)(2,1)}, bf16[3,128,256]{2,1,0:T(8,128)(2,1)S(1)}, u32[]{:S(2)}, u32[]{:S(2)}) %collective-permute-start.3) | collective-permute-done | bytes 196640 | tf_op jit(solution)/shard_map/ppermute | solution.py:32
  100.1 1.3 collective-permute-done.5
  101.7 5.1 %collective-permute-start.6 = (bf16[2,512,256]{2,1,0:T(8,128)(2,1)S(1)}, bf16[2,512,256]{2,1,0:T(8,128)(2,1)}, u32[]{:S(2)}, u32[]{:S(2)}) collective-permute-start(bf16[2,512,256]{2,1,0:T(8,128)(2,1)S(1)} %bitcast.57), channel_id=1, source_target_pairs={{0,4},{1,5},{2,6},{3,7},{4,8},{5,9},{6,10},{7,11},{8,12},{9,13},{1... | collective-permute-start | bytes 1572872 | tf_op jit(solution)/shard_map/ppermute | solution.py:23
  106.8 4.2 %collective-permute-start.8 = (bf16[2,512,256]{2,1,0:T(8,128)(2,1)S(1)}, bf16[2,512,256]{2,1,0:T(8,128)(2,1)}, u32[]{:S(2)}, u32[]{:S(2)}) collective-permute-start(bf16[2,512,256]{2,1,0:T(8,128)(2,1)S(1)} %bitcast.58), channel_id=1, source_target_pairs={{0,8},{1,9},{2,10},{3,11},{4,12},{5,13},{6,14},{7,15},{16,24},{17,... | collective-permute-start | bytes 1572872 | tf_op jit(solution)/shard_map/ppermute | solution.py:23
  111.0 4.3 %collective-permute-done.6.k2_ref.v2_ref = bf16[2,512,256]{2,1,0:T(8,128)(2,1)} collective-permute-done((bf16[2,512,256]{2,1,0:T(8,128)(2,1)S(1)}, bf16[2,512,256]{2,1,0:T(8,128)(2,1)}, u32[]{:S(2)}, u32[]{:S(2)}) %collective-permute-start.6) | collective-permute-done | bytes 524320 | tf_op jit(solution)/shard_map/ppermute | solution.py:23
  115.3 6.1 %collective-permute-start.7 = (bf16[2,512,256]{2,1,0:T(8,128)(2,1)}, bf16[2,512,256]{2,1,0:T(8,128)(2,1)}, u32[]{:S(2)}, u32[]{:S(2)}) collective-permute-start(bf16[2,512,256]{2,1,0:T(8,128)(2,1)} %collective-permute-done.6.k2_ref.v2_ref), channel_id=1, source_target_pairs={{0,8},{1,9},{2,10},{3,11},{4,12},{5,13},{6,14},{7,15},{16,24},{17,... | collective-permute-start | bytes 1572872 | tf_op jit(solution)/shard_map/ppermute | solution.py:23
  121.5 0.9 copy.8.qclip_ref
  123.1 0.7 slice.26
  123.8 2.8 %collective-permute-done.8.k1_ref.v1_ref = bf16[2,512,256]{2,1,0:T(8,128)(2,1)} collective-permute-done((bf16[2,512,256]{2,1,0:T(8,128)(2,1)S(1)}, bf16[2,512,256]{2,1,0:T(8,128)(2,1)}, u32[]{:S(2)}, u32[]{:S(2)}) %collective-permute-start.8) | collective-permute-done | bytes 524320 | tf_op jit(solution)/shard_map/ppermute | solution.py:23
  126.6 8.1 %collective-permute-done.7.k0_ref.v0_ref = bf16[2,512,256]{2,1,0:T(8,128)(2,1)} collective-permute-done((bf16[2,512,256]{2,1,0:T(8,128)(2,1)}, bf16[2,512,256]{2,1,0:T(8,128)(2,1)}, u32[]{:S(2)}, u32[]{:S(2)}) %collective-permute-start.7) | collective-permute-done | bytes 524320 | tf_op jit(solution)/shard_map/ppermute | solution.py:23
  134.7 6.8 %shard_map.47 = bf16[512,256]{1,0:T(8,128)(2,1)} custom-call(s32[512,1]{1,0:T(8,128)} %copy.8.qclip_ref, s32[1,2048]{1,0:T(1,128)} %bitcast.64, s32[1,2048]{1,0:T(1,128)} %bitcast.65, s32[1,2048]{1,0:T(1,128)} %bitcast.66, s32[1,2048]{1,0:T(1,128)} %bitcast.67, bf16[512,256]{1,0:T(8,128)(2,1)} %bitcast.62, ...), custom_call_target="tpu_custom_call" | custom-call | tf_op jit(solution)/shard_map/pallas_call | solution.py:212
  141.5 0.9 constant_dynamic-slice_fusion
  142.5 15.2 %collective-permute-start.9 = (bf16[128,256]{1,0:T(8,128)(2,1)S(1)}, bf16[128,256]{1,0:T(8,128)(2,1)S(1)}, u32[]{:S(2)}, u32[]{:S(2)}) collective-permute-start(bf16[128,256]{1,0:T(8,128)(2,1)S(1)} %get-tuple-element.16), channel_id=1, source_target_pairs={{0,3},{1,0},{2,1},{3,2},{4,7},{5,4},{6,5},{7,6},{8,11},{9,8},{10,9... | collective-permute-start | bytes 196616 | tf_op jit(solution)/shard_map/ppermute | solution.py:32
  157.7 1.1 collective-permute-start.10
  159.4 0.8 bitcast_dynamic-update-slice_fusion.14
  160.2 0.9 collective-permute-done.9
  161.8 0.9 bitcast_dynamic-update-slice_fusion.15
  163.4 18.0 %collective-permute-start.12 = (bf16[1,1024]{1,0:T(2,128)(2,1)S(1)}, bf16[1,1024]{1,0:T(2,128)(2,1)S(1)}, u32[]{:S(2)}, u32[]{:S(2)}) collective-permute-start(bf16[1,1024]{1,0:T(2,128)(2,1)S(1)} %slice.28), channel_id=1, source_target_pairs={{0,1},{1,2},{2,3},{3,4},{4,5},{5,6},{6,7},{7,8},{8,9},{9,10},{10,1... | collective-permute-start | bytes 6152 | tf_op jit(solution)/shard_map/ppermute | solution.py:23
  182.2 0.8 maximum_select_fusion.lift_ref
  183.0 2.4 %shard_map.48 = bf16[512,1024]{1,0:T(8,128)(2,1)} custom-call(bf16[512,1024]{1,0:T(8,128)(2,1)} %get-tuple-element.7.fine_ref, bf16[128,1024]{1,0:T(8,128)(2,1)} %maximum_select_fusion.lift_ref), custom_call_target="tpu_custom_call" | custom-call | tf_op jit(solution)/shard_map/pallas_call | solution.py:143
  (41 shorter events, 4.4 us)
Async XLA Ops:
  0.0 162.9 %copy-start = (bf16[1024,1024]{1,0:T(8,128)(2,1)S(1)}, bf16[1024,1024]{1,0:T(8,128)(2,1)}, u32[]{:S(2)}) copy-start(bf16[1024,1024]{1,0:T(8,128)(2,1)} %param.7) | copy-start | bytes 6291460
  0.0 56.8 %copy-start.2 = (s32[2048]{0:T(1024)S(1)}, s32[2048]{0:T(1024)}, u32[]{:S(2)}) copy-start(s32[2048]{0:T(1024)} %param.5) | copy-start | bytes 24580
  3.3 48.7 %collective-permute-start = (bf16[2,512,1024]{2,1,0:T(8,128)(2,1)}, bf16[2,512,1024]{2,1,0:T(8,128)(2,1)}, u32[]{:S(2)}, u32[]{:S(2)}) collective-permute-start(bf16[2,512,1024]{2,1,0:T(8,128)(2,1)} %slice.25), channel_id=1, source_target_pairs={{0,2},{1,3},{2,4},{3,5},{4,6},{5,7},{6,8},{7,9},{8,10},{9,11},{10,... | collective-permute-start | bytes 6291464 | tf_op jit(solution)/shard_map/ppermute | solution.py:23
  6.4 52.3 %collective-permute-start.1 = (bf16[2,512,1024]{2,1,0:T(8,128)(2,1)}, bf16[2,512,1024]{2,1,0:T(8,128)(2,1)}, u32[]{:S(2)}, u32[]{:S(2)}) collective-permute-start(bf16[2,512,1024]{2,1,0:T(8,128)(2,1)} %slice.25), channel_id=1, source_target_pairs={{0,1},{2,3},{4,5},{6,7},{8,9},{10,11},{12,13},{14,15},{16,17},{18,... | collective-permute-start | bytes 6291464 | tf_op jit(solution)/shard_map/ppermute | solution.py:159
  52.0 7.6 %collective-permute-start.2 = (bf16[2,512,1024]{2,1,0:T(8,128)(2,1)}, bf16[2,512,1024]{2,1,0:T(8,128)(2,1)}, u32[]{:S(2)}, u32[]{:S(2)}) collective-permute-start(bf16[2,512,1024]{2,1,0:T(8,128)(2,1)} %collective-permute-done.k0_ref.v0_ref), channel_id=1, source_target_pairs={{1,0},{3,2},{5,4},{7,6},{9,8},{11,10},{13,12},{15,14},{17,16},{19,... | collective-permute-start | bytes 6291464 | tf_op jit(solution)/shard_map/ppermute | solution.py:159
  92.4 7.6 %collective-permute-start.3 = (bf16[3,128,256]{2,1,0:T(8,128)(2,1)}, bf16[3,128,256]{2,1,0:T(8,128)(2,1)S(1)}, u32[]{:S(2)}, u32[]{:S(2)}) collective-permute-start(bf16[3,128,256]{2,1,0:T(8,128)(2,1)} %get-tuple-element.13), channel_id=1, source_target_pairs={{0,3},{1,0},{2,1},{3,2},{4,7},{5,4},{6,5},{7,6},{8,11},{9,8},{10,9... | collective-permute-start | bytes 589832 | tf_op jit(solution)/shard_map/ppermute | solution.py:32
  92.8 7.3 %collective-permute-start.4 = (bf16[3,128,256]{2,1,0:T(8,128)(2,1)S(1)}, bf16[3,128,256]{2,1,0:T(8,128)(2,1)S(1)}, u32[]{:S(2)}, u32[]{:S(2)}) collective-permute-start(bf16[3,128,256]{2,1,0:T(8,128)(2,1)S(1)} %get-tuple-element.12), channel_id=1, source_target_pairs={{0,2},{1,3},{2,0},{3,1},{4,6},{5,7},{6,4},{7,5},{8,10},{9,11},{10,... | collective-permute-start | bytes 589832 | tf_op jit(solution)/shard_map/ppermute | solution.py:32
  92.8 8.6 %collective-permute-start.5 = (bf16[3,128,256]{2,1,0:T(8,128)(2,1)S(1)}, bf16[3,128,256]{2,1,0:T(8,128)(2,1)S(1)}, u32[]{:S(2)}, u32[]{:S(2)}) collective-permute-start(bf16[3,128,256]{2,1,0:T(8,128)(2,1)S(1)} %get-tuple-element.11), channel_id=1, source_target_pairs={{0,1},{1,2},{2,3},{3,0},{4,5},{5,6},{6,7},{7,4},{8,9},{9,10},{10,1... | collective-permute-start | bytes 589832 | tf_op jit(solution)/shard_map/ppermute | solution.py:32
  101.7 33.0 %copy-start.1 = (bf16[2,4,128,256]{3,2,1,0:T(8,128)(2,1)}, bf16[2,4,128,256]{3,2,1,0:T(8,128)(2,1)S(1)}, u32[]{:S(2)}) copy-start(bf16[2,4,128,256]{3,2,1,0:T(8,128)(2,1)S(1)} %copy.7) | copy-start | bytes 1572868
  101.7 13.7 %collective-permute-start.6 = (bf16[2,512,256]{2,1,0:T(8,128)(2,1)S(1)}, bf16[2,512,256]{2,1,0:T(8,128)(2,1)}, u32[]{:S(2)}, u32[]{:S(2)}) collective-permute-start(bf16[2,512,256]{2,1,0:T(8,128)(2,1)S(1)} %bitcast.57), channel_id=1, source_target_pairs={{0,4},{1,5},{2,6},{3,7},{4,8},{5,9},{6,10},{7,11},{8,12},{9,13},{1... | collective-permute-start | bytes 1572872 | tf_op jit(solution)/shard_map/ppermute | solution.py:23
  106.8 19.8 %collective-permute-start.8 = (bf16[2,512,256]{2,1,0:T(8,128)(2,1)S(1)}, bf16[2,512,256]{2,1,0:T(8,128)(2,1)}, u32[]{:S(2)}, u32[]{:S(2)}) collective-permute-start(bf16[2,512,256]{2,1,0:T(8,128)(2,1)S(1)} %bitcast.58), channel_id=1, source_target_pairs={{0,8},{1,9},{2,10},{3,11},{4,12},{5,13},{6,14},{7,15},{16,24},{17,... | collective-permute-start | bytes 1572872 | tf_op jit(solution)/shard_map/ppermute | solution.py:23
  115.3 19.4 %collective-permute-start.7 = (bf16[2,512,256]{2,1,0:T(8,128)(2,1)}, bf16[2,512,256]{2,1,0:T(8,128)(2,1)}, u32[]{:S(2)}, u32[]{:S(2)}) collective-permute-start(bf16[2,512,256]{2,1,0:T(8,128)(2,1)} %collective-permute-done.6.k2_ref.v2_ref), channel_id=1, source_target_pairs={{0,8},{1,9},{2,10},{3,11},{4,12},{5,13},{6,14},{7,15},{16,24},{17,... | collective-permute-start | bytes 1572872 | tf_op jit(solution)/shard_map/ppermute | solution.py:23
  142.5 18.7 %collective-permute-start.9 = (bf16[128,256]{1,0:T(8,128)(2,1)S(1)}, bf16[128,256]{1,0:T(8,128)(2,1)S(1)}, u32[]{:S(2)}, u32[]{:S(2)}) collective-permute-start(bf16[128,256]{1,0:T(8,128)(2,1)S(1)} %get-tuple-element.16), channel_id=1, source_target_pairs={{0,3},{1,0},{2,1},{3,2},{4,7},{5,4},{6,5},{7,6},{8,11},{9,8},{10,9... | collective-permute-start | bytes 196616 | tf_op jit(solution)/shard_map/ppermute | solution.py:32
  157.7 4.1 %collective-permute-start.10 = (bf16[128,256]{1,0:T(8,128)(2,1)S(1)}, bf16[128,256]{1,0:T(8,128)(2,1)S(1)}, u32[]{:S(2)}, u32[]{:S(2)}) collective-permute-start(bf16[128,256]{1,0:T(8,128)(2,1)S(1)} %get-tuple-element.15), channel_id=1, source_target_pairs={{0,2},{1,3},{2,0},{3,1},{4,6},{5,7},{6,4},{7,5},{8,10},{9,11},{10,... | collective-permute-start | bytes 196616 | tf_op jit(solution)/shard_map/ppermute | solution.py:32
  158.8 3.0 %collective-permute-start.11 = (bf16[128,256]{1,0:T(8,128)(2,1)S(1)}, bf16[128,256]{1,0:T(8,128)(2,1)S(1)}, u32[]{:S(2)}, u32[]{:S(2)}) collective-permute-start(bf16[128,256]{1,0:T(8,128)(2,1)S(1)} %get-tuple-element.14), channel_id=1, source_target_pairs={{0,1},{1,2},{2,3},{3,0},{4,5},{5,6},{6,7},{7,4},{8,9},{9,10},{10,1... | collective-permute-start | bytes 196616 | tf_op jit(solution)/shard_map/ppermute | solution.py:32
  163.4 18.8 %collective-permute-start.12 = (bf16[1,1024]{1,0:T(2,128)(2,1)S(1)}, bf16[1,1024]{1,0:T(2,128)(2,1)S(1)}, u32[]{:S(2)}, u32[]{:S(2)}) collective-permute-start(bf16[1,1024]{1,0:T(2,128)(2,1)S(1)} %slice.28), channel_id=1, source_target_pairs={{0,1},{1,2},{2,3},{3,4},{4,5},{5,6},{6,7},{7,8},{8,9},{9,10},{10,1... | collective-permute-start | bytes 6152 | tf_op jit(solution)/shard_map/ppermute | solution.py:23

commit v9 on v6

--- a/solution.py
+++ b/solution.py
@@ -325,12 +325,15 @@
     )
     coarse_up = jnp.dot(att_rows, w_out, preferred_element_type=jnp.float32).astype(jnp.bfloat16)
     carried = passed_along(coarse_up[-1:], "seq", 1)
-    previous = jnp.concatenate([carried, coarse_up[:-1]], axis=0)
+    previous = jnp.concatenate([jnp.zeros_like(carried), coarse_up[:-1]], axis=0)
     clip_before = jnp.concatenate([jnp.full((1,), -1, jnp.int32), clip_ids])
     prev_clip = lax.dynamic_slice_in_dim(clip_before, position * coarse_rows, coarse_rows, 0)
     joined = prev_clip == own_clip
     lifted = jnp.where(joined[:, None], previous, jnp.zeros_like(previous))
-    return mix(fine_out, lifted)
+    mixed = mix(fine_out, lifted)
+    head_lift = jnp.where(joined[:1, None], carried, jnp.zeros_like(carried)).astype(jnp.float32)
+    head_rows = (fine_out[:POOL].astype(jnp.float32) + head_lift).astype(mixed.dtype)
+    return lax.dynamic_update_slice(mixed, head_rows, (0, 0))
 
 
 def solution(mesh):

time: 178 us -> 177 us (level)
  transfers between devices with their start and end apart: 13 -> 13, of which waited for: 8 -> 7; matrix products, arithmetic and copies ran while one was open for 3% -> 3% of each run, Pallas kernels for 0% -> 1%
where the time goes in v9:
time: 177 us; the launch traced here: 176 us
  waiting for transfers between devices  65.6 us (37%)
  starting transfers between devices  54.8 us (31%)
  Pallas kernels  37.4 us (21%)
  local copies, waits for them, and re-layouts  11.4 us (6%)
  matrix products  4.34 us (2%)
  other arithmetic  2.25 us (1%)
    ppermute x5, waiting for transfers between devices, passed_along(): lax.ppermute(value, axis, [(source, source + steps) for source in range(f...  56.7 us
    ppermute x5, starting transfers between devices, passed_along(): lax.ppermute(value, axis, [(source, source + steps) for source in range(f...  43.5 us
    pallas_call x1, Pallas kernels, fine_attention(): pl.pallas_call(kernel, grid=(pairs, nq), in_specs=[pl.BlockSpec((tile, 1)...  28.2 us
    ppermute x6, waiting for transfers between devices, within_group(): return lax.ppermute(value, axis, pairs)  8.03 us
    pallas_call x1, Pallas kernels, coarse_attention(): pl.pallas_call(kernel, grid=(heads, rows // tile), in_specs=[pl.BlockSpec...  6.8 us
    ppermute x2, starting transfers between devices, pair_swap(): lax.ppermute(value, axis, [(source, source + step) for source in range(st...  6.1 us
    ppermute x6, starting transfers between devices, within_group(): return lax.ppermute(value, axis, pairs)  5.21 us
    dot_general x1, matrix products, body(): jnp.einsum('rd,mdc->mrc', pooled, wplanes, preferred_element_type=jnp.flo...  3.87 us
  transfers between devices with their start and end apart: 13, of which 7 were waited for; matrix products, arithmetic and copies ran while one was open for 3% of the time, Pallas kernels for 1%

profile of v9, /device:TPU:7, one launch (start us, length us, event | category | flops | bytes accessed | tf_op | source)
XLA Modules:
  0.0 176.0 jit_solution(10246060479560859569)
XLA Ops:
  0.0 3.3 %slice.33 = bf16[2,512,1024]{2,1,0:T(8,128)(2,1)} slice(bf16[3,512,1024]{2,1,0:T(8,128)(2,1)} %bitcast.56), slice={[1:3], [0:512], [0:1024]} | slice | bytes 4194304 | tf_op jit(solution)/shard_map/slice | solution.py:274
  3.3 3.1 %collective-permute-start = (bf16[2,512,1024]{2,1,0:T(8,128)(2,1)}, bf16[2,512,1024]{2,1,0:T(8,128)(2,1)}, u32[]{:S(2)}, u32[]{:S(2)}) collective-permute-start(bf16[2,512,1024]{2,1,0:T(8,128)(2,1)} %slice.33), channel_id=1, source_target_pairs={{0,2},{1,3},{2,4},{3,5},{4,6},{5,7},{6,8},{7,9},{8,10},{9,11},{10,... | collective-permute-start | bytes 6291464 | tf_op jit(solution)/shard_map/ppermute | solution.py:23
  6.4 1.3 collective-permute-start.1
  7.7 44.3 %collective-permute-done.k0_ref.v0_ref = bf16[2,512,1024]{2,1,0:T(8,128)(2,1)} collective-permute-done((bf16[2,512,1024]{2,1,0:T(8,128)(2,1)}, bf16[2,512,1024]{2,1,0:T(8,128)(2,1)}, u32[]{:S(2)}, u32[]{:S(2)}) %collective-permute-start) | collective-permute-done | bytes 2097184 | tf_op jit(solution)/shard_map/ppermute | solution.py:23
  52.0 4.8 %collective-permute-start.2 = (bf16[2,512,1024]{2,1,0:T(8,128)(2,1)}, bf16[2,512,1024]{2,1,0:T(8,128)(2,1)}, u32[]{:S(2)}, u32[]{:S(2)}) collective-permute-start(bf16[2,512,1024]{2,1,0:T(8,128)(2,1)} %collective-permute-done.k0_ref.v0_ref), channel_id=1, source_target_pairs={{1,0},{3,2},{5,4},{7,6},{9,8},{11,10},{13,12},{15,14},{17,16},{19,... | collective-permute-start | bytes 6291464 | tf_op jit(solution)/shard_map/ppermute | solution.py:159
  56.9 0.8 reshape_reshape.8.qclip_ref
  58.0 0.8 reshape_reshape.7.kclip0_ref.kclip1_ref.kclip2_ref
  58.7 0.8 collective-permute-done.2.k1b_ref.v1b_ref
  59.5 28.2 %shard_map.46 = (bf16[512,1024]{1,0:T(8,128)(2,1)}, bf16[128,1024]{1,0:T(8,128)(2,1)}) custom-call(s32[512,1]{1,0:T(8,128)} %reshape_reshape.8.qclip_ref, s32[1,1536]{1,0:T(1,128)} %reshape_reshape.7.kclip0_ref.kclip1_ref.kclip2_ref, s32[1,1536]{1,0:T(1,128)} %reshape_reshape.7.kclip0_ref.kclip1_ref.kclip2_ref, ...), custom_call_target="tpu_custom_call" | custom-call | tf_op jit(solution)/shard_map/pallas_call | solution.py:104
  87.7 3.9 %fusion.2 = bf16[128,3,1024]{2,0,1:T(8,128)(2,1)S(1)} fusion(bf16[1024,3,1024]{2,0,1:T(8,128)(2,1)} %param.6, bf16[128,1024]{1,0:T(8,128)(2,1)} %get-tuple-element.8), kind=kOutput, calls=%fused_computation.2 | convolution fusion | flops 805699584 | bytes 7340032 | tf_op jit(solution)/shard_map/rd,mdc->mrc/dot_general | solution.py:291
  91.6 0.8 dynamic-slice_bitcast_fusion.2
  92.8 1.6 collective-permute-start.5
  94.4 5.6 %collective-permute-done.3 = bf16[3,128,256]{2,1,0:T(8,128)(2,1)S(1)} collective-permute-done((bf16[3,128,256]{2,1,0:T(8,128)(2,1)}, bf16[3,128,256]{2,1,0:T(8,128)(2,1)S(1)}, u32[]{:S(2)}, u32[]{:S(2)}) %collective-permute-start.3) | collective-permute-done | bytes 196640 | tf_op jit(solution)/shard_map/ppermute | solution.py:32
  100.1 1.3 collective-permute-done.5
  101.7 6.1 %collective-permute-start.6 = (bf16[2,512,256]{2,1,0:T(8,128)(2,1)S(1)}, bf16[2,512,256]{2,1,0:T(8,128)(2,1)}, u32[]{:S(2)}, u32[]{:S(2)}) collective-permute-start(bf16[2,512,256]{2,1,0:T(8,128)(2,1)S(1)} %bitcast.60), channel_id=1, source_target_pairs={{0,8},{1,9},{2,10},{3,11},{4,12},{5,13},{6,14},{7,15},{16,24},{17,... | collective-permute-start | bytes 1572872 | tf_op jit(solution)/shard_map/ppermute | solution.py:23
  107.8 4.0 %collective-permute-start.8 = (bf16[2,512,256]{2,1,0:T(8,128)(2,1)S(1)}, bf16[2,512,256]{2,1,0:T(8,128)(2,1)}, u32[]{:S(2)}, u32[]{:S(2)}) collective-permute-start(bf16[2,512,256]{2,1,0:T(8,128)(2,1)S(1)} %bitcast.61), channel_id=1, source_target_pairs={{0,4},{1,5},{2,6},{3,7},{4,8},{5,9},{6,10},{7,11},{8,12},{9,13},{1... | collective-permute-start | bytes 1572872 | tf_op jit(solution)/shard_map/ppermute | solution.py:23
  111.8 4.6 %collective-permute-done.6.k1_ref.v1_ref = bf16[2,512,256]{2,1,0:T(8,128)(2,1)} collective-permute-done((bf16[2,512,256]{2,1,0:T(8,128)(2,1)S(1)}, bf16[2,512,256]{2,1,0:T(8,128)(2,1)}, u32[]{:S(2)}, u32[]{:S(2)}) %collective-permute-start.6) | collective-permute-done | bytes 524320 | tf_op jit(solution)/shard_map/ppermute | solution.py:23
  116.4 17.3 %collective-permute-start.7 = (bf16[2,512,256]{2,1,0:T(8,128)(2,1)}, bf16[2,512,256]{2,1,0:T(8,128)(2,1)}, u32[]{:S(2)}, u32[]{:S(2)}) collective-permute-start(bf16[2,512,256]{2,1,0:T(8,128)(2,1)} %collective-permute-done.6.k1_ref.v1_ref), channel_id=1, source_target_pairs={{0,4},{1,5},{2,6},{3,7},{4,8},{5,9},{6,10},{7,11},{8,12},{9,13},{1... | collective-permute-start | bytes 1572872 | tf_op jit(solution)/shard_map/ppermute | solution.py:23
  133.9 0.9 copy.8.qclip_ref
  135.4 0.7 slice.34
  136.1 7.8 %collective-permute-done.7.k0_ref.v0_ref = bf16[2,512,256]{2,1,0:T(8,128)(2,1)} collective-permute-done((bf16[2,512,256]{2,1,0:T(8,128)(2,1)}, bf16[2,512,256]{2,1,0:T(8,128)(2,1)}, u32[]{:S(2)}, u32[]{:S(2)}) %collective-permute-start.7) | collective-permute-done | bytes 524320 | tf_op jit(solution)/shard_map/ppermute | solution.py:23
  144.0 6.8 %shard_map.47 = bf16[512,256]{1,0:T(8,128)(2,1)} custom-call(s32[512,1]{1,0:T(8,128)} %copy.8.qclip_ref, s32[1,2048]{1,0:T(1,128)} %bitcast.67, s32[1,2048]{1,0:T(1,128)} %bitcast.68, s32[1,2048]{1,0:T(1,128)} %bitcast.69, s32[1,2048]{1,0:T(1,128)} %bitcast.70, bf16[512,256]{1,0:T(8,128)(2,1)} %bitcast.65, ...), custom_call_target="tpu_custom_call" | custom-call | tf_op jit(solution)/shard_map/pallas_call | solution.py:212
  150.8 0.9 constant_dynamic-slice_fusion
  151.7 1.5 collective-permute-start.9
  153.6 1.3 collective-permute-start.11
  154.9 0.8 bitcast_dynamic-update-slice_fusion.14
  155.8 1.1 collective-permute-done.10
  156.9 0.9 bitcast_dynamic-update-slice_fusion.15
  158.5 12.9 %collective-permute-start.12 = (bf16[1,1024]{1,0:T(2,128)(2,1)S(1)}, bf16[1,1024]{1,0:T(2,128)(2,1)S(1)}, u32[]{:S(2)}, u32[]{:S(2)}) collective-permute-start(bf16[1,1024]{1,0:T(2,128)(2,1)S(1)} %slice.37), channel_id=1, source_target_pairs={{0,1},{1,2},{2,3},{3,4},{4,5},{5,6},{6,7},{7,8},{8,9},{9,10},{10,1... | collective-permute-start | bytes 6152 | tf_op jit(solution)/shard_map/ppermute | solution.py:23
  171.4 0.8 pad_select_fusion.lift_ref
  172.2 2.4 %shard_map.48 = bf16[512,1024]{1,0:T(8,128)(2,1)} custom-call(bf16[512,1024]{1,0:T(8,128)(2,1)} %get-tuple-element.7.fine_ref, bf16[128,1024]{1,0:T(8,128)(2,1)} %pad_select_fusion.lift_ref), custom_call_target="tpu_custom_call" | custom-call | tf_op jit(solution)/shard_map/pallas_call | solution.py:143
  174.7 1.3 fusion.6
  (43 shorter events, 2.9 us)
Async XLA Ops:
  0.0 158.0 %copy-start = (bf16[1024,1024]{1,0:T(8,128)(2,1)S(1)}, bf16[1024,1024]{1,0:T(8,128)(2,1)}, u32[]{:S(2)}) copy-start(bf16[1024,1024]{1,0:T(8,128)(2,1)} %param.7) | copy-start | bytes 6291460
  0.0 56.8 %copy-start.2 = (s32[2048]{0:T(1024)S(1)}, s32[2048]{0:T(1024)}, u32[]{:S(2)}) copy-start(s32[2048]{0:T(1024)} %param.5) | copy-start | bytes 24580
  3.3 48.7 %collective-permute-start = (bf16[2,512,1024]{2,1,0:T(8,128)(2,1)}, bf16[2,512,1024]{2,1,0:T(8,128)(2,1)}, u32[]{:S(2)}, u32[]{:S(2)}) collective-permute-start(bf16[2,512,1024]{2,1,0:T(8,128)(2,1)} %slice.33), channel_id=1, source_target_pairs={{0,2},{1,3},{2,4},{3,5},{4,6},{5,7},{6,8},{7,9},{8,10},{9,11},{10,... | collective-permute-start | bytes 6291464 | tf_op jit(solution)/shard_map/ppermute | solution.py:23
  6.4 52.3 %collective-permute-start.1 = (bf16[2,512,1024]{2,1,0:T(8,128)(2,1)}, bf16[2,512,1024]{2,1,0:T(8,128)(2,1)}, u32[]{:S(2)}, u32[]{:S(2)}) collective-permute-start(bf16[2,512,1024]{2,1,0:T(8,128)(2,1)} %slice.33), channel_id=1, source_target_pairs={{0,1},{2,3},{4,5},{6,7},{8,9},{10,11},{12,13},{14,15},{16,17},{18,... | collective-permute-start | bytes 6291464 | tf_op jit(solution)/shard_map/ppermute | solution.py:159
  52.0 7.6 %collective-permute-start.2 = (bf16[2,512,1024]{2,1,0:T(8,128)(2,1)}, bf16[2,512,1024]{2,1,0:T(8,128)(2,1)}, u32[]{:S(2)}, u32[]{:S(2)}) collective-permute-start(bf16[2,512,1024]{2,1,0:T(8,128)(2,1)} %collective-permute-done.k0_ref.v0_ref), channel_id=1, source_target_pairs={{1,0},{3,2},{5,4},{7,6},{9,8},{11,10},{13,12},{15,14},{17,16},{19,... | collective-permute-start | bytes 6291464 | tf_op jit(solution)/shard_map/ppermute | solution.py:159
  92.4 7.6 %collective-permute-start.3 = (bf16[3,128,256]{2,1,0:T(8,128)(2,1)}, bf16[3,128,256]{2,1,0:T(8,128)(2,1)S(1)}, u32[]{:S(2)}, u32[]{:S(2)}) collective-permute-start(bf16[3,128,256]{2,1,0:T(8,128)(2,1)} %get-tuple-element.13), channel_id=1, source_target_pairs={{0,3},{1,0},{2,1},{3,2},{4,7},{5,4},{6,5},{7,6},{8,11},{9,8},{10,9... | collective-permute-start | bytes 589832 | tf_op jit(solution)/shard_map/ppermute | solution.py:32
  92.8 7.3 %collective-permute-start.4 = (bf16[3,128,256]{2,1,0:T(8,128)(2,1)S(1)}, bf16[3,128,256]{2,1,0:T(8,128)(2,1)S(1)}, u32[]{:S(2)}, u32[]{:S(2)}) collective-permute-start(bf16[3,128,256]{2,1,0:T(8,128)(2,1)S(1)} %get-tuple-element.12), channel_id=1, source_target_pairs={{0,2},{1,3},{2,0},{3,1},{4,6},{5,7},{6,4},{7,5},{8,10},{9,11},{10,... | collective-permute-start | bytes 589832 | tf_op jit(solution)/shard_map/ppermute | solution.py:32
  92.8 8.6 %collective-permute-start.5 = (bf16[3,128,256]{2,1,0:T(8,128)(2,1)S(1)}, bf16[3,128,256]{2,1,0:T(8,128)(2,1)S(1)}, u32[]{:S(2)}, u32[]{:S(2)}) collective-permute-start(bf16[3,128,256]{2,1,0:T(8,128)(2,1)S(1)} %get-tuple-element.11), channel_id=1, source_target_pairs={{0,1},{1,2},{2,3},{3,0},{4,5},{5,6},{6,7},{7,4},{8,9},{9,10},{10,1... | collective-permute-start | bytes 589832 | tf_op jit(solution)/shard_map/ppermute | solution.py:32
  101.7 42.3 %copy-start.1 = (bf16[2,4,128,256]{3,2,1,0:T(8,128)(2,1)}, bf16[2,4,128,256]{3,2,1,0:T(8,128)(2,1)S(1)}, u32[]{:S(2)}) copy-start(bf16[2,4,128,256]{3,2,1,0:T(8,128)(2,1)S(1)} %copy.7) | copy-start | bytes 1572868
  101.7 14.8 %collective-permute-start.6 = (bf16[2,512,256]{2,1,0:T(8,128)(2,1)S(1)}, bf16[2,512,256]{2,1,0:T(8,128)(2,1)}, u32[]{:S(2)}, u32[]{:S(2)}) collective-permute-start(bf16[2,512,256]{2,1,0:T(8,128)(2,1)S(1)} %bitcast.60), channel_id=1, source_target_pairs={{0,8},{1,9},{2,10},{3,11},{4,12},{5,13},{6,14},{7,15},{16,24},{17,... | collective-permute-start | bytes 1572872 | tf_op jit(solution)/shard_map/ppermute | solution.py:23
  107.8 28.3 %collective-permute-start.8 = (bf16[2,512,256]{2,1,0:T(8,128)(2,1)S(1)}, bf16[2,512,256]{2,1,0:T(8,128)(2,1)}, u32[]{:S(2)}, u32[]{:S(2)}) collective-permute-start(bf16[2,512,256]{2,1,0:T(8,128)(2,1)S(1)} %bitcast.61), channel_id=1, source_target_pairs={{0,4},{1,5},{2,6},{3,7},{4,8},{5,9},{6,10},{7,11},{8,12},{9,13},{1... | collective-permute-start | bytes 1572872 | tf_op jit(solution)/shard_map/ppermute | solution.py:23
  116.4 27.5 %collective-permute-start.7 = (bf16[2,512,256]{2,1,0:T(8,128)(2,1)}, bf16[2,512,256]{2,1,0:T(8,128)(2,1)}, u32[]{:S(2)}, u32[]{:S(2)}) collective-permute-start(bf16[2,512,256]{2,1,0:T(8,128)(2,1)} %collective-permute-done.6.k1_ref.v1_ref), channel_id=1, source_target_pairs={{0,4},{1,5},{2,6},{3,7},{4,8},{5,9},{6,10},{7,11},{8,12},{9,13},{1... | collective-permute-start | bytes 1572872 | tf_op jit(solution)/shard_map/ppermute | solution.py:23
  151.7 4.1 %collective-permute-start.9 = (bf16[128,256]{1,0:T(8,128)(2,1)S(1)}, bf16[128,256]{1,0:T(8,128)(2,1)S(1)}, u32[]{:S(2)}, u32[]{:S(2)}) collective-permute-start(bf16[128,256]{1,0:T(8,128)(2,1)S(1)} %get-tuple-element.16), channel_id=1, source_target_pairs={{0,3},{1,0},{2,1},{3,2},{4,7},{5,4},{6,5},{7,6},{8,11},{9,8},{10,9... | collective-permute-start | bytes 196616 | tf_op jit(solution)/shard_map/ppermute | solution.py:32
  153.2 3.7 %collective-permute-start.10 = (bf16[128,256]{1,0:T(8,128)(2,1)S(1)}, bf16[128,256]{1,0:T(8,128)(2,1)S(1)}, u32[]{:S(2)}, u32[]{:S(2)}) collective-permute-start(bf16[128,256]{1,0:T(8,128)(2,1)S(1)} %get-tuple-element.15), channel_id=1, source_target_pairs={{0,2},{1,3},{2,0},{3,1},{4,6},{5,7},{6,4},{7,5},{8,10},{9,11},{10,... | collective-permute-start | bytes 196616 | tf_op jit(solution)/shard_map/ppermute | solution.py:32
  153.6 3.3 %collective-permute-start.11 = (bf16[128,256]{1,0:T(8,128)(2,1)S(1)}, bf16[128,256]{1,0:T(8,128)(2,1)S(1)}, u32[]{:S(2)}, u32[]{:S(2)}) collective-permute-start(bf16[128,256]{1,0:T(8,128)(2,1)S(1)} %get-tuple-element.14), channel_id=1, source_target_pairs={{0,1},{1,2},{2,3},{3,0},{4,5},{5,6},{6,7},{7,4},{8,9},{9,10},{10,1... | collective-permute-start | bytes 196616 | tf_op jit(solution)/shard_map/ppermute | solution.py:32
  158.5 16.1 %collective-permute-start.12 = (bf16[1,1024]{1,0:T(2,128)(2,1)S(1)}, bf16[1,1024]{1,0:T(2,128)(2,1)S(1)}, u32[]{:S(2)}, u32[]{:S(2)}) collective-permute-start(bf16[1,1024]{1,0:T(2,128)(2,1)S(1)} %slice.37), channel_id=1, source_target_pairs={{0,1},{1,2},{2,3},{3,4},{4,5},{5,6},{6,7},{7,8},{8,9},{9,10},{10,1... | collective-permute-start | bytes 6152 | tf_op jit(solution)/shard_map/ppermute | solution.py:23

commit v10 on v9

--- a/solution.py
+++ b/solution.py
@@ -34,36 +34,45 @@
 
 def fine_kernel(qclip_ref, kclip0_ref, kclip1_ref, kclip2_ref, q_ref,
                 k0_ref, v0_ref, k1_ref, v1_ref, k1b_ref, v1b_ref, k2_ref, v2_ref,
-                out_ref, pool_ref, *, scale):
+                out_ref, pool_ref, bias_ref, *, scale):
     tile = q_ref.shape[0]
     width = q_ref.shape[1]
     half = width // 2
+    seg = k0_ref.shape[0]
+    tile_index = pl.program_id(0)
+
+    @pl.when(pl.program_id(1) == 0)
+    def _():
+        qclip = qclip_ref[...]
+        qpos = tile_index * tile + lax.broadcasted_iota(jnp.int32, (tile, seg), 0)
+        kpos = lax.broadcasted_iota(jnp.int32, (tile, seg), 1)
+        allowed = (
+            kclip0_ref[...] == qclip,
+            kclip1_ref[...] == qclip,
+            (kclip2_ref[...] == qclip) & (kpos <= qpos),
+        )
+        for j in range(3):
+            bias_ref[:, j * seg:(j + 1) * seg] = jnp.where(allowed[j], 0.0, -1e30)
+
     q = q_ref[...] * jnp.asarray(scale, q_ref.dtype)
     lane = lax.broadcasted_iota(jnp.int32, (1, width), 1)
     low = lane < half
     zero = jnp.zeros_like(q)
     head_q = (jnp.where(low, q, zero), jnp.where(low, zero, q))
-    qclip = qclip_ref[...]
-    seg = k0_ref.shape[0]
 
     def run(step):
         own = (step + 1) * tile
         keys = (k0_ref[...], k1_ref[...] + k1b_ref[...], k2_ref[0:own, :])
         values = (v0_ref[...], v1_ref[...] + v1b_ref[...], v2_ref[0:own, :])
-        qpos = step * tile + lax.broadcasted_iota(jnp.int32, (tile, own), 0)
-        kpos = lax.broadcasted_iota(jnp.int32, (tile, own), 1)
-        masks = (
-            kclip0_ref[...] == qclip,
-            kclip1_ref[...] == qclip,
-            (kclip2_ref[:, 0:own] == qclip) & (kpos <= qpos),
-        )
+        spans = ((0, seg), (seg, seg), (2 * seg, own))
         results = []
         for h in range(2):
             scores = []
             for j in range(3):
                 s = lax.dot_general(head_q[h], keys[j], (((1,), (1,)), ((), ())),
                                     preferred_element_type=jnp.float32)
-                scores.append(jnp.where(masks[j], s, -1e30))
+                start, length = spans[j]
+                scores.append(s + bias_ref[:, start:start + length])
             top = jnp.max(scores[0], axis=1, keepdims=True)
             for j in range(1, 3):
                 top = jnp.maximum(top, jnp.max(scores[j], axis=1, keepdims=True))
@@ -86,7 +95,7 @@
             pool_ref.dtype)
 
     for step in range(seg // tile):
-        pl.when(pl.program_id(1) == step)(functools.partial(run, step))
+        pl.when(tile_index == step)(functools.partial(run, step))
 
 
 def fine_attention(planes, prev0, prev1a, prev1b, qclip, kclip, heads):
@@ -99,30 +108,31 @@
     kernel = functools.partial(fine_kernel, scale=1.0 / math.sqrt(head_dim))
 
     def plane_spec(plane):
-        return pl.BlockSpec((None, tok, pair), lambda h, i: (plane, 0, h))
+        return pl.BlockSpec((None, tok, pair), lambda i, h: (plane, 0, h))
 
     return pl.pallas_call(
         kernel,
-        grid=(pairs, nq),
+        grid=(nq, pairs),
         in_specs=[
-            pl.BlockSpec((tile, 1), lambda h, i: (i, 0)),
-            pl.BlockSpec((1, tok), lambda h, i: (0, 0)),
-            pl.BlockSpec((1, tok), lambda h, i: (0, 1)),
-            pl.BlockSpec((1, tok), lambda h, i: (0, 2)),
-            pl.BlockSpec((None, tile, pair), lambda h, i: (0, i, h)),
+            pl.BlockSpec((tile, 1), lambda i, h: (i, 0)),
+            pl.BlockSpec((1, tok), lambda i, h: (0, 0)),
+            pl.BlockSpec((1, tok), lambda i, h: (0, 1)),
+            pl.BlockSpec((1, tok), lambda i, h: (0, 2)),
+            pl.BlockSpec((None, tile, pair), lambda i, h: (0, i, h)),
             plane_spec(0), plane_spec(1),
             plane_spec(0), plane_spec(1),
             plane_spec(0), plane_spec(1),
             plane_spec(1), plane_spec(2),
         ],
         out_specs=[
-            pl.BlockSpec((tile, pair), lambda h, i: (i, h)),
-            pl.BlockSpec((tile // POOL, pair), lambda h, i: (i, h)),
+            pl.BlockSpec((tile, pair), lambda i, h: (i, h)),
+            pl.BlockSpec((tile // POOL, pair), lambda i, h: (i, h)),
         ],
         out_shape=[
             jax.ShapeDtypeStruct((tok, width), jnp.bfloat16),
             jax.ShapeDtypeStruct((tok // POOL, width), jnp.bfloat16),
         ],
+        scratch_shapes=[pltpu.VMEM((tile, 3 * tok), jnp.float32)],
     )(qclip, kclip, kclip, kclip, planes, prev0, prev0, prev1a, prev1a, prev1b, prev1b,
       planes, planes)
 

time: 177 us -> 178 us (level)
  no operation moved by 1% of the time
where the time goes in v10:
time: 178 us; the launch traced here: 176 us
  waiting for transfers between devices  65.5 us (37%)
  starting transfers between devices  54.9 us (31%)
  Pallas kernels  37.4 us (21%)
  local copies, waits for them, and re-layouts  11.4 us (6%)
  matrix products  4.35 us (2%)
  other arithmetic  2.25 us (1%)
    ppermute x5, waiting for transfers between devices, passed_along(): lax.ppermute(value, axis, [(source, source + steps) for source in range(f...  56.7 us
    ppermute x5, starting transfers between devices, passed_along(): lax.ppermute(value, axis, [(source, source + steps) for source in range(f...  43.5 us
    pallas_call x1, Pallas kernels, fine_attention(): pl.pallas_call(kernel, grid=(nq, pairs), in_specs=[pl.BlockSpec((tile, 1)...  28.2 us
    ppermute x6, waiting for transfers between devices, within_group(): return lax.ppermute(value, axis, pairs)  8.03 us
    pallas_call x1, Pallas kernels, coarse_attention(): pl.pallas_call(kernel, grid=(heads, rows // tile), in_specs=[pl.BlockSpec...  6.8 us
    ppermute x2, starting transfers between devices, pair_swap(): lax.ppermute(value, axis, [(source, source + step) for source in range(st...  6.1 us
    ppermute x6, starting transfers between devices, within_group(): return lax.ppermute(value, axis, pairs)  5.24 us
    dot_general x1, matrix products, body(): jnp.einsum('rd,mdc->mrc', pooled, wplanes, preferred_element_type=jnp.flo...  3.88 us
  transfers between devices with their start and end apart: 13, of which 7 were waited for; matrix products, arithmetic and copies ran while one was open for 3% of the time, Pallas kernels for 1%

profile of v10, /device:TPU:7, one launch (start us, length us, event | category | flops | bytes accessed | tf_op | source)
XLA Modules:
  0.0 176.1 jit_solution(911524005017657826)
XLA Ops:
  0.0 3.3 %slice.33 = bf16[2,512,1024]{2,1,0:T(8,128)(2,1)} slice(bf16[3,512,1024]{2,1,0:T(8,128)(2,1)} %bitcast.56), slice={[1:3], [0:512], [0:1024]} | slice | bytes 4194304 | tf_op jit(solution)/shard_map/slice | solution.py:284
  3.3 3.1 %collective-permute-start = (bf16[2,512,1024]{2,1,0:T(8,128)(2,1)}, bf16[2,512,1024]{2,1,0:T(8,128)(2,1)}, u32[]{:S(2)}, u32[]{:S(2)}) collective-permute-start(bf16[2,512,1024]{2,1,0:T(8,128)(2,1)} %slice.33), channel_id=1, source_target_pairs={{0,2},{1,3},{2,4},{3,5},{4,6},{5,7},{6,8},{7,9},{8,10},{9,11},{10,... | collective-permute-start | bytes 6291464 | tf_op jit(solution)/shard_map/ppermute | solution.py:23
  6.4 1.3 collective-permute-start.1
  7.7 44.3 %collective-permute-done.k0_ref.v0_ref = bf16[2,512,1024]{2,1,0:T(8,128)(2,1)} collective-permute-done((bf16[2,512,1024]{2,1,0:T(8,128)(2,1)}, bf16[2,512,1024]{2,1,0:T(8,128)(2,1)}, u32[]{:S(2)}, u32[]{:S(2)}) %collective-permute-start) | collective-permute-done | bytes 2097184 | tf_op jit(solution)/shard_map/ppermute | solution.py:23
  52.0 4.8 %collective-permute-start.2 = (bf16[2,512,1024]{2,1,0:T(8,128)(2,1)}, bf16[2,512,1024]{2,1,0:T(8,128)(2,1)}, u32[]{:S(2)}, u32[]{:S(2)}) collective-permute-start(bf16[2,512,1024]{2,1,0:T(8,128)(2,1)} %collective-permute-done.k0_ref.v0_ref), channel_id=1, source_target_pairs={{1,0},{3,2},{5,4},{7,6},{9,8},{11,10},{13,12},{15,14},{17,16},{19,... | collective-permute-start | bytes 6291464 | tf_op jit(solution)/shard_map/ppermute | solution.py:169
  56.9 0.8 reshape_reshape.8.qclip_ref
  58.0 0.8 reshape_reshape.7.kclip0_ref.kclip1_ref.kclip2_ref
  58.7 0.8 collective-permute-done.2.k1b_ref.v1b_ref
  59.5 28.2 %shard_map.46 = (bf16[512,1024]{1,0:T(8,128)(2,1)}, bf16[128,1024]{1,0:T(8,128)(2,1)}) custom-call(s32[512,1]{1,0:T(8,128)} %reshape_reshape.8.qclip_ref, s32[1,1536]{1,0:T(1,128)} %reshape_reshape.7.kclip0_ref.kclip1_ref.kclip2_ref, s32[1,1536]{1,0:T(1,128)} %reshape_reshape.7.kclip0_ref.kclip1_ref.kclip2_ref, ...), custom_call_target="tpu_custom_call" | custom-call | tf_op jit(solution)/shard_map/pallas_call | solution.py:113
  87.8 3.9 %fusion.2 = bf16[128,3,1024]{2,0,1:T(8,128)(2,1)S(1)} fusion(bf16[1024,3,1024]{2,0,1:T(8,128)(2,1)} %param.6, bf16[128,1024]{1,0:T(8,128)(2,1)} %get-tuple-element.8), kind=kOutput, calls=%fused_computation.2 | convolution fusion | flops 805699584 | bytes 7340032 | tf_op jit(solution)/shard_map/rd,mdc->mrc/dot_general | solution.py:301
  91.7 0.8 dynamic-slice_bitcast_fusion.2
  92.8 1.6 collective-permute-start.5
  94.5 5.6 %collective-permute-done.3 = bf16[3,128,256]{2,1,0:T(8,128)(2,1)S(1)} collective-permute-done((bf16[3,128,256]{2,1,0:T(8,128)(2,1)}, bf16[3,128,256]{2,1,0:T(8,128)(2,1)S(1)}, u32[]{:S(2)}, u32[]{:S(2)}) %collective-permute-start.3) | collective-permute-done | bytes 196640 | tf_op jit(solution)/shard_map/ppermute | solution.py:32
  100.1 1.4 collective-permute-done.5
  101.7 6.1 %collective-permute-start.6 = (bf16[2,512,256]{2,1,0:T(8,128)(2,1)S(1)}, bf16[2,512,256]{2,1,0:T(8,128)(2,1)}, u32[]{:S(2)}, u32[]{:S(2)}) collective-permute-start(bf16[2,512,256]{2,1,0:T(8,128)(2,1)S(1)} %bitcast.60), channel_id=1, source_target_pairs={{0,8},{1,9},{2,10},{3,11},{4,12},{5,13},{6,14},{7,15},{16,24},{17,... | collective-permute-start | bytes 1572872 | tf_op jit(solution)/shard_map/ppermute | solution.py:23
  107.9 4.0 %collective-permute-start.8 = (bf16[2,512,256]{2,1,0:T(8,128)(2,1)S(1)}, bf16[2,512,256]{2,1,0:T(8,128)(2,1)}, u32[]{:S(2)}, u32[]{:S(2)}) collective-permute-start(bf16[2,512,256]{2,1,0:T(8,128)(2,1)S(1)} %bitcast.61), channel_id=1, source_target_pairs={{0,4},{1,5},{2,6},{3,7},{4,8},{5,9},{6,10},{7,11},{8,12},{9,13},{1... | collective-permute-start | bytes 1572872 | tf_op jit(solution)/shard_map/ppermute | solution.py:23
  111.9 4.6 %collective-permute-done.6.k1_ref.v1_ref = bf16[2,512,256]{2,1,0:T(8,128)(2,1)} collective-permute-done((bf16[2,512,256]{2,1,0:T(8,128)(2,1)S(1)}, bf16[2,512,256]{2,1,0:T(8,128)(2,1)}, u32[]{:S(2)}, u32[]{:S(2)}) %collective-permute-start.6) | collective-permute-done | bytes 524320 | tf_op jit(solution)/shard_map/ppermute | solution.py:23
  116.5 17.4 %collective-permute-start.7 = (bf16[2,512,256]{2,1,0:T(8,128)(2,1)}, bf16[2,512,256]{2,1,0:T(8,128)(2,1)}, u32[]{:S(2)}, u32[]{:S(2)}) collective-permute-start(bf16[2,512,256]{2,1,0:T(8,128)(2,1)} %collective-permute-done.6.k1_ref.v1_ref), channel_id=1, source_target_pairs={{0,4},{1,5},{2,6},{3,7},{4,8},{5,9},{6,10},{7,11},{8,12},{9,13},{1... | collective-permute-start | bytes 1572872 | tf_op jit(solution)/shard_map/ppermute | solution.py:23
  133.9 0.9 copy.8.qclip_ref
  135.5 0.7 slice.34
  136.2 7.8 %collective-permute-done.7.k0_ref.v0_ref = bf16[2,512,256]{2,1,0:T(8,128)(2,1)} collective-permute-done((bf16[2,512,256]{2,1,0:T(8,128)(2,1)}, bf16[2,512,256]{2,1,0:T(8,128)(2,1)}, u32[]{:S(2)}, u32[]{:S(2)}) %collective-permute-start.7) | collective-permute-done | bytes 524320 | tf_op jit(solution)/shard_map/ppermute | solution.py:23
  144.0 6.8 %shard_map.47 = bf16[512,256]{1,0:T(8,128)(2,1)} custom-call(s32[512,1]{1,0:T(8,128)} %copy.8.qclip_ref, s32[1,2048]{1,0:T(1,128)} %bitcast.67, s32[1,2048]{1,0:T(1,128)} %bitcast.68, s32[1,2048]{1,0:T(1,128)} %bitcast.69, s32[1,2048]{1,0:T(1,128)} %bitcast.70, bf16[512,256]{1,0:T(8,128)(2,1)} %bitcast.65, ...), custom_call_target="tpu_custom_call" | custom-call | tf_op jit(solution)/shard_map/pallas_call | solution.py:222
  150.8 0.9 constant_dynamic-slice_fusion
  151.8 1.5 collective-permute-start.9
  153.7 1.3 collective-permute-start.11
  155.0 0.8 bitcast_dynamic-update-slice_fusion.14
  155.8 1.1 collective-permute-done.10
  157.0 0.9 bitcast_dynamic-update-slice_fusion.15
  158.6 12.9 %collective-permute-start.12 = (bf16[1,1024]{1,0:T(2,128)(2,1)S(1)}, bf16[1,1024]{1,0:T(2,128)(2,1)S(1)}, u32[]{:S(2)}, u32[]{:S(2)}) collective-permute-start(bf16[1,1024]{1,0:T(2,128)(2,1)S(1)} %slice.37), channel_id=1, source_target_pairs={{0,1},{1,2},{2,3},{3,4},{4,5},{5,6},{6,7},{7,8},{8,9},{9,10},{10,1... | collective-permute-start | bytes 6152 | tf_op jit(solution)/shard_map/ppermute | solution.py:23
  171.5 0.8 pad_select_fusion.lift_ref
  172.3 2.4 %shard_map.48 = bf16[512,1024]{1,0:T(8,128)(2,1)} custom-call(bf16[512,1024]{1,0:T(8,128)(2,1)} %get-tuple-element.7.fine_ref, bf16[128,1024]{1,0:T(8,128)(2,1)} %pad_select_fusion.lift_ref), custom_call_target="tpu_custom_call" | custom-call | tf_op jit(solution)/shard_map/pallas_call | solution.py:153
  174.7 1.3 fusion.6
  (43 shorter events, 3.0 us)
Async XLA Ops:
  0.0 158.1 %copy-start = (bf16[1024,1024]{1,0:T(8,128)(2,1)S(1)}, bf16[1024,1024]{1,0:T(8,128)(2,1)}, u32[]{:S(2)}) copy-start(bf16[1024,1024]{1,0:T(8,128)(2,1)} %param.7) | copy-start | bytes 6291460
  0.0 56.8 %copy-start.2 = (s32[2048]{0:T(1024)S(1)}, s32[2048]{0:T(1024)}, u32[]{:S(2)}) copy-start(s32[2048]{0:T(1024)} %param.5) | copy-start | bytes 24580
  3.3 48.7 %collective-permute-start = (bf16[2,512,1024]{2,1,0:T(8,128)(2,1)}, bf16[2,512,1024]{2,1,0:T(8,128)(2,1)}, u32[]{:S(2)}, u32[]{:S(2)}) collective-permute-start(bf16[2,512,1024]{2,1,0:T(8,128)(2,1)} %slice.33), channel_id=1, source_target_pairs={{0,2},{1,3},{2,4},{3,5},{4,6},{5,7},{6,8},{7,9},{8,10},{9,11},{10,... | collective-permute-start | bytes 6291464 | tf_op jit(solution)/shard_map/ppermute | solution.py:23
  6.4 52.3 %collective-permute-start.1 = (bf16[2,512,1024]{2,1,0:T(8,128)(2,1)}, bf16[2,512,1024]{2,1,0:T(8,128)(2,1)}, u32[]{:S(2)}, u32[]{:S(2)}) collective-permute-start(bf16[2,512,1024]{2,1,0:T(8,128)(2,1)} %slice.33), channel_id=1, source_target_pairs={{0,1},{2,3},{4,5},{6,7},{8,9},{10,11},{12,13},{14,15},{16,17},{18,... | collective-permute-start | bytes 6291464 | tf_op jit(solution)/shard_map/ppermute | solution.py:169
  52.0 7.6 %collective-permute-start.2 = (bf16[2,512,1024]{2,1,0:T(8,128)(2,1)}, bf16[2,512,1024]{2,1,0:T(8,128)(2,1)}, u32[]{:S(2)}, u32[]{:S(2)}) collective-permute-start(bf16[2,512,1024]{2,1,0:T(8,128)(2,1)} %collective-permute-done.k0_ref.v0_ref), channel_id=1, source_target_pairs={{1,0},{3,2},{5,4},{7,6},{9,8},{11,10},{13,12},{15,14},{17,16},{19,... | collective-permute-start | bytes 6291464 | tf_op jit(solution)/shard_map/ppermute | solution.py:169
  92.4 7.6 %collective-permute-start.3 = (bf16[3,128,256]{2,1,0:T(8,128)(2,1)}, bf16[3,128,256]{2,1,0:T(8,128)(2,1)S(1)}, u32[]{:S(2)}, u32[]{:S(2)}) collective-permute-start(bf16[3,128,256]{2,1,0:T(8,128)(2,1)} %get-tuple-element.13), channel_id=1, source_target_pairs={{0,3},{1,0},{2,1},{3,2},{4,7},{5,4},{6,5},{7,6},{8,11},{9,8},{10,9... | collective-permute-start | bytes 589832 | tf_op jit(solution)/shard_map/ppermute | solution.py:32
  92.8 7.2 %collective-permute-start.4 = (bf16[3,128,256]{2,1,0:T(8,128)(2,1)S(1)}, bf16[3,128,256]{2,1,0:T(8,128)(2,1)S(1)}, u32[]{:S(2)}, u32[]{:S(2)}) collective-permute-start(bf16[3,128,256]{2,1,0:T(8,128)(2,1)S(1)} %get-tuple-element.12), channel_id=1, source_target_pairs={{0,2},{1,3},{2,0},{3,1},{4,6},{5,7},{6,4},{7,5},{8,10},{9,11},{10,... | collective-permute-start | bytes 589832 | tf_op jit(solution)/shard_map/ppermute | solution.py:32
  92.8 8.6 %collective-permute-start.5 = (bf16[3,128,256]{2,1,0:T(8,128)(2,1)S(1)}, bf16[3,128,256]{2,1,0:T(8,128)(2,1)S(1)}, u32[]{:S(2)}, u32[]{:S(2)}) collective-permute-start(bf16[3,128,256]{2,1,0:T(8,128)(2,1)S(1)} %get-tuple-element.11), channel_id=1, source_target_pairs={{0,1},{1,2},{2,3},{3,0},{4,5},{5,6},{6,7},{7,4},{8,9},{9,10},{10,1... | collective-permute-start | bytes 589832 | tf_op jit(solution)/shard_map/ppermute | solution.py:32
  101.7 42.3 %copy-start.1 = (bf16[2,4,128,256]{3,2,1,0:T(8,128)(2,1)}, bf16[2,4,128,256]{3,2,1,0:T(8,128)(2,1)S(1)}, u32[]{:S(2)}) copy-start(bf16[2,4,128,256]{3,2,1,0:T(8,128)(2,1)S(1)} %copy.7) | copy-start | bytes 1572868
  101.7 14.7 %collective-permute-start.6 = (bf16[2,512,256]{2,1,0:T(8,128)(2,1)S(1)}, bf16[2,512,256]{2,1,0:T(8,128)(2,1)}, u32[]{:S(2)}, u32[]{:S(2)}) collective-permute-start(bf16[2,512,256]{2,1,0:T(8,128)(2,1)S(1)} %bitcast.60), channel_id=1, source_target_pairs={{0,8},{1,9},{2,10},{3,11},{4,12},{5,13},{6,14},{7,15},{16,24},{17,... | collective-permute-start | bytes 1572872 | tf_op jit(solution)/shard_map/ppermute | solution.py:23
  107.9 28.3 %collective-permute-start.8 = (bf16[2,512,256]{2,1,0:T(8,128)(2,1)S(1)}, bf16[2,512,256]{2,1,0:T(8,128)(2,1)}, u32[]{:S(2)}, u32[]{:S(2)}) collective-permute-start(bf16[2,512,256]{2,1,0:T(8,128)(2,1)S(1)} %bitcast.61), channel_id=1, source_target_pairs={{0,4},{1,5},{2,6},{3,7},{4,8},{5,9},{6,10},{7,11},{8,12},{9,13},{1... | collective-permute-start | bytes 1572872 | tf_op jit(solution)/shard_map/ppermute | solution.py:23
  116.5 27.6 %collective-permute-start.7 = (bf16[2,512,256]{2,1,0:T(8,128)(2,1)}, bf16[2,512,256]{2,1,0:T(8,128)(2,1)}, u32[]{:S(2)}, u32[]{:S(2)}) collective-permute-start(bf16[2,512,256]{2,1,0:T(8,128)(2,1)} %collective-permute-done.6.k1_ref.v1_ref), channel_id=1, source_target_pairs={{0,4},{1,5},{2,6},{3,7},{4,8},{5,9},{6,10},{7,11},{8,12},{9,13},{1... | collective-permute-start | bytes 1572872 | tf_op jit(solution)/shard_map/ppermute | solution.py:23
  151.8 4.1 %collective-permute-start.9 = (bf16[128,256]{1,0:T(8,128)(2,1)S(1)}, bf16[128,256]{1,0:T(8,128)(2,1)S(1)}, u32[]{:S(2)}, u32[]{:S(2)}) collective-permute-start(bf16[128,256]{1,0:T(8,128)(2,1)S(1)} %get-tuple-element.16), channel_id=1, source_target_pairs={{0,3},{1,0},{2,1},{3,2},{4,7},{5,4},{6,5},{7,6},{8,11},{9,8},{10,9... | collective-permute-start | bytes 196616 | tf_op jit(solution)/shard_map/ppermute | solution.py:32
  153.3 3.7 %collective-permute-start.10 = (bf16[128,256]{1,0:T(8,128)(2,1)S(1)}, bf16[128,256]{1,0:T(8,128)(2,1)S(1)}, u32[]{:S(2)}, u32[]{:S(2)}) collective-permute-start(bf16[128,256]{1,0:T(8,128)(2,1)S(1)} %get-tuple-element.15), channel_id=1, source_target_pairs={{0,2},{1,3},{2,0},{3,1},{4,6},{5,7},{6,4},{7,5},{8,10},{9,11},{10,... | collective-permute-start | bytes 196616 | tf_op jit(solution)/shard_map/ppermute | solution.py:32
  153.7 3.3 %collective-permute-start.11 = (bf16[128,256]{1,0:T(8,128)(2,1)S(1)}, bf16[128,256]{1,0:T(8,128)(2,1)S(1)}, u32[]{:S(2)}, u32[]{:S(2)}) collective-permute-start(bf16[128,256]{1,0:T(8,128)(2,1)S(1)} %get-tuple-element.14), channel_id=1, source_target_pairs={{0,1},{1,2},{2,3},{3,0},{4,5},{5,6},{6,7},{7,4},{8,9},{9,10},{10,1... | collective-permute-start | bytes 196616 | tf_op jit(solution)/shard_map/ppermute | solution.py:32
  158.6 16.1 %collective-permute-start.12 = (bf16[1,1024]{1,0:T(2,128)(2,1)S(1)}, bf16[1,1024]{1,0:T(2,128)(2,1)S(1)}, u32[]{:S(2)}, u32[]{:S(2)}) collective-permute-start(bf16[1,1024]{1,0:T(2,128)(2,1)S(1)} %slice.37), channel_id=1, source_target_pairs={{0,1},{1,2},{2,3},{3,4},{4,5},{5,6},{6,7},{7,8},{8,9},{9,10},{10,1... | collective-permute-start | bytes 6152 | tf_op jit(solution)/shard_map/ppermute | solution.py:23

commit v11 on v10

--- a/solution.py
+++ b/solution.py
@@ -15,6 +15,7 @@
 FREACH = 2
 CREACH = 3
 FINE_TILE = 256
+HALVES = 2
 
 
 def passed_along(value, axis, steps):
@@ -98,17 +99,20 @@
         pl.when(tile_index == step)(functools.partial(run, step))
 
 
-def fine_attention(planes, prev0, prev1a, prev1b, qclip, kclip, heads):
+def fine_attention(planes, prev0, prev1a, prev1b, qclip, kclip, heads, first_pair):
     _, tok, width = planes.shape
     head_dim = width // heads
     pair = 2 * head_dim
-    pairs = width // pair
+    pairs = prev0.shape[2] // pair
     tile = min(FINE_TILE, tok)
     nq = tok // tile
     kernel = functools.partial(fine_kernel, scale=1.0 / math.sqrt(head_dim))
 
     def plane_spec(plane):
         return pl.BlockSpec((None, tok, pair), lambda i, h: (plane, 0, h))
+
+    def own_spec(plane):
+        return pl.BlockSpec((None, tok, pair), lambda i, h: (plane, 0, first_pair + h))
 
     return pl.pallas_call(
         kernel,
@@ -118,19 +122,19 @@
             pl.BlockSpec((1, tok), lambda i, h: (0, 0)),
             pl.BlockSpec((1, tok), lambda i, h: (0, 1)),
             pl.BlockSpec((1, tok), lambda i, h: (0, 2)),
-            pl.BlockSpec((None, tile, pair), lambda i, h: (0, i, h)),
+            pl.BlockSpec((None, tile, pair), lambda i, h: (0, i, first_pair + h)),
             plane_spec(0), plane_spec(1),
             plane_spec(0), plane_spec(1),
             plane_spec(0), plane_spec(1),
-            plane_spec(1), plane_spec(2),
+            own_spec(1), own_spec(2),
         ],
         out_specs=[
             pl.BlockSpec((tile, pair), lambda i, h: (i, h)),
             pl.BlockSpec((tile // POOL, pair), lambda i, h: (i, h)),
         ],
         out_shape=[
-            jax.ShapeDtypeStruct((tok, width), jnp.bfloat16),
-            jax.ShapeDtypeStruct((tok // POOL, width), jnp.bfloat16),
+            jax.ShapeDtypeStruct((tok, pairs * pair), jnp.bfloat16),
+            jax.ShapeDtypeStruct((tok // POOL, pairs * pair), jnp.bfloat16),
         ],
         scratch_shapes=[pltpu.VMEM((tile, 3 * tok), jnp.float32)],
     )(qclip, kclip, kclip, kclip, planes, prev0, prev0, prev1a, prev1a, prev1b, prev1b,
@@ -281,10 +285,6 @@
     quarter = position % QUARTERS
     cycle_place = position // QUARTERS
     planes = jnp.transpose(fine_qkv, (1, 0, 2))
-    own_pairs = planes[1:]
-    prev0 = passed_along(own_pairs, "seq", 2)
-    prev1a = pair_swap(own_pairs, "seq", False)
-    prev1b = pair_swap(prev0, "seq", True)
     clip_front = jnp.concatenate([jnp.full((FREACH * coarse_rows,), -1, jnp.int32), clip_ids])
     key_clip = jnp.repeat(
         lax.dynamic_slice_in_dim(clip_front, position * coarse_rows, (FREACH + 1) * coarse_rows, 0),
@@ -292,10 +292,30 @@
     )
     own_clip = lax.dynamic_slice_in_dim(clip_ids, position * coarse_rows, coarse_rows, 0)
     query_clip = jnp.repeat(own_clip, POOL)
-    fine_out, pooled = fine_attention(
-        planes, prev0, prev1a, prev1b, query_clip.reshape(tok_count, 1),
-        key_clip.reshape(1, (FREACH + 1) * tok_count), FHEADS,
-    )
+    head_pair_width = 2 * feat_width // FHEADS
+    part_width = feat_width // HALVES
+    outs = []
+    pools = []
+    gate = None
+    for part in range(HALVES):
+        own_pairs = planes[1:, :, part * part_width:(part + 1) * part_width]
+        if gate is not None:
+            own_pairs, _ = lax.optimization_barrier((own_pairs, gate))
+        prev0 = passed_along(own_pairs, "seq", 2)
+        gate = prev0
+        if outs:
+            prev0, _ = lax.optimization_barrier((prev0, outs[-1]))
+        prev1a = pair_swap(own_pairs, "seq", False)
+        prev1b = pair_swap(prev0, "seq", True)
+        part_out, part_pool = fine_attention(
+            planes, prev0, prev1a, prev1b, query_clip.reshape(tok_count, 1),
+            key_clip.reshape(1, (FREACH + 1) * tok_count), FHEADS,
+            part * part_width // head_pair_width,
+        )
+        outs.append(part_out)
+        pools.append(part_pool)
+    fine_out = jnp.concatenate(outs, axis=1)
+    pooled = jnp.concatenate(pools, axis=1)
     quarter_width = w_coarse.shape[2] // QUARTERS
     wplanes = jnp.transpose(w_coarse, (1, 0, 2))
     projected = jnp.einsum(

time: 178 us -> 170 us (0.955)
  waiting for transfers between devices: 65.5 us -> 45 us
  starting transfers between devices: 54.9 us -> 62.3 us
  Pallas kernels: 37.4 us -> 39.9 us
  local copies, waits for them, and re-layouts: 11.4 us -> 13.9 us
    ppermute x5 -> x6, waiting for transfers between devices: 56.7 us -> 35.6 us  [passed_along(): lax.ppermute(value, axis, [(source, source + steps) for source in range(f...]
    ppermute x5 -> x6, starting transfers between devices: 43.5 us -> 47.8 us  [passed_along(): lax.ppermute(value, axis, [(source, source + steps) for source in range(f...]
    ppermute x2 -> x4, starting transfers between devices: 6.1 us -> 9.26 us  [pair_swap(): lax.ppermute(value, axis, [(source, source + step) for source in range(st...]
    pallas_call x1 -> x2, Pallas kernels: 28.2 us -> 30.7 us  [fine_attention(): pl.pallas_call(kernel, grid=(nq, pairs), in_specs=[pl.BlockSpec((tile, 1)...]
  transfers between devices with their start and end apart: 13 -> 16, of which waited for: 7 -> 8; matrix products, arithmetic and copies ran while one was open for 3% -> 5% of each run, Pallas kernels for 1% -> 11%
where the time goes in v11:
time: 170 us; the launch traced here: 168 us
  starting transfers between devices  62.3 us (37%)
  waiting for transfers between devices  45 us (26%)
  Pallas kernels  39.9 us (23%)
  local copies, waits for them, and re-layouts  13.9 us (8%)
  matrix products  4.32 us (3%)
  other arithmetic  2.25 us (1%)
    ppermute x6, starting transfers between devices, passed_along(): lax.ppermute(value, axis, [(source, source + steps) for source in range(f...  47.8 us
    ppermute x6, waiting for transfers between devices, passed_along(): lax.ppermute(value, axis, [(source, source + steps) for source in range(f...  35.6 us
    pallas_call x2, Pallas kernels, fine_attention(): pl.pallas_call(kernel, grid=(nq, pairs), in_specs=[pl.BlockSpec((tile, 1)...  30.7 us
    ppermute x4, starting transfers between devices, pair_swap(): lax.ppermute(value, axis, [(source, source + step) for source in range(st...  9.26 us
    ppermute x6, waiting for transfers between devices, within_group(): return lax.ppermute(value, axis, pairs)  8.03 us
    pallas_call x1, Pallas kernels, coarse_attention(): pl.pallas_call(kernel, grid=(heads, rows // tile), in_specs=[pl.BlockSpec...  6.8 us
    ppermute x6, starting transfers between devices, within_group(): return lax.ppermute(value, axis, pairs)  5.22 us
    dot_general x1, matrix products, body(): jnp.einsum('rd,mdc->mrc', pooled, wplanes, preferred_element_type=jnp.flo...  3.85 us
  transfers between devices with their start and end apart: 16, of which 8 were waited for; matrix products, arithmetic and copies ran while one was open for 5% of the time, Pallas kernels for 11%

profile of v11, /device:TPU:7, one launch (start us, length us, event | category | flops | bytes accessed | tf_op | source)
XLA Modules:
  0.0 168.0 jit_solution(10360225132440335744)
XLA Ops:
  0.0 3.2 %fusion.12 = (bf16[2,512,512]{2,1,0:T(8,128)(2,1)}, bf16[2,512,512]{2,1,0:T(8,128)(2,1)}) fusion(bf16[3,512,1024]{2,1,0:T(8,128)(2,1)} %bitcast.56), kind=kLoop, calls=%fused_computation.44 | loop fusion | bytes 4194304 | tf_op jit(solution)/shard_map/slice | solution.py:301
  3.2 3.1 %collective-permute-start = (bf16[2,512,512]{2,1,0:T(8,128)(2,1)}, bf16[2,512,512]{2,1,0:T(8,128)(2,1)}, u32[]{:S(2)}, u32[]{:S(2)}) collective-permute-start(bf16[2,512,512]{2,1,0:T(8,128)(2,1)} %get-tuple-element.20), channel_id=1, source_target_pairs={{0,2},{1,3},{2,4},{3,5},{4,6},{5,7},{6,8},{7,9},{8,10},{9,11},{10,... | collective-permute-start | bytes 3145736 | tf_op jit(solution)/shard_map/ppermute | solution.py:24
  6.3 1.3 collective-permute-start.1
  7.6 21.8 %collective-permute-done.k0_ref.v0_ref = bf16[2,512,512]{2,1,0:T(8,128)(2,1)} collective-permute-done((bf16[2,512,512]{2,1,0:T(8,128)(2,1)}, bf16[2,512,512]{2,1,0:T(8,128)(2,1)}, u32[]{:S(2)}, u32[]{:S(2)}) %collective-permute-start) | collective-permute-done | bytes 1048608 | tf_op jit(solution)/shard_map/ppermute | solution.py:24
  29.4 4.4 %collective-permute-start.2 = (bf16[2,512,512]{2,1,0:T(8,128)(2,1)}, bf16[2,512,512]{2,1,0:T(8,128)(2,1)}, u32[]{:S(2)}, u32[]{:S(2)}) collective-permute-start(bf16[2,512,512]{2,1,0:T(8,128)(2,1)} %collective-permute-done.k0_ref.v0_ref), channel_id=1, source_target_pairs={{1,0},{3,2},{5,4},{7,6},{9,8},{11,10},{13,12},{15,14},{17,16},{19,... | collective-permute-start | bytes 3145736 | tf_op jit(solution)/shard_map/ppermute | solution.py:173
  33.8 4.0 %collective-permute-start.3 = (bf16[2,512,512]{2,1,0:T(8,128)(2,1)}, bf16[2,512,512]{2,1,0:T(8,128)(2,1)S(1)}, u32[]{:S(2)}, u32[]{:S(2)}) collective-permute-start(bf16[2,512,512]{2,1,0:T(8,128)(2,1)} %get-tuple-element.12), channel_id=1, source_target_pairs={{0,2},{1,3},{2,4},{3,5},{4,6},{5,7},{6,8},{7,9},{8,10},{9,11},{10,... | collective-permute-start | bytes 3145736 | tf_op jit(solution)/shard_map/ppermute | solution.py:24
  39.8 1.3 collective-permute-start.4
  41.1 15.3 %shard_map.46 = (bf16[512,512]{1,0:T(8,128)(2,1)}, bf16[128,512]{1,0:T(8,128)(2,1)}) custom-call(s32[512,1]{1,0:T(8,128)} %reshape_reshape.10.qclip_ref, s32[1,1536]{1,0:T(1,128)} %reshape_reshape.9.kclip0_ref.kclip1_ref.kclip2_ref, s32[1,1536]{1,0:T(1,128)} %reshape_reshape.9.kclip0_ref.kclip1_ref.kclip2_ref, ...), custom_call_target="tpu_custom_call" | custom-call | tf_op jit(solution)/shard_map/pallas_call | solution.py:117
  56.5 3.6 %collective-permute-done.3.k0_ref.v0_ref = bf16[2,512,512]{2,1,0:T(8,128)(2,1)S(1)} collective-permute-done((bf16[2,512,512]{2,1,0:T(8,128)(2,1)}, bf16[2,512,512]{2,1,0:T(8,128)(2,1)S(1)}, u32[]{:S(2)}, u32[]{:S(2)}) %collective-permute-start.3) | collective-permute-done | bytes 1048608 | tf_op jit(solution)/shard_map/ppermute | solution.py:24
  60.0 2.3 %collective-permute-start.5 = (bf16[2,512,512]{2,1,0:T(8,128)(2,1)S(1)}, bf16[2,512,512]{2,1,0:T(8,128)(2,1)}, u32[]{:S(2)}, u32[]{:S(2)}) collective-permute-start(bf16[2,512,512]{2,1,0:T(8,128)(2,1)S(1)} %collective-permute-done.3.k0_ref.v0_ref), channel_id=1, source_target_pairs={{1,0},{3,2},{5,4},{7,6},{9,8},{11,10},{13,12},{15,14},{17,16},{19,... | collective-permute-start | bytes 3145736 | tf_op jit(solution)/shard_map/ppermute | solution.py:173
  62.3 1.4 collective-permute-done.5.k1b_ref.v1b_ref
  63.7 15.4 %shard_map.47 = (bf16[512,512]{1,0:T(8,128)(2,1)}, bf16[128,512]{1,0:T(8,128)(2,1)}) custom-call(s32[512,1]{1,0:T(8,128)} %reshape_reshape.10.qclip_ref, s32[1,1536]{1,0:T(1,128)} %reshape_reshape.9.kclip0_ref.kclip1_ref.kclip2_ref, s32[1,1536]{1,0:T(1,128)} %reshape_reshape.9.kclip0_ref.kclip1_ref.kclip2_ref, ...), custom_call_target="tpu_custom_call" | custom-call | tf_op jit(solution)/shard_map/pallas_call | solution.py:117
  79.1 3.9 %fusion.2 = bf16[128,3,1024]{2,0,1:T(8,128)(2,1)S(1)} fusion(bf16[1024,3,1024]{2,0,1:T(8,128)(2,1)} %param.6, bf16[128,512]{1,0:T(8,128)(2,1)} %get-tuple-element.16, bf16[128,512]{1,0:T(8,128)(2,1)S(1)} %copy-done.4), kind=kOutput, calls=%fused_computation.2 | convolution fusion | flops 806223872 | bytes 7340032 | tf_op jit(solution)/shard_map/rd,mdc->mrc/dot_general | solution.py:321
  84.1 1.6 collective-permute-start.8
  85.8 5.6 %collective-permute-done.6 = bf16[3,128,256]{2,1,0:T(8,128)(2,1)S(1)} collective-permute-done((bf16[3,128,256]{2,1,0:T(8,128)(2,1)}, bf16[3,128,256]{2,1,0:T(8,128)(2,1)S(1)}, u32[]{:S(2)}, u32[]{:S(2)}) %collective-permute-start.6) | collective-permute-done | bytes 196640 | tf_op jit(solution)/shard_map/ppermute | solution.py:33
  91.4 1.3 collective-permute-done.8
  93.1 6.9 %collective-permute-start.9 = (bf16[2,512,256]{2,1,0:T(8,128)(2,1)S(1)}, bf16[2,512,256]{2,1,0:T(8,128)(2,1)}, u32[]{:S(2)}, u32[]{:S(2)}) collective-permute-start(bf16[2,512,256]{2,1,0:T(8,128)(2,1)S(1)} %bitcast.63), channel_id=1, source_target_pairs={{0,8},{1,9},{2,10},{3,11},{4,12},{5,13},{6,14},{7,15},{16,24},{17,... | collective-permute-start | bytes 1572872 | tf_op jit(solution)/shard_map/ppermute | solution.py:24
  99.9 4.0 %collective-permute-start.11 = (bf16[2,512,256]{2,1,0:T(8,128)(2,1)S(1)}, bf16[2,512,256]{2,1,0:T(8,128)(2,1)}, u32[]{:S(2)}, u32[]{:S(2)}) collective-permute-start(bf16[2,512,256]{2,1,0:T(8,128)(2,1)S(1)} %bitcast.64), channel_id=1, source_target_pairs={{0,4},{1,5},{2,6},{3,7},{4,8},{5,9},{6,10},{7,11},{8,12},{9,13},{1... | collective-permute-start | bytes 1572872 | tf_op jit(solution)/shard_map/ppermute | solution.py:24
  103.9 5.0 %collective-permute-done.9.k1_ref.v1_ref = bf16[2,512,256]{2,1,0:T(8,128)(2,1)} collective-permute-done((bf16[2,512,256]{2,1,0:T(8,128)(2,1)S(1)}, bf16[2,512,256]{2,1,0:T(8,128)(2,1)}, u32[]{:S(2)}, u32[]{:S(2)}) %collective-permute-start.9) | collective-permute-done | bytes 524320 | tf_op jit(solution)/shard_map/ppermute | solution.py:24
  108.9 17.0 %collective-permute-start.10 = (bf16[2,512,256]{2,1,0:T(8,128)(2,1)}, bf16[2,512,256]{2,1,0:T(8,128)(2,1)}, u32[]{:S(2)}, u32[]{:S(2)}) collective-permute-start(bf16[2,512,256]{2,1,0:T(8,128)(2,1)} %collective-permute-done.9.k1_ref.v1_ref), channel_id=1, source_target_pairs={{0,4},{1,5},{2,6},{3,7},{4,8},{5,9},{6,10},{7,11},{8,12},{9,13},{1... | collective-permute-start | bytes 1572872 | tf_op jit(solution)/shard_map/ppermute | solution.py:24
  126.0 0.9 copy.9.qclip_ref
  127.5 1.1 constant_dynamic-update-slice_fusion.1
  128.6 1.1 constant_dynamic-update-slice_fusion.fine_ref
  130.8 5.3 %collective-permute-done.10.k0_ref.v0_ref = bf16[2,512,256]{2,1,0:T(8,128)(2,1)} collective-permute-done((bf16[2,512,256]{2,1,0:T(8,128)(2,1)}, bf16[2,512,256]{2,1,0:T(8,128)(2,1)}, u32[]{:S(2)}, u32[]{:S(2)}) %collective-permute-start.10) | collective-permute-done | bytes 524320 | tf_op jit(solution)/shard_map/ppermute | solution.py:24
  136.1 6.8 %shard_map.48 = bf16[512,256]{1,0:T(8,128)(2,1)} custom-call(s32[512,1]{1,0:T(8,128)} %copy.9.qclip_ref, s32[1,2048]{1,0:T(1,128)} %bitcast.70, s32[1,2048]{1,0:T(1,128)} %bitcast.71, s32[1,2048]{1,0:T(1,128)} %bitcast.72, s32[1,2048]{1,0:T(1,128)} %bitcast.73, bf16[512,256]{1,0:T(8,128)(2,1)} %bitcast.68, ...), custom_call_target="tpu_custom_call" | custom-call | tf_op jit(solution)/shard_map/pallas_call | solution.py:226
  142.9 0.9 constant_dynamic-slice_fusion
  143.8 1.5 collective-permute-start.12
  145.4 1.7 %collective-permute-start.14 = (bf16[128,256]{1,0:T(8,128)(2,1)S(1)}, bf16[128,256]{1,0:T(8,128)(2,1)S(1)}, u32[]{:S(2)}, u32[]{:S(2)}) collective-permute-start(bf16[128,256]{1,0:T(8,128)(2,1)S(1)} %get-tuple-element.24), channel_id=1, source_target_pairs={{0,1},{1,2},{2,3},{3,0},{4,5},{5,6},{6,7},{7,4},{8,9},{9,10},{10,1... | collective-permute-start | bytes 196616 | tf_op jit(solution)/shard_map/ppermute | solution.py:33
  147.9 1.1 collective-permute-done.13
  150.6 12.8 %collective-permute-start.15 = (bf16[1,1024]{1,0:T(2,128)(2,1)S(1)}, bf16[1,1024]{1,0:T(2,128)(2,1)S(1)}, u32[]{:S(2)}, u32[]{:S(2)}) collective-permute-start(bf16[1,1024]{1,0:T(2,128)(2,1)S(1)} %slice.43), channel_id=1, source_target_pairs={{0,1},{1,2},{2,3},{3,4},{4,5},{5,6},{6,7},{7,8},{8,9},{9,10},{10,1... | collective-permute-start | bytes 6152 | tf_op jit(solution)/shard_map/ppermute | solution.py:24
  164.2 2.4 %shard_map.49 = bf16[512,1024]{1,0:T(8,128)(2,1)} custom-call(bf16[512,1024]{1,0:T(8,128)(2,1)} %copy-done.3, bf16[128,1024]{1,0:T(8,128)(2,1)} %pad_select_fusion.lift_ref), custom_call_target="tpu_custom_call" | custom-call | tf_op jit(solution)/shard_map/pallas_call | solution.py:157
  166.7 1.3 fusion.7
  (58 shorter events, 8.5 us)
Async XLA Ops:
  0.0 150.1 %copy-start = (bf16[1024,1024]{1,0:T(8,128)(2,1)S(1)}, bf16[1024,1024]{1,0:T(8,128)(2,1)}, u32[]{:S(2)}) copy-start(bf16[1024,1024]{1,0:T(8,128)(2,1)} %param.7) | copy-start | bytes 6291460
  0.0 37.9 %copy-start.5 = (s32[2048]{0:T(1024)S(1)}, s32[2048]{0:T(1024)}, u32[]{:S(2)}) copy-start(s32[2048]{0:T(1024)} %param.5) | copy-start | bytes 24580
  3.2 26.2 %collective-permute-start = (bf16[2,512,512]{2,1,0:T(8,128)(2,1)}, bf16[2,512,512]{2,1,0:T(8,128)(2,1)}, u32[]{:S(2)}, u32[]{:S(2)}) collective-permute-start(bf16[2,512,512]{2,1,0:T(8,128)(2,1)} %get-tuple-element.20), channel_id=1, source_target_pairs={{0,2},{1,3},{2,4},{3,5},{4,6},{5,7},{6,8},{7,9},{8,10},{9,11},{10,... | collective-permute-start | bytes 3145736 | tf_op jit(solution)/shard_map/ppermute | solution.py:24
  6.3 34.8 %collective-permute-start.1 = (bf16[2,512,512]{2,1,0:T(8,128)(2,1)}, bf16[2,512,512]{2,1,0:T(8,128)(2,1)}, u32[]{:S(2)}, u32[]{:S(2)}) collective-permute-start(bf16[2,512,512]{2,1,0:T(8,128)(2,1)} %get-tuple-element.20), channel_id=1, source_target_pairs={{0,1},{2,3},{4,5},{6,7},{8,9},{10,11},{12,13},{14,15},{16,17},{18,... | collective-permute-start | bytes 3145736 | tf_op jit(solution)/shard_map/ppermute | solution.py:173
  29.4 11.7 %collective-permute-start.2 = (bf16[2,512,512]{2,1,0:T(8,128)(2,1)}, bf16[2,512,512]{2,1,0:T(8,128)(2,1)}, u32[]{:S(2)}, u32[]{:S(2)}) collective-permute-start(bf16[2,512,512]{2,1,0:T(8,128)(2,1)} %collective-permute-done.k0_ref.v0_ref), channel_id=1, source_target_pairs={{1,0},{3,2},{5,4},{7,6},{9,8},{11,10},{13,12},{15,14},{17,16},{19,... | collective-permute-start | bytes 3145736 | tf_op jit(solution)/shard_map/ppermute | solution.py:173
  33.8 26.2 %collective-permute-start.3 = (bf16[2,512,512]{2,1,0:T(8,128)(2,1)}, bf16[2,512,512]{2,1,0:T(8,128)(2,1)S(1)}, u32[]{:S(2)}, u32[]{:S(2)}) collective-permute-start(bf16[2,512,512]{2,1,0:T(8,128)(2,1)} %get-tuple-element.12), channel_id=1, source_target_pairs={{0,2},{1,3},{2,4},{3,5},{4,6},{5,7},{6,8},{7,9},{8,10},{9,11},{10,... | collective-permute-start | bytes 3145736 | tf_op jit(solution)/shard_map/ppermute | solution.py:24
  39.8 22.5 %collective-permute-start.4 = (bf16[2,512,512]{2,1,0:T(8,128)(2,1)}, bf16[2,512,512]{2,1,0:T(8,128)(2,1)}, u32[]{:S(2)}, u32[]{:S(2)}) collective-permute-start(bf16[2,512,512]{2,1,0:T(8,128)(2,1)} %get-tuple-element.12), channel_id=1, source_target_pairs={{0,1},{2,3},{4,5},{6,7},{8,9},{10,11},{12,13},{14,15},{16,17},{18,... | collective-permute-start | bytes 3145736 | tf_op jit(solution)/shard_map/ppermute | solution.py:173
  60.0 3.7 %copy-start.2 = (bf16[2,512,512]{2,1,0:T(8,128)(2,1)}, bf16[2,512,512]{2,1,0:T(8,128)(2,1)S(1)}, u32[]{:S(2)}) copy-start(bf16[2,512,512]{2,1,0:T(8,128)(2,1)S(1)} %collective-permute-done.3.k0_ref.v0_ref) | copy-start | bytes 3145732
  60.0 3.7 %collective-permute-start.5 = (bf16[2,512,512]{2,1,0:T(8,128)(2,1)S(1)}, bf16[2,512,512]{2,1,0:T(8,128)(2,1)}, u32[]{:S(2)}, u32[]{:S(2)}) collective-permute-start(bf16[2,512,512]{2,1,0:T(8,128)(2,1)S(1)} %collective-permute-done.3.k0_ref.v0_ref), channel_id=1, source_target_pairs={{1,0},{3,2},{5,4},{7,6},{9,8},{11,10},{13,12},{15,14},{17,16},{19,... | collective-permute-start | bytes 3145736 | tf_op jit(solution)/shard_map/ppermute | solution.py:173
  62.3 16.8 %copy-start.4 = (bf16[128,512]{1,0:T(8,128)(2,1)S(1)}, bf16[128,512]{1,0:T(8,128)(2,1)}, u32[]{:S(2)}) copy-start(bf16[128,512]{1,0:T(8,128)(2,1)} %get-tuple-element.15) | copy-start | bytes 393220
  83.8 7.6 %collective-permute-start.6 = (bf16[3,128,256]{2,1,0:T(8,128)(2,1)}, bf16[3,128,256]{2,1,0:T(8,128)(2,1)S(1)}, u32[]{:S(2)}, u32[]{:S(2)}) collective-permute-start(bf16[3,128,256]{2,1,0:T(8,128)(2,1)} %get-tuple-element.23), channel_id=1, source_target_pairs={{0,3},{1,0},{2,1},{3,2},{4,7},{5,4},{6,5},{7,6},{8,11},{9,8},{10,9... | collective-permute-start | bytes 589832 | tf_op jit(solution)/shard_map/ppermute | solution.py:33
  84.1 7.3 %collective-permute-start.7 = (bf16[3,128,256]{2,1,0:T(8,128)(2,1)S(1)}, bf16[3,128,256]{2,1,0:T(8,128)(2,1)S(1)}, u32[]{:S(2)}, u32[]{:S(2)}) collective-permute-start(bf16[3,128,256]{2,1,0:T(8,128)(2,1)S(1)} %get-tuple-element.22), channel_id=1, source_target_pairs={{0,2},{1,3},{2,0},{3,1},{4,6},{5,7},{6,4},{7,5},{8,10},{9,11},{10,... | collective-permute-start | bytes 589832 | tf_op jit(solution)/shard_map/ppermute | solution.py:33
  84.1 8.6 %collective-permute-start.8 = (bf16[3,128,256]{2,1,0:T(8,128)(2,1)S(1)}, bf16[3,128,256]{2,1,0:T(8,128)(2,1)S(1)}, u32[]{:S(2)}, u32[]{:S(2)}) collective-permute-start(bf16[3,128,256]{2,1,0:T(8,128)(2,1)S(1)} %get-tuple-element.21), channel_id=1, source_target_pairs={{0,1},{1,2},{2,3},{3,0},{4,5},{5,6},{6,7},{7,4},{8,9},{9,10},{10,1... | collective-permute-start | bytes 589832 | tf_op jit(solution)/shard_map/ppermute | solution.py:33
  93.1 43.1 %copy-start.1 = (bf16[2,4,128,256]{3,2,1,0:T(8,128)(2,1)}, bf16[2,4,128,256]{3,2,1,0:T(8,128)(2,1)S(1)}, u32[]{:S(2)}) copy-start(bf16[2,4,128,256]{3,2,1,0:T(8,128)(2,1)S(1)} %copy.8) | copy-start | bytes 1572868
  93.1 15.8 %collective-permute-start.9 = (bf16[2,512,256]{2,1,0:T(8,128)(2,1)S(1)}, bf16[2,512,256]{2,1,0:T(8,128)(2,1)}, u32[]{:S(2)}, u32[]{:S(2)}) collective-permute-start(bf16[2,512,256]{2,1,0:T(8,128)(2,1)S(1)} %bitcast.63), channel_id=1, source_target_pairs={{0,8},{1,9},{2,10},{3,11},{4,12},{5,13},{6,14},{7,15},{16,24},{17,... | collective-permute-start | bytes 1572872 | tf_op jit(solution)/shard_map/ppermute | solution.py:24
  99.9 30.6 %collective-permute-start.11 = (bf16[2,512,256]{2,1,0:T(8,128)(2,1)S(1)}, bf16[2,512,256]{2,1,0:T(8,128)(2,1)}, u32[]{:S(2)}, u32[]{:S(2)}) collective-permute-start(bf16[2,512,256]{2,1,0:T(8,128)(2,1)S(1)} %bitcast.64), channel_id=1, source_target_pairs={{0,4},{1,5},{2,6},{3,7},{4,8},{5,9},{6,10},{7,11},{8,12},{9,13},{1... | collective-permute-start | bytes 1572872 | tf_op jit(solution)/shard_map/ppermute | solution.py:24
  108.9 27.2 %collective-permute-start.10 = (bf16[2,512,256]{2,1,0:T(8,128)(2,1)}, bf16[2,512,256]{2,1,0:T(8,128)(2,1)}, u32[]{:S(2)}, u32[]{:S(2)}) collective-permute-start(bf16[2,512,256]{2,1,0:T(8,128)(2,1)} %collective-permute-done.9.k1_ref.v1_ref), channel_id=1, source_target_pairs={{0,4},{1,5},{2,6},{3,7},{4,8},{5,9},{6,10},{7,11},{8,12},{9,13},{1... | collective-permute-start | bytes 1572872 | tf_op jit(solution)/shard_map/ppermute | solution.py:24
  129.7 1.1 copy-start.3
  143.8 4.1 %collective-permute-start.12 = (bf16[128,256]{1,0:T(8,128)(2,1)S(1)}, bf16[128,256]{1,0:T(8,128)(2,1)S(1)}, u32[]{:S(2)}, u32[]{:S(2)}) collective-permute-start(bf16[128,256]{1,0:T(8,128)(2,1)S(1)} %get-tuple-element.26), channel_id=1, source_target_pairs={{0,3},{1,0},{2,1},{3,2},{4,7},{5,4},{6,5},{7,6},{8,11},{9,8},{10,9... | collective-permute-start | bytes 196616 | tf_op jit(solution)/shard_map/ppermute | solution.py:33
  145.3 3.7 %collective-permute-start.13 = (bf16[128,256]{1,0:T(8,128)(2,1)S(1)}, bf16[128,256]{1,0:T(8,128)(2,1)S(1)}, u32[]{:S(2)}, u32[]{:S(2)}) collective-permute-start(bf16[128,256]{1,0:T(8,128)(2,1)S(1)} %get-tuple-element.25), channel_id=1, source_target_pairs={{0,2},{1,3},{2,0},{3,1},{4,6},{5,7},{6,4},{7,5},{8,10},{9,11},{10,... | collective-permute-start | bytes 196616 | tf_op jit(solution)/shard_map/ppermute | solution.py:33
  145.4 3.7 %collective-permute-start.14 = (bf16[128,256]{1,0:T(8,128)(2,1)S(1)}, bf16[128,256]{1,0:T(8,128)(2,1)S(1)}, u32[]{:S(2)}, u32[]{:S(2)}) collective-permute-start(bf16[128,256]{1,0:T(8,128)(2,1)S(1)} %get-tuple-element.24), channel_id=1, source_target_pairs={{0,1},{1,2},{2,3},{3,0},{4,5},{5,6},{6,7},{7,4},{8,9},{9,10},{10,1... | collective-permute-start | bytes 196616 | tf_op jit(solution)/shard_map/ppermute | solution.py:33
  150.6 16.0 %collective-permute-start.15 = (bf16[1,1024]{1,0:T(2,128)(2,1)S(1)}, bf16[1,1024]{1,0:T(2,128)(2,1)S(1)}, u32[]{:S(2)}, u32[]{:S(2)}) collective-permute-start(bf16[1,1024]{1,0:T(2,128)(2,1)S(1)} %slice.43), channel_id=1, source_target_pairs={{0,1},{1,2},{2,3},{3,4},{4,5},{5,6},{6,7},{7,8},{8,9},{9,10},{10,1... | collective-permute-start | bytes 6152 | tf_op jit(solution)/shard_map/ppermute | solution.py:24

commit v12 on v11

--- a/solution.py
+++ b/solution.py
@@ -15,7 +15,7 @@
 FREACH = 2
 CREACH = 3
 FINE_TILE = 256
-HALVES = 2
+HALVES = 4
 
 
 def passed_along(value, axis, steps):

time: 170 us -> 178 us (1.047)
  starting transfers between devices: 62.3 us -> 76.8 us
  waiting for transfers between devices: 45 us -> 32.4 us
  Pallas kernels: 39.9 us -> 44.5 us
    ppermute x6 -> x8, waiting for transfers between devices: 35.6 us -> 23.6 us  [passed_along(): lax.ppermute(value, axis, [(source, source + steps) for source in range(f...]
    ppermute x4 -> x8, starting transfers between devices: 9.26 us -> 18.8 us  [pair_swap(): lax.ppermute(value, axis, [(source, source + step) for source in range(st...]
    ppermute x6 -> x8, starting transfers between devices: 47.8 us -> 52.5 us  [passed_along(): lax.ppermute(value, axis, [(source, source + steps) for source in range(f...]
    pallas_call x2 -> x4, Pallas kernels: 30.7 us -> 35.3 us  [fine_attention(): pl.pallas_call(kernel, grid=(nq, pairs), in_specs=[pl.BlockSpec((tile, 1)...]
    unnamed x27 -> x43, local copies, waits for them, and re-layouts: 3.3 us -> 6.03 us
  transfers between devices with their start and end apart: 16 -> 22, of which waited for: 8 -> 9; matrix products, arithmetic and copies ran while one was open for 5% -> 5% of each run, Pallas kernels for 11% -> 16%
where the time goes in v12:
time: 178 us; the launch traced here: 176 us
  starting transfers between devices  76.8 us (43%)
  Pallas kernels  44.5 us (25%)
  waiting for transfers between devices  32.4 us (18%)
  local copies, waits for them, and re-layouts  15.4 us (9%)
  matrix products  4.29 us (2%)
  other arithmetic  2.27 us (1%)
    ppermute x8, starting transfers between devices, passed_along(): lax.ppermute(value, axis, [(source, source + steps) for source in range(f...  52.5 us
    pallas_call x4, Pallas kernels, fine_attention(): pl.pallas_call(kernel, grid=(nq, pairs), in_specs=[pl.BlockSpec((tile, 1)...  35.3 us
    ppermute x8, waiting for transfers between devices, passed_along(): lax.ppermute(value, axis, [(source, source + steps) for source in range(f...  23.6 us
    ppermute x8, starting transfers between devices, pair_swap(): lax.ppermute(value, axis, [(source, source + step) for source in range(st...  18.8 us
    ppermute x6, waiting for transfers between devices, within_group(): return lax.ppermute(value, axis, pairs)  7.99 us
    pallas_call x1, Pallas kernels, coarse_attention(): pl.pallas_call(kernel, grid=(heads, rows // tile), in_specs=[pl.BlockSpec...  6.8 us
    unnamed x43, local copies, waits for them, and re-layouts  6.03 us
    ppermute x6, starting transfers between devices, within_group(): return lax.ppermute(value, axis, pairs)  5.49 us
  transfers between devices with their start and end apart: 22, of which 9 were waited for; matrix products, arithmetic and copies ran while one was open for 5% of the time, Pallas kernels for 16%

profile of v12, /device:TPU:7, one launch (start us, length us, event | category | flops | bytes accessed | tf_op | source)
XLA Modules:
  0.0 176.2 jit_solution(7901804138321764634)
XLA Ops:
  0.0 3.1 %fusion.16 = (bf16[2,512,256]{2,1,0:T(8,128)(2,1)}, bf16[2,512,256]{2,1,0:T(8,128)(2,1)}, bf16[2,512,256]{2,1,0:T(8,128)(2,1)}, bf16[2,512,256]{2,1,0:T(8,128)(2,1)}) fusion(bf16[3,512,1024]{2,1,0:T(8,128)(2,1)} %bitcast.56), kind=kLoop, calls=%fused_computation.50 | loop fusion | bytes 4194304 | tf_op jit(solution)/shard_map/slice | solution.py:301
  3.1 3.1 %collective-permute-start = (bf16[2,512,256]{2,1,0:T(8,128)(2,1)}, bf16[2,512,256]{2,1,0:T(8,128)(2,1)S(1)}, u32[]{:S(2)}, u32[]{:S(2)}) collective-permute-start(bf16[2,512,256]{2,1,0:T(8,128)(2,1)} %get-tuple-element.38), channel_id=1, source_target_pairs={{0,2},{1,3},{2,4},{3,5},{4,6},{5,7},{6,8},{7,9},{8,10},{9,11},{10,... | collective-permute-start | bytes 1572872 | tf_op jit(solution)/shard_map/ppermute | solution.py:24
  6.2 1.3 collective-permute-start.1
  7.5 10.4 %collective-permute-done.k0_ref.v0_ref = bf16[2,512,256]{2,1,0:T(8,128)(2,1)S(1)} collective-permute-done((bf16[2,512,256]{2,1,0:T(8,128)(2,1)}, bf16[2,512,256]{2,1,0:T(8,128)(2,1)S(1)}, u32[]{:S(2)}, u32[]{:S(2)}) %collective-permute-start) | collective-permute-done | bytes 524320 | tf_op jit(solution)/shard_map/ppermute | solution.py:24
  18.0 4.2 %collective-permute-start.2 = (bf16[2,512,256]{2,1,0:T(8,128)(2,1)S(1)}, bf16[2,512,256]{2,1,0:T(8,128)(2,1)}, u32[]{:S(2)}, u32[]{:S(2)}) collective-permute-start(bf16[2,512,256]{2,1,0:T(8,128)(2,1)S(1)} %collective-permute-done.k0_ref.v0_ref), channel_id=1, source_target_pairs={{1,0},{3,2},{5,4},{7,6},{9,8},{11,10},{13,12},{15,14},{17,16},{19,... | collective-permute-start | bytes 1572872 | tf_op jit(solution)/shard_map/ppermute | solution.py:173
  22.2 4.0 %collective-permute-start.3 = (bf16[2,512,256]{2,1,0:T(8,128)(2,1)}, bf16[2,512,256]{2,1,0:T(8,128)(2,1)S(1)}, u32[]{:S(2)}, u32[]{:S(2)}) collective-permute-start(bf16[2,512,256]{2,1,0:T(8,128)(2,1)} %get-tuple-element.20), channel_id=1, source_target_pairs={{0,2},{1,3},{2,4},{3,5},{4,6},{5,7},{6,8},{7,9},{8,10},{9,11},{10,... | collective-permute-start | bytes 1572872 | tf_op jit(solution)/shard_map/ppermute | solution.py:24
  29.5 8.8 %shard_map.46 = (bf16[512,256]{1,0:T(8,128)(2,1)}, bf16[128,256]{1,0:T(8,128)(2,1)}) custom-call(s32[512,1]{1,0:T(8,128)} %reshape_reshape.6.qclip_ref, s32[1,1536]{1,0:T(1,128)} %reshape_reshape.5.kclip0_ref.kclip1_ref.kclip2_ref, s32[1,1536]{1,0:T(1,128)} %reshape_reshape.5.kclip0_ref.kclip1_ref.kclip2_ref, ...), custom_call_target="tpu_custom_call" | custom-call | tf_op jit(solution)/shard_map/pallas_call | solution.py:117
  38.3 3.8 %collective-permute-start.5 = (bf16[2,512,256]{2,1,0:T(8,128)(2,1)S(1)}, bf16[2,512,256]{2,1,0:T(8,128)(2,1)S(1)}, u32[]{:S(2)}, u32[]{:S(2)}) collective-permute-start(bf16[2,512,256]{2,1,0:T(8,128)(2,1)S(1)} %collective-permute-done.3.k0_ref.v0_ref), channel_id=1, source_target_pairs={{1,0},{3,2},{5,4},{7,6},{9,8},{11,10},{13,12},{15,14},{17,16},{19,... | collective-permute-start | bytes 1572872 | tf_op jit(solution)/shard_map/ppermute | solution.py:173
  42.2 2.2 %collective-permute-start.6 = (bf16[2,512,256]{2,1,0:T(8,128)(2,1)}, bf16[2,512,256]{2,1,0:T(8,128)(2,1)}, u32[]{:S(2)}, u32[]{:S(2)}) collective-permute-start(bf16[2,512,256]{2,1,0:T(8,128)(2,1)} %get-tuple-element.23), channel_id=1, source_target_pairs={{0,2},{1,3},{2,4},{3,5},{4,6},{5,7},{6,8},{7,9},{8,10},{9,11},{10,... | collective-permute-start | bytes 1572872 | tf_op jit(solution)/shard_map/ppermute | solution.py:24
  46.6 8.8 %shard_map.47 = (bf16[512,256]{1,0:T(8,128)(2,1)}, bf16[128,256]{1,0:T(8,128)(2,1)}) custom-call(s32[512,1]{1,0:T(8,128)} %reshape_reshape.6.qclip_ref, s32[1,1536]{1,0:T(1,128)} %reshape_reshape.5.kclip0_ref.kclip1_ref.kclip2_ref, s32[1,1536]{1,0:T(1,128)} %reshape_reshape.5.kclip0_ref.kclip1_ref.kclip2_ref, ...), custom_call_target="tpu_custom_call" | custom-call | tf_op jit(solution)/shard_map/pallas_call | solution.py:117
  55.4 2.5 %collective-permute-done.6.k0_ref.v0_ref = bf16[2,512,256]{2,1,0:T(8,128)(2,1)} collective-permute-done((bf16[2,512,256]{2,1,0:T(8,128)(2,1)}, bf16[2,512,256]{2,1,0:T(8,128)(2,1)}, u32[]{:S(2)}, u32[]{:S(2)}) %collective-permute-start.6) | collective-permute-done | bytes 524320 | tf_op jit(solution)/shard_map/ppermute | solution.py:24
  58.0 3.1 %collective-permute-start.8 = (bf16[2,512,256]{2,1,0:T(8,128)(2,1)}, bf16[2,512,256]{2,1,0:T(8,128)(2,1)}, u32[]{:S(2)}, u32[]{:S(2)}) collective-permute-start(bf16[2,512,256]{2,1,0:T(8,128)(2,1)} %collective-permute-done.6.k0_ref.v0_ref), channel_id=1, source_target_pairs={{1,0},{3,2},{5,4},{7,6},{9,8},{11,10},{13,12},{15,14},{17,16},{19,... | collective-permute-start | bytes 1572872 | tf_op jit(solution)/shard_map/ppermute | solution.py:173
  61.1 3.1 %collective-permute-start.9 = (bf16[2,512,256]{2,1,0:T(8,128)(2,1)}, bf16[2,512,256]{2,1,0:T(8,128)(2,1)S(1)}, u32[]{:S(2)}, u32[]{:S(2)}) collective-permute-start(bf16[2,512,256]{2,1,0:T(8,128)(2,1)} %get-tuple-element.26), channel_id=1, source_target_pairs={{0,2},{1,3},{2,4},{3,5},{4,6},{5,7},{6,8},{7,9},{8,10},{9,11},{10,... | collective-permute-start | bytes 1572872 | tf_op jit(solution)/shard_map/ppermute | solution.py:24
  65.6 8.8 %shard_map.48 = (bf16[512,256]{1,0:T(8,128)(2,1)}, bf16[128,256]{1,0:T(8,128)(2,1)}) custom-call(s32[512,1]{1,0:T(8,128)} %reshape_reshape.6.qclip_ref, s32[1,1536]{1,0:T(1,128)} %reshape_reshape.5.kclip0_ref.kclip1_ref.kclip2_ref, s32[1,1536]{1,0:T(1,128)} %reshape_reshape.5.kclip0_ref.kclip1_ref.kclip2_ref, ...), custom_call_target="tpu_custom_call" | custom-call | tf_op jit(solution)/shard_map/pallas_call | solution.py:117
  74.4 1.5 collective-permute-done.9.k0_ref.v0_ref
  75.9 2.5 %collective-permute-start.11 = (bf16[2,512,256]{2,1,0:T(8,128)(2,1)S(1)}, bf16[2,512,256]{2,1,0:T(8,128)(2,1)}, u32[]{:S(2)}, u32[]{:S(2)}) collective-permute-start(bf16[2,512,256]{2,1,0:T(8,128)(2,1)S(1)} %collective-permute-done.9.k0_ref.v0_ref), channel_id=1, source_target_pairs={{1,0},{3,2},{5,4},{7,6},{9,8},{11,10},{13,12},{15,14},{17,16},{19,... | collective-permute-start | bytes 1572872 | tf_op jit(solution)/shard_map/ppermute | solution.py:173
  79.2 8.8 %shard_map.49 = (bf16[512,256]{1,0:T(8,128)(2,1)}, bf16[128,256]{1,0:T(8,128)(2,1)}) custom-call(s32[512,1]{1,0:T(8,128)} %reshape_reshape.6.qclip_ref, s32[1,1536]{1,0:T(1,128)} %reshape_reshape.5.kclip0_ref.kclip1_ref.kclip2_ref, s32[1,1536]{1,0:T(1,128)} %reshape_reshape.5.kclip0_ref.kclip1_ref.kclip2_ref, ...), custom_call_target="tpu_custom_call" | custom-call | tf_op jit(solution)/shard_map/pallas_call | solution.py:117
  88.0 3.8 %fusion.2 = bf16[128,3,1024]{2,0,1:T(8,128)(2,1)S(1)} fusion(bf16[1024,3,1024]{2,0,1:T(8,128)(2,1)} %param.6, bf16[128,256]{1,0:T(8,128)(2,1)} %get-tuple-element.32, bf16[128,256]{1,0:T(8,128)(2,1)S(1)} %copy-done.12, bf16[128,256]{1,0:T(8,128)(2,1)S(1)} %copy-done.11, bf16[128,256]{1,0:T(8,128)(2,1)S(1)} %copy-done.10), kind=kOutput, calls=%fused_computation.2 | convolution fusion | flops 806748160 | bytes 7340032 | tf_op jit(solution)/shard_map/rd,mdc->mrc/dot_general | solution.py:321
  93.2 1.6 collective-permute-start.14
  94.9 5.3 %collective-permute-done.12 = bf16[3,128,256]{2,1,0:T(8,128)(2,1)S(1)} collective-permute-done((bf16[3,128,256]{2,1,0:T(8,128)(2,1)}, bf16[3,128,256]{2,1,0:T(8,128)(2,1)S(1)}, u32[]{:S(2)}, u32[]{:S(2)}) %collective-permute-start.12) | collective-permute-done | bytes 196640 | tf_op jit(solution)/shard_map/ppermute | solution.py:33
  100.3 1.6 collective-permute-done.14
  102.2 5.9 %collective-permute-start.15 = (bf16[2,512,256]{2,1,0:T(8,128)(2,1)S(1)}, bf16[2,512,256]{2,1,0:T(8,128)(2,1)}, u32[]{:S(2)}, u32[]{:S(2)}) collective-permute-start(bf16[2,512,256]{2,1,0:T(8,128)(2,1)S(1)} %bitcast.69), channel_id=1, source_target_pairs={{0,8},{1,9},{2,10},{3,11},{4,12},{5,13},{6,14},{7,15},{16,24},{17,... | collective-permute-start | bytes 1572872 | tf_op jit(solution)/shard_map/ppermute | solution.py:24
  108.1 3.9 %collective-permute-start.17 = (bf16[2,512,256]{2,1,0:T(8,128)(2,1)S(1)}, bf16[2,512,256]{2,1,0:T(8,128)(2,1)}, u32[]{:S(2)}, u32[]{:S(2)}) collective-permute-start(bf16[2,512,256]{2,1,0:T(8,128)(2,1)S(1)} %bitcast.70), channel_id=1, source_target_pairs={{0,4},{1,5},{2,6},{3,7},{4,8},{5,9},{6,10},{7,11},{8,12},{9,13},{1... | collective-permute-start | bytes 1572872 | tf_op jit(solution)/shard_map/ppermute | solution.py:24
  112.0 4.8 %collective-permute-done.15.k1_ref.v1_ref = bf16[2,512,256]{2,1,0:T(8,128)(2,1)} collective-permute-done((bf16[2,512,256]{2,1,0:T(8,128)(2,1)S(1)}, bf16[2,512,256]{2,1,0:T(8,128)(2,1)}, u32[]{:S(2)}, u32[]{:S(2)}) %collective-permute-start.15) | collective-permute-done | bytes 524320 | tf_op jit(solution)/shard_map/ppermute | solution.py:24
  116.8 17.3 %collective-permute-start.16 = (bf16[2,512,256]{2,1,0:T(8,128)(2,1)}, bf16[2,512,256]{2,1,0:T(8,128)(2,1)}, u32[]{:S(2)}, u32[]{:S(2)}) collective-permute-start(bf16[2,512,256]{2,1,0:T(8,128)(2,1)} %collective-permute-done.15.k1_ref.v1_ref), channel_id=1, source_target_pairs={{0,4},{1,5},{2,6},{3,7},{4,8},{5,9},{6,10},{7,11},{8,12},{9,13},{1... | collective-permute-start | bytes 1572872 | tf_op jit(solution)/shard_map/ppermute | solution.py:24
  139.8 4.5 %collective-permute-done.16.k0_ref.v0_ref = bf16[2,512,256]{2,1,0:T(8,128)(2,1)} collective-permute-done((bf16[2,512,256]{2,1,0:T(8,128)(2,1)}, bf16[2,512,256]{2,1,0:T(8,128)(2,1)}, u32[]{:S(2)}, u32[]{:S(2)}) %collective-permute-start.16) | collective-permute-done | bytes 524320 | tf_op jit(solution)/shard_map/ppermute | solution.py:24
  144.3 6.8 %shard_map.50 = bf16[512,256]{1,0:T(8,128)(2,1)} custom-call(s32[512,1]{1,0:T(8,128)} %copy.11.qclip_ref, s32[1,2048]{1,0:T(1,128)} %bitcast.76, s32[1,2048]{1,0:T(1,128)} %bitcast.77, s32[1,2048]{1,0:T(1,128)} %bitcast.78, s32[1,2048]{1,0:T(1,128)} %bitcast.79, bf16[512,256]{1,0:T(8,128)(2,1)} %bitcast.74, ...), custom_call_target="tpu_custom_call" | custom-call | tf_op jit(solution)/shard_map/pallas_call | solution.py:226
  152.0 1.5 collective-permute-start.18
  153.5 1.7 collective-permute-start.20
  158.8 12.8 %collective-permute-start.21 = (bf16[1,1024]{1,0:T(2,128)(2,1)S(1)}, bf16[1,1024]{1,0:T(2,128)(2,1)S(1)}, u32[]{:S(2)}, u32[]{:S(2)}) collective-permute-start(bf16[1,1024]{1,0:T(2,128)(2,1)S(1)} %slice.53), channel_id=1, source_target_pairs={{0,1},{1,2},{2,3},{3,4},{4,5},{5,6},{6,7},{7,8},{8,9},{9,10},{10,1... | collective-permute-start | bytes 6152 | tf_op jit(solution)/shard_map/ppermute | solution.py:24
  172.4 2.4 %shard_map.51 = bf16[512,1024]{1,0:T(8,128)(2,1)} custom-call(bf16[512,1024]{1,0:T(8,128)(2,1)} %copy-done.7, bf16[128,1024]{1,0:T(8,128)(2,1)} %pad_select_fusion.lift_ref), custom_call_target="tpu_custom_call" | custom-call | tf_op jit(solution)/shard_map/pallas_call | solution.py:157
  174.9 1.3 fusion.11
  (88 shorter events, 20.2 us)
Async XLA Ops:
  0.0 158.3 %copy-start = (bf16[1024,1024]{1,0:T(8,128)(2,1)S(1)}, bf16[1024,1024]{1,0:T(8,128)(2,1)}, u32[]{:S(2)}) copy-start(bf16[1024,1024]{1,0:T(8,128)(2,1)} %param.7) | copy-start | bytes 6291460
  0.0 26.2 %copy-start.9 = (s32[2048]{0:T(1024)S(1)}, s32[2048]{0:T(1024)}, u32[]{:S(2)}) copy-start(s32[2048]{0:T(1024)} %param.5) | copy-start | bytes 24580
  3.1 14.9 %collective-permute-start = (bf16[2,512,256]{2,1,0:T(8,128)(2,1)}, bf16[2,512,256]{2,1,0:T(8,128)(2,1)S(1)}, u32[]{:S(2)}, u32[]{:S(2)}) collective-permute-start(bf16[2,512,256]{2,1,0:T(8,128)(2,1)} %get-tuple-element.38), channel_id=1, source_target_pairs={{0,2},{1,3},{2,4},{3,5},{4,6},{5,7},{6,8},{7,9},{8,10},{9,11},{10,... | collective-permute-start | bytes 1572872 | tf_op jit(solution)/shard_map/ppermute | solution.py:24
  6.2 23.3 %collective-permute-start.1 = (bf16[2,512,256]{2,1,0:T(8,128)(2,1)}, bf16[2,512,256]{2,1,0:T(8,128)(2,1)}, u32[]{:S(2)}, u32[]{:S(2)}) collective-permute-start(bf16[2,512,256]{2,1,0:T(8,128)(2,1)} %get-tuple-element.38), channel_id=1, source_target_pairs={{0,1},{2,3},{4,5},{6,7},{8,9},{10,11},{12,13},{14,15},{16,17},{18,... | collective-permute-start | bytes 1572872 | tf_op jit(solution)/shard_map/ppermute | solution.py:173
  17.9 11.6 %copy-start.5 = (bf16[2,512,256]{2,1,0:T(8,128)(2,1)}, bf16[2,512,256]{2,1,0:T(8,128)(2,1)S(1)}, u32[]{:S(2)}) copy-start(bf16[2,512,256]{2,1,0:T(8,128)(2,1)S(1)} %collective-permute-done.k0_ref.v0_ref) | copy-start | bytes 1572868
  18.0 11.5 %collective-permute-start.2 = (bf16[2,512,256]{2,1,0:T(8,128)(2,1)S(1)}, bf16[2,512,256]{2,1,0:T(8,128)(2,1)}, u32[]{:S(2)}, u32[]{:S(2)}) collective-permute-start(bf16[2,512,256]{2,1,0:T(8,128)(2,1)S(1)} %collective-permute-done.k0_ref.v0_ref), channel_id=1, source_target_pairs={{1,0},{3,2},{5,4},{7,6},{9,8},{11,10},{13,12},{15,14},{17,16},{19,... | collective-permute-start | bytes 1572872 | tf_op jit(solution)/shard_map/ppermute | solution.py:173
  22.2 16.1 %collective-permute-start.3 = (bf16[2,512,256]{2,1,0:T(8,128)(2,1)}, bf16[2,512,256]{2,1,0:T(8,128)(2,1)S(1)}, u32[]{:S(2)}, u32[]{:S(2)}) collective-permute-start(bf16[2,512,256]{2,1,0:T(8,128)(2,1)} %get-tuple-element.20), channel_id=1, source_target_pairs={{0,2},{1,3},{2,4},{3,5},{4,6},{5,7},{6,8},{7,9},{8,10},{9,11},{10,... | collective-permute-start | bytes 1572872 | tf_op jit(solution)/shard_map/ppermute | solution.py:24
  28.2 17.6 %collective-permute-start.4 = (bf16[2,512,256]{2,1,0:T(8,128)(2,1)}, bf16[2,512,256]{2,1,0:T(8,128)(2,1)}, u32[]{:S(2)}, u32[]{:S(2)}) collective-permute-start(bf16[2,512,256]{2,1,0:T(8,128)(2,1)} %get-tuple-element.20), channel_id=1, source_target_pairs={{0,1},{2,3},{4,5},{6,7},{8,9},{10,11},{12,13},{14,15},{16,17},{18,... | collective-permute-start | bytes 1572872 | tf_op jit(solution)/shard_map/ppermute | solution.py:173
  38.3 7.4 %copy-start.4 = (bf16[2,512,256]{2,1,0:T(8,128)(2,1)}, bf16[2,512,256]{2,1,0:T(8,128)(2,1)S(1)}, u32[]{:S(2)}) copy-start(bf16[2,512,256]{2,1,0:T(8,128)(2,1)S(1)} %collective-permute-done.3.k0_ref.v0_ref) | copy-start | bytes 1572868
  38.3 7.4 %collective-permute-start.5 = (bf16[2,512,256]{2,1,0:T(8,128)(2,1)S(1)}, bf16[2,512,256]{2,1,0:T(8,128)(2,1)S(1)}, u32[]{:S(2)}, u32[]{:S(2)}) collective-permute-start(bf16[2,512,256]{2,1,0:T(8,128)(2,1)S(1)} %collective-permute-done.3.k0_ref.v0_ref), channel_id=1, source_target_pairs={{1,0},{3,2},{5,4},{7,6},{9,8},{11,10},{13,12},{15,14},{17,16},{19,... | collective-permute-start | bytes 1572872 | tf_op jit(solution)/shard_map/ppermute | solution.py:173
  42.2 15.8 %collective-permute-start.6 = (bf16[2,512,256]{2,1,0:T(8,128)(2,1)}, bf16[2,512,256]{2,1,0:T(8,128)(2,1)}, u32[]{:S(2)}, u32[]{:S(2)}) collective-permute-start(bf16[2,512,256]{2,1,0:T(8,128)(2,1)} %get-tuple-element.23), channel_id=1, source_target_pairs={{0,2},{1,3},{2,4},{3,5},{4,6},{5,7},{6,8},{7,9},{8,10},{9,11},{10,... | collective-permute-start | bytes 1572872 | tf_op jit(solution)/shard_map/ppermute | solution.py:24
  44.4 21.1 %collective-permute-start.7 = (bf16[2,512,256]{2,1,0:T(8,128)(2,1)}, bf16[2,512,256]{2,1,0:T(8,128)(2,1)}, u32[]{:S(2)}, u32[]{:S(2)}) collective-permute-start(bf16[2,512,256]{2,1,0:T(8,128)(2,1)} %get-tuple-element.23), channel_id=1, source_target_pairs={{0,1},{2,3},{4,5},{6,7},{8,9},{10,11},{12,13},{14,15},{16,17},{18,... | collective-permute-start | bytes 1572872 | tf_op jit(solution)/shard_map/ppermute | solution.py:173
  58.0 7.6 %collective-permute-start.8 = (bf16[2,512,256]{2,1,0:T(8,128)(2,1)}, bf16[2,512,256]{2,1,0:T(8,128)(2,1)}, u32[]{:S(2)}, u32[]{:S(2)}) collective-permute-start(bf16[2,512,256]{2,1,0:T(8,128)(2,1)} %collective-permute-done.6.k0_ref.v0_ref), channel_id=1, source_target_pairs={{1,0},{3,2},{5,4},{7,6},{9,8},{11,10},{13,12},{15,14},{17,16},{19,... | collective-permute-start | bytes 1572872 | tf_op jit(solution)/shard_map/ppermute | solution.py:173
  61.1 14.8 %collective-permute-start.9 = (bf16[2,512,256]{2,1,0:T(8,128)(2,1)}, bf16[2,512,256]{2,1,0:T(8,128)(2,1)S(1)}, u32[]{:S(2)}, u32[]{:S(2)}) collective-permute-start(bf16[2,512,256]{2,1,0:T(8,128)(2,1)} %get-tuple-element.26), channel_id=1, source_target_pairs={{0,2},{1,3},{2,4},{3,5},{4,6},{5,7},{6,8},{7,9},{8,10},{9,11},{10,... | collective-permute-start | bytes 1572872 | tf_op jit(solution)/shard_map/ppermute | solution.py:24
  64.2 14.1 %collective-permute-start.10 = (bf16[2,512,256]{2,1,0:T(8,128)(2,1)}, bf16[2,512,256]{2,1,0:T(8,128)(2,1)S(1)}, u32[]{:S(2)}, u32[]{:S(2)}) collective-permute-start(bf16[2,512,256]{2,1,0:T(8,128)(2,1)} %get-tuple-element.26), channel_id=1, source_target_pairs={{0,1},{2,3},{4,5},{6,7},{8,9},{10,11},{12,13},{14,15},{16,17},{18,... | collective-permute-start | bytes 1572872 | tf_op jit(solution)/shard_map/ppermute | solution.py:173
  75.9 3.3 %copy-start.2 = (bf16[2,512,256]{2,1,0:T(8,128)(2,1)}, bf16[2,512,256]{2,1,0:T(8,128)(2,1)S(1)}, u32[]{:S(2)}) copy-start(bf16[2,512,256]{2,1,0:T(8,128)(2,1)S(1)} %collective-permute-done.9.k0_ref.v0_ref) | copy-start | bytes 1572868
  75.9 3.3 %collective-permute-start.11 = (bf16[2,512,256]{2,1,0:T(8,128)(2,1)S(1)}, bf16[2,512,256]{2,1,0:T(8,128)(2,1)}, u32[]{:S(2)}, u32[]{:S(2)}) collective-permute-start(bf16[2,512,256]{2,1,0:T(8,128)(2,1)S(1)} %collective-permute-done.9.k0_ref.v0_ref), channel_id=1, source_target_pairs={{1,0},{3,2},{5,4},{7,6},{9,8},{11,10},{13,12},{15,14},{17,16},{19,... | collective-permute-start | bytes 1572872 | tf_op jit(solution)/shard_map/ppermute | solution.py:173
  78.3 9.7 %copy-start.10 = (bf16[128,256]{1,0:T(8,128)(2,1)S(1)}, bf16[128,256]{1,0:T(8,128)(2,1)}, u32[]{:S(2)}) copy-start(bf16[128,256]{1,0:T(8,128)(2,1)} %get-tuple-element.29) | copy-start | bytes 196612
  78.3 9.7 %copy-start.11 = (bf16[128,256]{1,0:T(8,128)(2,1)S(1)}, bf16[128,256]{1,0:T(8,128)(2,1)}, u32[]{:S(2)}) copy-start(bf16[128,256]{1,0:T(8,128)(2,1)} %get-tuple-element.30) | copy-start | bytes 196612
  78.3 9.7 %copy-start.12 = (bf16[128,256]{1,0:T(8,128)(2,1)S(1)}, bf16[128,256]{1,0:T(8,128)(2,1)}, u32[]{:S(2)}) copy-start(bf16[128,256]{1,0:T(8,128)(2,1)} %get-tuple-element.31) | copy-start | bytes 196612
  92.6 7.6 %collective-permute-start.12 = (bf16[3,128,256]{2,1,0:T(8,128)(2,1)}, bf16[3,128,256]{2,1,0:T(8,128)(2,1)S(1)}, u32[]{:S(2)}, u32[]{:S(2)}) collective-permute-start(bf16[3,128,256]{2,1,0:T(8,128)(2,1)} %get-tuple-element.41), channel_id=1, source_target_pairs={{0,3},{1,0},{2,1},{3,2},{4,7},{5,4},{6,5},{7,6},{8,11},{9,8},{10,9... | collective-permute-start | bytes 589832 | tf_op jit(solution)/shard_map/ppermute | solution.py:33
  93.0 7.3 %collective-permute-start.13 = (bf16[3,128,256]{2,1,0:T(8,128)(2,1)S(1)}, bf16[3,128,256]{2,1,0:T(8,128)(2,1)S(1)}, u32[]{:S(2)}, u32[]{:S(2)}) collective-permute-start(bf16[3,128,256]{2,1,0:T(8,128)(2,1)S(1)} %get-tuple-element.40), channel_id=1, source_target_pairs={{0,2},{1,3},{2,0},{3,1},{4,6},{5,7},{6,4},{7,5},{8,10},{9,11},{10,... | collective-permute-start | bytes 589832 | tf_op jit(solution)/shard_map/ppermute | solution.py:33
  93.2 8.6 %collective-permute-start.14 = (bf16[3,128,256]{2,1,0:T(8,128)(2,1)S(1)}, bf16[3,128,256]{2,1,0:T(8,128)(2,1)S(1)}, u32[]{:S(2)}, u32[]{:S(2)}) collective-permute-start(bf16[3,128,256]{2,1,0:T(8,128)(2,1)S(1)} %get-tuple-element.39), channel_id=1, source_target_pairs={{0,1},{1,2},{2,3},{3,0},{4,5},{5,6},{6,7},{7,4},{8,9},{9,10},{10,1... | collective-permute-start | bytes 589832 | tf_op jit(solution)/shard_map/ppermute | solution.py:33
  102.1 42.1 %copy-start.1 = (bf16[2,4,128,256]{3,2,1,0:T(8,128)(2,1)}, bf16[2,4,128,256]{3,2,1,0:T(8,128)(2,1)S(1)}, u32[]{:S(2)}) copy-start(bf16[2,4,128,256]{3,2,1,0:T(8,128)(2,1)S(1)} %copy.10) | copy-start | bytes 1572868
  102.2 14.6 %collective-permute-start.15 = (bf16[2,512,256]{2,1,0:T(8,128)(2,1)S(1)}, bf16[2,512,256]{2,1,0:T(8,128)(2,1)}, u32[]{:S(2)}, u32[]{:S(2)}) collective-permute-start(bf16[2,512,256]{2,1,0:T(8,128)(2,1)S(1)} %bitcast.69), channel_id=1, source_target_pairs={{0,8},{1,9},{2,10},{3,11},{4,12},{5,13},{6,14},{7,15},{16,24},{17,... | collective-permute-start | bytes 1572872 | tf_op jit(solution)/shard_map/ppermute | solution.py:24
  108.1 31.4 %collective-permute-start.17 = (bf16[2,512,256]{2,1,0:T(8,128)(2,1)S(1)}, bf16[2,512,256]{2,1,0:T(8,128)(2,1)}, u32[]{:S(2)}, u32[]{:S(2)}) collective-permute-start(bf16[2,512,256]{2,1,0:T(8,128)(2,1)S(1)} %bitcast.70), channel_id=1, source_target_pairs={{0,4},{1,5},{2,6},{3,7},{4,8},{5,9},{6,10},{7,11},{8,12},{9,13},{1... | collective-permute-start | bytes 1572872 | tf_op jit(solution)/shard_map/ppermute | solution.py:24
  116.8 27.5 %collective-permute-start.16 = (bf16[2,512,256]{2,1,0:T(8,128)(2,1)}, bf16[2,512,256]{2,1,0:T(8,128)(2,1)}, u32[]{:S(2)}, u32[]{:S(2)}) collective-permute-start(bf16[2,512,256]{2,1,0:T(8,128)(2,1)} %collective-permute-done.15.k1_ref.v1_ref), channel_id=1, source_target_pairs={{0,4},{1,5},{2,6},{3,7},{4,8},{5,9},{6,10},{7,11},{8,12},{9,13},{1... | collective-permute-start | bytes 1572872 | tf_op jit(solution)/shard_map/ppermute | solution.py:24
  135.7 3.0 %copy-start.8 = (bf16[512,256]{1,0:T(8,128)(2,1)S(1)}, bf16[512,256]{1,0:T(8,128)(2,1)}, u32[]{:S(2)}) copy-start(bf16[512,256]{1,0:T(8,128)(2,1)} %get-tuple-element.28) | copy-start | bytes 786436
  152.0 4.1 %collective-permute-start.18 = (bf16[128,256]{1,0:T(8,128)(2,1)S(1)}, bf16[128,256]{1,0:T(8,128)(2,1)S(1)}, u32[]{:S(2)}, u32[]{:S(2)}) collective-permute-start(bf16[128,256]{1,0:T(8,128)(2,1)S(1)} %get-tuple-element.44), channel_id=1, source_target_pairs={{0,3},{1,0},{2,1},{3,2},{4,7},{5,4},{6,5},{7,6},{8,11},{9,8},{10,9... | collective-permute-start | bytes 196616 | tf_op jit(solution)/shard_map/ppermute | solution.py:33
  153.5 3.7 %collective-permute-start.19 = (bf16[128,256]{1,0:T(8,128)(2,1)S(1)}, bf16[128,256]{1,0:T(8,128)(2,1)S(1)}, u32[]{:S(2)}, u32[]{:S(2)}) collective-permute-start(bf16[128,256]{1,0:T(8,128)(2,1)S(1)} %get-tuple-element.43), channel_id=1, source_target_pairs={{0,2},{1,3},{2,0},{3,1},{4,6},{5,7},{6,4},{7,5},{8,10},{9,11},{10,... | collective-permute-start | bytes 196616 | tf_op jit(solution)/shard_map/ppermute | solution.py:33
  153.5 3.7 %collective-permute-start.20 = (bf16[128,256]{1,0:T(8,128)(2,1)S(1)}, bf16[128,256]{1,0:T(8,128)(2,1)S(1)}, u32[]{:S(2)}, u32[]{:S(2)}) collective-permute-start(bf16[128,256]{1,0:T(8,128)(2,1)S(1)} %get-tuple-element.42), channel_id=1, source_target_pairs={{0,1},{1,2},{2,3},{3,0},{4,5},{5,6},{6,7},{7,4},{8,9},{9,10},{10,1... | collective-permute-start | bytes 196616 | tf_op jit(solution)/shard_map/ppermute | solution.py:33
  158.8 16.0 %collective-permute-start.21 = (bf16[1,1024]{1,0:T(2,128)(2,1)S(1)}, bf16[1,1024]{1,0:T(2,128)(2,1)S(1)}, u32[]{:S(2)}, u32[]{:S(2)}) collective-permute-start(bf16[1,1024]{1,0:T(2,128)(2,1)S(1)} %slice.53), channel_id=1, source_target_pairs={{0,1},{1,2},{2,3},{3,4},{4,5},{5,6},{6,7},{7,8},{8,9},{9,10},{10,1... | collective-permute-start | bytes 6152 | tf_op jit(solution)/shard_map/ppermute | solution.py:24
  (3 other events, 2.7 us)

commit v13 on v11

--- a/solution.py
+++ b/solution.py
@@ -305,7 +305,10 @@
         gate = prev0
         if outs:
             prev0, _ = lax.optimization_barrier((prev0, outs[-1]))
-        prev1a = pair_swap(own_pairs, "seq", False)
+        local_pairs = own_pairs
+        if outs:
+            local_pairs, _ = lax.optimization_barrier((own_pairs, outs[-1]))
+        prev1a = pair_swap(local_pairs, "seq", False)
         prev1b = pair_swap(prev0, "seq", True)
         part_out, part_pool = fine_attention(
             planes, prev0, prev1a, prev1b, query_clip.reshape(tok_count, 1),

time: 170 us -> 173 us (1.018)
  waiting for transfers between devices: 45 us -> 48.1 us
    ppermute x4, waiting for transfers between devices: 1.41 us -> 3.52 us  [pair_swap(): lax.ppermute(value, axis, [(source, source + step) for source in range(st...]
  transfers between devices with their start and end apart: 16 -> 16, of which waited for: 8 -> 8; matrix products, arithmetic and copies ran while one was open for 5% -> 5% of each run, Pallas kernels for 11% -> 10%
where the time goes in v13:
time: 173 us; the launch traced here: 171 us
  starting transfers between devices  62.2 us (36%)
  waiting for transfers between devices  48.1 us (28%)
  Pallas kernels  39.9 us (23%)
  local copies, waits for them, and re-layouts  13.8 us (8%)
  matrix products  4.32 us (2%)
  other arithmetic  2.25 us (1%)
    ppermute x6, starting transfers between devices, passed_along(): lax.ppermute(value, axis, [(source, source + steps) for source in range(f...  47.9 us
    ppermute x6, waiting for transfers between devices, passed_along(): lax.ppermute(value, axis, [(source, source + steps) for source in range(f...  36.6 us
    pallas_call x2, Pallas kernels, fine_attention(): pl.pallas_call(kernel, grid=(nq, pairs), in_specs=[pl.BlockSpec((tile, 1)...  30.7 us
    ppermute x4, starting transfers between devices, pair_swap(): lax.ppermute(value, axis, [(source, source + step) for source in range(st...  9.3 us
    ppermute x6, waiting for transfers between devices, within_group(): return lax.ppermute(value, axis, pairs)  8 us
    pallas_call x1, Pallas kernels, coarse_attention(): pl.pallas_call(kernel, grid=(heads, rows // tile), in_specs=[pl.BlockSpec...  6.79 us
    ppermute x6, starting transfers between devices, within_group(): return lax.ppermute(value, axis, pairs)  5.01 us
    dot_general x1, matrix products, body(): jnp.einsum('rd,mdc->mrc', pooled, wplanes, preferred_element_type=jnp.flo...  3.86 us
  transfers between devices with their start and end apart: 16, of which 8 were waited for; matrix products, arithmetic and copies ran while one was open for 5% of the time, Pallas kernels for 10%

profile of v13, /device:TPU:7, one launch (start us, length us, event | category | flops | bytes accessed | tf_op | source)
XLA Modules:
  0.0 171.0 jit_solution(1283912581993265795)
XLA Ops:
  0.0 3.1 %fusion.12 = (bf16[2,512,512]{2,1,0:T(8,128)(2,1)}, bf16[2,512,512]{2,1,0:T(8,128)(2,1)}) fusion(bf16[3,512,1024]{2,1,0:T(8,128)(2,1)} %bitcast.56), kind=kLoop, calls=%fused_computation.44 | loop fusion | bytes 4194304 | tf_op jit(solution)/shard_map/slice | solution.py:301
  3.1 3.1 %collective-permute-start = (bf16[2,512,512]{2,1,0:T(8,128)(2,1)}, bf16[2,512,512]{2,1,0:T(8,128)(2,1)}, u32[]{:S(2)}, u32[]{:S(2)}) collective-permute-start(bf16[2,512,512]{2,1,0:T(8,128)(2,1)} %get-tuple-element.22), channel_id=1, source_target_pairs={{0,2},{1,3},{2,4},{3,5},{4,6},{5,7},{6,8},{7,9},{8,10},{9,11},{10,... | collective-permute-start | bytes 3145736 | tf_op jit(solution)/shard_map/ppermute | solution.py:24
  6.3 1.3 collective-permute-start.1
  7.6 21.8 %collective-permute-done.k0_ref.v0_ref = bf16[2,512,512]{2,1,0:T(8,128)(2,1)} collective-permute-done((bf16[2,512,512]{2,1,0:T(8,128)(2,1)}, bf16[2,512,512]{2,1,0:T(8,128)(2,1)}, u32[]{:S(2)}, u32[]{:S(2)}) %collective-permute-start) | collective-permute-done | bytes 1048608 | tf_op jit(solution)/shard_map/ppermute | solution.py:24
  29.4 4.4 %collective-permute-start.2 = (bf16[2,512,512]{2,1,0:T(8,128)(2,1)}, bf16[2,512,512]{2,1,0:T(8,128)(2,1)}, u32[]{:S(2)}, u32[]{:S(2)}) collective-permute-start(bf16[2,512,512]{2,1,0:T(8,128)(2,1)} %collective-permute-done.k0_ref.v0_ref), channel_id=1, source_target_pairs={{1,0},{3,2},{5,4},{7,6},{9,8},{11,10},{13,12},{15,14},{17,16},{19,... | collective-permute-start | bytes 3145736 | tf_op jit(solution)/shard_map/ppermute | solution.py:173
  33.8 4.0 %collective-permute-start.3 = (bf16[2,512,512]{2,1,0:T(8,128)(2,1)}, bf16[2,512,512]{2,1,0:T(8,128)(2,1)S(1)}, u32[]{:S(2)}, u32[]{:S(2)}) collective-permute-start(bf16[2,512,512]{2,1,0:T(8,128)(2,1)} %get-tuple-element.15), channel_id=1, source_target_pairs={{0,2},{1,3},{2,4},{3,5},{4,6},{5,7},{6,8},{7,9},{8,10},{9,11},{10,... | collective-permute-start | bytes 3145736 | tf_op jit(solution)/shard_map/ppermute | solution.py:24
  39.8 15.3 %shard_map.46 = (bf16[512,512]{1,0:T(8,128)(2,1)}, bf16[128,512]{1,0:T(8,128)(2,1)}) custom-call(s32[512,1]{1,0:T(8,128)} %reshape_reshape.10.qclip_ref, s32[1,1536]{1,0:T(1,128)} %reshape_reshape.9.kclip0_ref.kclip1_ref.kclip2_ref, s32[1,1536]{1,0:T(1,128)} %reshape_reshape.9.kclip0_ref.kclip1_ref.kclip2_ref, ...), custom_call_target="tpu_custom_call" | custom-call | tf_op jit(solution)/shard_map/pallas_call | solution.py:117
  55.1 4.8 %collective-permute-done.3.k0_ref.v0_ref = bf16[2,512,512]{2,1,0:T(8,128)(2,1)S(1)} collective-permute-done((bf16[2,512,512]{2,1,0:T(8,128)(2,1)}, bf16[2,512,512]{2,1,0:T(8,128)(2,1)S(1)}, u32[]{:S(2)}, u32[]{:S(2)}) %collective-permute-start.3) | collective-permute-done | bytes 1048608 | tf_op jit(solution)/shard_map/ppermute | solution.py:24
  60.0 2.3 %collective-permute-start.5 = (bf16[2,512,512]{2,1,0:T(8,128)(2,1)S(1)}, bf16[2,512,512]{2,1,0:T(8,128)(2,1)}, u32[]{:S(2)}, u32[]{:S(2)}) collective-permute-start(bf16[2,512,512]{2,1,0:T(8,128)(2,1)S(1)} %collective-permute-done.3.k0_ref.v0_ref), channel_id=1, source_target_pairs={{1,0},{3,2},{5,4},{7,6},{9,8},{11,10},{13,12},{15,14},{17,16},{19,... | collective-permute-start | bytes 3145736 | tf_op jit(solution)/shard_map/ppermute | solution.py:173
  62.3 1.3 collective-permute-start.4
  63.7 3.5 %collective-permute-done.4.k1_ref.v1_ref = bf16[2,512,512]{2,1,0:T(8,128)(2,1)} collective-permute-done((bf16[2,512,512]{2,1,0:T(8,128)(2,1)}, bf16[2,512,512]{2,1,0:T(8,128)(2,1)}, u32[]{:S(2)}, u32[]{:S(2)}) %collective-permute-start.4) | collective-permute-done | bytes 1048608 | tf_op jit(solution)/shard_map/ppermute | solution.py:173
  67.2 15.4 %shard_map.47 = (bf16[512,512]{1,0:T(8,128)(2,1)}, bf16[128,512]{1,0:T(8,128)(2,1)}) custom-call(s32[512,1]{1,0:T(8,128)} %reshape_reshape.10.qclip_ref, s32[1,1536]{1,0:T(1,128)} %reshape_reshape.9.kclip0_ref.kclip1_ref.kclip2_ref, s32[1,1536]{1,0:T(1,128)} %reshape_reshape.9.kclip0_ref.kclip1_ref.kclip2_ref, ...), custom_call_target="tpu_custom_call" | custom-call | tf_op jit(solution)/shard_map/pallas_call | solution.py:117
  82.6 3.9 %fusion.2 = bf16[128,3,1024]{2,0,1:T(8,128)(2,1)S(1)} fusion(bf16[1024,3,1024]{2,0,1:T(8,128)(2,1)} %param.6, bf16[128,512]{1,0:T(8,128)(2,1)} %get-tuple-element.18, bf16[128,512]{1,0:T(8,128)(2,1)S(1)} %copy-done.4), kind=kOutput, calls=%fused_computation.2 | convolution fusion | flops 806223872 | bytes 7340032 | tf_op jit(solution)/shard_map/rd,mdc->mrc/dot_general | solution.py:324
  87.3 1.7 collective-permute-start.8
  89.0 5.8 %collective-permute-done.6 = bf16[3,128,256]{2,1,0:T(8,128)(2,1)S(1)} collective-permute-done((bf16[3,128,256]{2,1,0:T(8,128)(2,1)}, bf16[3,128,256]{2,1,0:T(8,128)(2,1)S(1)}, u32[]{:S(2)}, u32[]{:S(2)}) %collective-permute-start.6) | collective-permute-done | bytes 196640 | tf_op jit(solution)/shard_map/ppermute | solution.py:33
  94.9 1.1 collective-permute-done.8
  96.3 6.5 %collective-permute-start.9 = (bf16[2,512,256]{2,1,0:T(8,128)(2,1)S(1)}, bf16[2,512,256]{2,1,0:T(8,128)(2,1)}, u32[]{:S(2)}, u32[]{:S(2)}) collective-permute-start(bf16[2,512,256]{2,1,0:T(8,128)(2,1)S(1)} %bitcast.63), channel_id=1, source_target_pairs={{0,8},{1,9},{2,10},{3,11},{4,12},{5,13},{6,14},{7,15},{16,24},{17,... | collective-permute-start | bytes 1572872 | tf_op jit(solution)/shard_map/ppermute | solution.py:24
  102.8 4.0 %collective-permute-start.11 = (bf16[2,512,256]{2,1,0:T(8,128)(2,1)S(1)}, bf16[2,512,256]{2,1,0:T(8,128)(2,1)}, u32[]{:S(2)}, u32[]{:S(2)}) collective-permute-start(bf16[2,512,256]{2,1,0:T(8,128)(2,1)S(1)} %bitcast.64), channel_id=1, source_target_pairs={{0,4},{1,5},{2,6},{3,7},{4,8},{5,9},{6,10},{7,11},{8,12},{9,13},{1... | collective-permute-start | bytes 1572872 | tf_op jit(solution)/shard_map/ppermute | solution.py:24
  106.8 4.7 %collective-permute-done.9.k1_ref.v1_ref = bf16[2,512,256]{2,1,0:T(8,128)(2,1)} collective-permute-done((bf16[2,512,256]{2,1,0:T(8,128)(2,1)S(1)}, bf16[2,512,256]{2,1,0:T(8,128)(2,1)}, u32[]{:S(2)}, u32[]{:S(2)}) %collective-permute-start.9) | collective-permute-done | bytes 524320 | tf_op jit(solution)/shard_map/ppermute | solution.py:24
  111.5 17.3 %collective-permute-start.10 = (bf16[2,512,256]{2,1,0:T(8,128)(2,1)}, bf16[2,512,256]{2,1,0:T(8,128)(2,1)}, u32[]{:S(2)}, u32[]{:S(2)}) collective-permute-start(bf16[2,512,256]{2,1,0:T(8,128)(2,1)} %collective-permute-done.9.k1_ref.v1_ref), channel_id=1, source_target_pairs={{0,4},{1,5},{2,6},{3,7},{4,8},{5,9},{6,10},{7,11},{8,12},{9,13},{1... | collective-permute-start | bytes 1572872 | tf_op jit(solution)/shard_map/ppermute | solution.py:24
  130.4 1.1 constant_dynamic-update-slice_fusion.1
  131.5 1.1 constant_dynamic-update-slice_fusion.fine_ref
  133.7 5.3 %collective-permute-done.10.k0_ref.v0_ref = bf16[2,512,256]{2,1,0:T(8,128)(2,1)} collective-permute-done((bf16[2,512,256]{2,1,0:T(8,128)(2,1)}, bf16[2,512,256]{2,1,0:T(8,128)(2,1)}, u32[]{:S(2)}, u32[]{:S(2)}) %collective-permute-start.10) | collective-permute-done | bytes 524320 | tf_op jit(solution)/shard_map/ppermute | solution.py:24
  139.0 6.8 %shard_map.48 = bf16[512,256]{1,0:T(8,128)(2,1)} custom-call(s32[512,1]{1,0:T(8,128)} %copy.9.qclip_ref, s32[1,2048]{1,0:T(1,128)} %bitcast.70, s32[1,2048]{1,0:T(1,128)} %bitcast.71, s32[1,2048]{1,0:T(1,128)} %bitcast.72, s32[1,2048]{1,0:T(1,128)} %bitcast.73, bf16[512,256]{1,0:T(8,128)(2,1)} %bitcast.68, ...), custom_call_target="tpu_custom_call" | custom-call | tf_op jit(solution)/shard_map/pallas_call | solution.py:226
  145.8 0.9 constant_dynamic-slice_fusion
  146.7 1.5 collective-permute-start.12
  148.5 1.4 collective-permute-start.14
  150.8 1.1 collective-permute-done.13
  151.9 0.9 bitcast_dynamic-update-slice_fusion.15
  153.5 12.9 %collective-permute-start.15 = (bf16[1,1024]{1,0:T(2,128)(2,1)S(1)}, bf16[1,1024]{1,0:T(2,128)(2,1)S(1)}, u32[]{:S(2)}, u32[]{:S(2)}) collective-permute-start(bf16[1,1024]{1,0:T(2,128)(2,1)S(1)} %slice.43), channel_id=1, source_target_pairs={{0,1},{1,2},{2,3},{3,4},{4,5},{5,6},{6,7},{7,8},{8,9},{9,10},{10,1... | collective-permute-start | bytes 6152 | tf_op jit(solution)/shard_map/ppermute | solution.py:24
  167.2 2.4 %shard_map.49 = bf16[512,1024]{1,0:T(8,128)(2,1)} custom-call(bf16[512,1024]{1,0:T(8,128)(2,1)} %copy-done.3, bf16[128,1024]{1,0:T(8,128)(2,1)} %pad_select_fusion.lift_ref), custom_call_target="tpu_custom_call" | custom-call | tf_op jit(solution)/shard_map/pallas_call | solution.py:157
  169.7 1.3 fusion.7
  (58 shorter events, 8.6 us)
Async XLA Ops:
  0.0 153.0 %copy-start = (bf16[1024,1024]{1,0:T(8,128)(2,1)S(1)}, bf16[1024,1024]{1,0:T(8,128)(2,1)}, u32[]{:S(2)}) copy-start(bf16[1024,1024]{1,0:T(8,128)(2,1)} %param.7) | copy-start | bytes 6291460
  0.0 37.9 %copy-start.5 = (s32[2048]{0:T(1024)S(1)}, s32[2048]{0:T(1024)}, u32[]{:S(2)}) copy-start(s32[2048]{0:T(1024)} %param.5) | copy-start | bytes 24580
  3.1 26.2 %collective-permute-start = (bf16[2,512,512]{2,1,0:T(8,128)(2,1)}, bf16[2,512,512]{2,1,0:T(8,128)(2,1)}, u32[]{:S(2)}, u32[]{:S(2)}) collective-permute-start(bf16[2,512,512]{2,1,0:T(8,128)(2,1)} %get-tuple-element.22), channel_id=1, source_target_pairs={{0,2},{1,3},{2,4},{3,5},{4,6},{5,7},{6,8},{7,9},{8,10},{9,11},{10,... | collective-permute-start | bytes 3145736 | tf_op jit(solution)/shard_map/ppermute | solution.py:24
  6.3 33.5 %collective-permute-start.1 = (bf16[2,512,512]{2,1,0:T(8,128)(2,1)}, bf16[2,512,512]{2,1,0:T(8,128)(2,1)}, u32[]{:S(2)}, u32[]{:S(2)}) collective-permute-start(bf16[2,512,512]{2,1,0:T(8,128)(2,1)} %get-tuple-element.22), channel_id=1, source_target_pairs={{0,1},{2,3},{4,5},{6,7},{8,9},{10,11},{12,13},{14,15},{16,17},{18,... | collective-permute-start | bytes 3145736 | tf_op jit(solution)/shard_map/ppermute | solution.py:173
  29.4 10.5 %collective-permute-start.2 = (bf16[2,512,512]{2,1,0:T(8,128)(2,1)}, bf16[2,512,512]{2,1,0:T(8,128)(2,1)}, u32[]{:S(2)}, u32[]{:S(2)}) collective-permute-start(bf16[2,512,512]{2,1,0:T(8,128)(2,1)} %collective-permute-done.k0_ref.v0_ref), channel_id=1, source_target_pairs={{1,0},{3,2},{5,4},{7,6},{9,8},{11,10},{13,12},{15,14},{17,16},{19,... | collective-permute-start | bytes 3145736 | tf_op jit(solution)/shard_map/ppermute | solution.py:173
  33.8 26.2 %collective-permute-start.3 = (bf16[2,512,512]{2,1,0:T(8,128)(2,1)}, bf16[2,512,512]{2,1,0:T(8,128)(2,1)S(1)}, u32[]{:S(2)}, u32[]{:S(2)}) collective-permute-start(bf16[2,512,512]{2,1,0:T(8,128)(2,1)} %get-tuple-element.15), channel_id=1, source_target_pairs={{0,2},{1,3},{2,4},{3,5},{4,6},{5,7},{6,8},{7,9},{8,10},{9,11},{10,... | collective-permute-start | bytes 3145736 | tf_op jit(solution)/shard_map/ppermute | solution.py:24
  60.0 7.2 %copy-start.2 = (bf16[2,512,512]{2,1,0:T(8,128)(2,1)}, bf16[2,512,512]{2,1,0:T(8,128)(2,1)S(1)}, u32[]{:S(2)}) copy-start(bf16[2,512,512]{2,1,0:T(8,128)(2,1)S(1)} %collective-permute-done.3.k0_ref.v0_ref) | copy-start | bytes 3145732
  60.0 3.7 %collective-permute-start.5 = (bf16[2,512,512]{2,1,0:T(8,128)(2,1)S(1)}, bf16[2,512,512]{2,1,0:T(8,128)(2,1)}, u32[]{:S(2)}, u32[]{:S(2)}) collective-permute-start(bf16[2,512,512]{2,1,0:T(8,128)(2,1)S(1)} %collective-permute-done.3.k0_ref.v0_ref), channel_id=1, source_target_pairs={{1,0},{3,2},{5,4},{7,6},{9,8},{11,10},{13,12},{15,14},{17,16},{19,... | collective-permute-start | bytes 3145736 | tf_op jit(solution)/shard_map/ppermute | solution.py:173
  62.3 4.9 %collective-permute-start.4 = (bf16[2,512,512]{2,1,0:T(8,128)(2,1)}, bf16[2,512,512]{2,1,0:T(8,128)(2,1)}, u32[]{:S(2)}, u32[]{:S(2)}) collective-permute-start(bf16[2,512,512]{2,1,0:T(8,128)(2,1)} %get-tuple-element.15), channel_id=1, source_target_pairs={{0,1},{2,3},{4,5},{6,7},{8,9},{10,11},{12,13},{14,15},{16,17},{18,... | collective-permute-start | bytes 3145736 | tf_op jit(solution)/shard_map/ppermute | solution.py:173
  63.6 18.9 %copy-start.4 = (bf16[128,512]{1,0:T(8,128)(2,1)S(1)}, bf16[128,512]{1,0:T(8,128)(2,1)}, u32[]{:S(2)}) copy-start(bf16[128,512]{1,0:T(8,128)(2,1)} %get-tuple-element.17) | copy-start | bytes 393220
  87.2 7.7 %collective-permute-start.6 = (bf16[3,128,256]{2,1,0:T(8,128)(2,1)}, bf16[3,128,256]{2,1,0:T(8,128)(2,1)S(1)}, u32[]{:S(2)}, u32[]{:S(2)}) collective-permute-start(bf16[3,128,256]{2,1,0:T(8,128)(2,1)} %get-tuple-element.25), channel_id=1, source_target_pairs={{0,3},{1,0},{2,1},{3,2},{4,7},{5,4},{6,5},{7,6},{8,11},{9,8},{10,9... | collective-permute-start | bytes 589832 | tf_op jit(solution)/shard_map/ppermute | solution.py:33
  87.3 7.5 %collective-permute-start.7 = (bf16[3,128,256]{2,1,0:T(8,128)(2,1)S(1)}, bf16[3,128,256]{2,1,0:T(8,128)(2,1)S(1)}, u32[]{:S(2)}, u32[]{:S(2)}) collective-permute-start(bf16[3,128,256]{2,1,0:T(8,128)(2,1)S(1)} %get-tuple-element.24), channel_id=1, source_target_pairs={{0,2},{1,3},{2,0},{3,1},{4,6},{5,7},{6,4},{7,5},{8,10},{9,11},{10,... | collective-permute-start | bytes 589832 | tf_op jit(solution)/shard_map/ppermute | solution.py:33
  87.3 8.6 %collective-permute-start.8 = (bf16[3,128,256]{2,1,0:T(8,128)(2,1)S(1)}, bf16[3,128,256]{2,1,0:T(8,128)(2,1)S(1)}, u32[]{:S(2)}, u32[]{:S(2)}) collective-permute-start(bf16[3,128,256]{2,1,0:T(8,128)(2,1)S(1)} %get-tuple-element.23), channel_id=1, source_target_pairs={{0,1},{1,2},{2,3},{3,0},{4,5},{5,6},{6,7},{7,4},{8,9},{9,10},{10,1... | collective-permute-start | bytes 589832 | tf_op jit(solution)/shard_map/ppermute | solution.py:33
  96.3 42.7 %copy-start.1 = (bf16[2,4,128,256]{3,2,1,0:T(8,128)(2,1)}, bf16[2,4,128,256]{3,2,1,0:T(8,128)(2,1)S(1)}, u32[]{:S(2)}) copy-start(bf16[2,4,128,256]{3,2,1,0:T(8,128)(2,1)S(1)} %copy.8) | copy-start | bytes 1572868
  96.3 15.3 %collective-permute-start.9 = (bf16[2,512,256]{2,1,0:T(8,128)(2,1)S(1)}, bf16[2,512,256]{2,1,0:T(8,128)(2,1)}, u32[]{:S(2)}, u32[]{:S(2)}) collective-permute-start(bf16[2,512,256]{2,1,0:T(8,128)(2,1)S(1)} %bitcast.63), channel_id=1, source_target_pairs={{0,8},{1,9},{2,10},{3,11},{4,12},{5,13},{6,14},{7,15},{16,24},{17,... | collective-permute-start | bytes 1572872 | tf_op jit(solution)/shard_map/ppermute | solution.py:24
  102.8 30.6 %collective-permute-start.11 = (bf16[2,512,256]{2,1,0:T(8,128)(2,1)S(1)}, bf16[2,512,256]{2,1,0:T(8,128)(2,1)}, u32[]{:S(2)}, u32[]{:S(2)}) collective-permute-start(bf16[2,512,256]{2,1,0:T(8,128)(2,1)S(1)} %bitcast.64), channel_id=1, source_target_pairs={{0,4},{1,5},{2,6},{3,7},{4,8},{5,9},{6,10},{7,11},{8,12},{9,13},{1... | collective-permute-start | bytes 1572872 | tf_op jit(solution)/shard_map/ppermute | solution.py:24
  111.5 27.5 %collective-permute-start.10 = (bf16[2,512,256]{2,1,0:T(8,128)(2,1)}, bf16[2,512,256]{2,1,0:T(8,128)(2,1)}, u32[]{:S(2)}, u32[]{:S(2)}) collective-permute-start(bf16[2,512,256]{2,1,0:T(8,128)(2,1)} %collective-permute-done.9.k1_ref.v1_ref), channel_id=1, source_target_pairs={{0,4},{1,5},{2,6},{3,7},{4,8},{5,9},{6,10},{7,11},{8,12},{9,13},{1... | collective-permute-start | bytes 1572872 | tf_op jit(solution)/shard_map/ppermute | solution.py:24
  132.6 1.1 copy-start.3
  146.7 4.1 %collective-permute-start.12 = (bf16[128,256]{1,0:T(8,128)(2,1)S(1)}, bf16[128,256]{1,0:T(8,128)(2,1)S(1)}, u32[]{:S(2)}, u32[]{:S(2)}) collective-permute-start(bf16[128,256]{1,0:T(8,128)(2,1)S(1)} %get-tuple-element.28), channel_id=1, source_target_pairs={{0,3},{1,0},{2,1},{3,2},{4,7},{5,4},{6,5},{7,6},{8,11},{9,8},{10,9... | collective-permute-start | bytes 196616 | tf_op jit(solution)/shard_map/ppermute | solution.py:33
  148.2 3.7 %collective-permute-start.13 = (bf16[128,256]{1,0:T(8,128)(2,1)S(1)}, bf16[128,256]{1,0:T(8,128)(2,1)S(1)}, u32[]{:S(2)}, u32[]{:S(2)}) collective-permute-start(bf16[128,256]{1,0:T(8,128)(2,1)S(1)} %get-tuple-element.27), channel_id=1, source_target_pairs={{0,2},{1,3},{2,0},{3,1},{4,6},{5,7},{6,4},{7,5},{8,10},{9,11},{10,... | collective-permute-start | bytes 196616 | tf_op jit(solution)/shard_map/ppermute | solution.py:33
  148.5 3.3 %collective-permute-start.14 = (bf16[128,256]{1,0:T(8,128)(2,1)S(1)}, bf16[128,256]{1,0:T(8,128)(2,1)S(1)}, u32[]{:S(2)}, u32[]{:S(2)}) collective-permute-start(bf16[128,256]{1,0:T(8,128)(2,1)S(1)} %get-tuple-element.26), channel_id=1, source_target_pairs={{0,1},{1,2},{2,3},{3,0},{4,5},{5,6},{6,7},{7,4},{8,9},{9,10},{10,1... | collective-permute-start | bytes 196616 | tf_op jit(solution)/shard_map/ppermute | solution.py:33
  153.5 16.1 %collective-permute-start.15 = (bf16[1,1024]{1,0:T(2,128)(2,1)S(1)}, bf16[1,1024]{1,0:T(2,128)(2,1)S(1)}, u32[]{:S(2)}, u32[]{:S(2)}) collective-permute-start(bf16[1,1024]{1,0:T(2,128)(2,1)S(1)} %slice.43), channel_id=1, source_target_pairs={{0,1},{1,2},{2,3},{3,4},{4,5},{5,6},{6,7},{7,8},{8,9},{9,10},{10,1... | collective-permute-start | bytes 6152 | tf_op jit(solution)/shard_map/ppermute | solution.py:24

commit v14 on v11

--- a/solution.py
+++ b/solution.py
@@ -34,7 +34,7 @@
 
 
 def fine_kernel(qclip_ref, kclip0_ref, kclip1_ref, kclip2_ref, q_ref,
-                k0_ref, v0_ref, k1_ref, v1_ref, k1b_ref, v1b_ref, k2_ref, v2_ref,
+                k0_ref, v0_ref, k1_ref, v1_ref, k2_ref, v2_ref,
                 out_ref, pool_ref, bias_ref, *, scale):
     tile = q_ref.shape[0]
     width = q_ref.shape[1]
@@ -63,8 +63,8 @@
 
     def run(step):
         own = (step + 1) * tile
-        keys = (k0_ref[...], k1_ref[...] + k1b_ref[...], k2_ref[0:own, :])
-        values = (v0_ref[...], v1_ref[...] + v1b_ref[...], v2_ref[0:own, :])
+        keys = (k0_ref[...], k1_ref[...], k2_ref[0:own, :])
+        values = (v0_ref[...], v1_ref[...], v2_ref[0:own, :])
         spans = ((0, seg), (seg, seg), (2 * seg, own))
         results = []
         for h in range(2):
@@ -99,7 +99,7 @@
         pl.when(tile_index == step)(functools.partial(run, step))
 
 
-def fine_attention(planes, prev0, prev1a, prev1b, qclip, kclip, heads, first_pair):
+def fine_attention(planes, prev0, prev1, qclip, kclip, heads, first_pair):
     _, tok, width = planes.shape
     head_dim = width // heads
     pair = 2 * head_dim
@@ -123,7 +123,6 @@
             pl.BlockSpec((1, tok), lambda i, h: (0, 1)),
             pl.BlockSpec((1, tok), lambda i, h: (0, 2)),
             pl.BlockSpec((None, tile, pair), lambda i, h: (0, i, first_pair + h)),
-            plane_spec(0), plane_spec(1),
             plane_spec(0), plane_spec(1),
             plane_spec(0), plane_spec(1),
             own_spec(1), own_spec(2),
@@ -137,8 +136,7 @@
             jax.ShapeDtypeStruct((tok // POOL, pairs * pair), jnp.bfloat16),
         ],
         scratch_shapes=[pltpu.VMEM((tile, 3 * tok), jnp.float32)],
-    )(qclip, kclip, kclip, kclip, planes, prev0, prev0, prev1a, prev1a, prev1b, prev1b,
-      planes, planes)
+    )(qclip, kclip, kclip, kclip, planes, prev0, prev0, prev1, prev1, planes, planes)
 
 
 def mix_kernel(fine_ref, lift_ref, out_ref):
@@ -293,6 +291,7 @@
     own_clip = lax.dynamic_slice_in_dim(clip_ids, position * coarse_rows, coarse_rows, 0)
     query_clip = jnp.repeat(own_clip, POOL)
     head_pair_width = 2 * feat_width // FHEADS
+    seq_count = lax.axis_size("seq")
     part_width = feat_width // HALVES
     outs = []
     pools = []
@@ -305,10 +304,10 @@
         gate = prev0
         if outs:
             prev0, _ = lax.optimization_barrier((prev0, outs[-1]))
-        prev1a = pair_swap(own_pairs, "seq", False)
-        prev1b = pair_swap(prev0, "seq", True)
+        outgoing = jnp.where(position % 2 == 0, own_pairs, prev0)
+        prev1 = lax.ppermute(outgoing, "seq", [(source, source ^ 1) for source in range(seq_count)])
         part_out, part_pool = fine_attention(
-            planes, prev0, prev1a, prev1b, query_clip.reshape(tok_count, 1),
+            planes, prev0, prev1, query_clip.reshape(tok_count, 1),
             key_clip.reshape(1, (FREACH + 1) * tok_count), FHEADS,
             part * part_width // head_pair_width,
         )

time: 170 us -> 172 us (1.012)
  starting transfers between devices: 62.3 us -> 56.9 us
  waiting for transfers between devices: 45 us -> 49.7 us
  other arithmetic: 2.25 us -> 6.9 us
    ppermute x4 -> x2, starting transfers between devices: 9.26 us -> 3.69 us  [body(): lax.ppermute(outgoing, 'seq', [(source, source ^ 1) for source in range(s...]
    ppermute x6, waiting for transfers between devices: 35.6 us -> 39.1 us  [passed_along(): lax.ppermute(value, axis, [(source, source + steps) for source in range(f...]
    slice x0 -> x1, other arithmetic: none -> 3.47 us  [body(): own_pairs = planes[1:, :, part * part_width:(part + 1) * part_width]]
  transfers between devices with their start and end apart: 16 -> 14, of which waited for: 8 -> 8; matrix products, arithmetic and copies ran while one was open for 5% -> 5% of each run, Pallas kernels for 11% -> 10%
where the time goes in v14:
time: 172 us; the launch traced here: 171 us
  starting transfers between devices  56.9 us (33%)
  waiting for transfers between devices  49.7 us (29%)
  Pallas kernels  39.4 us (23%)
  local copies, waits for them, and re-layouts  13.2 us (8%)
  other arithmetic  6.9 us (4%)
  matrix products  4.32 us (3%)
    ppermute x6, starting transfers between devices, passed_along(): lax.ppermute(value, axis, [(source, source + steps) for source in range(f...  48 us
    ppermute x6, waiting for transfers between devices, passed_along(): lax.ppermute(value, axis, [(source, source + steps) for source in range(f...  39.1 us
    pallas_call x2, Pallas kernels, fine_attention(): pl.pallas_call(kernel, grid=(nq, pairs), in_specs=[pl.BlockSpec((tile, 1)...  30.2 us
    ppermute x6, waiting for transfers between devices, within_group(): return lax.ppermute(value, axis, pairs)  8.03 us
    pallas_call x1, Pallas kernels, coarse_attention(): pl.pallas_call(kernel, grid=(heads, rows // tile), in_specs=[pl.BlockSpec...  6.79 us
    ppermute x6, starting transfers between devices, within_group(): return lax.ppermute(value, axis, pairs)  5.22 us
    dot_general x1, matrix products, body(): jnp.einsum('rd,mdc->mrc', pooled, wplanes, preferred_element_type=jnp.flo...  3.85 us
    ppermute x2, starting transfers between devices, body(): lax.ppermute(outgoing, 'seq', [(source, source ^ 1) for source in range(s...  3.69 us
  transfers between devices with their start and end apart: 14, of which 8 were waited for; matrix products, arithmetic and copies ran while one was open for 5% of the time, Pallas kernels for 10%

profile of v14, /device:TPU:7, one launch (start us, length us, event | category | flops | bytes accessed | tf_op | source)
XLA Modules:
  0.0 170.8 jit_solution(9042077406282072432)
XLA Ops:
  0.0 2.4 %slice.37 = bf16[2,512,512]{2,1,0:T(8,128)(2,1)} slice(bf16[3,512,1024]{2,1,0:T(8,128)(2,1)} %bitcast.56), slice={[1:3], [0:512], [0:512]} | slice | bytes 2097152 | tf_op jit(solution)/shard_map/slice | solution.py:300
  2.4 3.1 %collective-permute-start = (bf16[2,512,512]{2,1,0:T(8,128)(2,1)}, bf16[2,512,512]{2,1,0:T(8,128)(2,1)S(1)}, u32[]{:S(2)}, u32[]{:S(2)}) collective-permute-start(bf16[2,512,512]{2,1,0:T(8,128)(2,1)} %slice.37), channel_id=1, source_target_pairs={{0,2},{1,3},{2,4},{3,5},{4,6},{5,7},{6,8},{7,9},{8,10},{9,11},{10,... | collective-permute-start | bytes 3145736 | tf_op jit(solution)/shard_map/ppermute | solution.py:24
  5.6 23.0 %collective-permute-done.k0_ref.v0_ref = bf16[2,512,512]{2,1,0:T(8,128)(2,1)S(1)} collective-permute-done((bf16[2,512,512]{2,1,0:T(8,128)(2,1)}, bf16[2,512,512]{2,1,0:T(8,128)(2,1)S(1)}, u32[]{:S(2)}, u32[]{:S(2)}) %collective-permute-start) | collective-permute-done | bytes 1048608 | tf_op jit(solution)/shard_map/ppermute | solution.py:24
  28.5 3.5 %fusion.12 = (bf16[2,512,512]{2,1,0:T(8,128)(2,1)}, bf16[2,512,512]{2,1,0:T(8,128)(2,1)}) fusion(bf16[3,512,1024]{2,1,0:T(8,128)(2,1)} %bitcast.57, bf16[2,512,512]{2,1,0:T(8,128)(2,1)S(1)} %collective-permute-done.k0_ref.v0_ref, pred[]{:T(512)S(6)} %eq.24), kind=kLoop, calls=%fused_computation.46 | loop fusion | flops 524288 | bytes 5242881 | tf_op jit(solution)/shard_map/slice | solution.py:300
  32.0 1.5 collective-permute-start.1
  33.6 4.0 %collective-permute-start.2 = (bf16[2,512,512]{2,1,0:T(8,128)(2,1)}, bf16[2,512,512]{2,1,0:T(8,128)(2,1)S(1)}, u32[]{:S(2)}, u32[]{:S(2)}) collective-permute-start(bf16[2,512,512]{2,1,0:T(8,128)(2,1)} %get-tuple-element.12), channel_id=1, source_target_pairs={{0,2},{1,3},{2,4},{3,5},{4,6},{5,7},{6,8},{7,9},{8,10},{9,11},{10,... | collective-permute-start | bytes 3145736 | tf_op jit(solution)/shard_map/ppermute | solution.py:24
  39.6 15.0 %shard_map.46 = (bf16[512,512]{1,0:T(8,128)(2,1)}, bf16[128,512]{1,0:T(8,128)(2,1)}) custom-call(s32[512,1]{1,0:T(8,128)} %reshape_reshape.10.qclip_ref, s32[1,1536]{1,0:T(1,128)} %reshape_reshape.9.kclip0_ref.kclip1_ref.kclip2_ref, s32[1,1536]{1,0:T(1,128)} %reshape_reshape.9.kclip0_ref.kclip1_ref.kclip2_ref, ...), custom_call_target="tpu_custom_call" | custom-call | tf_op jit(solution)/shard_map/pallas_call | solution.py:117
  54.6 5.9 %collective-permute-done.2.k0_ref.v0_ref = bf16[2,512,512]{2,1,0:T(8,128)(2,1)S(1)} collective-permute-done((bf16[2,512,512]{2,1,0:T(8,128)(2,1)}, bf16[2,512,512]{2,1,0:T(8,128)(2,1)S(1)}, u32[]{:S(2)}, u32[]{:S(2)}) %collective-permute-start.2) | collective-permute-done | bytes 1048608 | tf_op jit(solution)/shard_map/ppermute | solution.py:24
  60.5 1.2 broadcast_select_fusion
  61.8 2.1 %collective-permute-start.3 = (bf16[2,512,512]{2,1,0:T(8,128)(2,1)}, bf16[2,512,512]{2,1,0:T(8,128)(2,1)}, u32[]{:S(2)}, u32[]{:S(2)}) collective-permute-start(bf16[2,512,512]{2,1,0:T(8,128)(2,1)} %broadcast_select_fusion), channel_id=1, source_target_pairs={{0,1},{1,0},{2,3},{3,2},{4,5},{5,4},{6,7},{7,6},{8,9},{9,8},{10,11... | collective-permute-start | bytes 3145736 | tf_op jit(solution)/shard_map/ppermute | solution.py:308
  63.9 2.6 %collective-permute-done.3.k1_ref.v1_ref = bf16[2,512,512]{2,1,0:T(8,128)(2,1)} collective-permute-done((bf16[2,512,512]{2,1,0:T(8,128)(2,1)}, bf16[2,512,512]{2,1,0:T(8,128)(2,1)}, u32[]{:S(2)}, u32[]{:S(2)}) %collective-permute-start.3) | collective-permute-done | bytes 1048608 | tf_op jit(solution)/shard_map/ppermute | solution.py:308
  66.6 15.2 %shard_map.47 = (bf16[512,512]{1,0:T(8,128)(2,1)}, bf16[128,512]{1,0:T(8,128)(2,1)}) custom-call(s32[512,1]{1,0:T(8,128)} %reshape_reshape.10.qclip_ref, s32[1,1536]{1,0:T(1,128)} %reshape_reshape.9.kclip0_ref.kclip1_ref.kclip2_ref, s32[1,1536]{1,0:T(1,128)} %reshape_reshape.9.kclip0_ref.kclip1_ref.kclip2_ref, ...), custom_call_target="tpu_custom_call" | custom-call | tf_op jit(solution)/shard_map/pallas_call | solution.py:117
  81.8 3.9 %fusion.2 = bf16[128,3,1024]{2,0,1:T(8,128)(2,1)S(1)} fusion(bf16[1024,3,1024]{2,0,1:T(8,128)(2,1)} %param.6, bf16[128,512]{1,0:T(8,128)(2,1)} %get-tuple-element.16, bf16[128,512]{1,0:T(8,128)(2,1)S(1)} %copy-done.5), kind=kOutput, calls=%fused_computation.2 | convolution fusion | flops 806223872 | bytes 7340032 | tf_op jit(solution)/shard_map/rd,mdc->mrc/dot_general | solution.py:320
  86.8 1.6 collective-permute-start.6
  88.4 5.6 %collective-permute-done.4 = bf16[3,128,256]{2,1,0:T(8,128)(2,1)S(1)} collective-permute-done((bf16[3,128,256]{2,1,0:T(8,128)(2,1)}, bf16[3,128,256]{2,1,0:T(8,128)(2,1)S(1)}, u32[]{:S(2)}, u32[]{:S(2)}) %collective-permute-start.4) | collective-permute-done | bytes 196640 | tf_op jit(solution)/shard_map/ppermute | solution.py:33
  94.1 1.3 collective-permute-done.6
  95.7 7.0 %collective-permute-start.7 = (bf16[2,512,256]{2,1,0:T(8,128)(2,1)S(1)}, bf16[2,512,256]{2,1,0:T(8,128)(2,1)}, u32[]{:S(2)}, u32[]{:S(2)}) collective-permute-start(bf16[2,512,256]{2,1,0:T(8,128)(2,1)S(1)} %bitcast.64), channel_id=1, source_target_pairs={{0,8},{1,9},{2,10},{3,11},{4,12},{5,13},{6,14},{7,15},{16,24},{17,... | collective-permute-start | bytes 1572872 | tf_op jit(solution)/shard_map/ppermute | solution.py:24
  102.7 4.0 %collective-permute-start.9 = (bf16[2,512,256]{2,1,0:T(8,128)(2,1)S(1)}, bf16[2,512,256]{2,1,0:T(8,128)(2,1)}, u32[]{:S(2)}, u32[]{:S(2)}) collective-permute-start(bf16[2,512,256]{2,1,0:T(8,128)(2,1)S(1)} %bitcast.65), channel_id=1, source_target_pairs={{0,4},{1,5},{2,6},{3,7},{4,8},{5,9},{6,10},{7,11},{8,12},{9,13},{1... | collective-permute-start | bytes 1572872 | tf_op jit(solution)/shard_map/ppermute | solution.py:24
  106.7 5.0 %collective-permute-done.7.k1_ref.v1_ref = bf16[2,512,256]{2,1,0:T(8,128)(2,1)} collective-permute-done((bf16[2,512,256]{2,1,0:T(8,128)(2,1)S(1)}, bf16[2,512,256]{2,1,0:T(8,128)(2,1)}, u32[]{:S(2)}, u32[]{:S(2)}) %collective-permute-start.7) | collective-permute-done | bytes 524320 | tf_op jit(solution)/shard_map/ppermute | solution.py:24
  111.7 17.0 %collective-permute-start.8 = (bf16[2,512,256]{2,1,0:T(8,128)(2,1)}, bf16[2,512,256]{2,1,0:T(8,128)(2,1)}, u32[]{:S(2)}, u32[]{:S(2)}) collective-permute-start(bf16[2,512,256]{2,1,0:T(8,128)(2,1)} %collective-permute-done.7.k1_ref.v1_ref), channel_id=1, source_target_pairs={{0,4},{1,5},{2,6},{3,7},{4,8},{5,9},{6,10},{7,11},{8,12},{9,13},{1... | collective-permute-start | bytes 1572872 | tf_op jit(solution)/shard_map/ppermute | solution.py:24
  128.8 0.9 copy.9.qclip_ref
  130.3 1.1 constant_dynamic-update-slice_fusion.1
  131.4 1.1 constant_dynamic-update-slice_fusion.fine_ref
  133.6 5.3 %collective-permute-done.8.k0_ref.v0_ref = bf16[2,512,256]{2,1,0:T(8,128)(2,1)} collective-permute-done((bf16[2,512,256]{2,1,0:T(8,128)(2,1)}, bf16[2,512,256]{2,1,0:T(8,128)(2,1)}, u32[]{:S(2)}, u32[]{:S(2)}) %collective-permute-start.8) | collective-permute-done | bytes 524320 | tf_op jit(solution)/shard_map/ppermute | solution.py:24
  138.9 6.8 %shard_map.48 = bf16[512,256]{1,0:T(8,128)(2,1)} custom-call(s32[512,1]{1,0:T(8,128)} %copy.9.qclip_ref, s32[1,2048]{1,0:T(1,128)} %bitcast.71, s32[1,2048]{1,0:T(1,128)} %bitcast.72, s32[1,2048]{1,0:T(1,128)} %bitcast.73, s32[1,2048]{1,0:T(1,128)} %bitcast.74, bf16[512,256]{1,0:T(8,128)(2,1)} %bitcast.69, ...), custom_call_target="tpu_custom_call" | custom-call | tf_op jit(solution)/shard_map/pallas_call | solution.py:224
  145.7 0.9 constant_dynamic-slice_fusion
  146.6 1.5 collective-permute-start.10
  148.1 1.7 collective-permute-start.12
  150.7 1.1 collective-permute-done.11
  153.4 12.8 %collective-permute-start.13 = (bf16[1,1024]{1,0:T(2,128)(2,1)S(1)}, bf16[1,1024]{1,0:T(2,128)(2,1)S(1)}, u32[]{:S(2)}, u32[]{:S(2)}) collective-permute-start(bf16[1,1024]{1,0:T(2,128)(2,1)S(1)} %slice.43), channel_id=1, source_target_pairs={{0,1},{1,2},{2,3},{3,4},{4,5},{5,6},{6,7},{7,8},{8,9},{9,10},{10,1... | collective-permute-start | bytes 6152 | tf_op jit(solution)/shard_map/ppermute | solution.py:24
  167.0 2.4 %shard_map.49 = bf16[512,1024]{1,0:T(8,128)(2,1)} custom-call(bf16[512,1024]{1,0:T(8,128)(2,1)} %copy-done.4, bf16[128,1024]{1,0:T(8,128)(2,1)} %pad_select_fusion.lift_ref), custom_call_target="tpu_custom_call" | custom-call | tf_op jit(solution)/shard_map/pallas_call | solution.py:155
  169.5 1.3 fusion.7
  (58 shorter events, 8.7 us)
Async XLA Ops:
  0.0 152.9 %copy-start = (bf16[1024,1024]{1,0:T(8,128)(2,1)S(1)}, bf16[1024,1024]{1,0:T(8,128)(2,1)}, u32[]{:S(2)}) copy-start(bf16[1024,1024]{1,0:T(8,128)(2,1)} %param.7) | copy-start | bytes 6291460
  2.4 26.1 %collective-permute-start = (bf16[2,512,512]{2,1,0:T(8,128)(2,1)}, bf16[2,512,512]{2,1,0:T(8,128)(2,1)S(1)}, u32[]{:S(2)}, u32[]{:S(2)}) collective-permute-start(bf16[2,512,512]{2,1,0:T(8,128)(2,1)} %slice.37), channel_id=1, source_target_pairs={{0,2},{1,3},{2,4},{3,5},{4,6},{5,7},{6,8},{7,9},{8,10},{9,11},{10,... | collective-permute-start | bytes 3145736 | tf_op jit(solution)/shard_map/ppermute | solution.py:24
  5.6 32.0 %copy-start.6 = (s32[2048]{0:T(1024)S(1)}, s32[2048]{0:T(1024)}, u32[]{:S(2)}) copy-start(s32[2048]{0:T(1024)} %param.5) | copy-start | bytes 24580
  28.5 3.5 %copy-start.2 = (bf16[2,512,512]{2,1,0:T(8,128)(2,1)}, bf16[2,512,512]{2,1,0:T(8,128)(2,1)S(1)}, u32[]{:S(2)}) copy-start(bf16[2,512,512]{2,1,0:T(8,128)(2,1)S(1)} %collective-permute-done.k0_ref.v0_ref) | copy-start | bytes 3145732
  32.0 7.5 %collective-permute-start.1 = (bf16[2,512,512]{2,1,0:T(8,128)(2,1)}, bf16[2,512,512]{2,1,0:T(8,128)(2,1)}, u32[]{:S(2)}, u32[]{:S(2)}) collective-permute-start(bf16[2,512,512]{2,1,0:T(8,128)(2,1)} %get-tuple-element.20), channel_id=1, source_target_pairs={{0,1},{1,0},{2,3},{3,2},{4,5},{5,4},{6,7},{7,6},{8,9},{9,8},{10,11... | collective-permute-start | bytes 3145736 | tf_op jit(solution)/shard_map/ppermute | solution.py:308
  33.6 26.9 %collective-permute-start.2 = (bf16[2,512,512]{2,1,0:T(8,128)(2,1)}, bf16[2,512,512]{2,1,0:T(8,128)(2,1)S(1)}, u32[]{:S(2)}, u32[]{:S(2)}) collective-permute-start(bf16[2,512,512]{2,1,0:T(8,128)(2,1)} %get-tuple-element.12), channel_id=1, source_target_pairs={{0,2},{1,3},{2,4},{3,5},{4,6},{5,7},{6,8},{7,9},{8,10},{9,11},{10,... | collective-permute-start | bytes 3145736 | tf_op jit(solution)/shard_map/ppermute | solution.py:24
  60.5 1.3 copy-start.1
  61.8 4.8 %collective-permute-start.3 = (bf16[2,512,512]{2,1,0:T(8,128)(2,1)}, bf16[2,512,512]{2,1,0:T(8,128)(2,1)}, u32[]{:S(2)}, u32[]{:S(2)}) collective-permute-start(bf16[2,512,512]{2,1,0:T(8,128)(2,1)} %broadcast_select_fusion), channel_id=1, source_target_pairs={{0,1},{1,0},{2,3},{3,2},{4,5},{5,4},{6,7},{7,6},{8,9},{9,8},{10,11... | collective-permute-start | bytes 3145736 | tf_op jit(solution)/shard_map/ppermute | solution.py:308
  63.9 17.8 %copy-start.5 = (bf16[128,512]{1,0:T(8,128)(2,1)S(1)}, bf16[128,512]{1,0:T(8,128)(2,1)}, u32[]{:S(2)}) copy-start(bf16[128,512]{1,0:T(8,128)(2,1)} %get-tuple-element.15) | copy-start | bytes 393220
  86.4 7.6 %collective-permute-start.4 = (bf16[3,128,256]{2,1,0:T(8,128)(2,1)}, bf16[3,128,256]{2,1,0:T(8,128)(2,1)S(1)}, u32[]{:S(2)}, u32[]{:S(2)}) collective-permute-start(bf16[3,128,256]{2,1,0:T(8,128)(2,1)} %get-tuple-element.23), channel_id=1, source_target_pairs={{0,3},{1,0},{2,1},{3,2},{4,7},{5,4},{6,5},{7,6},{8,11},{9,8},{10,9... | collective-permute-start | bytes 589832 | tf_op jit(solution)/shard_map/ppermute | solution.py:33
  86.8 7.3 %collective-permute-start.5 = (bf16[3,128,256]{2,1,0:T(8,128)(2,1)S(1)}, bf16[3,128,256]{2,1,0:T(8,128)(2,1)S(1)}, u32[]{:S(2)}, u32[]{:S(2)}) collective-permute-start(bf16[3,128,256]{2,1,0:T(8,128)(2,1)S(1)} %get-tuple-element.22), channel_id=1, source_target_pairs={{0,2},{1,3},{2,0},{3,1},{4,6},{5,7},{6,4},{7,5},{8,10},{9,11},{10,... | collective-permute-start | bytes 589832 | tf_op jit(solution)/shard_map/ppermute | solution.py:33
  86.8 8.6 %collective-permute-start.6 = (bf16[3,128,256]{2,1,0:T(8,128)(2,1)S(1)}, bf16[3,128,256]{2,1,0:T(8,128)(2,1)S(1)}, u32[]{:S(2)}, u32[]{:S(2)}) collective-permute-start(bf16[3,128,256]{2,1,0:T(8,128)(2,1)S(1)} %get-tuple-element.21), channel_id=1, source_target_pairs={{0,1},{1,2},{2,3},{3,0},{4,5},{5,6},{6,7},{7,4},{8,9},{9,10},{10,1... | collective-permute-start | bytes 589832 | tf_op jit(solution)/shard_map/ppermute | solution.py:33
  95.7 43.2 %copy-start.3 = (bf16[2,4,128,256]{3,2,1,0:T(8,128)(2,1)}, bf16[2,4,128,256]{3,2,1,0:T(8,128)(2,1)S(1)}, u32[]{:S(2)}) copy-start(bf16[2,4,128,256]{3,2,1,0:T(8,128)(2,1)S(1)} %copy.8) | copy-start | bytes 1572868
  95.7 16.0 %collective-permute-start.7 = (bf16[2,512,256]{2,1,0:T(8,128)(2,1)S(1)}, bf16[2,512,256]{2,1,0:T(8,128)(2,1)}, u32[]{:S(2)}, u32[]{:S(2)}) collective-permute-start(bf16[2,512,256]{2,1,0:T(8,128)(2,1)S(1)} %bitcast.64), channel_id=1, source_target_pairs={{0,8},{1,9},{2,10},{3,11},{4,12},{5,13},{6,14},{7,15},{16,24},{17,... | collective-permute-start | bytes 1572872 | tf_op jit(solution)/shard_map/ppermute | solution.py:24
  102.7 30.6 %collective-permute-start.9 = (bf16[2,512,256]{2,1,0:T(8,128)(2,1)S(1)}, bf16[2,512,256]{2,1,0:T(8,128)(2,1)}, u32[]{:S(2)}, u32[]{:S(2)}) collective-permute-start(bf16[2,512,256]{2,1,0:T(8,128)(2,1)S(1)} %bitcast.65), channel_id=1, source_target_pairs={{0,4},{1,5},{2,6},{3,7},{4,8},{5,9},{6,10},{7,11},{8,12},{9,13},{1... | collective-permute-start | bytes 1572872 | tf_op jit(solution)/shard_map/ppermute | solution.py:24
  111.7 27.2 %collective-permute-start.8 = (bf16[2,512,256]{2,1,0:T(8,128)(2,1)}, bf16[2,512,256]{2,1,0:T(8,128)(2,1)}, u32[]{:S(2)}, u32[]{:S(2)}) collective-permute-start(bf16[2,512,256]{2,1,0:T(8,128)(2,1)} %collective-permute-done.7.k1_ref.v1_ref), channel_id=1, source_target_pairs={{0,4},{1,5},{2,6},{3,7},{4,8},{5,9},{6,10},{7,11},{8,12},{9,13},{1... | collective-permute-start | bytes 1572872 | tf_op jit(solution)/shard_map/ppermute | solution.py:24
  132.5 1.1 copy-start.4
  146.6 4.1 %collective-permute-start.10 = (bf16[128,256]{1,0:T(8,128)(2,1)S(1)}, bf16[128,256]{1,0:T(8,128)(2,1)S(1)}, u32[]{:S(2)}, u32[]{:S(2)}) collective-permute-start(bf16[128,256]{1,0:T(8,128)(2,1)S(1)} %get-tuple-element.26), channel_id=1, source_target_pairs={{0,3},{1,0},{2,1},{3,2},{4,7},{5,4},{6,5},{7,6},{8,11},{9,8},{10,9... | collective-permute-start | bytes 196616 | tf_op jit(solution)/shard_map/ppermute | solution.py:33
  148.1 3.7 %collective-permute-start.11 = (bf16[128,256]{1,0:T(8,128)(2,1)S(1)}, bf16[128,256]{1,0:T(8,128)(2,1)S(1)}, u32[]{:S(2)}, u32[]{:S(2)}) collective-permute-start(bf16[128,256]{1,0:T(8,128)(2,1)S(1)} %get-tuple-element.25), channel_id=1, source_target_pairs={{0,2},{1,3},{2,0},{3,1},{4,6},{5,7},{6,4},{7,5},{8,10},{9,11},{10,... | collective-permute-start | bytes 196616 | tf_op jit(solution)/shard_map/ppermute | solution.py:33
  148.1 3.7 %collective-permute-start.12 = (bf16[128,256]{1,0:T(8,128)(2,1)S(1)}, bf16[128,256]{1,0:T(8,128)(2,1)S(1)}, u32[]{:S(2)}, u32[]{:S(2)}) collective-permute-start(bf16[128,256]{1,0:T(8,128)(2,1)S(1)} %get-tuple-element.24), channel_id=1, source_target_pairs={{0,1},{1,2},{2,3},{3,0},{4,5},{5,6},{6,7},{7,4},{8,9},{9,10},{10,1... | collective-permute-start | bytes 196616 | tf_op jit(solution)/shard_map/ppermute | solution.py:33
  153.4 16.0 %collective-permute-start.13 = (bf16[1,1024]{1,0:T(2,128)(2,1)S(1)}, bf16[1,1024]{1,0:T(2,128)(2,1)S(1)}, u32[]{:S(2)}, u32[]{:S(2)}) collective-permute-start(bf16[1,1024]{1,0:T(2,128)(2,1)S(1)} %slice.43), channel_id=1, source_target_pairs={{0,1},{1,2},{2,3},{3,4},{4,5},{5,6},{6,7},{7,8},{8,9},{9,10},{10,1... | collective-permute-start | bytes 6152 | tf_op jit(solution)/shard_map/ppermute | solution.py:24

commit v15 on v11

--- a/solution.py
+++ b/solution.py
@@ -295,7 +295,8 @@
     head_pair_width = 2 * feat_width // FHEADS
     part_width = feat_width // HALVES
     outs = []
-    pools = []
+    projected = None
+    wplanes = jnp.transpose(w_coarse, (1, 0, 2))
     gate = None
     for part in range(HALVES):
         own_pairs = planes[1:, :, part * part_width:(part + 1) * part_width]
@@ -304,7 +305,7 @@
         prev0 = passed_along(own_pairs, "seq", 2)
         gate = prev0
         if outs:
-            prev0, _ = lax.optimization_barrier((prev0, outs[-1]))
+            prev0, _ = lax.optimization_barrier((prev0, projected))
         prev1a = pair_swap(own_pairs, "seq", False)
         prev1b = pair_swap(prev0, "seq", True)
         part_out, part_pool = fine_attention(
@@ -313,14 +314,14 @@
             part * part_width // head_pair_width,
         )
         outs.append(part_out)
-        pools.append(part_pool)
+        part_weight = wplanes[:, part * part_width:(part + 1) * part_width, :]
+        contribution = jnp.einsum(
+            "rd,mdc->mrc", part_pool, part_weight, preferred_element_type=jnp.float32
+        )
+        projected = contribution if projected is None else projected + contribution
     fine_out = jnp.concatenate(outs, axis=1)
-    pooled = jnp.concatenate(pools, axis=1)
     quarter_width = w_coarse.shape[2] // QUARTERS
-    wplanes = jnp.transpose(w_coarse, (1, 0, 2))
-    projected = jnp.einsum(
-        "rd,mdc->mrc", pooled, wplanes, preferred_element_type=jnp.float32
-    ).astype(jnp.bfloat16)
+    projected = projected.astype(jnp.bfloat16)
     pieces = []
     for shift in range(QUARTERS):
         piece = lax.dynamic_slice_in_dim(

time: 170 us -> 169 us (level)
  waiting for transfers between devices: 45 us -> 39.4 us
  matrix products: 4.32 us -> 7.23 us
  starting transfers between devices: 62.3 us -> 64.3 us
    ppermute x6, waiting for transfers between devices: 35.6 us -> 29.9 us  [passed_along(): lax.ppermute(value, axis, [(source, source + steps) for source in range(f...]
    dot_general x1 -> x2, matrix products: 3.85 us -> 6.76 us  [body(): jnp.einsum('rd,mdc->mrc', part_pool, part_weight, preferred_element_type=...]
    ppermute x4, starting transfers between devices: 9.26 us -> 11.9 us  [pair_swap(): lax.ppermute(value, axis, [(source, source + step) for source in range(st...]
    ppermute x6, starting transfers between devices: 47.8 us -> 45.8 us  [passed_along(): lax.ppermute(value, axis, [(source, source + steps) for source in range(f...]
  transfers between devices with their start and end apart: 16 -> 16, of which waited for: 8 -> 7; matrix products, arithmetic and copies ran while one was open for 5% -> 7% of each run, Pallas kernels for 11% -> 11%
where the time goes in v15:
time: 169 us; the launch traced here: 167 us
  starting transfers between devices  64.3 us (38%)
  Pallas kernels  39.9 us (24%)
  waiting for transfers between devices  39.4 us (23%)
  local copies, waits for them, and re-layouts  13.8 us (8%)
  matrix products  7.23 us (4%)
  other arithmetic  2.27 us (1%)
    ppermute x6, starting transfers between devices, passed_along(): lax.ppermute(value, axis, [(source, source + steps) for source in range(f...  45.8 us
    pallas_call x2, Pallas kernels, fine_attention(): pl.pallas_call(kernel, grid=(nq, pairs), in_specs=[pl.BlockSpec((tile, 1)...  30.7 us
    ppermute x6, waiting for transfers between devices, passed_along(): lax.ppermute(value, axis, [(source, source + steps) for source in range(f...  29.9 us
    ppermute x4, starting transfers between devices, pair_swap(): lax.ppermute(value, axis, [(source, source + step) for source in range(st...  11.9 us
    ppermute x6, waiting for transfers between devices, within_group(): return lax.ppermute(value, axis, pairs)  8.03 us
    pallas_call x1, Pallas kernels, coarse_attention(): pl.pallas_call(kernel, grid=(heads, rows // tile), in_specs=[pl.BlockSpec...  6.8 us
    dot_general x2, matrix products, body(): jnp.einsum('rd,mdc->mrc', part_pool, part_weight, preferred_element_type=...  6.76 us
    ppermute x6, starting transfers between devices, within_group(): return lax.ppermute(value, axis, pairs)  6.56 us
  transfers between devices with their start and end apart: 16, of which 7 were waited for; matrix products, arithmetic and copies ran while one was open for 7% of the time, Pallas kernels for 11%

profile of v15, /device:TPU:7, one launch (start us, length us, event | category | flops | bytes accessed | tf_op | source)
XLA Modules:
  0.0 167.3 jit_solution(6073627561854165266)
XLA Ops:
  0.0 3.2 %fusion.16 = (bf16[2,512,512]{2,1,0:T(8,128)(2,1)}, bf16[2,512,512]{2,1,0:T(8,128)(2,1)}) fusion(bf16[3,512,1024]{2,1,0:T(8,128)(2,1)} %bitcast.53), kind=kLoop, calls=%fused_computation.46 | loop fusion | bytes 4194304 | tf_op jit(solution)/shard_map/slice | solution.py:302
  3.2 3.1 %collective-permute-start = (bf16[2,512,512]{2,1,0:T(8,128)(2,1)}, bf16[2,512,512]{2,1,0:T(8,128)(2,1)}, u32[]{:S(2)}, u32[]{:S(2)}) collective-permute-start(bf16[2,512,512]{2,1,0:T(8,128)(2,1)} %get-tuple-element.20), channel_id=1, source_target_pairs={{0,2},{1,3},{2,4},{3,5},{4,6},{5,7},{6,8},{7,9},{8,10},{9,11},{10,... | collective-permute-start | bytes 3145736 | tf_op jit(solution)/shard_map/ppermute | solution.py:24
  6.3 1.3 collective-permute-start.1
  7.6 21.8 %collective-permute-done.k0_ref.v0_ref = bf16[2,512,512]{2,1,0:T(8,128)(2,1)} collective-permute-done((bf16[2,512,512]{2,1,0:T(8,128)(2,1)}, bf16[2,512,512]{2,1,0:T(8,128)(2,1)}, u32[]{:S(2)}, u32[]{:S(2)}) %collective-permute-start) | collective-permute-done | bytes 1048608 | tf_op jit(solution)/shard_map/ppermute | solution.py:24
  29.4 4.4 %collective-permute-start.2 = (bf16[2,512,512]{2,1,0:T(8,128)(2,1)}, bf16[2,512,512]{2,1,0:T(8,128)(2,1)}, u32[]{:S(2)}, u32[]{:S(2)}) collective-permute-start(bf16[2,512,512]{2,1,0:T(8,128)(2,1)} %collective-permute-done.k0_ref.v0_ref), channel_id=1, source_target_pairs={{1,0},{3,2},{5,4},{7,6},{9,8},{11,10},{13,12},{15,14},{17,16},{19,... | collective-permute-start | bytes 3145736 | tf_op jit(solution)/shard_map/ppermute | solution.py:173
  33.8 4.0 %collective-permute-start.3 = (bf16[2,512,512]{2,1,0:T(8,128)(2,1)}, bf16[2,512,512]{2,1,0:T(8,128)(2,1)S(1)}, u32[]{:S(2)}, u32[]{:S(2)}) collective-permute-start(bf16[2,512,512]{2,1,0:T(8,128)(2,1)} %get-tuple-element.12), channel_id=1, source_target_pairs={{0,2},{1,3},{2,4},{3,5},{4,6},{5,7},{6,8},{7,9},{8,10},{9,11},{10,... | collective-permute-start | bytes 3145736 | tf_op jit(solution)/shard_map/ppermute | solution.py:24
  39.8 1.3 collective-permute-start.4
  41.1 15.3 %shard_map.46 = (bf16[512,512]{1,0:T(8,128)(2,1)}, bf16[128,512]{1,0:T(8,128)(2,1)}) custom-call(s32[512,1]{1,0:T(8,128)} %reshape_reshape.10.qclip_ref, s32[1,1536]{1,0:T(1,128)} %reshape_reshape.9.kclip0_ref.kclip1_ref.kclip2_ref, s32[1,1536]{1,0:T(1,128)} %reshape_reshape.9.kclip0_ref.kclip1_ref.kclip2_ref, ...), custom_call_target="tpu_custom_call" | custom-call | tf_op jit(solution)/shard_map/pallas_call | solution.py:117
  56.5 3.7 %fusion.5 = f32[3,128,1024]{2,1,0:T(8,128)} fusion(bf16[3,1024,1024]{2,1,0:T(8,128)(2,1)} %bitcast.60, bf16[128,512]{1,0:T(8,128)(2,1)} %get-tuple-element.13), kind=kOutput, calls=%fused_computation.6 | convolution fusion | flops 402653184 | bytes 4849664 | tf_op jit(solution)/shard_map/rd,mdc->mrc/dot_general | solution.py:318
  60.2 4.9 %collective-permute-start.5 = (bf16[2,512,512]{2,1,0:T(8,128)(2,1)S(1)}, bf16[2,512,512]{2,1,0:T(8,128)(2,1)}, u32[]{:S(2)}, u32[]{:S(2)}) collective-permute-start(bf16[2,512,512]{2,1,0:T(8,128)(2,1)S(1)} %collective-permute-done.3.k0_ref.v0_ref), channel_id=1, source_target_pairs={{1,0},{3,2},{5,4},{7,6},{9,8},{11,10},{13,12},{15,14},{17,16},{19,... | collective-permute-start | bytes 3145736 | tf_op jit(solution)/shard_map/ppermute | solution.py:173
  65.2 1.4 collective-permute-done.5.k1b_ref.v1b_ref
  66.6 15.4 %shard_map.47 = (bf16[512,512]{1,0:T(8,128)(2,1)}, bf16[128,512]{1,0:T(8,128)(2,1)}) custom-call(s32[512,1]{1,0:T(8,128)} %reshape_reshape.10.qclip_ref, s32[1,1536]{1,0:T(1,128)} %reshape_reshape.9.kclip0_ref.kclip1_ref.kclip2_ref, s32[1,1536]{1,0:T(1,128)} %reshape_reshape.9.kclip0_ref.kclip1_ref.kclip2_ref, ...), custom_call_target="tpu_custom_call" | custom-call | tf_op jit(solution)/shard_map/pallas_call | solution.py:117
  82.0 3.0 %fusion.4 = bf16[3,128,1024]{2,1,0:T(8,128)(2,1)S(1)} fusion(f32[3,128,1024]{2,1,0:T(8,128)} %fusion.5, bf16[3,1024,1024]{2,1,0:T(8,128)(2,1)} %bitcast.61, bf16[128,512]{1,0:T(8,128)(2,1)} %get-tuple-element.16), kind=kOutput, calls=%fused_computation.5 | convolution fusion | flops 403439616 | bytes 5636096 | tf_op jit(solution)/shard_map/rd,mdc->mrc/dot_general | solution.py:318
  86.1 1.6 collective-permute-start.8
  87.8 5.6 %collective-permute-done.6 = bf16[3,128,256]{2,1,0:T(8,128)(2,1)S(1)} collective-permute-done((bf16[3,128,256]{2,1,0:T(8,128)(2,1)}, bf16[3,128,256]{2,1,0:T(8,128)(2,1)S(1)}, u32[]{:S(2)}, u32[]{:S(2)}) %collective-permute-start.6) | collective-permute-done | bytes 196640 | tf_op jit(solution)/shard_map/ppermute | solution.py:33
  93.4 1.4 collective-permute-done.8
  95.1 5.0 %collective-permute-start.9 = (bf16[2,512,256]{2,1,0:T(8,128)(2,1)S(1)}, bf16[2,512,256]{2,1,0:T(8,128)(2,1)}, u32[]{:S(2)}, u32[]{:S(2)}) collective-permute-start(bf16[2,512,256]{2,1,0:T(8,128)(2,1)S(1)} %bitcast.62), channel_id=1, source_target_pairs={{0,8},{1,9},{2,10},{3,11},{4,12},{5,13},{6,14},{7,15},{16,24},{17,... | collective-permute-start | bytes 1572872 | tf_op jit(solution)/shard_map/ppermute | solution.py:24
  100.1 3.3 %collective-permute-start.11 = (bf16[2,512,256]{2,1,0:T(8,128)(2,1)S(1)}, bf16[2,512,256]{2,1,0:T(8,128)(2,1)}, u32[]{:S(2)}, u32[]{:S(2)}) collective-permute-start(bf16[2,512,256]{2,1,0:T(8,128)(2,1)S(1)} %bitcast.63), channel_id=1, source_target_pairs={{0,4},{1,5},{2,6},{3,7},{4,8},{5,9},{6,10},{7,11},{8,12},{9,13},{1... | collective-permute-start | bytes 1572872 | tf_op jit(solution)/shard_map/ppermute | solution.py:24
  103.4 4.2 %collective-permute-done.9.k1_ref.v1_ref = bf16[2,512,256]{2,1,0:T(8,128)(2,1)} collective-permute-done((bf16[2,512,256]{2,1,0:T(8,128)(2,1)S(1)}, bf16[2,512,256]{2,1,0:T(8,128)(2,1)}, u32[]{:S(2)}, u32[]{:S(2)}) %collective-permute-start.9) | collective-permute-done | bytes 524320 | tf_op jit(solution)/shard_map/ppermute | solution.py:24
  107.6 17.2 %collective-permute-start.10 = (bf16[2,512,256]{2,1,0:T(8,128)(2,1)}, bf16[2,512,256]{2,1,0:T(8,128)(2,1)}, u32[]{:S(2)}, u32[]{:S(2)}) collective-permute-start(bf16[2,512,256]{2,1,0:T(8,128)(2,1)} %collective-permute-done.9.k1_ref.v1_ref), channel_id=1, source_target_pairs={{0,4},{1,5},{2,6},{3,7},{4,8},{5,9},{6,10},{7,11},{8,12},{9,13},{1... | collective-permute-start | bytes 1572872 | tf_op jit(solution)/shard_map/ppermute | solution.py:24
  124.9 0.9 copy.9.qclip_ref
  126.4 1.1 constant_dynamic-update-slice_fusion.1
  127.5 1.1 constant_dynamic-update-slice_fusion.fine_ref
  129.8 3.9 %collective-permute-done.10.k0_ref.v0_ref = bf16[2,512,256]{2,1,0:T(8,128)(2,1)} collective-permute-done((bf16[2,512,256]{2,1,0:T(8,128)(2,1)}, bf16[2,512,256]{2,1,0:T(8,128)(2,1)}, u32[]{:S(2)}, u32[]{:S(2)}) %collective-permute-start.10) | collective-permute-done | bytes 524320 | tf_op jit(solution)/shard_map/ppermute | solution.py:24
  133.7 6.8 %shard_map.48 = bf16[512,256]{1,0:T(8,128)(2,1)} custom-call(s32[512,1]{1,0:T(8,128)} %copy.9.qclip_ref, s32[1,2048]{1,0:T(1,128)} %bitcast.69, s32[1,2048]{1,0:T(1,128)} %bitcast.70, s32[1,2048]{1,0:T(1,128)} %bitcast.71, s32[1,2048]{1,0:T(1,128)} %bitcast.72, bf16[512,256]{1,0:T(8,128)(2,1)} %bitcast.67, ...), custom_call_target="tpu_custom_call" | custom-call | tf_op jit(solution)/shard_map/pallas_call | solution.py:226
  140.5 0.9 constant_dynamic-slice_fusion
  141.4 2.8 %collective-permute-start.12 = (bf16[128,256]{1,0:T(8,128)(2,1)S(1)}, bf16[128,256]{1,0:T(8,128)(2,1)S(1)}, u32[]{:S(2)}, u32[]{:S(2)}) collective-permute-start(bf16[128,256]{1,0:T(8,128)(2,1)S(1)} %get-tuple-element.26), channel_id=1, source_target_pairs={{0,3},{1,0},{2,1},{3,2},{4,7},{5,4},{6,5},{7,6},{8,11},{9,8},{10,9... | collective-permute-start | bytes 196616 | tf_op jit(solution)/shard_map/ppermute | solution.py:33
  144.3 1.7 %collective-permute-start.14 = (bf16[128,256]{1,0:T(8,128)(2,1)S(1)}, bf16[128,256]{1,0:T(8,128)(2,1)S(1)}, u32[]{:S(2)}, u32[]{:S(2)}) collective-permute-start(bf16[128,256]{1,0:T(8,128)(2,1)S(1)} %get-tuple-element.24), channel_id=1, source_target_pairs={{0,1},{1,2},{2,3},{3,0},{4,5},{5,6},{6,7},{7,4},{8,9},{9,10},{10,1... | collective-permute-start | bytes 196616 | tf_op jit(solution)/shard_map/ppermute | solution.py:33
  146.8 1.1 collective-permute-done.13
  149.6 13.1 %collective-permute-start.15 = (bf16[1,1024]{1,0:T(2,128)(2,1)S(1)}, bf16[1,1024]{1,0:T(2,128)(2,1)S(1)}, u32[]{:S(2)}, u32[]{:S(2)}) collective-permute-start(bf16[1,1024]{1,0:T(2,128)(2,1)S(1)} %slice.53), channel_id=1, source_target_pairs={{0,1},{1,2},{2,3},{3,4},{4,5},{5,6},{6,7},{7,8},{8,9},{9,10},{10,1... | collective-permute-start | bytes 6152 | tf_op jit(solution)/shard_map/ppermute | solution.py:24
  163.5 2.4 %shard_map.49 = bf16[512,1024]{1,0:T(8,128)(2,1)} custom-call(bf16[512,1024]{1,0:T(8,128)(2,1)} %copy-done.3, bf16[128,1024]{1,0:T(8,128)(2,1)} %pad_select_fusion.lift_ref), custom_call_target="tpu_custom_call" | custom-call | tf_op jit(solution)/shard_map/pallas_call | solution.py:157
  166.0 1.3 fusion.12
  (57 shorter events, 8.5 us)
Async XLA Ops:
  0.0 149.1 %copy-start = (bf16[1024,1024]{1,0:T(8,128)(2,1)S(1)}, bf16[1024,1024]{1,0:T(8,128)(2,1)}, u32[]{:S(2)}) copy-start(bf16[1024,1024]{1,0:T(8,128)(2,1)} %param.7) | copy-start | bytes 6291460
  0.0 37.9 %copy-start.4 = (s32[2048]{0:T(1024)S(1)}, s32[2048]{0:T(1024)}, u32[]{:S(2)}) copy-start(s32[2048]{0:T(1024)} %param.5) | copy-start | bytes 24580
  3.2 26.2 %collective-permute-start = (bf16[2,512,512]{2,1,0:T(8,128)(2,1)}, bf16[2,512,512]{2,1,0:T(8,128)(2,1)}, u32[]{:S(2)}, u32[]{:S(2)}) collective-permute-start(bf16[2,512,512]{2,1,0:T(8,128)(2,1)} %get-tuple-element.20), channel_id=1, source_target_pairs={{0,2},{1,3},{2,4},{3,5},{4,6},{5,7},{6,8},{7,9},{8,10},{9,11},{10,... | collective-permute-start | bytes 3145736 | tf_op jit(solution)/shard_map/ppermute | solution.py:24
  6.3 34.8 %collective-permute-start.1 = (bf16[2,512,512]{2,1,0:T(8,128)(2,1)}, bf16[2,512,512]{2,1,0:T(8,128)(2,1)}, u32[]{:S(2)}, u32[]{:S(2)}) collective-permute-start(bf16[2,512,512]{2,1,0:T(8,128)(2,1)} %get-tuple-element.20), channel_id=1, source_target_pairs={{0,1},{2,3},{4,5},{6,7},{8,9},{10,11},{12,13},{14,15},{16,17},{18,... | collective-permute-start | bytes 3145736 | tf_op jit(solution)/shard_map/ppermute | solution.py:173
  29.4 11.7 %collective-permute-start.2 = (bf16[2,512,512]{2,1,0:T(8,128)(2,1)}, bf16[2,512,512]{2,1,0:T(8,128)(2,1)}, u32[]{:S(2)}, u32[]{:S(2)}) collective-permute-start(bf16[2,512,512]{2,1,0:T(8,128)(2,1)} %collective-permute-done.k0_ref.v0_ref), channel_id=1, source_target_pairs={{1,0},{3,2},{5,4},{7,6},{9,8},{11,10},{13,12},{15,14},{17,16},{19,... | collective-permute-start | bytes 3145736 | tf_op jit(solution)/shard_map/ppermute | solution.py:173
  33.8 26.4 %collective-permute-start.3 = (bf16[2,512,512]{2,1,0:T(8,128)(2,1)}, bf16[2,512,512]{2,1,0:T(8,128)(2,1)S(1)}, u32[]{:S(2)}, u32[]{:S(2)}) collective-permute-start(bf16[2,512,512]{2,1,0:T(8,128)(2,1)} %get-tuple-element.12), channel_id=1, source_target_pairs={{0,2},{1,3},{2,4},{3,5},{4,6},{5,7},{6,8},{7,9},{8,10},{9,11},{10,... | collective-permute-start | bytes 3145736 | tf_op jit(solution)/shard_map/ppermute | solution.py:24
  39.8 25.3 %collective-permute-start.4 = (bf16[2,512,512]{2,1,0:T(8,128)(2,1)}, bf16[2,512,512]{2,1,0:T(8,128)(2,1)}, u32[]{:S(2)}, u32[]{:S(2)}) collective-permute-start(bf16[2,512,512]{2,1,0:T(8,128)(2,1)} %get-tuple-element.12), channel_id=1, source_target_pairs={{0,1},{2,3},{4,5},{6,7},{8,9},{10,11},{12,13},{14,15},{16,17},{18,... | collective-permute-start | bytes 3145736 | tf_op jit(solution)/shard_map/ppermute | solution.py:173
  60.2 6.4 %copy-start.2 = (bf16[2,512,512]{2,1,0:T(8,128)(2,1)}, bf16[2,512,512]{2,1,0:T(8,128)(2,1)S(1)}, u32[]{:S(2)}) copy-start(bf16[2,512,512]{2,1,0:T(8,128)(2,1)S(1)} %collective-permute-done.3.k0_ref.v0_ref) | copy-start | bytes 3145732
  60.2 6.4 %collective-permute-start.5 = (bf16[2,512,512]{2,1,0:T(8,128)(2,1)S(1)}, bf16[2,512,512]{2,1,0:T(8,128)(2,1)}, u32[]{:S(2)}, u32[]{:S(2)}) collective-permute-start(bf16[2,512,512]{2,1,0:T(8,128)(2,1)S(1)} %collective-permute-done.3.k0_ref.v0_ref), channel_id=1, source_target_pairs={{1,0},{3,2},{5,4},{7,6},{9,8},{11,10},{13,12},{15,14},{17,16},{19,... | collective-permute-start | bytes 3145736 | tf_op jit(solution)/shard_map/ppermute | solution.py:173
  85.8 7.6 %collective-permute-start.6 = (bf16[3,128,256]{2,1,0:T(8,128)(2,1)}, bf16[3,128,256]{2,1,0:T(8,128)(2,1)S(1)}, u32[]{:S(2)}, u32[]{:S(2)}) collective-permute-start(bf16[3,128,256]{2,1,0:T(8,128)(2,1)} %get-tuple-element.23), channel_id=1, source_target_pairs={{0,3},{1,0},{2,1},{3,2},{4,7},{5,4},{6,5},{7,6},{8,11},{9,8},{10,9... | collective-permute-start | bytes 589832 | tf_op jit(solution)/shard_map/ppermute | solution.py:33
  86.1 7.2 %collective-permute-start.7 = (bf16[3,128,256]{2,1,0:T(8,128)(2,1)S(1)}, bf16[3,128,256]{2,1,0:T(8,128)(2,1)S(1)}, u32[]{:S(2)}, u32[]{:S(2)}) collective-permute-start(bf16[3,128,256]{2,1,0:T(8,128)(2,1)S(1)} %get-tuple-element.22), channel_id=1, source_target_pairs={{0,2},{1,3},{2,0},{3,1},{4,6},{5,7},{6,4},{7,5},{8,10},{9,11},{10,... | collective-permute-start | bytes 589832 | tf_op jit(solution)/shard_map/ppermute | solution.py:33
  86.1 8.6 %collective-permute-start.8 = (bf16[3,128,256]{2,1,0:T(8,128)(2,1)S(1)}, bf16[3,128,256]{2,1,0:T(8,128)(2,1)S(1)}, u32[]{:S(2)}, u32[]{:S(2)}) collective-permute-start(bf16[3,128,256]{2,1,0:T(8,128)(2,1)S(1)} %get-tuple-element.21), channel_id=1, source_target_pairs={{0,1},{1,2},{2,3},{3,0},{4,5},{5,6},{6,7},{7,4},{8,9},{9,10},{10,1... | collective-permute-start | bytes 589832 | tf_op jit(solution)/shard_map/ppermute | solution.py:33
  95.1 38.6 %copy-start.1 = (bf16[2,4,128,256]{3,2,1,0:T(8,128)(2,1)}, bf16[2,4,128,256]{3,2,1,0:T(8,128)(2,1)S(1)}, u32[]{:S(2)}) copy-start(bf16[2,4,128,256]{3,2,1,0:T(8,128)(2,1)S(1)} %copy.8) | copy-start | bytes 1572868
  95.1 12.6 %collective-permute-start.9 = (bf16[2,512,256]{2,1,0:T(8,128)(2,1)S(1)}, bf16[2,512,256]{2,1,0:T(8,128)(2,1)}, u32[]{:S(2)}, u32[]{:S(2)}) collective-permute-start(bf16[2,512,256]{2,1,0:T(8,128)(2,1)S(1)} %bitcast.62), channel_id=1, source_target_pairs={{0,8},{1,9},{2,10},{3,11},{4,12},{5,13},{6,14},{7,15},{16,24},{17,... | collective-permute-start | bytes 1572872 | tf_op jit(solution)/shard_map/ppermute | solution.py:24
  100.1 29.3 %collective-permute-start.11 = (bf16[2,512,256]{2,1,0:T(8,128)(2,1)S(1)}, bf16[2,512,256]{2,1,0:T(8,128)(2,1)}, u32[]{:S(2)}, u32[]{:S(2)}) collective-permute-start(bf16[2,512,256]{2,1,0:T(8,128)(2,1)S(1)} %bitcast.63), channel_id=1, source_target_pairs={{0,4},{1,5},{2,6},{3,7},{4,8},{5,9},{6,10},{7,11},{8,12},{9,13},{1... | collective-permute-start | bytes 1572872 | tf_op jit(solution)/shard_map/ppermute | solution.py:24
  107.6 26.0 %collective-permute-start.10 = (bf16[2,512,256]{2,1,0:T(8,128)(2,1)}, bf16[2,512,256]{2,1,0:T(8,128)(2,1)}, u32[]{:S(2)}, u32[]{:S(2)}) collective-permute-start(bf16[2,512,256]{2,1,0:T(8,128)(2,1)} %collective-permute-done.9.k1_ref.v1_ref), channel_id=1, source_target_pairs={{0,4},{1,5},{2,6},{3,7},{4,8},{5,9},{6,10},{7,11},{8,12},{9,13},{1... | collective-permute-start | bytes 1572872 | tf_op jit(solution)/shard_map/ppermute | solution.py:24
  128.7 1.1 copy-start.3
  141.4 5.4 %collective-permute-start.12 = (bf16[128,256]{1,0:T(8,128)(2,1)S(1)}, bf16[128,256]{1,0:T(8,128)(2,1)S(1)}, u32[]{:S(2)}, u32[]{:S(2)}) collective-permute-start(bf16[128,256]{1,0:T(8,128)(2,1)S(1)} %get-tuple-element.26), channel_id=1, source_target_pairs={{0,3},{1,0},{2,1},{3,2},{4,7},{5,4},{6,5},{7,6},{8,11},{9,8},{10,9... | collective-permute-start | bytes 196616 | tf_op jit(solution)/shard_map/ppermute | solution.py:33
  144.3 3.7 %collective-permute-start.13 = (bf16[128,256]{1,0:T(8,128)(2,1)S(1)}, bf16[128,256]{1,0:T(8,128)(2,1)S(1)}, u32[]{:S(2)}, u32[]{:S(2)}) collective-permute-start(bf16[128,256]{1,0:T(8,128)(2,1)S(1)} %get-tuple-element.25), channel_id=1, source_target_pairs={{0,2},{1,3},{2,0},{3,1},{4,6},{5,7},{6,4},{7,5},{8,10},{9,11},{10,... | collective-permute-start | bytes 196616 | tf_op jit(solution)/shard_map/ppermute | solution.py:33
  144.3 3.7 %collective-permute-start.14 = (bf16[128,256]{1,0:T(8,128)(2,1)S(1)}, bf16[128,256]{1,0:T(8,128)(2,1)S(1)}, u32[]{:S(2)}, u32[]{:S(2)}) collective-permute-start(bf16[128,256]{1,0:T(8,128)(2,1)S(1)} %get-tuple-element.24), channel_id=1, source_target_pairs={{0,1},{1,2},{2,3},{3,0},{4,5},{5,6},{6,7},{7,4},{8,9},{9,10},{10,1... | collective-permute-start | bytes 196616 | tf_op jit(solution)/shard_map/ppermute | solution.py:33
  149.6 16.4 %collective-permute-start.15 = (bf16[1,1024]{1,0:T(2,128)(2,1)S(1)}, bf16[1,1024]{1,0:T(2,128)(2,1)S(1)}, u32[]{:S(2)}, u32[]{:S(2)}) collective-permute-start(bf16[1,1024]{1,0:T(2,128)(2,1)S(1)} %slice.53), channel_id=1, source_target_pairs={{0,1},{1,2},{2,3},{3,4},{4,5},{5,6},{6,7},{7,8},{8,9},{9,10},{10,1... | collective-permute-start | bytes 6152 | tf_op jit(solution)/shard_map/ppermute | solution.py:24

commit v16 on v15

--- a/solution.py
+++ b/solution.py
@@ -333,7 +333,7 @@
     coarse_queries = grouped[0]
     coarse_pairs = grouped[1:]
     one_back = passed_along(coarse_pairs, "seq", QUARTERS)
-    two_back = passed_along(coarse_pairs, "seq", 2 * QUARTERS)
+    two_back = passed_along(one_back, "seq", QUARTERS)
     three_back = passed_along(two_back, "seq", QUARTERS)
     earlier = [three_back, two_back, one_back]
     clip_back = jnp.concatenate([jnp.full((CREACH * group_rows,), -1, jnp.int32), clip_ids])

time: 169 us -> 163 us (0.964)
  starting transfers between devices: 64.3 us -> 50.7 us
  waiting for transfers between devices: 39.4 us -> 47.6 us
    ppermute x6, starting transfers between devices: 45.8 us -> 26.6 us  [passed_along(): lax.ppermute(value, axis, [(source, source + steps) for source in range(f...]
    ppermute x6, waiting for transfers between devices: 29.9 us -> 37.6 us  [passed_along(): lax.ppermute(value, axis, [(source, source + steps) for source in range(f...]
    ppermute x6, starting transfers between devices: 6.56 us -> 12.1 us  [within_group(): return lax.ppermute(value, axis, pairs)]
    unnamed x25 -> x27, local copies, waits for them, and re-layouts: 3.3 us -> 4.09 us
  transfers between devices with their start and end apart: 16 -> 16, of which waited for: 7 -> 9; matrix products, arithmetic and copies ran while one was open for 7% -> 7% of each run, Pallas kernels for 11% -> 11%
where the time goes in v16:
time: 163 us
  starting transfers between devices  50.7 us (31%)
  waiting for transfers between devices  47.6 us (29%)
  Pallas kernels  39.9 us (24%)
  local copies, waits for them, and re-layouts  14.7 us (9%)
  matrix products  7.22 us (4%)
  other arithmetic  2.25 us (1%)
    ppermute x6, waiting for transfers between devices, passed_along(): lax.ppermute(value, axis, [(source, source + steps) for source in range(f...  37.6 us
    pallas_call x2, Pallas kernels, fine_attention(): pl.pallas_call(kernel, grid=(nq, pairs), in_specs=[pl.BlockSpec((tile, 1)...  30.7 us
    ppermute x6, starting transfers between devices, passed_along(): lax.ppermute(value, axis, [(source, source + steps) for source in range(f...  26.6 us
    ppermute x6, starting transfers between devices, within_group(): return lax.ppermute(value, axis, pairs)  12.1 us
    ppermute x4, starting transfers between devices, pair_swap(): lax.ppermute(value, axis, [(source, source + step) for source in range(st...  11.9 us
    ppermute x6, waiting for transfers between devices, within_group(): return lax.ppermute(value, axis, pairs)  8.63 us
    pallas_call x1, Pallas kernels, coarse_attention(): pl.pallas_call(kernel, grid=(heads, rows // tile), in_specs=[pl.BlockSpec...  6.79 us
    dot_general x2, matrix products, body(): jnp.einsum('rd,mdc->mrc', part_pool, part_weight, preferred_element_type=...  6.75 us
  transfers between devices with their start and end apart: 16, of which 9 were waited for; matrix products, arithmetic and copies ran while one was open for 7% of the time, Pallas kernels for 11%

profile of v16, /device:TPU:7, one launch (start us, length us, event | category | flops | bytes accessed | tf_op | source)
XLA Modules:
  0.0 162.7 jit_solution(17691547416908930184)
XLA Ops:
  0.0 3.2 %fusion.16 = (bf16[2,512,512]{2,1,0:T(8,128)(2,1)}, bf16[2,512,512]{2,1,0:T(8,128)(2,1)}) fusion(bf16[3,512,1024]{2,1,0:T(8,128)(2,1)} %bitcast.53), kind=kLoop, calls=%fused_computation.46 | loop fusion | bytes 4194304 | tf_op jit(solution)/shard_map/slice | solution.py:302
  3.2 3.1 %collective-permute-start = (bf16[2,512,512]{2,1,0:T(8,128)(2,1)}, bf16[2,512,512]{2,1,0:T(8,128)(2,1)}, u32[]{:S(2)}, u32[]{:S(2)}) collective-permute-start(bf16[2,512,512]{2,1,0:T(8,128)(2,1)} %get-tuple-element.20), channel_id=1, source_target_pairs={{0,2},{1,3},{2,4},{3,5},{4,6},{5,7},{6,8},{7,9},{8,10},{9,11},{10,... | collective-permute-start | bytes 3145736 | tf_op jit(solution)/shard_map/ppermute | solution.py:24
  6.3 1.3 collective-permute-start.1
  7.6 21.8 %collective-permute-done.k0_ref.v0_ref = bf16[2,512,512]{2,1,0:T(8,128)(2,1)} collective-permute-done((bf16[2,512,512]{2,1,0:T(8,128)(2,1)}, bf16[2,512,512]{2,1,0:T(8,128)(2,1)}, u32[]{:S(2)}, u32[]{:S(2)}) %collective-permute-start) | collective-permute-done | bytes 1048608 | tf_op jit(solution)/shard_map/ppermute | solution.py:24
  29.4 4.4 %collective-permute-start.2 = (bf16[2,512,512]{2,1,0:T(8,128)(2,1)}, bf16[2,512,512]{2,1,0:T(8,128)(2,1)}, u32[]{:S(2)}, u32[]{:S(2)}) collective-permute-start(bf16[2,512,512]{2,1,0:T(8,128)(2,1)} %collective-permute-done.k0_ref.v0_ref), channel_id=1, source_target_pairs={{1,0},{3,2},{5,4},{7,6},{9,8},{11,10},{13,12},{15,14},{17,16},{19,... | collective-permute-start | bytes 3145736 | tf_op jit(solution)/shard_map/ppermute | solution.py:173
  33.8 4.0 %collective-permute-start.3 = (bf16[2,512,512]{2,1,0:T(8,128)(2,1)}, bf16[2,512,512]{2,1,0:T(8,128)(2,1)S(1)}, u32[]{:S(2)}, u32[]{:S(2)}) collective-permute-start(bf16[2,512,512]{2,1,0:T(8,128)(2,1)} %get-tuple-element.12), channel_id=1, source_target_pairs={{0,2},{1,3},{2,4},{3,5},{4,6},{5,7},{6,8},{7,9},{8,10},{9,11},{10,... | collective-permute-start | bytes 3145736 | tf_op jit(solution)/shard_map/ppermute | solution.py:24
  39.8 1.3 collective-permute-start.4
  41.1 15.3 %shard_map.46 = (bf16[512,512]{1,0:T(8,128)(2,1)}, bf16[128,512]{1,0:T(8,128)(2,1)}) custom-call(s32[512,1]{1,0:T(8,128)} %reshape_reshape.10.qclip_ref, s32[1,1536]{1,0:T(1,128)} %reshape_reshape.9.kclip0_ref.kclip1_ref.kclip2_ref, s32[1,1536]{1,0:T(1,128)} %reshape_reshape.9.kclip0_ref.kclip1_ref.kclip2_ref, ...), custom_call_target="tpu_custom_call" | custom-call | tf_op jit(solution)/shard_map/pallas_call | solution.py:117
  56.4 3.7 %fusion.5 = f32[3,128,1024]{2,1,0:T(8,128)} fusion(bf16[3,1024,1024]{2,1,0:T(8,128)(2,1)} %bitcast.60, bf16[128,512]{1,0:T(8,128)(2,1)} %get-tuple-element.13), kind=kOutput, calls=%fused_computation.6 | convolution fusion | flops 402653184 | bytes 4849664 | tf_op jit(solution)/shard_map/rd,mdc->mrc/dot_general | solution.py:318
  60.2 5.0 %collective-permute-start.5 = (bf16[2,512,512]{2,1,0:T(8,128)(2,1)S(1)}, bf16[2,512,512]{2,1,0:T(8,128)(2,1)}, u32[]{:S(2)}, u32[]{:S(2)}) collective-permute-start(bf16[2,512,512]{2,1,0:T(8,128)(2,1)S(1)} %collective-permute-done.3.k0_ref.v0_ref), channel_id=1, source_target_pairs={{1,0},{3,2},{5,4},{7,6},{9,8},{11,10},{13,12},{15,14},{17,16},{19,... | collective-permute-start | bytes 3145736 | tf_op jit(solution)/shard_map/ppermute | solution.py:173
  65.1 1.4 collective-permute-done.5.k1b_ref.v1b_ref
  66.6 15.4 %shard_map.47 = (bf16[512,512]{1,0:T(8,128)(2,1)}, bf16[128,512]{1,0:T(8,128)(2,1)}) custom-call(s32[512,1]{1,0:T(8,128)} %reshape_reshape.10.qclip_ref, s32[1,1536]{1,0:T(1,128)} %reshape_reshape.9.kclip0_ref.kclip1_ref.kclip2_ref, s32[1,1536]{1,0:T(1,128)} %reshape_reshape.9.kclip0_ref.kclip1_ref.kclip2_ref, ...), custom_call_target="tpu_custom_call" | custom-call | tf_op jit(solution)/shard_map/pallas_call | solution.py:117
  82.0 3.0 %fusion.4 = bf16[3,128,1024]{2,1,0:T(8,128)(2,1)S(1)} fusion(f32[3,128,1024]{2,1,0:T(8,128)} %fusion.5, bf16[3,1024,1024]{2,1,0:T(8,128)(2,1)} %bitcast.61, bf16[128,512]{1,0:T(8,128)(2,1)} %get-tuple-element.16), kind=kOutput, calls=%fused_computation.5 | convolution fusion | flops 403439616 | bytes 5636096 | tf_op jit(solution)/shard_map/rd,mdc->mrc/dot_general | solution.py:318
  86.1 1.6 %collective-permute-start.8 = (bf16[3,128,256]{2,1,0:T(8,128)(2,1)S(1)}, bf16[3,128,256]{2,1,0:T(8,128)(2,1)S(1)}, u32[]{:S(2)}, u32[]{:S(2)}) collective-permute-start(bf16[3,128,256]{2,1,0:T(8,128)(2,1)S(1)} %get-tuple-element.21), channel_id=1, source_target_pairs={{0,1},{1,2},{2,3},{3,0},{4,5},{5,6},{6,7},{7,4},{8,9},{9,10},{10,1... | collective-permute-start | bytes 589832 | tf_op jit(solution)/shard_map/ppermute | solution.py:33
  87.8 5.6 %collective-permute-done.6 = bf16[3,128,256]{2,1,0:T(8,128)(2,1)S(1)} collective-permute-done((bf16[3,128,256]{2,1,0:T(8,128)(2,1)}, bf16[3,128,256]{2,1,0:T(8,128)(2,1)S(1)}, u32[]{:S(2)}, u32[]{:S(2)}) %collective-permute-start.6) | collective-permute-done | bytes 196640 | tf_op jit(solution)/shard_map/ppermute | solution.py:33
  93.4 1.3 collective-permute-done.8
  95.1 3.2 %collective-permute-start.9 = (bf16[2,512,256]{2,1,0:T(8,128)(2,1)S(1)}, bf16[2,512,256]{2,1,0:T(8,128)(2,1)S(1)}, u32[]{:S(2)}, u32[]{:S(2)}) collective-permute-start(bf16[2,512,256]{2,1,0:T(8,128)(2,1)S(1)} %bitcast.62), channel_id=1, source_target_pairs={{0,4},{1,5},{2,6},{3,7},{4,8},{5,9},{6,10},{7,11},{8,12},{9,13},{1... | collective-permute-start | bytes 1572872 | tf_op jit(solution)/shard_map/ppermute | solution.py:24
  98.3 8.2 %collective-permute-done.9.k2_ref.v2_ref = bf16[2,512,256]{2,1,0:T(8,128)(2,1)S(1)} collective-permute-done((bf16[2,512,256]{2,1,0:T(8,128)(2,1)S(1)}, bf16[2,512,256]{2,1,0:T(8,128)(2,1)S(1)}, u32[]{:S(2)}, u32[]{:S(2)}) %collective-permute-start.9) | collective-permute-done | bytes 524320 | tf_op jit(solution)/shard_map/ppermute | solution.py:24
  107.3 4.9 %collective-permute-start.10 = (bf16[2,512,256]{2,1,0:T(8,128)(2,1)S(1)}, bf16[2,512,256]{2,1,0:T(8,128)(2,1)}, u32[]{:S(2)}, u32[]{:S(2)}) collective-permute-start(bf16[2,512,256]{2,1,0:T(8,128)(2,1)S(1)} %collective-permute-done.9.k2_ref.v2_ref), channel_id=1, source_target_pairs={{0,4},{1,5},{2,6},{3,7},{4,8},{5,9},{6,10},{7,11},{8,12},{9,13},{1... | collective-permute-start | bytes 1572872 | tf_op jit(solution)/shard_map/ppermute | solution.py:24
  112.2 6.5 %collective-permute-done.10.k1_ref.v1_ref = bf16[2,512,256]{2,1,0:T(8,128)(2,1)} collective-permute-done((bf16[2,512,256]{2,1,0:T(8,128)(2,1)S(1)}, bf16[2,512,256]{2,1,0:T(8,128)(2,1)}, u32[]{:S(2)}, u32[]{:S(2)}) %collective-permute-start.10) | collective-permute-done | bytes 524320 | tf_op jit(solution)/shard_map/ppermute | solution.py:24
  118.8 5.0 %collective-permute-start.11 = (bf16[2,512,256]{2,1,0:T(8,128)(2,1)}, bf16[2,512,256]{2,1,0:T(8,128)(2,1)}, u32[]{:S(2)}, u32[]{:S(2)}) collective-permute-start(bf16[2,512,256]{2,1,0:T(8,128)(2,1)} %collective-permute-done.10.k1_ref.v1_ref), channel_id=1, source_target_pairs={{0,4},{1,5},{2,6},{3,7},{4,8},{5,9},{6,10},{7,11},{8,12},{9,13},{1... | collective-permute-start | bytes 1572872 | tf_op jit(solution)/shard_map/ppermute | solution.py:24
  125.4 1.1 constant_dynamic-update-slice_fusion.1
  126.5 1.1 constant_dynamic-update-slice_fusion.fine_ref
  128.7 1.0 collective-permute-done.11.k0_ref.v0_ref
  129.7 6.8 %shard_map.48 = bf16[512,256]{1,0:T(8,128)(2,1)} custom-call(s32[512,1]{1,0:T(8,128)} %copy.9.qclip_ref, s32[1,2048]{1,0:T(1,128)} %bitcast.68, s32[1,2048]{1,0:T(1,128)} %bitcast.69, s32[1,2048]{1,0:T(1,128)} %bitcast.70, s32[1,2048]{1,0:T(1,128)} %bitcast.71, bf16[512,256]{1,0:T(8,128)(2,1)} %bitcast.66, ...), custom_call_target="tpu_custom_call" | custom-call | tf_op jit(solution)/shard_map/pallas_call | solution.py:226
  136.5 0.9 constant_dynamic-slice_fusion
  137.5 5.8 %collective-permute-start.12 = (bf16[128,256]{1,0:T(8,128)(2,1)S(1)}, bf16[128,256]{1,0:T(8,128)(2,1)S(1)}, u32[]{:S(2)}, u32[]{:S(2)}) collective-permute-start(bf16[128,256]{1,0:T(8,128)(2,1)S(1)} %get-tuple-element.26), channel_id=1, source_target_pairs={{0,3},{1,0},{2,1},{3,2},{4,7},{5,4},{6,5},{7,6},{8,11},{9,8},{10,9... | collective-permute-start | bytes 196616 | tf_op jit(solution)/shard_map/ppermute | solution.py:33
  143.2 4.4 %collective-permute-start.13 = (bf16[128,256]{1,0:T(8,128)(2,1)S(1)}, bf16[128,256]{1,0:T(8,128)(2,1)S(1)}, u32[]{:S(2)}, u32[]{:S(2)}) collective-permute-start(bf16[128,256]{1,0:T(8,128)(2,1)S(1)} %get-tuple-element.25), channel_id=1, source_target_pairs={{0,2},{1,3},{2,0},{3,1},{4,6},{5,7},{6,4},{7,5},{8,10},{9,11},{10,... | collective-permute-start | bytes 196616 | tf_op jit(solution)/shard_map/ppermute | solution.py:33
  148.4 1.5 collective-permute-done.12
  151.8 6.3 %collective-permute-start.15 = (bf16[1,1024]{1,0:T(2,128)(2,1)S(1)}, bf16[1,1024]{1,0:T(2,128)(2,1)S(1)}, u32[]{:S(2)}, u32[]{:S(2)}) collective-permute-start(bf16[1,1024]{1,0:T(2,128)(2,1)S(1)} %slice.53), channel_id=1, source_target_pairs={{0,1},{1,2},{2,3},{3,4},{4,5},{5,6},{6,7},{7,8},{8,9},{9,10},{10,1... | collective-permute-start | bytes 6152 | tf_op jit(solution)/shard_map/ppermute | solution.py:24
  158.9 2.4 %shard_map.49 = bf16[512,1024]{1,0:T(8,128)(2,1)} custom-call(bf16[512,1024]{1,0:T(8,128)(2,1)} %copy-done.3, bf16[128,1024]{1,0:T(8,128)(2,1)} %pad_select_fusion.lift_ref), custom_call_target="tpu_custom_call" | custom-call | tf_op jit(solution)/shard_map/pallas_call | solution.py:157
  161.4 1.3 fusion.12
  (59 shorter events, 10.4 us)
Async XLA Ops:
  0.0 151.3 %copy-start = (bf16[1024,1024]{1,0:T(8,128)(2,1)S(1)}, bf16[1024,1024]{1,0:T(8,128)(2,1)}, u32[]{:S(2)}) copy-start(bf16[1024,1024]{1,0:T(8,128)(2,1)} %param.7) | copy-start | bytes 6291460
  0.0 37.9 %copy-start.5 = (s32[2048]{0:T(1024)S(1)}, s32[2048]{0:T(1024)}, u32[]{:S(2)}) copy-start(s32[2048]{0:T(1024)} %param.5) | copy-start | bytes 24580
  3.2 26.2 %collective-permute-start = (bf16[2,512,512]{2,1,0:T(8,128)(2,1)}, bf16[2,512,512]{2,1,0:T(8,128)(2,1)}, u32[]{:S(2)}, u32[]{:S(2)}) collective-permute-start(bf16[2,512,512]{2,1,0:T(8,128)(2,1)} %get-tuple-element.20), channel_id=1, source_target_pairs={{0,2},{1,3},{2,4},{3,5},{4,6},{5,7},{6,8},{7,9},{8,10},{9,11},{10,... | collective-permute-start | bytes 3145736 | tf_op jit(solution)/shard_map/ppermute | solution.py:24
  6.3 34.8 %collective-permute-start.1 = (bf16[2,512,512]{2,1,0:T(8,128)(2,1)}, bf16[2,512,512]{2,1,0:T(8,128)(2,1)}, u32[]{:S(2)}, u32[]{:S(2)}) collective-permute-start(bf16[2,512,512]{2,1,0:T(8,128)(2,1)} %get-tuple-element.20), channel_id=1, source_target_pairs={{0,1},{2,3},{4,5},{6,7},{8,9},{10,11},{12,13},{14,15},{16,17},{18,... | collective-permute-start | bytes 3145736 | tf_op jit(solution)/shard_map/ppermute | solution.py:173
  29.4 11.7 %collective-permute-start.2 = (bf16[2,512,512]{2,1,0:T(8,128)(2,1)}, bf16[2,512,512]{2,1,0:T(8,128)(2,1)}, u32[]{:S(2)}, u32[]{:S(2)}) collective-permute-start(bf16[2,512,512]{2,1,0:T(8,128)(2,1)} %collective-permute-done.k0_ref.v0_ref), channel_id=1, source_target_pairs={{1,0},{3,2},{5,4},{7,6},{9,8},{11,10},{13,12},{15,14},{17,16},{19,... | collective-permute-start | bytes 3145736 | tf_op jit(solution)/shard_map/ppermute | solution.py:173
  33.8 26.4 %collective-permute-start.3 = (bf16[2,512,512]{2,1,0:T(8,128)(2,1)}, bf16[2,512,512]{2,1,0:T(8,128)(2,1)S(1)}, u32[]{:S(2)}, u32[]{:S(2)}) collective-permute-start(bf16[2,512,512]{2,1,0:T(8,128)(2,1)} %get-tuple-element.12), channel_id=1, source_target_pairs={{0,2},{1,3},{2,4},{3,5},{4,6},{5,7},{6,8},{7,9},{8,10},{9,11},{10,... | collective-permute-start | bytes 3145736 | tf_op jit(solution)/shard_map/ppermute | solution.py:24
  39.8 25.3 %collective-permute-start.4 = (bf16[2,512,512]{2,1,0:T(8,128)(2,1)}, bf16[2,512,512]{2,1,0:T(8,128)(2,1)}, u32[]{:S(2)}, u32[]{:S(2)}) collective-permute-start(bf16[2,512,512]{2,1,0:T(8,128)(2,1)} %get-tuple-element.12), channel_id=1, source_target_pairs={{0,1},{2,3},{4,5},{6,7},{8,9},{10,11},{12,13},{14,15},{16,17},{18,... | collective-permute-start | bytes 3145736 | tf_op jit(solution)/shard_map/ppermute | solution.py:173
  60.2 6.4 %copy-start.2 = (bf16[2,512,512]{2,1,0:T(8,128)(2,1)}, bf16[2,512,512]{2,1,0:T(8,128)(2,1)S(1)}, u32[]{:S(2)}) copy-start(bf16[2,512,512]{2,1,0:T(8,128)(2,1)S(1)} %collective-permute-done.3.k0_ref.v0_ref) | copy-start | bytes 3145732
  60.2 6.4 %collective-permute-start.5 = (bf16[2,512,512]{2,1,0:T(8,128)(2,1)S(1)}, bf16[2,512,512]{2,1,0:T(8,128)(2,1)}, u32[]{:S(2)}, u32[]{:S(2)}) collective-permute-start(bf16[2,512,512]{2,1,0:T(8,128)(2,1)S(1)} %collective-permute-done.3.k0_ref.v0_ref), channel_id=1, source_target_pairs={{1,0},{3,2},{5,4},{7,6},{9,8},{11,10},{13,12},{15,14},{17,16},{19,... | collective-permute-start | bytes 3145736 | tf_op jit(solution)/shard_map/ppermute | solution.py:173
  85.8 7.6 %collective-permute-start.6 = (bf16[3,128,256]{2,1,0:T(8,128)(2,1)}, bf16[3,128,256]{2,1,0:T(8,128)(2,1)S(1)}, u32[]{:S(2)}, u32[]{:S(2)}) collective-permute-start(bf16[3,128,256]{2,1,0:T(8,128)(2,1)} %get-tuple-element.23), channel_id=1, source_target_pairs={{0,3},{1,0},{2,1},{3,2},{4,7},{5,4},{6,5},{7,6},{8,11},{9,8},{10,9... | collective-permute-start | bytes 589832 | tf_op jit(solution)/shard_map/ppermute | solution.py:33
  86.1 7.3 %collective-permute-start.7 = (bf16[3,128,256]{2,1,0:T(8,128)(2,1)S(1)}, bf16[3,128,256]{2,1,0:T(8,128)(2,1)S(1)}, u32[]{:S(2)}, u32[]{:S(2)}) collective-permute-start(bf16[3,128,256]{2,1,0:T(8,128)(2,1)S(1)} %get-tuple-element.22), channel_id=1, source_target_pairs={{0,2},{1,3},{2,0},{3,1},{4,6},{5,7},{6,4},{7,5},{8,10},{9,11},{10,... | collective-permute-start | bytes 589832 | tf_op jit(solution)/shard_map/ppermute | solution.py:33
  86.1 8.6 %collective-permute-start.8 = (bf16[3,128,256]{2,1,0:T(8,128)(2,1)S(1)}, bf16[3,128,256]{2,1,0:T(8,128)(2,1)S(1)}, u32[]{:S(2)}, u32[]{:S(2)}) collective-permute-start(bf16[3,128,256]{2,1,0:T(8,128)(2,1)S(1)} %get-tuple-element.21), channel_id=1, source_target_pairs={{0,1},{1,2},{2,3},{3,0},{4,5},{5,6},{6,7},{7,4},{8,9},{9,10},{10,1... | collective-permute-start | bytes 589832 | tf_op jit(solution)/shard_map/ppermute | solution.py:33
  95.1 34.7 %copy-start.1 = (bf16[2,4,128,256]{3,2,1,0:T(8,128)(2,1)}, bf16[2,4,128,256]{3,2,1,0:T(8,128)(2,1)S(1)}, u32[]{:S(2)}) copy-start(bf16[2,4,128,256]{3,2,1,0:T(8,128)(2,1)S(1)} %copy.8) | copy-start | bytes 1572868
  95.1 11.5 %collective-permute-start.9 = (bf16[2,512,256]{2,1,0:T(8,128)(2,1)S(1)}, bf16[2,512,256]{2,1,0:T(8,128)(2,1)S(1)}, u32[]{:S(2)}, u32[]{:S(2)}) collective-permute-start(bf16[2,512,256]{2,1,0:T(8,128)(2,1)S(1)} %bitcast.62), channel_id=1, source_target_pairs={{0,4},{1,5},{2,6},{3,7},{4,8},{5,9},{6,10},{7,11},{8,12},{9,13},{1... | collective-permute-start | bytes 1572872 | tf_op jit(solution)/shard_map/ppermute | solution.py:24
  106.5 0.8 copy-start.4
  107.3 11.4 %collective-permute-start.10 = (bf16[2,512,256]{2,1,0:T(8,128)(2,1)S(1)}, bf16[2,512,256]{2,1,0:T(8,128)(2,1)}, u32[]{:S(2)}, u32[]{:S(2)}) collective-permute-start(bf16[2,512,256]{2,1,0:T(8,128)(2,1)S(1)} %collective-permute-done.9.k2_ref.v2_ref), channel_id=1, source_target_pairs={{0,4},{1,5},{2,6},{3,7},{4,8},{5,9},{6,10},{7,11},{8,12},{9,13},{1... | collective-permute-start | bytes 1572872 | tf_op jit(solution)/shard_map/ppermute | solution.py:24
  118.8 10.9 %collective-permute-start.11 = (bf16[2,512,256]{2,1,0:T(8,128)(2,1)}, bf16[2,512,256]{2,1,0:T(8,128)(2,1)}, u32[]{:S(2)}, u32[]{:S(2)}) collective-permute-start(bf16[2,512,256]{2,1,0:T(8,128)(2,1)} %collective-permute-done.10.k1_ref.v1_ref), channel_id=1, source_target_pairs={{0,4},{1,5},{2,6},{3,7},{4,8},{5,9},{6,10},{7,11},{8,12},{9,13},{1... | collective-permute-start | bytes 1572872 | tf_op jit(solution)/shard_map/ppermute | solution.py:24
  127.6 1.1 copy-start.3
  137.5 12.4 %collective-permute-start.12 = (bf16[128,256]{1,0:T(8,128)(2,1)S(1)}, bf16[128,256]{1,0:T(8,128)(2,1)S(1)}, u32[]{:S(2)}, u32[]{:S(2)}) collective-permute-start(bf16[128,256]{1,0:T(8,128)(2,1)S(1)} %get-tuple-element.26), channel_id=1, source_target_pairs={{0,3},{1,0},{2,1},{3,2},{4,7},{5,4},{6,5},{7,6},{8,11},{9,8},{10,9... | collective-permute-start | bytes 196616 | tf_op jit(solution)/shard_map/ppermute | solution.py:33
  143.2 6.7 %collective-permute-start.13 = (bf16[128,256]{1,0:T(8,128)(2,1)S(1)}, bf16[128,256]{1,0:T(8,128)(2,1)S(1)}, u32[]{:S(2)}, u32[]{:S(2)}) collective-permute-start(bf16[128,256]{1,0:T(8,128)(2,1)S(1)} %get-tuple-element.25), channel_id=1, source_target_pairs={{0,2},{1,3},{2,0},{3,1},{4,6},{5,7},{6,4},{7,5},{8,10},{9,11},{10,... | collective-permute-start | bytes 196616 | tf_op jit(solution)/shard_map/ppermute | solution.py:33
  147.6 2.6 %collective-permute-start.14 = (bf16[128,256]{1,0:T(8,128)(2,1)S(1)}, bf16[128,256]{1,0:T(8,128)(2,1)S(1)}, u32[]{:S(2)}, u32[]{:S(2)}) collective-permute-start(bf16[128,256]{1,0:T(8,128)(2,1)S(1)} %get-tuple-element.24), channel_id=1, source_target_pairs={{0,1},{1,2},{2,3},{3,0},{4,5},{5,6},{6,7},{7,4},{8,9},{9,10},{10,1... | collective-permute-start | bytes 196616 | tf_op jit(solution)/shard_map/ppermute | solution.py:33
  151.8 9.5 %collective-permute-start.15 = (bf16[1,1024]{1,0:T(2,128)(2,1)S(1)}, bf16[1,1024]{1,0:T(2,128)(2,1)S(1)}, u32[]{:S(2)}, u32[]{:S(2)}) collective-permute-start(bf16[1,1024]{1,0:T(2,128)(2,1)S(1)} %slice.53), channel_id=1, source_target_pairs={{0,1},{1,2},{2,3},{3,4},{4,5},{5,6},{6,7},{7,8},{8,9},{9,10},{10,1... | collective-permute-start | bytes 6152 | tf_op jit(solution)/shard_map/ppermute | solution.py:24

commit v17 on v16

--- a/solution.py
+++ b/solution.py
@@ -323,16 +323,28 @@
     quarter_width = w_coarse.shape[2] // QUARTERS
     projected = projected.astype(jnp.bfloat16)
     pieces = []
+    pieces_kv = []
     for shift in range(QUARTERS):
         piece = lax.dynamic_slice_in_dim(
             projected, ((quarter + shift) % QUARTERS) * quarter_width, quarter_width, 2
         )
+        pieces_kv.append(piece[1:])
         pieces.append(piece if shift == 0 else within_group(piece, "seq", shift))
     grouped = group_order(pieces, quarter)
     grouped = jnp.transpose(grouped, (1, 0, 2, 3)).reshape(3, group_rows, quarter_width)
     coarse_queries = grouped[0]
     coarse_pairs = grouped[1:]
-    one_back = passed_along(coarse_pairs, "seq", QUARTERS)
+    seq_count = lax.axis_size("seq")
+    forward = []
+    for shift in range(QUARTERS):
+        pairs = [
+            (source, source - source % QUARTERS + QUARTERS + (source + shift) % QUARTERS)
+            for source in range(seq_count - QUARTERS)
+        ]
+        forward.append(lax.ppermute(pieces_kv[shift], "seq", pairs))
+    one_back = jnp.transpose(group_order(forward, quarter), (1, 0, 2, 3)).reshape(
+        2, group_rows, quarter_width
+    )
     two_back = passed_along(one_back, "seq", QUARTERS)
     three_back = passed_along(two_back, "seq", QUARTERS)
     earlier = [three_back, two_back, one_back]

time: 163 us -> 164 us (level)
    ppermute x0 -> x4, starting transfers between devices: none -> 13.7 us  [body(): forward.append(lax.ppermute(pieces_kv[shift], 'seq', pairs))]
    ppermute x6, starting transfers between devices: 12.1 us -> 4.77 us  [within_group(): return lax.ppermute(value, axis, pairs)]
    ppermute x6, waiting for transfers between devices: 8.63 us -> 1.27 us  [within_group(): return lax.ppermute(value, axis, pairs)]
    ppermute x6 -> x5, starting transfers between devices: 26.6 us -> 21.6 us  [passed_along(): lax.ppermute(value, axis, [(source, source + steps) for source in range(f...]
    ppermute x6 -> x5, waiting for transfers between devices: 37.6 us -> 42.2 us  [passed_along(): lax.ppermute(value, axis, [(source, source + steps) for source in range(f...]
    ppermute x0 -> x4, waiting for transfers between devices: none -> 2.77 us  [body(): forward.append(lax.ppermute(pieces_kv[shift], 'seq', pairs))]
    unnamed x27 -> x40, local copies, waits for them, and re-layouts: 4.09 us -> 4.65 us
  transfers between devices with their start and end apart: 16 -> 19, of which waited for: 9 -> 6; matrix products, arithmetic and copies ran while one was open for 7% -> 8% of each run, Pallas kernels for 11% -> 11%
where the time goes in v17:
time: 164 us; the launch traced here: 163 us
  starting transfers between devices  52 us (32%)
  waiting for transfers between devices  46.2 us (28%)
  Pallas kernels  40 us (24%)
  local copies, waits for them, and re-layouts  14.4 us (9%)
  matrix products  7.22 us (4%)
  other arithmetic  2.26 us (1%)
    ppermute x5, waiting for transfers between devices, passed_along(): lax.ppermute(value, axis, [(source, source + steps) for source in range(f...  42.2 us
    pallas_call x2, Pallas kernels, fine_attention(): pl.pallas_call(kernel, grid=(nq, pairs), in_specs=[pl.BlockSpec((tile, 1)...  30.7 us
    ppermute x5, starting transfers between devices, passed_along(): lax.ppermute(value, axis, [(source, source + steps) for source in range(f...  21.6 us
    ppermute x4, starting transfers between devices, body(): forward.append(lax.ppermute(pieces_kv[shift], 'seq', pairs))  13.7 us
    ppermute x4, starting transfers between devices, pair_swap(): lax.ppermute(value, axis, [(source, source + step) for source in range(st...  12 us
    pallas_call x1, Pallas kernels, coarse_attention(): pl.pallas_call(kernel, grid=(heads, rows // tile), in_specs=[pl.BlockSpec...  6.81 us
    dot_general x2, matrix products, body(): jnp.einsum('rd,mdc->mrc', part_pool, part_weight, preferred_element_type=...  6.75 us
    ppermute x6, starting transfers between devices, within_group(): return lax.ppermute(value, axis, pairs)  4.77 us
  transfers between devices with their start and end apart: 19, of which 6 were waited for; matrix products, arithmetic and copies ran while one was open for 8% of the time, Pallas kernels for 11%

profile of v17, /device:TPU:7, one launch (start us, length us, event | category | flops | bytes accessed | tf_op | source)
XLA Modules:
  0.0 162.7 jit_solution(14826571941282736120)
XLA Ops:
  0.0 3.2 %fusion.16 = (bf16[2,512,512]{2,1,0:T(8,128)(2,1)}, bf16[2,512,512]{2,1,0:T(8,128)(2,1)}) fusion(bf16[3,512,1024]{2,1,0:T(8,128)(2,1)} %bitcast.68), kind=kLoop, calls=%fused_computation.59 | loop fusion | bytes 4194304 | tf_op jit(solution)/shard_map/slice | solution.py:302
  3.2 3.1 %collective-permute-start = (bf16[2,512,512]{2,1,0:T(8,128)(2,1)}, bf16[2,512,512]{2,1,0:T(8,128)(2,1)}, u32[]{:S(2)}, u32[]{:S(2)}) collective-permute-start(bf16[2,512,512]{2,1,0:T(8,128)(2,1)} %get-tuple-element.20), channel_id=1, source_target_pairs={{0,2},{1,3},{2,4},{3,5},{4,6},{5,7},{6,8},{7,9},{8,10},{9,11},{10,... | collective-permute-start | bytes 3145736 | tf_op jit(solution)/shard_map/ppermute | solution.py:24
  6.3 1.3 collective-permute-start.1
  7.6 21.8 %collective-permute-done.k0_ref.v0_ref = bf16[2,512,512]{2,1,0:T(8,128)(2,1)} collective-permute-done((bf16[2,512,512]{2,1,0:T(8,128)(2,1)}, bf16[2,512,512]{2,1,0:T(8,128)(2,1)}, u32[]{:S(2)}, u32[]{:S(2)}) %collective-permute-start) | collective-permute-done | bytes 1048608 | tf_op jit(solution)/shard_map/ppermute | solution.py:24
  29.4 4.4 %collective-permute-start.2 = (bf16[2,512,512]{2,1,0:T(8,128)(2,1)}, bf16[2,512,512]{2,1,0:T(8,128)(2,1)}, u32[]{:S(2)}, u32[]{:S(2)}) collective-permute-start(bf16[2,512,512]{2,1,0:T(8,128)(2,1)} %collective-permute-done.k0_ref.v0_ref), channel_id=1, source_target_pairs={{1,0},{3,2},{5,4},{7,6},{9,8},{11,10},{13,12},{15,14},{17,16},{19,... | collective-permute-start | bytes 3145736 | tf_op jit(solution)/shard_map/ppermute | solution.py:173
  33.8 4.0 %collective-permute-start.3 = (bf16[2,512,512]{2,1,0:T(8,128)(2,1)}, bf16[2,512,512]{2,1,0:T(8,128)(2,1)S(1)}, u32[]{:S(2)}, u32[]{:S(2)}) collective-permute-start(bf16[2,512,512]{2,1,0:T(8,128)(2,1)} %get-tuple-element.12), channel_id=1, source_target_pairs={{0,2},{1,3},{2,4},{3,5},{4,6},{5,7},{6,8},{7,9},{8,10},{9,11},{10,... | collective-permute-start | bytes 3145736 | tf_op jit(solution)/shard_map/ppermute | solution.py:24
  39.9 1.3 collective-permute-start.4
  41.2 15.3 %shard_map.46 = (bf16[512,512]{1,0:T(8,128)(2,1)}, bf16[128,512]{1,0:T(8,128)(2,1)}) custom-call(s32[512,1]{1,0:T(8,128)} %reshape_reshape.10.qclip_ref, s32[1,1536]{1,0:T(1,128)} %reshape_reshape.9.kclip0_ref.kclip1_ref.kclip2_ref, s32[1,1536]{1,0:T(1,128)} %reshape_reshape.9.kclip0_ref.kclip1_ref.kclip2_ref, ...), custom_call_target="tpu_custom_call" | custom-call | tf_op jit(solution)/shard_map/pallas_call | solution.py:117
  56.5 3.7 %fusion.5 = f32[3,128,1024]{2,1,0:T(8,128)} fusion(bf16[3,1024,1024]{2,1,0:T(8,128)(2,1)} %bitcast.75, bf16[128,512]{1,0:T(8,128)(2,1)} %get-tuple-element.13), kind=kOutput, calls=%fused_computation.6 | convolution fusion | flops 402653184 | bytes 4849664 | tf_op jit(solution)/shard_map/rd,mdc->mrc/dot_general | solution.py:318
  60.2 5.0 %collective-permute-start.5 = (bf16[2,512,512]{2,1,0:T(8,128)(2,1)S(1)}, bf16[2,512,512]{2,1,0:T(8,128)(2,1)}, u32[]{:S(2)}, u32[]{:S(2)}) collective-permute-start(bf16[2,512,512]{2,1,0:T(8,128)(2,1)S(1)} %collective-permute-done.3.k0_ref.v0_ref), channel_id=1, source_target_pairs={{1,0},{3,2},{5,4},{7,6},{9,8},{11,10},{13,12},{15,14},{17,16},{19,... | collective-permute-start | bytes 3145736 | tf_op jit(solution)/shard_map/ppermute | solution.py:173
  65.3 0.9 copy.11.qclip_ref
  66.9 1.9 %constant_dynamic-update-slice_fusion.1 = bf16[512,1024]{1,0:T(8,128)(2,1)} fusion(bf16[512,512]{1,0:T(8,128)(2,1)} %get-tuple-element.11), kind=kLoop, calls=%fused_computation.39 | loop fusion | bytes 1048576
  68.7 15.4 %shard_map.47 = (bf16[512,512]{1,0:T(8,128)(2,1)}, bf16[128,512]{1,0:T(8,128)(2,1)}) custom-call(s32[512,1]{1,0:T(8,128)} %reshape_reshape.10.qclip_ref, s32[1,1536]{1,0:T(1,128)} %reshape_reshape.9.kclip0_ref.kclip1_ref.kclip2_ref, s32[1,1536]{1,0:T(1,128)} %reshape_reshape.9.kclip0_ref.kclip1_ref.kclip2_ref, ...), custom_call_target="tpu_custom_call" | custom-call | tf_op jit(solution)/shard_map/pallas_call | solution.py:117
  84.2 3.0 %fusion.4 = bf16[3,128,1024]{2,1,0:T(8,128)(2,1)S(1)} fusion(f32[3,128,1024]{2,1,0:T(8,128)} %fusion.5, bf16[3,1024,1024]{2,1,0:T(8,128)(2,1)} %bitcast.76, bf16[128,512]{1,0:T(8,128)(2,1)} %get-tuple-element.16), kind=kOutput, calls=%fused_computation.5 | convolution fusion | flops 403439616 | bytes 5636096 | tf_op jit(solution)/shard_map/rd,mdc->mrc/dot_general | solution.py:318
  87.4 3.3 %collective-permute-start.9 = (bf16[2,128,256]{2,1,0:T(8,128)(2,1)S(1)}, bf16[2,128,256]{2,1,0:T(8,128)(2,1)S(1)}, u32[]{:S(2)}, u32[]{:S(2)}) collective-permute-start(bf16[2,128,256]{2,1,0:T(8,128)(2,1)S(1)} %get-tuple-element.24), channel_id=1, source_target_pairs={{0,4},{1,5},{2,6},{3,7},{4,8},{5,9},{6,10},{7,11},{8,12},{9,13},{1... | collective-permute-start | bytes 393224 | tf_op jit(solution)/shard_map/ppermute | solution.py:344
  90.9 1.7 %collective-permute-start.8 = (bf16[3,128,256]{2,1,0:T(8,128)(2,1)S(1)}, bf16[3,128,256]{2,1,0:T(8,128)(2,1)S(1)}, u32[]{:S(2)}, u32[]{:S(2)}) collective-permute-start(bf16[3,128,256]{2,1,0:T(8,128)(2,1)S(1)} %get-tuple-element.25), channel_id=1, source_target_pairs={{0,1},{1,2},{2,3},{3,0},{4,5},{5,6},{6,7},{7,4},{8,9},{9,10},{10,1... | collective-permute-start | bytes 589832 | tf_op jit(solution)/shard_map/ppermute | solution.py:33
  92.6 3.4 %collective-permute-start.10 = (bf16[2,128,256]{2,1,0:T(8,128)(2,1)S(1)}, bf16[2,128,256]{2,1,0:T(8,128)(2,1)S(1)}, u32[]{:S(2)}, u32[]{:S(2)}) collective-permute-start(bf16[2,128,256]{2,1,0:T(8,128)(2,1)S(1)} %get-tuple-element.23), channel_id=1, source_target_pairs={{0,7},{1,4},{2,5},{3,6},{4,11},{5,8},{6,9},{7,10},{8,15},{9,12},{1... | collective-permute-start | bytes 393224 | tf_op jit(solution)/shard_map/ppermute | solution.py:344
  96.2 3.1 %collective-permute-start.11 = (bf16[2,128,256]{2,1,0:T(8,128)(2,1)S(1)}, bf16[2,128,256]{2,1,0:T(8,128)(2,1)S(1)}, u32[]{:S(2)}, u32[]{:S(2)}) collective-permute-start(bf16[2,128,256]{2,1,0:T(8,128)(2,1)S(1)} %get-tuple-element.22), channel_id=1, source_target_pairs={{0,6},{1,7},{2,4},{3,5},{4,10},{5,11},{6,8},{7,9},{8,14},{9,15},{1... | collective-permute-start | bytes 393224 | tf_op jit(solution)/shard_map/ppermute | solution.py:344
  99.3 3.8 %collective-permute-start.12 = (bf16[2,128,256]{2,1,0:T(8,128)(2,1)S(1)}, bf16[2,128,256]{2,1,0:T(8,128)(2,1)S(1)}, u32[]{:S(2)}, u32[]{:S(2)}) collective-permute-start(bf16[2,128,256]{2,1,0:T(8,128)(2,1)S(1)} %get-tuple-element.21), channel_id=1, source_target_pairs={{0,5},{1,6},{2,7},{3,4},{4,9},{5,10},{6,11},{7,8},{8,13},{9,14},{1... | collective-permute-start | bytes 393224 | tf_op jit(solution)/shard_map/ppermute | solution.py:344
  103.2 2.8 %collective-permute-done.12 = bf16[2,128,256]{2,1,0:T(8,128)(2,1)S(1)} collective-permute-done((bf16[2,128,256]{2,1,0:T(8,128)(2,1)S(1)}, bf16[2,128,256]{2,1,0:T(8,128)(2,1)S(1)}, u32[]{:S(2)}, u32[]{:S(2)}) %collective-permute-start.12) | collective-permute-done | bytes 131104 | tf_op jit(solution)/shard_map/ppermute | solution.py:344
  106.1 4.6 %collective-permute-start.13 = (bf16[2,512,256]{2,1,0:T(8,128)(2,1)S(1)}, bf16[2,512,256]{2,1,0:T(8,128)(2,1)S(1)}, u32[]{:S(2)}, u32[]{:S(2)}) collective-permute-start(bf16[2,512,256]{2,1,0:T(8,128)(2,1)S(1)} %bitcast.77), channel_id=1, source_target_pairs={{0,4},{1,5},{2,6},{3,7},{4,8},{5,9},{6,10},{7,11},{8,12},{9,13},{1... | collective-permute-start | bytes 1572872 | tf_op jit(solution)/shard_map/ppermute | solution.py:24
  110.9 11.2 %collective-permute-done.13.k1_ref.v1_ref = bf16[2,512,256]{2,1,0:T(8,128)(2,1)S(1)} collective-permute-done((bf16[2,512,256]{2,1,0:T(8,128)(2,1)S(1)}, bf16[2,512,256]{2,1,0:T(8,128)(2,1)S(1)}, u32[]{:S(2)}, u32[]{:S(2)}) %collective-permute-start.13) | collective-permute-done | bytes 524320 | tf_op jit(solution)/shard_map/ppermute | solution.py:24
  122.1 3.8 %collective-permute-start.14 = (bf16[2,512,256]{2,1,0:T(8,128)(2,1)S(1)}, bf16[2,512,256]{2,1,0:T(8,128)(2,1)S(1)}, u32[]{:S(2)}, u32[]{:S(2)}) collective-permute-start(bf16[2,512,256]{2,1,0:T(8,128)(2,1)S(1)} %collective-permute-done.13.k1_ref.v1_ref), channel_id=1, source_target_pairs={{0,4},{1,5},{2,6},{3,7},{4,8},{5,9},{6,10},{7,11},{8,12},{9,13},{1... | collective-permute-start | bytes 1572872 | tf_op jit(solution)/shard_map/ppermute | solution.py:24
  127.7 9.2 %collective-permute-done.14.k0_ref.v0_ref = bf16[2,512,256]{2,1,0:T(8,128)(2,1)S(1)} collective-permute-done((bf16[2,512,256]{2,1,0:T(8,128)(2,1)S(1)}, bf16[2,512,256]{2,1,0:T(8,128)(2,1)S(1)}, u32[]{:S(2)}, u32[]{:S(2)}) %collective-permute-start.14) | collective-permute-done | bytes 524320 | tf_op jit(solution)/shard_map/ppermute | solution.py:24
  137.7 6.8 %shard_map.48 = bf16[512,256]{1,0:T(8,128)(2,1)} custom-call(s32[512,1]{1,0:T(8,128)} %copy.11.qclip_ref, s32[1,2048]{1,0:T(1,128)} %bitcast.85, s32[1,2048]{1,0:T(1,128)} %bitcast.86, s32[1,2048]{1,0:T(1,128)} %bitcast.87, s32[1,2048]{1,0:T(1,128)} %bitcast.88, bf16[512,256]{1,0:T(8,128)(2,1)} %bitcast.83, bf16[2,512,256]{2,1,0:T(8,128)(2,1)} %copy-done.6, ...), custom_call_target="tpu_custom_call" | custom-call | tf_op jit(solution)/shard_map/pallas_call | solution.py:226
  144.5 0.9 constant_dynamic-slice_fusion.4
  145.4 1.2 collective-permute-start.15
  147.1 1.2 collective-permute-start.17
  149.3 1.2 collective-permute-done.16
  152.1 6.0 %collective-permute-start.18 = (bf16[1,1024]{1,0:T(2,128)(2,1)S(1)}, bf16[1,1024]{1,0:T(2,128)(2,1)S(1)}, u32[]{:S(2)}, u32[]{:S(2)}) collective-permute-start(bf16[1,1024]{1,0:T(2,128)(2,1)S(1)} %slice.69), channel_id=1, source_target_pairs={{0,1},{1,2},{2,3},{3,4},{4,5},{5,6},{6,7},{7,8},{8,9},{9,10},{10,1... | collective-permute-start | bytes 6152 | tf_op jit(solution)/shard_map/ppermute | solution.py:24
  158.9 2.4 %shard_map.49 = bf16[512,1024]{1,0:T(8,128)(2,1)} custom-call(bf16[512,1024]{1,0:T(8,128)(2,1)} %copy-done.4, bf16[128,1024]{1,0:T(8,128)(2,1)} %pad_select_fusion.lift_ref), custom_call_target="tpu_custom_call" | custom-call | tf_op jit(solution)/shard_map/pallas_call | solution.py:157
  161.4 1.3 fusion.12
  (82 shorter events, 9.7 us)
Async XLA Ops:
  0.0 151.6 %copy-start = (bf16[1024,1024]{1,0:T(8,128)(2,1)S(1)}, bf16[1024,1024]{1,0:T(8,128)(2,1)}, u32[]{:S(2)}) copy-start(bf16[1024,1024]{1,0:T(8,128)(2,1)} %param.7) | copy-start | bytes 6291460
  0.0 37.9 %copy-start.8 = (s32[2048]{0:T(1024)S(1)}, s32[2048]{0:T(1024)}, u32[]{:S(2)}) copy-start(s32[2048]{0:T(1024)} %param.5) | copy-start | bytes 24580
  3.2 26.2 %collective-permute-start = (bf16[2,512,512]{2,1,0:T(8,128)(2,1)}, bf16[2,512,512]{2,1,0:T(8,128)(2,1)}, u32[]{:S(2)}, u32[]{:S(2)}) collective-permute-start(bf16[2,512,512]{2,1,0:T(8,128)(2,1)} %get-tuple-element.20), channel_id=1, source_target_pairs={{0,2},{1,3},{2,4},{3,5},{4,6},{5,7},{6,8},{7,9},{8,10},{9,11},{10,... | collective-permute-start | bytes 3145736 | tf_op jit(solution)/shard_map/ppermute | solution.py:24
  6.3 34.8 %collective-permute-start.1 = (bf16[2,512,512]{2,1,0:T(8,128)(2,1)}, bf16[2,512,512]{2,1,0:T(8,128)(2,1)}, u32[]{:S(2)}, u32[]{:S(2)}) collective-permute-start(bf16[2,512,512]{2,1,0:T(8,128)(2,1)} %get-tuple-element.20), channel_id=1, source_target_pairs={{0,1},{2,3},{4,5},{6,7},{8,9},{10,11},{12,13},{14,15},{16,17},{18,... | collective-permute-start | bytes 3145736 | tf_op jit(solution)/shard_map/ppermute | solution.py:173
  29.4 11.7 %collective-permute-start.2 = (bf16[2,512,512]{2,1,0:T(8,128)(2,1)}, bf16[2,512,512]{2,1,0:T(8,128)(2,1)}, u32[]{:S(2)}, u32[]{:S(2)}) collective-permute-start(bf16[2,512,512]{2,1,0:T(8,128)(2,1)} %collective-permute-done.k0_ref.v0_ref), channel_id=1, source_target_pairs={{1,0},{3,2},{5,4},{7,6},{9,8},{11,10},{13,12},{15,14},{17,16},{19,... | collective-permute-start | bytes 3145736 | tf_op jit(solution)/shard_map/ppermute | solution.py:173
  33.8 26.4 %collective-permute-start.3 = (bf16[2,512,512]{2,1,0:T(8,128)(2,1)}, bf16[2,512,512]{2,1,0:T(8,128)(2,1)S(1)}, u32[]{:S(2)}, u32[]{:S(2)}) collective-permute-start(bf16[2,512,512]{2,1,0:T(8,128)(2,1)} %get-tuple-element.12), channel_id=1, source_target_pairs={{0,2},{1,3},{2,4},{3,5},{4,6},{5,7},{6,8},{7,9},{8,10},{9,11},{10,... | collective-permute-start | bytes 3145736 | tf_op jit(solution)/shard_map/ppermute | solution.py:24
  39.9 28.9 %collective-permute-start.4 = (bf16[2,512,512]{2,1,0:T(8,128)(2,1)}, bf16[2,512,512]{2,1,0:T(8,128)(2,1)}, u32[]{:S(2)}, u32[]{:S(2)}) collective-permute-start(bf16[2,512,512]{2,1,0:T(8,128)(2,1)} %get-tuple-element.12), channel_id=1, source_target_pairs={{0,1},{2,3},{4,5},{6,7},{8,9},{10,11},{12,13},{14,15},{16,17},{18,... | collective-permute-start | bytes 3145736 | tf_op jit(solution)/shard_map/ppermute | solution.py:173
  60.2 8.5 %copy-start.2 = (bf16[2,512,512]{2,1,0:T(8,128)(2,1)}, bf16[2,512,512]{2,1,0:T(8,128)(2,1)S(1)}, u32[]{:S(2)}) copy-start(bf16[2,512,512]{2,1,0:T(8,128)(2,1)S(1)} %collective-permute-done.3.k0_ref.v0_ref) | copy-start | bytes 3145732
  60.2 8.5 %collective-permute-start.5 = (bf16[2,512,512]{2,1,0:T(8,128)(2,1)S(1)}, bf16[2,512,512]{2,1,0:T(8,128)(2,1)}, u32[]{:S(2)}, u32[]{:S(2)}) collective-permute-start(bf16[2,512,512]{2,1,0:T(8,128)(2,1)S(1)} %collective-permute-done.3.k0_ref.v0_ref), channel_id=1, source_target_pairs={{1,0},{3,2},{5,4},{7,6},{9,8},{11,10},{13,12},{15,14},{17,16},{19,... | collective-permute-start | bytes 3145736 | tf_op jit(solution)/shard_map/ppermute | solution.py:173
  87.2 8.9 %copy-start.3 = (bf16[512,1024]{1,0:T(8,128)(2,1)S(1)}, bf16[512,1024]{1,0:T(8,128)(2,1)}, u32[]{:S(2)}) copy-start(bf16[512,1024]{1,0:T(8,128)(2,1)} %constant_dynamic-update-slice_fusion.1) | copy-start | bytes 3145732
  87.2 8.9 %copy-start.7 = (bf16[512,512]{1,0:T(8,128)(2,1)S(1)}, bf16[512,512]{1,0:T(8,128)(2,1)}, u32[]{:S(2)}) copy-start(bf16[512,512]{1,0:T(8,128)(2,1)} %get-tuple-element.15) | copy-start | bytes 1572868
  87.4 8.8 %collective-permute-start.9 = (bf16[2,128,256]{2,1,0:T(8,128)(2,1)S(1)}, bf16[2,128,256]{2,1,0:T(8,128)(2,1)S(1)}, u32[]{:S(2)}, u32[]{:S(2)}) collective-permute-start(bf16[2,128,256]{2,1,0:T(8,128)(2,1)S(1)} %get-tuple-element.24), channel_id=1, source_target_pairs={{0,4},{1,5},{2,6},{3,7},{4,8},{5,9},{6,10},{7,11},{8,12},{9,13},{1... | collective-permute-start | bytes 393224 | tf_op jit(solution)/shard_map/ppermute | solution.py:344
  90.8 20.0 %collective-permute-start.6 = (bf16[3,128,256]{2,1,0:T(8,128)(2,1)S(1)}, bf16[3,128,256]{2,1,0:T(8,128)(2,1)S(1)}, u32[]{:S(2)}, u32[]{:S(2)}) collective-permute-start(bf16[3,128,256]{2,1,0:T(8,128)(2,1)S(1)} %get-tuple-element.27), channel_id=1, source_target_pairs={{0,3},{1,0},{2,1},{3,2},{4,7},{5,4},{6,5},{7,6},{8,11},{9,8},{10,9... | collective-permute-start | bytes 589832 | tf_op jit(solution)/shard_map/ppermute | solution.py:33
  90.8 20.0 %collective-permute-start.7 = (bf16[3,128,256]{2,1,0:T(8,128)(2,1)S(1)}, bf16[3,128,256]{2,1,0:T(8,128)(2,1)S(1)}, u32[]{:S(2)}, u32[]{:S(2)}) collective-permute-start(bf16[3,128,256]{2,1,0:T(8,128)(2,1)S(1)} %get-tuple-element.26), channel_id=1, source_target_pairs={{0,2},{1,3},{2,0},{3,1},{4,6},{5,7},{6,4},{7,5},{8,10},{9,11},{10,... | collective-permute-start | bytes 589832 | tf_op jit(solution)/shard_map/ppermute | solution.py:33
  90.9 19.9 %collective-permute-start.8 = (bf16[3,128,256]{2,1,0:T(8,128)(2,1)S(1)}, bf16[3,128,256]{2,1,0:T(8,128)(2,1)S(1)}, u32[]{:S(2)}, u32[]{:S(2)}) collective-permute-start(bf16[3,128,256]{2,1,0:T(8,128)(2,1)S(1)} %get-tuple-element.25), channel_id=1, source_target_pairs={{0,1},{1,2},{2,3},{3,0},{4,5},{5,6},{6,7},{7,4},{8,9},{9,10},{10,1... | collective-permute-start | bytes 589832 | tf_op jit(solution)/shard_map/ppermute | solution.py:33
  92.6 6.7 %collective-permute-start.10 = (bf16[2,128,256]{2,1,0:T(8,128)(2,1)S(1)}, bf16[2,128,256]{2,1,0:T(8,128)(2,1)S(1)}, u32[]{:S(2)}, u32[]{:S(2)}) collective-permute-start(bf16[2,128,256]{2,1,0:T(8,128)(2,1)S(1)} %get-tuple-element.23), channel_id=1, source_target_pairs={{0,7},{1,4},{2,5},{3,6},{4,11},{5,8},{6,9},{7,10},{8,15},{9,12},{1... | collective-permute-start | bytes 393224 | tf_op jit(solution)/shard_map/ppermute | solution.py:344
  96.1 9.9 %copy-start.4 = (bf16[512,1024]{1,0:T(8,128)(2,1)}, bf16[512,1024]{1,0:T(8,128)(2,1)S(1)}, u32[]{:S(2)}) copy-start(bf16[512,1024]{1,0:T(8,128)(2,1)S(1)} %constant_dynamic-update-slice_fusion.fine_ref) | copy-start | bytes 3145732
  96.2 7.0 %collective-permute-start.11 = (bf16[2,128,256]{2,1,0:T(8,128)(2,1)S(1)}, bf16[2,128,256]{2,1,0:T(8,128)(2,1)S(1)}, u32[]{:S(2)}, u32[]{:S(2)}) collective-permute-start(bf16[2,128,256]{2,1,0:T(8,128)(2,1)S(1)} %get-tuple-element.22), channel_id=1, source_target_pairs={{0,6},{1,7},{2,4},{3,5},{4,10},{5,11},{6,8},{7,9},{8,14},{9,15},{1... | collective-permute-start | bytes 393224 | tf_op jit(solution)/shard_map/ppermute | solution.py:344
  99.3 6.6 %collective-permute-start.12 = (bf16[2,128,256]{2,1,0:T(8,128)(2,1)S(1)}, bf16[2,128,256]{2,1,0:T(8,128)(2,1)S(1)}, u32[]{:S(2)}, u32[]{:S(2)}) collective-permute-start(bf16[2,128,256]{2,1,0:T(8,128)(2,1)S(1)} %get-tuple-element.21), channel_id=1, source_target_pairs={{0,5},{1,6},{2,7},{3,4},{4,9},{5,10},{6,11},{7,8},{8,13},{9,14},{1... | collective-permute-start | bytes 393224 | tf_op jit(solution)/shard_map/ppermute | solution.py:344
  106.1 20.0 %copy-start.1 = (bf16[2,4,128,256]{3,2,1,0:T(8,128)(2,1)}, bf16[2,4,128,256]{3,2,1,0:T(8,128)(2,1)S(1)}, u32[]{:S(2)}) copy-start(bf16[2,4,128,256]{3,2,1,0:T(8,128)(2,1)S(1)} %copy.9) | copy-start | bytes 1572868
  106.1 16.0 %collective-permute-start.13 = (bf16[2,512,256]{2,1,0:T(8,128)(2,1)S(1)}, bf16[2,512,256]{2,1,0:T(8,128)(2,1)S(1)}, u32[]{:S(2)}, u32[]{:S(2)}) collective-permute-start(bf16[2,512,256]{2,1,0:T(8,128)(2,1)S(1)} %bitcast.77), channel_id=1, source_target_pairs={{0,4},{1,5},{2,6},{3,7},{4,8},{5,9},{6,10},{7,11},{8,12},{9,13},{1... | collective-permute-start | bytes 1572872 | tf_op jit(solution)/shard_map/ppermute | solution.py:24
  122.1 4.7 %copy-start.5 = (bf16[2,512,256]{2,1,0:T(8,128)(2,1)}, bf16[2,512,256]{2,1,0:T(8,128)(2,1)S(1)}, u32[]{:S(2)}) copy-start(bf16[2,512,256]{2,1,0:T(8,128)(2,1)S(1)} %collective-permute-done.13.k1_ref.v1_ref) | copy-start | bytes 1572868
  122.1 14.7 %collective-permute-start.14 = (bf16[2,512,256]{2,1,0:T(8,128)(2,1)S(1)}, bf16[2,512,256]{2,1,0:T(8,128)(2,1)S(1)}, u32[]{:S(2)}, u32[]{:S(2)}) collective-permute-start(bf16[2,512,256]{2,1,0:T(8,128)(2,1)S(1)} %collective-permute-done.13.k1_ref.v1_ref), channel_id=1, source_target_pairs={{0,4},{1,5},{2,6},{3,7},{4,8},{5,9},{6,10},{7,11},{8,12},{9,13},{1... | collective-permute-start | bytes 1572872 | tf_op jit(solution)/shard_map/ppermute | solution.py:24
  136.9 0.8 copy-start.6
  145.4 3.9 %collective-permute-start.15 = (bf16[128,256]{1,0:T(8,128)(2,1)S(1)}, bf16[128,256]{1,0:T(8,128)(2,1)S(1)}, u32[]{:S(2)}, u32[]{:S(2)}) collective-permute-start(bf16[128,256]{1,0:T(8,128)(2,1)S(1)} %get-tuple-element.30), channel_id=1, source_target_pairs={{0,3},{1,0},{2,1},{3,2},{4,7},{5,4},{6,5},{7,6},{8,11},{9,8},{10,9... | collective-permute-start | bytes 196616 | tf_op jit(solution)/shard_map/ppermute | solution.py:33
  146.6 3.8 %collective-permute-start.16 = (bf16[128,256]{1,0:T(8,128)(2,1)S(1)}, bf16[128,256]{1,0:T(8,128)(2,1)S(1)}, u32[]{:S(2)}, u32[]{:S(2)}) collective-permute-start(bf16[128,256]{1,0:T(8,128)(2,1)S(1)} %get-tuple-element.29), channel_id=1, source_target_pairs={{0,2},{1,3},{2,0},{3,1},{4,6},{5,7},{6,4},{7,5},{8,10},{9,11},{10,... | collective-permute-start | bytes 196616 | tf_op jit(solution)/shard_map/ppermute | solution.py:33
  147.1 3.3 %collective-permute-start.17 = (bf16[128,256]{1,0:T(8,128)(2,1)S(1)}, bf16[128,256]{1,0:T(8,128)(2,1)S(1)}, u32[]{:S(2)}, u32[]{:S(2)}) collective-permute-start(bf16[128,256]{1,0:T(8,128)(2,1)S(1)} %get-tuple-element.28), channel_id=1, source_target_pairs={{0,1},{1,2},{2,3},{3,0},{4,5},{5,6},{6,7},{7,4},{8,9},{9,10},{10,1... | collective-permute-start | bytes 196616 | tf_op jit(solution)/shard_map/ppermute | solution.py:33
  152.1 9.2 %collective-permute-start.18 = (bf16[1,1024]{1,0:T(2,128)(2,1)S(1)}, bf16[1,1024]{1,0:T(2,128)(2,1)S(1)}, u32[]{:S(2)}, u32[]{:S(2)}) collective-permute-start(bf16[1,1024]{1,0:T(2,128)(2,1)S(1)} %slice.69), channel_id=1, source_target_pairs={{0,1},{1,2},{2,3},{3,4},{4,5},{5,6},{6,7},{7,8},{8,9},{9,10},{10,1... | collective-permute-start | bytes 6152 | tf_op jit(solution)/shard_map/ppermute | solution.py:24

commit v18 on v16

--- a/solution.py
+++ b/solution.py
@@ -124,7 +124,7 @@
             pl.BlockSpec((1, tok), lambda i, h: (0, 2)),
             pl.BlockSpec((None, tile, pair), lambda i, h: (0, i, first_pair + h)),
             plane_spec(0), plane_spec(1),
-            plane_spec(0), plane_spec(1),
+            own_spec(1), own_spec(2),
             plane_spec(0), plane_spec(1),
             own_spec(1), own_spec(2),
         ],
@@ -298,6 +298,7 @@
     projected = None
     wplanes = jnp.transpose(w_coarse, (1, 0, 2))
     gate = None
+    prev1a = pair_swap(planes, "seq", False)
     for part in range(HALVES):
         own_pairs = planes[1:, :, part * part_width:(part + 1) * part_width]
         if gate is not None:
@@ -306,7 +307,6 @@
         gate = prev0
         if outs:
             prev0, _ = lax.optimization_barrier((prev0, projected))
-        prev1a = pair_swap(own_pairs, "seq", False)
         prev1b = pair_swap(prev0, "seq", True)
         part_out, part_pool = fine_attention(
             planes, prev0, prev1a, prev1b, query_clip.reshape(tok_count, 1),

time: 163 us -> 163 us (level)
  starting transfers between devices: 50.7 us -> 46.4 us
  waiting for transfers between devices: 47.6 us -> 51.4 us
    ppermute x6, waiting for transfers between devices: 37.6 us -> 42 us  [passed_along(): lax.ppermute(value, axis, [(source, source + steps) for source in range(f...]
    ppermute x6, starting transfers between devices: 12.1 us -> 8.04 us  [within_group(): return lax.ppermute(value, axis, pairs)]
    ppermute x4 -> x3, starting transfers between devices: 11.9 us -> 10.3 us  [pair_swap(): lax.ppermute(value, axis, [(source, source + step) for source in range(st...]
  transfers between devices with their start and end apart: 16 -> 15, of which waited for: 9 -> 9; matrix products, arithmetic and copies ran while one was open for 7% -> 9% of each run, Pallas kernels for 11% -> 11%
where the time goes in v18:
time: 163 us; the launch traced here: 162 us
  waiting for transfers between devices  51.4 us (32%)
  starting transfers between devices  46.4 us (28%)
  Pallas kernels  40 us (25%)
  local copies, waits for them, and re-layouts  14.2 us (9%)
  matrix products  7.22 us (4%)
  other arithmetic  2.28 us (1%)
    ppermute x6, waiting for transfers between devices, passed_along(): lax.ppermute(value, axis, [(source, source + steps) for source in range(f...  42 us
    pallas_call x2, Pallas kernels, fine_attention(): pl.pallas_call(kernel, grid=(nq, pairs), in_specs=[pl.BlockSpec((tile, 1)...  30.8 us
    ppermute x6, starting transfers between devices, passed_along(): lax.ppermute(value, axis, [(source, source + steps) for source in range(f...  28.1 us
    ppermute x3, starting transfers between devices, pair_swap(): lax.ppermute(value, axis, [(source, source + step) for source in range(st...  10.3 us
    ppermute x6, starting transfers between devices, within_group(): return lax.ppermute(value, axis, pairs)  8.04 us
    ppermute x6, waiting for transfers between devices, within_group(): return lax.ppermute(value, axis, pairs)  8.03 us
    pallas_call x1, Pallas kernels, coarse_attention(): pl.pallas_call(kernel, grid=(heads, rows // tile), in_specs=[pl.BlockSpec...  6.8 us
    dot_general x2, matrix products, body(): jnp.einsum('rd,mdc->mrc', part_pool, part_weight, preferred_element_type=...  6.75 us
  transfers between devices with their start and end apart: 15, of which 9 were waited for; matrix products, arithmetic and copies ran while one was open for 9% of the time, Pallas kernels for 11%

profile of v18, /device:TPU:7, one launch (start us, length us, event | category | flops | bytes accessed | tf_op | source)
XLA Modules:
  0.0 161.8 jit_solution(16662077360891106295)
XLA Ops:
  0.0 1.4 collective-permute-start.1
  1.4 2.7 %fusion.16 = (bf16[2,512,512]{2,1,0:T(8,128)(2,1)}, bf16[2,512,512]{2,1,0:T(8,128)(2,1)S(1)}) fusion(bf16[3,512,1024]{2,1,0:T(8,128)(2,1)} %bitcast.54), kind=kLoop, calls=%fused_computation.46 | loop fusion | bytes 4194304 | tf_op jit(solution)/shard_map/slice | solution.py:303
  4.1 3.1 %collective-permute-start = (bf16[2,512,512]{2,1,0:T(8,128)(2,1)S(1)}, bf16[2,512,512]{2,1,0:T(8,128)(2,1)}, u32[]{:S(2)}, u32[]{:S(2)}) collective-permute-start(bf16[2,512,512]{2,1,0:T(8,128)(2,1)S(1)} %get-tuple-element.20), channel_id=1, source_target_pairs={{0,2},{1,3},{2,4},{3,5},{4,6},{5,7},{6,8},{7,9},{8,10},{9,11},{10,... | collective-permute-start | bytes 3145736 | tf_op jit(solution)/shard_map/ppermute | solution.py:24
  7.3 20.7 %collective-permute-done.k0_ref.v0_ref = bf16[2,512,512]{2,1,0:T(8,128)(2,1)} collective-permute-done((bf16[2,512,512]{2,1,0:T(8,128)(2,1)S(1)}, bf16[2,512,512]{2,1,0:T(8,128)(2,1)}, u32[]{:S(2)}, u32[]{:S(2)}) %collective-permute-start) | collective-permute-done | bytes 1048608 | tf_op jit(solution)/shard_map/ppermute | solution.py:24
  28.0 6.6 %collective-permute-start.2 = (bf16[2,512,512]{2,1,0:T(8,128)(2,1)}, bf16[2,512,512]{2,1,0:T(8,128)(2,1)}, u32[]{:S(2)}, u32[]{:S(2)}) collective-permute-start(bf16[2,512,512]{2,1,0:T(8,128)(2,1)} %collective-permute-done.k0_ref.v0_ref), channel_id=1, source_target_pairs={{1,0},{3,2},{5,4},{7,6},{9,8},{11,10},{13,12},{15,14},{17,16},{19,... | collective-permute-start | bytes 3145736 | tf_op jit(solution)/shard_map/ppermute | solution.py:173
  34.6 4.0 %collective-permute-start.3 = (bf16[2,512,512]{2,1,0:T(8,128)(2,1)}, bf16[2,512,512]{2,1,0:T(8,128)(2,1)S(1)}, u32[]{:S(2)}, u32[]{:S(2)}) collective-permute-start(bf16[2,512,512]{2,1,0:T(8,128)(2,1)} %get-tuple-element.12), channel_id=1, source_target_pairs={{0,2},{1,3},{2,4},{3,5},{4,6},{5,7},{6,8},{7,9},{8,10},{9,11},{10,... | collective-permute-start | bytes 3145736 | tf_op jit(solution)/shard_map/ppermute | solution.py:24
  40.6 15.3 %shard_map.46 = (bf16[512,512]{1,0:T(8,128)(2,1)}, bf16[128,512]{1,0:T(8,128)(2,1)}) custom-call(s32[512,1]{1,0:T(8,128)} %reshape_reshape.10.qclip_ref, s32[1,1536]{1,0:T(1,128)} %reshape_reshape.9.kclip0_ref.kclip1_ref.kclip2_ref, s32[1,1536]{1,0:T(1,128)} %reshape_reshape.9.kclip0_ref.kclip1_ref.kclip2_ref, ...), custom_call_target="tpu_custom_call" | custom-call | tf_op jit(solution)/shard_map/pallas_call | solution.py:117
  55.9 3.7 %fusion.5 = f32[3,128,1024]{2,1,0:T(8,128)} fusion(bf16[3,1024,1024]{2,1,0:T(8,128)(2,1)} %bitcast.61, bf16[128,512]{1,0:T(8,128)(2,1)} %get-tuple-element.13), kind=kOutput, calls=%fused_computation.6 | convolution fusion | flops 402653184 | bytes 4849664 | tf_op jit(solution)/shard_map/rd,mdc->mrc/dot_general | solution.py:318
  59.7 1.1 collective-permute-done.3.k0_ref.v0_ref
  60.8 2.3 %collective-permute-start.4 = (bf16[2,512,512]{2,1,0:T(8,128)(2,1)S(1)}, bf16[2,512,512]{2,1,0:T(8,128)(2,1)}, u32[]{:S(2)}, u32[]{:S(2)}) collective-permute-start(bf16[2,512,512]{2,1,0:T(8,128)(2,1)S(1)} %collective-permute-done.3.k0_ref.v0_ref), channel_id=1, source_target_pairs={{1,0},{3,2},{5,4},{7,6},{9,8},{11,10},{13,12},{15,14},{17,16},{19,... | collective-permute-start | bytes 3145736 | tf_op jit(solution)/shard_map/ppermute | solution.py:173
  63.1 1.4 collective-permute-done.4.k1b_ref.v1b_ref
  64.5 15.5 %shard_map.47 = (bf16[512,512]{1,0:T(8,128)(2,1)}, bf16[128,512]{1,0:T(8,128)(2,1)}) custom-call(s32[512,1]{1,0:T(8,128)} %reshape_reshape.10.qclip_ref, s32[1,1536]{1,0:T(1,128)} %reshape_reshape.9.kclip0_ref.kclip1_ref.kclip2_ref, s32[1,1536]{1,0:T(1,128)} %reshape_reshape.9.kclip0_ref.kclip1_ref.kclip2_ref, ...), custom_call_target="tpu_custom_call" | custom-call | tf_op jit(solution)/shard_map/pallas_call | solution.py:117
  79.9 3.0 %fusion.4 = bf16[3,128,1024]{2,1,0:T(8,128)(2,1)S(1)} fusion(f32[3,128,1024]{2,1,0:T(8,128)} %fusion.5, bf16[3,1024,1024]{2,1,0:T(8,128)(2,1)} %bitcast.62, bf16[128,512]{1,0:T(8,128)(2,1)} %get-tuple-element.16), kind=kOutput, calls=%fused_computation.5 | convolution fusion | flops 403439616 | bytes 5636096 | tf_op jit(solution)/shard_map/rd,mdc->mrc/dot_general | solution.py:318
  84.1 1.6 %collective-permute-start.7 = (bf16[3,128,256]{2,1,0:T(8,128)(2,1)S(1)}, bf16[3,128,256]{2,1,0:T(8,128)(2,1)S(1)}, u32[]{:S(2)}, u32[]{:S(2)}) collective-permute-start(bf16[3,128,256]{2,1,0:T(8,128)(2,1)S(1)} %get-tuple-element.21), channel_id=1, source_target_pairs={{0,1},{1,2},{2,3},{3,0},{4,5},{5,6},{6,7},{7,4},{8,9},{9,10},{10,1... | collective-permute-start | bytes 589832 | tf_op jit(solution)/shard_map/ppermute | solution.py:33
  85.8 5.6 %collective-permute-done.5 = bf16[3,128,256]{2,1,0:T(8,128)(2,1)S(1)} collective-permute-done((bf16[3,128,256]{2,1,0:T(8,128)(2,1)}, bf16[3,128,256]{2,1,0:T(8,128)(2,1)S(1)}, u32[]{:S(2)}, u32[]{:S(2)}) %collective-permute-start.5) | collective-permute-done | bytes 196640 | tf_op jit(solution)/shard_map/ppermute | solution.py:33
  91.4 1.4 collective-permute-done.7
  93.0 5.0 %collective-permute-start.8 = (bf16[2,512,256]{2,1,0:T(8,128)(2,1)S(1)}, bf16[2,512,256]{2,1,0:T(8,128)(2,1)S(1)}, u32[]{:S(2)}, u32[]{:S(2)}) collective-permute-start(bf16[2,512,256]{2,1,0:T(8,128)(2,1)S(1)} %bitcast.63), channel_id=1, source_target_pairs={{0,4},{1,5},{2,6},{3,7},{4,8},{5,9},{6,10},{7,11},{8,12},{9,13},{1... | collective-permute-start | bytes 1572872 | tf_op jit(solution)/shard_map/ppermute | solution.py:24
  98.1 9.7 %collective-permute-done.8.k2_ref.v2_ref = bf16[2,512,256]{2,1,0:T(8,128)(2,1)S(1)} collective-permute-done((bf16[2,512,256]{2,1,0:T(8,128)(2,1)S(1)}, bf16[2,512,256]{2,1,0:T(8,128)(2,1)S(1)}, u32[]{:S(2)}, u32[]{:S(2)}) %collective-permute-start.8) | collective-permute-done | bytes 524320 | tf_op jit(solution)/shard_map/ppermute | solution.py:24
  108.6 4.9 %collective-permute-start.9 = (bf16[2,512,256]{2,1,0:T(8,128)(2,1)S(1)}, bf16[2,512,256]{2,1,0:T(8,128)(2,1)}, u32[]{:S(2)}, u32[]{:S(2)}) collective-permute-start(bf16[2,512,256]{2,1,0:T(8,128)(2,1)S(1)} %collective-permute-done.8.k2_ref.v2_ref), channel_id=1, source_target_pairs={{0,4},{1,5},{2,6},{3,7},{4,8},{5,9},{6,10},{7,11},{8,12},{9,13},{1... | collective-permute-start | bytes 1572872 | tf_op jit(solution)/shard_map/ppermute | solution.py:24
  113.5 8.0 %collective-permute-done.9.k1_ref.v1_ref = bf16[2,512,256]{2,1,0:T(8,128)(2,1)} collective-permute-done((bf16[2,512,256]{2,1,0:T(8,128)(2,1)S(1)}, bf16[2,512,256]{2,1,0:T(8,128)(2,1)}, u32[]{:S(2)}, u32[]{:S(2)}) %collective-permute-start.9) | collective-permute-done | bytes 524320 | tf_op jit(solution)/shard_map/ppermute | solution.py:24
  121.5 5.0 %collective-permute-start.10 = (bf16[2,512,256]{2,1,0:T(8,128)(2,1)}, bf16[2,512,256]{2,1,0:T(8,128)(2,1)}, u32[]{:S(2)}, u32[]{:S(2)}) collective-permute-start(bf16[2,512,256]{2,1,0:T(8,128)(2,1)} %collective-permute-done.9.k1_ref.v1_ref), channel_id=1, source_target_pairs={{0,4},{1,5},{2,6},{3,7},{4,8},{5,9},{6,10},{7,11},{8,12},{9,13},{1... | collective-permute-start | bytes 1572872 | tf_op jit(solution)/shard_map/ppermute | solution.py:24
  128.1 1.1 constant_dynamic-update-slice_fusion.1
  129.2 1.1 constant_dynamic-update-slice_fusion.fine_ref
  131.4 2.5 %collective-permute-done.10.k0_ref.v0_ref = bf16[2,512,256]{2,1,0:T(8,128)(2,1)} collective-permute-done((bf16[2,512,256]{2,1,0:T(8,128)(2,1)}, bf16[2,512,256]{2,1,0:T(8,128)(2,1)}, u32[]{:S(2)}, u32[]{:S(2)}) %collective-permute-start.10) | collective-permute-done | bytes 524320 | tf_op jit(solution)/shard_map/ppermute | solution.py:24
  133.9 6.8 %shard_map.48 = bf16[512,256]{1,0:T(8,128)(2,1)} custom-call(s32[512,1]{1,0:T(8,128)} %copy.9.qclip_ref, s32[1,2048]{1,0:T(1,128)} %bitcast.69, s32[1,2048]{1,0:T(1,128)} %bitcast.70, s32[1,2048]{1,0:T(1,128)} %bitcast.71, s32[1,2048]{1,0:T(1,128)} %bitcast.72, bf16[512,256]{1,0:T(8,128)(2,1)} %bitcast.67, ...), custom_call_target="tpu_custom_call" | custom-call | tf_op jit(solution)/shard_map/pallas_call | solution.py:226
  140.7 0.9 constant_dynamic-slice_fusion
  141.6 4.3 %collective-permute-start.11 = (bf16[128,256]{1,0:T(8,128)(2,1)S(1)}, bf16[128,256]{1,0:T(8,128)(2,1)S(1)}, u32[]{:S(2)}, u32[]{:S(2)}) collective-permute-start(bf16[128,256]{1,0:T(8,128)(2,1)S(1)} %get-tuple-element.26), channel_id=1, source_target_pairs={{0,3},{1,0},{2,1},{3,2},{4,7},{5,4},{6,5},{7,6},{8,11},{9,8},{10,9... | collective-permute-start | bytes 196616 | tf_op jit(solution)/shard_map/ppermute | solution.py:33
  145.9 1.7 %collective-permute-start.13 = (bf16[128,256]{1,0:T(8,128)(2,1)S(1)}, bf16[128,256]{1,0:T(8,128)(2,1)S(1)}, u32[]{:S(2)}, u32[]{:S(2)}) collective-permute-start(bf16[128,256]{1,0:T(8,128)(2,1)S(1)} %get-tuple-element.24), channel_id=1, source_target_pairs={{0,1},{1,2},{2,3},{3,0},{4,5},{5,6},{6,7},{7,4},{8,9},{9,10},{10,1... | collective-permute-start | bytes 196616 | tf_op jit(solution)/shard_map/ppermute | solution.py:33
  148.5 1.1 collective-permute-done.12
  151.2 5.9 %collective-permute-start.14 = (bf16[1,1024]{1,0:T(2,128)(2,1)S(1)}, bf16[1,1024]{1,0:T(2,128)(2,1)S(1)}, u32[]{:S(2)}, u32[]{:S(2)}) collective-permute-start(bf16[1,1024]{1,0:T(2,128)(2,1)S(1)} %slice.53), channel_id=1, source_target_pairs={{0,1},{1,2},{2,3},{3,4},{4,5},{5,6},{6,7},{7,8},{8,9},{9,10},{10,1... | collective-permute-start | bytes 6152 | tf_op jit(solution)/shard_map/ppermute | solution.py:24
  158.0 2.4 %shard_map.49 = bf16[512,1024]{1,0:T(8,128)(2,1)} custom-call(bf16[512,1024]{1,0:T(8,128)(2,1)} %copy-done.3, bf16[128,1024]{1,0:T(8,128)(2,1)} %pad_select_fusion.lift_ref), custom_call_target="tpu_custom_call" | custom-call | tf_op jit(solution)/shard_map/pallas_call | solution.py:157
  160.4 1.3 fusion.12
  (57 shorter events, 10.2 us)
Async XLA Ops:
  0.0 150.7 %copy-start = (bf16[1024,1024]{1,0:T(8,128)(2,1)S(1)}, bf16[1024,1024]{1,0:T(8,128)(2,1)}, u32[]{:S(2)}) copy-start(bf16[1024,1024]{1,0:T(8,128)(2,1)} %param.7) | copy-start | bytes 6291460
  0.0 38.7 %copy-start.5 = (s32[2048]{0:T(1024)S(1)}, s32[2048]{0:T(1024)}, u32[]{:S(2)}) copy-start(s32[2048]{0:T(1024)} %param.5) | copy-start | bytes 24580
  0.0 40.6 %collective-permute-start.1 = (bf16[3,512,1024]{2,1,0:T(8,128)(2,1)}, bf16[3,512,1024]{2,1,0:T(8,128)(2,1)}, u32[]{:S(2)}, u32[]{:S(2)}) collective-permute-start(bf16[3,512,1024]{2,1,0:T(8,128)(2,1)} %bitcast.53), channel_id=1, source_target_pairs={{0,1},{2,3},{4,5},{6,7},{8,9},{10,11},{12,13},{14,15},{16,17},{18,... | collective-permute-start | bytes 9437192 | tf_op jit(solution)/shard_map/ppermute | solution.py:173
  4.1 23.9 %collective-permute-start = (bf16[2,512,512]{2,1,0:T(8,128)(2,1)S(1)}, bf16[2,512,512]{2,1,0:T(8,128)(2,1)}, u32[]{:S(2)}, u32[]{:S(2)}) collective-permute-start(bf16[2,512,512]{2,1,0:T(8,128)(2,1)S(1)} %get-tuple-element.20), channel_id=1, source_target_pairs={{0,2},{1,3},{2,4},{3,5},{4,6},{5,7},{6,8},{7,9},{8,10},{9,11},{10,... | collective-permute-start | bytes 3145736 | tf_op jit(solution)/shard_map/ppermute | solution.py:24
  28.0 12.6 %collective-permute-start.2 = (bf16[2,512,512]{2,1,0:T(8,128)(2,1)}, bf16[2,512,512]{2,1,0:T(8,128)(2,1)}, u32[]{:S(2)}, u32[]{:S(2)}) collective-permute-start(bf16[2,512,512]{2,1,0:T(8,128)(2,1)} %collective-permute-done.k0_ref.v0_ref), channel_id=1, source_target_pairs={{1,0},{3,2},{5,4},{7,6},{9,8},{11,10},{13,12},{15,14},{17,16},{19,... | collective-permute-start | bytes 3145736 | tf_op jit(solution)/shard_map/ppermute | solution.py:173
  34.6 26.2 %collective-permute-start.3 = (bf16[2,512,512]{2,1,0:T(8,128)(2,1)}, bf16[2,512,512]{2,1,0:T(8,128)(2,1)S(1)}, u32[]{:S(2)}, u32[]{:S(2)}) collective-permute-start(bf16[2,512,512]{2,1,0:T(8,128)(2,1)} %get-tuple-element.12), channel_id=1, source_target_pairs={{0,2},{1,3},{2,4},{3,5},{4,6},{5,7},{6,8},{7,9},{8,10},{9,11},{10,... | collective-permute-start | bytes 3145736 | tf_op jit(solution)/shard_map/ppermute | solution.py:24
  60.8 3.7 %copy-start.2 = (bf16[2,512,512]{2,1,0:T(8,128)(2,1)}, bf16[2,512,512]{2,1,0:T(8,128)(2,1)S(1)}, u32[]{:S(2)}) copy-start(bf16[2,512,512]{2,1,0:T(8,128)(2,1)S(1)} %collective-permute-done.3.k0_ref.v0_ref) | copy-start | bytes 3145732
  60.8 3.7 %collective-permute-start.4 = (bf16[2,512,512]{2,1,0:T(8,128)(2,1)S(1)}, bf16[2,512,512]{2,1,0:T(8,128)(2,1)}, u32[]{:S(2)}, u32[]{:S(2)}) collective-permute-start(bf16[2,512,512]{2,1,0:T(8,128)(2,1)S(1)} %collective-permute-done.3.k0_ref.v0_ref), channel_id=1, source_target_pairs={{1,0},{3,2},{5,4},{7,6},{9,8},{11,10},{13,12},{15,14},{17,16},{19,... | collective-permute-start | bytes 3145736 | tf_op jit(solution)/shard_map/ppermute | solution.py:173
  83.7 7.6 %collective-permute-start.5 = (bf16[3,128,256]{2,1,0:T(8,128)(2,1)}, bf16[3,128,256]{2,1,0:T(8,128)(2,1)S(1)}, u32[]{:S(2)}, u32[]{:S(2)}) collective-permute-start(bf16[3,128,256]{2,1,0:T(8,128)(2,1)} %get-tuple-element.23), channel_id=1, source_target_pairs={{0,3},{1,0},{2,1},{3,2},{4,7},{5,4},{6,5},{7,6},{8,11},{9,8},{10,9... | collective-permute-start | bytes 589832 | tf_op jit(solution)/shard_map/ppermute | solution.py:33
  84.1 7.2 %collective-permute-start.6 = (bf16[3,128,256]{2,1,0:T(8,128)(2,1)S(1)}, bf16[3,128,256]{2,1,0:T(8,128)(2,1)S(1)}, u32[]{:S(2)}, u32[]{:S(2)}) collective-permute-start(bf16[3,128,256]{2,1,0:T(8,128)(2,1)S(1)} %get-tuple-element.22), channel_id=1, source_target_pairs={{0,2},{1,3},{2,0},{3,1},{4,6},{5,7},{6,4},{7,5},{8,10},{9,11},{10,... | collective-permute-start | bytes 589832 | tf_op jit(solution)/shard_map/ppermute | solution.py:33
  84.1 8.6 %collective-permute-start.7 = (bf16[3,128,256]{2,1,0:T(8,128)(2,1)S(1)}, bf16[3,128,256]{2,1,0:T(8,128)(2,1)S(1)}, u32[]{:S(2)}, u32[]{:S(2)}) collective-permute-start(bf16[3,128,256]{2,1,0:T(8,128)(2,1)S(1)} %get-tuple-element.21), channel_id=1, source_target_pairs={{0,1},{1,2},{2,3},{3,0},{4,5},{5,6},{6,7},{7,4},{8,9},{9,10},{10,1... | collective-permute-start | bytes 589832 | tf_op jit(solution)/shard_map/ppermute | solution.py:33
  93.0 40.8 %copy-start.1 = (bf16[2,4,128,256]{3,2,1,0:T(8,128)(2,1)}, bf16[2,4,128,256]{3,2,1,0:T(8,128)(2,1)S(1)}, u32[]{:S(2)}) copy-start(bf16[2,4,128,256]{3,2,1,0:T(8,128)(2,1)S(1)} %copy.8) | copy-start | bytes 1572868
  93.0 14.7 %collective-permute-start.8 = (bf16[2,512,256]{2,1,0:T(8,128)(2,1)S(1)}, bf16[2,512,256]{2,1,0:T(8,128)(2,1)S(1)}, u32[]{:S(2)}, u32[]{:S(2)}) collective-permute-start(bf16[2,512,256]{2,1,0:T(8,128)(2,1)S(1)} %bitcast.63), channel_id=1, source_target_pairs={{0,4},{1,5},{2,6},{3,7},{4,8},{5,9},{6,10},{7,11},{8,12},{9,13},{1... | collective-permute-start | bytes 1572872 | tf_op jit(solution)/shard_map/ppermute | solution.py:24
  107.8 0.8 copy-start.4
  108.6 12.9 %collective-permute-start.9 = (bf16[2,512,256]{2,1,0:T(8,128)(2,1)S(1)}, bf16[2,512,256]{2,1,0:T(8,128)(2,1)}, u32[]{:S(2)}, u32[]{:S(2)}) collective-permute-start(bf16[2,512,256]{2,1,0:T(8,128)(2,1)S(1)} %collective-permute-done.8.k2_ref.v2_ref), channel_id=1, source_target_pairs={{0,4},{1,5},{2,6},{3,7},{4,8},{5,9},{6,10},{7,11},{8,12},{9,13},{1... | collective-permute-start | bytes 1572872 | tf_op jit(solution)/shard_map/ppermute | solution.py:24
  121.5 12.4 %collective-permute-start.10 = (bf16[2,512,256]{2,1,0:T(8,128)(2,1)}, bf16[2,512,256]{2,1,0:T(8,128)(2,1)}, u32[]{:S(2)}, u32[]{:S(2)}) collective-permute-start(bf16[2,512,256]{2,1,0:T(8,128)(2,1)} %collective-permute-done.9.k1_ref.v1_ref), channel_id=1, source_target_pairs={{0,4},{1,5},{2,6},{3,7},{4,8},{5,9},{6,10},{7,11},{8,12},{9,13},{1... | collective-permute-start | bytes 1572872 | tf_op jit(solution)/shard_map/ppermute | solution.py:24
  130.3 1.1 copy-start.3
  141.6 6.9 %collective-permute-start.11 = (bf16[128,256]{1,0:T(8,128)(2,1)S(1)}, bf16[128,256]{1,0:T(8,128)(2,1)S(1)}, u32[]{:S(2)}, u32[]{:S(2)}) collective-permute-start(bf16[128,256]{1,0:T(8,128)(2,1)S(1)} %get-tuple-element.26), channel_id=1, source_target_pairs={{0,3},{1,0},{2,1},{3,2},{4,7},{5,4},{6,5},{7,6},{8,11},{9,8},{10,9... | collective-permute-start | bytes 196616 | tf_op jit(solution)/shard_map/ppermute | solution.py:33
  145.9 3.7 %collective-permute-start.12 = (bf16[128,256]{1,0:T(8,128)(2,1)S(1)}, bf16[128,256]{1,0:T(8,128)(2,1)S(1)}, u32[]{:S(2)}, u32[]{:S(2)}) collective-permute-start(bf16[128,256]{1,0:T(8,128)(2,1)S(1)} %get-tuple-element.25), channel_id=1, source_target_pairs={{0,2},{1,3},{2,0},{3,1},{4,6},{5,7},{6,4},{7,5},{8,10},{9,11},{10,... | collective-permute-start | bytes 196616 | tf_op jit(solution)/shard_map/ppermute | solution.py:33
  145.9 3.7 %collective-permute-start.13 = (bf16[128,256]{1,0:T(8,128)(2,1)S(1)}, bf16[128,256]{1,0:T(8,128)(2,1)S(1)}, u32[]{:S(2)}, u32[]{:S(2)}) collective-permute-start(bf16[128,256]{1,0:T(8,128)(2,1)S(1)} %get-tuple-element.24), channel_id=1, source_target_pairs={{0,1},{1,2},{2,3},{3,0},{4,5},{5,6},{6,7},{7,4},{8,9},{9,10},{10,1... | collective-permute-start | bytes 196616 | tf_op jit(solution)/shard_map/ppermute | solution.py:33
  151.2 9.2 %collective-permute-start.14 = (bf16[1,1024]{1,0:T(2,128)(2,1)S(1)}, bf16[1,1024]{1,0:T(2,128)(2,1)S(1)}, u32[]{:S(2)}, u32[]{:S(2)}) collective-permute-start(bf16[1,1024]{1,0:T(2,128)(2,1)S(1)} %slice.53), channel_id=1, source_target_pairs={{0,1},{1,2},{2,3},{3,4},{4,5},{5,6},{6,7},{7,8},{8,9},{9,10},{10,1... | collective-permute-start | bytes 6152 | tf_op jit(solution)/shard_map/ppermute | solution.py:24

commit v19 on v18

--- a/solution.py
+++ b/solution.py
@@ -141,17 +141,18 @@
       planes, planes)
 
 
-def mix_kernel(fine_ref, lift_ref, out_ref):
+def mix_kernel(fine_ref, up_ref, join_ref, out_ref):
     tile = fine_ref.shape[0]
-    rows = lift_ref.shape[0]
-    spread_row = lax.broadcasted_iota(jnp.int32, (tile, rows), 0)
+    rows = up_ref.shape[0]
+    fine_row = pl.program_id(0) * tile + lax.broadcasted_iota(jnp.int32, (tile, rows), 0)
     spread_col = lax.broadcasted_iota(jnp.int32, (tile, rows), 1)
-    spread = jnp.where(spread_row // POOL == spread_col, 1.0, 0.0).astype(jnp.bfloat16)
-    lifted = jnp.dot(spread, lift_ref[...], preferred_element_type=jnp.float32)
+    hit = (spread_col == fine_row // POOL - 1) & (join_ref[...] != 0)
+    spread = jnp.where(hit, 1.0, 0.0).astype(jnp.bfloat16)
+    lifted = jnp.dot(spread, up_ref[...], preferred_element_type=jnp.float32)
     out_ref[...] = (fine_ref[...].astype(jnp.float32) + lifted).astype(out_ref.dtype)
 
 
-def mix(fine_out, lifted):
+def mix(fine_out, coarse_up, join_rows):
     tok, width = fine_out.shape
     tile = min(FINE_TILE, tok)
     return pl.pallas_call(
@@ -159,11 +160,36 @@
         grid=(tok // tile,),
         in_specs=[
             pl.BlockSpec((tile, width), lambda i: (i, 0)),
-            pl.BlockSpec((tile // POOL, width), lambda i: (i, 0)),
+            pl.BlockSpec(coarse_up.shape, lambda i: (0, 0)),
+            pl.BlockSpec((tile, 1), lambda i: (i, 0)),
         ],
         out_specs=pl.BlockSpec((tile, width), lambda i: (i, 0)),
         out_shape=jax.ShapeDtypeStruct((tok, width), fine_out.dtype),
-    )(fine_out, lifted)
+    )(fine_out, coarse_up, join_rows)
+
+
+def patch_kernel(mixed_ref, fine_ref, lift_ref, out_ref):
+    rows = out_ref.shape[0]
+    row = lax.broadcasted_iota(jnp.int32, (rows, 1), 0)
+    head = (fine_ref[...].astype(jnp.float32) + lift_ref[...].astype(jnp.float32)).astype(out_ref.dtype)
+    out_ref[...] = jnp.where(row < POOL, head, mixed_ref[...])
+
+
+def patch(mixed, fine_out, head_lift):
+    width = mixed.shape[1]
+    rows = 16
+    return pl.pallas_call(
+        patch_kernel,
+        grid=(1,),
+        in_specs=[
+            pl.BlockSpec((rows, width), lambda i: (0, 0)),
+            pl.BlockSpec((rows, width), lambda i: (0, 0)),
+            pl.BlockSpec((1, width), lambda i: (0, 0)),
+        ],
+        out_specs=pl.BlockSpec((rows, width), lambda i: (0, 0)),
+        out_shape=jax.ShapeDtypeStruct(mixed.shape, mixed.dtype),
+        input_output_aliases={0: 0},
+    )(mixed, fine_out, head_lift)
 
 
 def pair_swap(value, axis, from_odd):
@@ -356,15 +382,13 @@
     )
     coarse_up = jnp.dot(att_rows, w_out, preferred_element_type=jnp.float32).astype(jnp.bfloat16)
     carried = passed_along(coarse_up[-1:], "seq", 1)
-    previous = jnp.concatenate([jnp.zeros_like(carried), coarse_up[:-1]], axis=0)
     clip_before = jnp.concatenate([jnp.full((1,), -1, jnp.int32), clip_ids])
     prev_clip = lax.dynamic_slice_in_dim(clip_before, position * coarse_rows, coarse_rows, 0)
     joined = prev_clip == own_clip
-    lifted = jnp.where(joined[:, None], previous, jnp.zeros_like(previous))
-    mixed = mix(fine_out, lifted)
-    head_lift = jnp.where(joined[:1, None], carried, jnp.zeros_like(carried)).astype(jnp.float32)
-    head_rows = (fine_out[:POOL].astype(jnp.float32) + head_lift).astype(mixed.dtype)
-    return lax.dynamic_update_slice(mixed, head_rows, (0, 0))
+    join_rows = jnp.repeat(joined.astype(jnp.int32), POOL).reshape(tok_count, 1)
+    mixed = mix(fine_out, coarse_up, join_rows)
+    head_lift = jnp.where(joined[:1, None], carried, jnp.zeros_like(carried))
+    return patch(mixed, fine_out, head_lift)
 
 
 def solution(mesh):

time: 163 us -> 166 us (1.018)
  local copies, waits for them, and re-layouts: 14.2 us -> 16.4 us
  Pallas kernels: 40 us -> 41.8 us
    unnamed x27 -> x33, local copies, waits for them, and re-layouts: 4.11 us -> 4.86 us
where the time goes in v19:
time: 166 us; the launch traced here: 165 us
  waiting for transfers between devices  51 us (31%)
  starting transfers between devices  46.4 us (28%)
  Pallas kernels  41.8 us (25%)
  local copies, waits for them, and re-layouts  16.4 us (10%)
  matrix products  8.23 us (5%)
    ppermute x6, waiting for transfers between devices, passed_along(): lax.ppermute(value, axis, [(source, source + steps) for source in range(f...  41.6 us
    pallas_call x2, Pallas kernels, fine_attention(): pl.pallas_call(kernel, grid=(nq, pairs), in_specs=[pl.BlockSpec((tile, 1)...  30.7 us
    ppermute x6, starting transfers between devices, passed_along(): lax.ppermute(value, axis, [(source, source + steps) for source in range(f...  28.1 us
    ppermute x3, starting transfers between devices, pair_swap(): lax.ppermute(value, axis, [(source, source + step) for source in range(st...  10.3 us
    ppermute x6, starting transfers between devices, within_group(): return lax.ppermute(value, axis, pairs)  8.04 us
    ppermute x6, waiting for transfers between devices, within_group(): return lax.ppermute(value, axis, pairs)  8.03 us
    pallas_call x1, Pallas kernels, coarse_attention(): pl.pallas_call(kernel, grid=(heads, rows // tile), in_specs=[pl.BlockSpec...  6.8 us
    dot_general x2, matrix products, body(): jnp.einsum('rd,mdc->mrc', part_pool, part_weight, preferred_element_type=...  6.75 us
  transfers between devices with their start and end apart: 15, of which 9 were waited for; matrix products, arithmetic and copies ran while one was open for 9% of the time, Pallas kernels for 11%

profile of v19, /device:TPU:7, one launch (start us, length us, event | category | flops | bytes accessed | tf_op | source)
XLA Modules:
  0.0 164.8 jit_solution(3775909492439467846)
XLA Ops:
  0.0 1.4 collective-permute-start.1
  1.4 2.7 %fusion.16 = (bf16[2,512,512]{2,1,0:T(8,128)(2,1)}, bf16[2,512,512]{2,1,0:T(8,128)(2,1)S(1)}) fusion(bf16[3,512,1024]{2,1,0:T(8,128)(2,1)} %bitcast.52), kind=kLoop, calls=%fused_computation.43 | loop fusion | bytes 4194304 | tf_op jit(solution)/shard_map/slice | solution.py:329
  4.1 3.1 %collective-permute-start = (bf16[2,512,512]{2,1,0:T(8,128)(2,1)S(1)}, bf16[2,512,512]{2,1,0:T(8,128)(2,1)}, u32[]{:S(2)}, u32[]{:S(2)}) collective-permute-start(bf16[2,512,512]{2,1,0:T(8,128)(2,1)S(1)} %get-tuple-element.21), channel_id=1, source_target_pairs={{0,2},{1,3},{2,4},{3,5},{4,6},{5,7},{6,8},{7,9},{8,10},{9,11},{10,... | collective-permute-start | bytes 3145736 | tf_op jit(solution)/shard_map/ppermute | solution.py:24
  7.3 20.7 %collective-permute-done.k0_ref.v0_ref = bf16[2,512,512]{2,1,0:T(8,128)(2,1)} collective-permute-done((bf16[2,512,512]{2,1,0:T(8,128)(2,1)S(1)}, bf16[2,512,512]{2,1,0:T(8,128)(2,1)}, u32[]{:S(2)}, u32[]{:S(2)}) %collective-permute-start) | collective-permute-done | bytes 1048608 | tf_op jit(solution)/shard_map/ppermute | solution.py:24
  28.0 6.6 %collective-permute-start.2 = (bf16[2,512,512]{2,1,0:T(8,128)(2,1)}, bf16[2,512,512]{2,1,0:T(8,128)(2,1)}, u32[]{:S(2)}, u32[]{:S(2)}) collective-permute-start(bf16[2,512,512]{2,1,0:T(8,128)(2,1)} %collective-permute-done.k0_ref.v0_ref), channel_id=1, source_target_pairs={{1,0},{3,2},{5,4},{7,6},{9,8},{11,10},{13,12},{15,14},{17,16},{19,... | collective-permute-start | bytes 3145736 | tf_op jit(solution)/shard_map/ppermute | solution.py:199
  34.6 4.0 %collective-permute-start.3 = (bf16[2,512,512]{2,1,0:T(8,128)(2,1)}, bf16[2,512,512]{2,1,0:T(8,128)(2,1)S(1)}, u32[]{:S(2)}, u32[]{:S(2)}) collective-permute-start(bf16[2,512,512]{2,1,0:T(8,128)(2,1)} %get-tuple-element.12), channel_id=1, source_target_pairs={{0,2},{1,3},{2,4},{3,5},{4,6},{5,7},{6,8},{7,9},{8,10},{9,11},{10,... | collective-permute-start | bytes 3145736 | tf_op jit(solution)/shard_map/ppermute | solution.py:24
  40.6 15.3 %shard_map.46 = (bf16[512,512]{1,0:T(8,128)(2,1)}, bf16[128,512]{1,0:T(8,128)(2,1)}) custom-call(s32[512,1]{1,0:T(8,128)} %reshape_reshape.15.qclip_ref, s32[1,1536]{1,0:T(1,128)} %reshape_reshape.12.kclip0_ref.kclip1_ref.kclip2_ref, s32[1,1536]{1,0:T(1,128)} %reshape_reshape.12.kclip0_ref.kclip1_ref.kclip2_ref, ...), custom_call_target="tpu_custom_call" | custom-call | tf_op jit(solution)/shard_map/pallas_call | solution.py:117
  55.9 3.7 %fusion.5 = f32[3,128,1024]{2,1,0:T(8,128)} fusion(bf16[3,1024,1024]{2,1,0:T(8,128)(2,1)} %bitcast.59, bf16[128,512]{1,0:T(8,128)(2,1)} %get-tuple-element.13), kind=kOutput, calls=%fused_computation.6 | convolution fusion | flops 402653184 | bytes 4849664 | tf_op jit(solution)/shard_map/rd,mdc->mrc/dot_general | solution.py:344
  59.7 1.1 collective-permute-done.3.k0_ref.v0_ref
  60.8 2.3 %collective-permute-start.4 = (bf16[2,512,512]{2,1,0:T(8,128)(2,1)S(1)}, bf16[2,512,512]{2,1,0:T(8,128)(2,1)}, u32[]{:S(2)}, u32[]{:S(2)}) collective-permute-start(bf16[2,512,512]{2,1,0:T(8,128)(2,1)S(1)} %collective-permute-done.3.k0_ref.v0_ref), channel_id=1, source_target_pairs={{1,0},{3,2},{5,4},{7,6},{9,8},{11,10},{13,12},{15,14},{17,16},{19,... | collective-permute-start | bytes 3145736 | tf_op jit(solution)/shard_map/ppermute | solution.py:199
  63.1 1.4 collective-permute-done.4.k1b_ref.v1b_ref
  64.5 15.4 %shard_map.47 = (bf16[512,512]{1,0:T(8,128)(2,1)}, bf16[128,512]{1,0:T(8,128)(2,1)}) custom-call(s32[512,1]{1,0:T(8,128)} %reshape_reshape.15.qclip_ref, s32[1,1536]{1,0:T(1,128)} %reshape_reshape.12.kclip0_ref.kclip1_ref.kclip2_ref, s32[1,1536]{1,0:T(1,128)} %reshape_reshape.12.kclip0_ref.kclip1_ref.kclip2_ref, ...), custom_call_target="tpu_custom_call" | custom-call | tf_op jit(solution)/shard_map/pallas_call | solution.py:117
  79.9 3.0 %fusion.4 = bf16[3,128,1024]{2,1,0:T(8,128)(2,1)S(1)} fusion(f32[3,128,1024]{2,1,0:T(8,128)} %fusion.5, bf16[3,1024,1024]{2,1,0:T(8,128)(2,1)} %bitcast.60, bf16[128,512]{1,0:T(8,128)(2,1)} %get-tuple-element.16), kind=kOutput, calls=%fused_computation.5 | convolution fusion | flops 403439616 | bytes 5636096 | tf_op jit(solution)/shard_map/rd,mdc->mrc/dot_general | solution.py:344
  84.1 1.6 collective-permute-start.7
  85.7 5.6 %collective-permute-done.5 = bf16[3,128,256]{2,1,0:T(8,128)(2,1)S(1)} collective-permute-done((bf16[3,128,256]{2,1,0:T(8,128)(2,1)}, bf16[3,128,256]{2,1,0:T(8,128)(2,1)S(1)}, u32[]{:S(2)}, u32[]{:S(2)}) %collective-permute-start.5) | collective-permute-done | bytes 196640 | tf_op jit(solution)/shard_map/ppermute | solution.py:33
  91.3 1.4 collective-permute-done.7
  93.9 5.0 %collective-permute-start.8 = (bf16[2,512,256]{2,1,0:T(8,128)(2,1)S(1)}, bf16[2,512,256]{2,1,0:T(8,128)(2,1)S(1)}, u32[]{:S(2)}, u32[]{:S(2)}) collective-permute-start(bf16[2,512,256]{2,1,0:T(8,128)(2,1)S(1)} %bitcast.61), channel_id=1, source_target_pairs={{0,4},{1,5},{2,6},{3,7},{4,8},{5,9},{6,10},{7,11},{8,12},{9,13},{1... | collective-permute-start | bytes 1572872 | tf_op jit(solution)/shard_map/ppermute | solution.py:24
  98.9 9.7 %collective-permute-done.8.k2_ref.v2_ref = bf16[2,512,256]{2,1,0:T(8,128)(2,1)S(1)} collective-permute-done((bf16[2,512,256]{2,1,0:T(8,128)(2,1)S(1)}, bf16[2,512,256]{2,1,0:T(8,128)(2,1)S(1)}, u32[]{:S(2)}, u32[]{:S(2)}) %collective-permute-start.8) | collective-permute-done | bytes 524320 | tf_op jit(solution)/shard_map/ppermute | solution.py:24
  108.6 4.9 %collective-permute-start.9 = (bf16[2,512,256]{2,1,0:T(8,128)(2,1)S(1)}, bf16[2,512,256]{2,1,0:T(8,128)(2,1)}, u32[]{:S(2)}, u32[]{:S(2)}) collective-permute-start(bf16[2,512,256]{2,1,0:T(8,128)(2,1)S(1)} %collective-permute-done.8.k2_ref.v2_ref), channel_id=1, source_target_pairs={{0,4},{1,5},{2,6},{3,7},{4,8},{5,9},{6,10},{7,11},{8,12},{9,13},{1... | collective-permute-start | bytes 1572872 | tf_op jit(solution)/shard_map/ppermute | solution.py:24
  113.5 8.0 %collective-permute-done.9.k1_ref.v1_ref = bf16[2,512,256]{2,1,0:T(8,128)(2,1)} collective-permute-done((bf16[2,512,256]{2,1,0:T(8,128)(2,1)S(1)}, bf16[2,512,256]{2,1,0:T(8,128)(2,1)}, u32[]{:S(2)}, u32[]{:S(2)}) %collective-permute-start.9) | collective-permute-done | bytes 524320 | tf_op jit(solution)/shard_map/ppermute | solution.py:24
  121.5 5.0 %collective-permute-start.10 = (bf16[2,512,256]{2,1,0:T(8,128)(2,1)}, bf16[2,512,256]{2,1,0:T(8,128)(2,1)}, u32[]{:S(2)}, u32[]{:S(2)}) collective-permute-start(bf16[2,512,256]{2,1,0:T(8,128)(2,1)} %collective-permute-done.9.k1_ref.v1_ref), channel_id=1, source_target_pairs={{0,4},{1,5},{2,6},{3,7},{4,8},{5,9},{6,10},{7,11},{8,12},{9,13},{1... | collective-permute-start | bytes 1572872 | tf_op jit(solution)/shard_map/ppermute | solution.py:24
  129.1 1.1 constant_dynamic-update-slice_fusion.1
  130.2 1.7 %slice.41 = bf16[1,4,128,256]{3,2,0,1:T(8,128)(2,1)} slice(bf16[3,4,128,256]{3,2,0,1:T(8,128)(2,1)} %copy-done.4), slice={[0:1], [0:4], [0:128], [0:256]} | slice | bytes 524288 | tf_op jit(solution)/shard_map/slice | solution.py:359
  131.9 2.1 %collective-permute-done.10.k0_ref.v0_ref = bf16[2,512,256]{2,1,0:T(8,128)(2,1)} collective-permute-done((bf16[2,512,256]{2,1,0:T(8,128)(2,1)}, bf16[2,512,256]{2,1,0:T(8,128)(2,1)}, u32[]{:S(2)}, u32[]{:S(2)}) %collective-permute-start.10) | collective-permute-done | bytes 524320 | tf_op jit(solution)/shard_map/ppermute | solution.py:24
  133.9 6.8 %shard_map.48 = bf16[512,256]{1,0:T(8,128)(2,1)} custom-call(s32[512,1]{1,0:T(8,128)} %copy.10.qclip_ref, s32[1,2048]{1,0:T(1,128)} %bitcast.66, s32[1,2048]{1,0:T(1,128)} %bitcast.67, s32[1,2048]{1,0:T(1,128)} %bitcast.68, s32[1,2048]{1,0:T(1,128)} %bitcast.69, bf16[512,256]{1,0:T(8,128)(2,1)} %bitcast.64, ...), custom_call_target="tpu_custom_call" | custom-call | tf_op jit(solution)/shard_map/pallas_call | solution.py:252
  141.7 4.3 %collective-permute-start.11 = (bf16[128,256]{1,0:T(8,128)(2,1)S(1)}, bf16[128,256]{1,0:T(8,128)(2,1)S(1)}, u32[]{:S(2)}, u32[]{:S(2)}) collective-permute-start(bf16[128,256]{1,0:T(8,128)(2,1)S(1)} %get-tuple-element.27), channel_id=1, source_target_pairs={{0,3},{1,0},{2,1},{3,2},{4,7},{5,4},{6,5},{7,6},{8,11},{9,8},{10,9... | collective-permute-start | bytes 196616 | tf_op jit(solution)/shard_map/ppermute | solution.py:33
  146.0 1.7 %collective-permute-start.13 = (bf16[128,256]{1,0:T(8,128)(2,1)S(1)}, bf16[128,256]{1,0:T(8,128)(2,1)S(1)}, u32[]{:S(2)}, u32[]{:S(2)}) collective-permute-start(bf16[128,256]{1,0:T(8,128)(2,1)S(1)} %get-tuple-element.25), channel_id=1, source_target_pairs={{0,1},{1,2},{2,3},{3,0},{4,5},{5,6},{6,7},{7,4},{8,9},{9,10},{10,1... | collective-permute-start | bytes 196616 | tf_op jit(solution)/shard_map/ppermute | solution.py:33
  148.5 1.1 collective-permute-done.12
  151.4 1.5 convolution_convert_fusion.up_ref
  152.9 5.9 %collective-permute-start.14 = (bf16[1,1024]{1,0:T(2,128)(2,1)S(1)}, bf16[1,1024]{1,0:T(2,128)(2,1)S(1)}, u32[]{:S(2)}, u32[]{:S(2)}) collective-permute-start(bf16[1,1024]{1,0:T(2,128)(2,1)S(1)} %slice.43), channel_id=1, source_target_pairs={{0,1},{1,2},{2,3},{3,4},{4,5},{5,6},{6,7},{7,8},{8,9},{9,10},{10,1... | collective-permute-start | bytes 6152 | tf_op jit(solution)/shard_map/ppermute | solution.py:24
  160.0 2.8 %shard_map.49.mixed_ref = bf16[512,1024]{1,0:T(8,128)(2,1)} custom-call(bf16[512,1024]{1,0:T(8,128)(2,1)} %copy-done.1, bf16[128,1024]{1,0:T(8,128)(2,1)} %copy-done.6, s32[512,1]{1,0:T(8,128)} %reshape_reshape.14.join_ref), custom_call_target="tpu_custom_call" | custom-call | tf_op jit(solution)/shard_map/pallas_call | solution.py:158
  163.4 1.4 shard_map.50
  (64 shorter events, 12.1 us)
Async XLA Ops:
  0.0 151.4 %copy-start = (bf16[1024,1024]{1,0:T(8,128)(2,1)S(1)}, bf16[1024,1024]{1,0:T(8,128)(2,1)}, u32[]{:S(2)}) copy-start(bf16[1024,1024]{1,0:T(8,128)(2,1)} %param.7) | copy-start | bytes 6291460
  0.0 38.7 %copy-start.8 = (s32[2048]{0:T(1024)S(1)}, s32[2048]{0:T(1024)}, u32[]{:S(2)}) copy-start(s32[2048]{0:T(1024)} %param.5) | copy-start | bytes 24580
  0.0 40.6 %collective-permute-start.1 = (bf16[3,512,1024]{2,1,0:T(8,128)(2,1)}, bf16[3,512,1024]{2,1,0:T(8,128)(2,1)}, u32[]{:S(2)}, u32[]{:S(2)}) collective-permute-start(bf16[3,512,1024]{2,1,0:T(8,128)(2,1)} %bitcast.51), channel_id=1, source_target_pairs={{0,1},{2,3},{4,5},{6,7},{8,9},{10,11},{12,13},{14,15},{16,17},{18,... | collective-permute-start | bytes 9437192 | tf_op jit(solution)/shard_map/ppermute | solution.py:199
  4.1 23.9 %collective-permute-start = (bf16[2,512,512]{2,1,0:T(8,128)(2,1)S(1)}, bf16[2,512,512]{2,1,0:T(8,128)(2,1)}, u32[]{:S(2)}, u32[]{:S(2)}) collective-permute-start(bf16[2,512,512]{2,1,0:T(8,128)(2,1)S(1)} %get-tuple-element.21), channel_id=1, source_target_pairs={{0,2},{1,3},{2,4},{3,5},{4,6},{5,7},{6,8},{7,9},{8,10},{9,11},{10,... | collective-permute-start | bytes 3145736 | tf_op jit(solution)/shard_map/ppermute | solution.py:24
  28.0 12.6 %collective-permute-start.2 = (bf16[2,512,512]{2,1,0:T(8,128)(2,1)}, bf16[2,512,512]{2,1,0:T(8,128)(2,1)}, u32[]{:S(2)}, u32[]{:S(2)}) collective-permute-start(bf16[2,512,512]{2,1,0:T(8,128)(2,1)} %collective-permute-done.k0_ref.v0_ref), channel_id=1, source_target_pairs={{1,0},{3,2},{5,4},{7,6},{9,8},{11,10},{13,12},{15,14},{17,16},{19,... | collective-permute-start | bytes 3145736 | tf_op jit(solution)/shard_map/ppermute | solution.py:199
  34.6 26.2 %collective-permute-start.3 = (bf16[2,512,512]{2,1,0:T(8,128)(2,1)}, bf16[2,512,512]{2,1,0:T(8,128)(2,1)S(1)}, u32[]{:S(2)}, u32[]{:S(2)}) collective-permute-start(bf16[2,512,512]{2,1,0:T(8,128)(2,1)} %get-tuple-element.12), channel_id=1, source_target_pairs={{0,2},{1,3},{2,4},{3,5},{4,6},{5,7},{6,8},{7,9},{8,10},{9,11},{10,... | collective-permute-start | bytes 3145736 | tf_op jit(solution)/shard_map/ppermute | solution.py:24
  60.8 3.7 %copy-start.3 = (bf16[2,512,512]{2,1,0:T(8,128)(2,1)}, bf16[2,512,512]{2,1,0:T(8,128)(2,1)S(1)}, u32[]{:S(2)}) copy-start(bf16[2,512,512]{2,1,0:T(8,128)(2,1)S(1)} %collective-permute-done.3.k0_ref.v0_ref) | copy-start | bytes 3145732
  60.8 3.7 %collective-permute-start.4 = (bf16[2,512,512]{2,1,0:T(8,128)(2,1)S(1)}, bf16[2,512,512]{2,1,0:T(8,128)(2,1)}, u32[]{:S(2)}, u32[]{:S(2)}) collective-permute-start(bf16[2,512,512]{2,1,0:T(8,128)(2,1)S(1)} %collective-permute-done.3.k0_ref.v0_ref), channel_id=1, source_target_pairs={{1,0},{3,2},{5,4},{7,6},{9,8},{11,10},{13,12},{15,14},{17,16},{19,... | collective-permute-start | bytes 3145736 | tf_op jit(solution)/shard_map/ppermute | solution.py:199
  83.7 7.6 %collective-permute-start.5 = (bf16[3,128,256]{2,1,0:T(8,128)(2,1)}, bf16[3,128,256]{2,1,0:T(8,128)(2,1)S(1)}, u32[]{:S(2)}, u32[]{:S(2)}) collective-permute-start(bf16[3,128,256]{2,1,0:T(8,128)(2,1)} %get-tuple-element.24), channel_id=1, source_target_pairs={{0,3},{1,0},{2,1},{3,2},{4,7},{5,4},{6,5},{7,6},{8,11},{9,8},{10,9... | collective-permute-start | bytes 589832 | tf_op jit(solution)/shard_map/ppermute | solution.py:33
  84.1 7.2 %collective-permute-start.6 = (bf16[3,128,256]{2,1,0:T(8,128)(2,1)S(1)}, bf16[3,128,256]{2,1,0:T(8,128)(2,1)S(1)}, u32[]{:S(2)}, u32[]{:S(2)}) collective-permute-start(bf16[3,128,256]{2,1,0:T(8,128)(2,1)S(1)} %get-tuple-element.23), channel_id=1, source_target_pairs={{0,2},{1,3},{2,0},{3,1},{4,6},{5,7},{6,4},{7,5},{8,10},{9,11},{10,... | collective-permute-start | bytes 589832 | tf_op jit(solution)/shard_map/ppermute | solution.py:33
  84.1 8.6 %collective-permute-start.7 = (bf16[3,128,256]{2,1,0:T(8,128)(2,1)S(1)}, bf16[3,128,256]{2,1,0:T(8,128)(2,1)S(1)}, u32[]{:S(2)}, u32[]{:S(2)}) collective-permute-start(bf16[3,128,256]{2,1,0:T(8,128)(2,1)S(1)} %get-tuple-element.22), channel_id=1, source_target_pairs={{0,1},{1,2},{2,3},{3,0},{4,5},{5,6},{6,7},{7,4},{8,9},{9,10},{10,1... | collective-permute-start | bytes 589832 | tf_op jit(solution)/shard_map/ppermute | solution.py:33
  92.9 15.7 %copy-start.4 = (bf16[3,4,128,256]{3,2,0,1:T(8,128)(2,1)}, bf16[3,4,128,256]{3,2,0,1:T(8,128)(2,1)S(1)}, u32[]{:S(2)}) copy-start(bf16[3,4,128,256]{3,2,0,1:T(8,128)(2,1)S(1)} %dynamic-slice_bitcast_fusion) | copy-start | bytes 2359300
  93.0 0.9 copy-start.2
  93.9 14.7 %collective-permute-start.8 = (bf16[2,512,256]{2,1,0:T(8,128)(2,1)S(1)}, bf16[2,512,256]{2,1,0:T(8,128)(2,1)S(1)}, u32[]{:S(2)}, u32[]{:S(2)}) collective-permute-start(bf16[2,512,256]{2,1,0:T(8,128)(2,1)S(1)} %bitcast.61), channel_id=1, source_target_pairs={{0,4},{1,5},{2,6},{3,7},{4,8},{5,9},{6,10},{7,11},{8,12},{9,13},{1... | collective-permute-start | bytes 1572872 | tf_op jit(solution)/shard_map/ppermute | solution.py:24
  108.6 4.9 %copy-start.5 = (bf16[2,512,256]{2,1,0:T(8,128)(2,1)}, bf16[2,512,256]{2,1,0:T(8,128)(2,1)S(1)}, u32[]{:S(2)}) copy-start(bf16[2,512,256]{2,1,0:T(8,128)(2,1)S(1)} %collective-permute-done.8.k2_ref.v2_ref) | copy-start | bytes 1572868
  108.6 12.9 %collective-permute-start.9 = (bf16[2,512,256]{2,1,0:T(8,128)(2,1)S(1)}, bf16[2,512,256]{2,1,0:T(8,128)(2,1)}, u32[]{:S(2)}, u32[]{:S(2)}) collective-permute-start(bf16[2,512,256]{2,1,0:T(8,128)(2,1)S(1)} %collective-permute-done.8.k2_ref.v2_ref), channel_id=1, source_target_pairs={{0,4},{1,5},{2,6},{3,7},{4,8},{5,9},{6,10},{7,11},{8,12},{9,13},{1... | collective-permute-start | bytes 1572872 | tf_op jit(solution)/shard_map/ppermute | solution.py:24
  121.5 12.4 %collective-permute-start.10 = (bf16[2,512,256]{2,1,0:T(8,128)(2,1)}, bf16[2,512,256]{2,1,0:T(8,128)(2,1)}, u32[]{:S(2)}, u32[]{:S(2)}) collective-permute-start(bf16[2,512,256]{2,1,0:T(8,128)(2,1)} %collective-permute-done.9.k1_ref.v1_ref), channel_id=1, source_target_pairs={{0,4},{1,5},{2,6},{3,7},{4,8},{5,9},{6,10},{7,11},{8,12},{9,13},{1... | collective-permute-start | bytes 1572872 | tf_op jit(solution)/shard_map/ppermute | solution.py:24
  141.7 6.9 %collective-permute-start.11 = (bf16[128,256]{1,0:T(8,128)(2,1)S(1)}, bf16[128,256]{1,0:T(8,128)(2,1)S(1)}, u32[]{:S(2)}, u32[]{:S(2)}) collective-permute-start(bf16[128,256]{1,0:T(8,128)(2,1)S(1)} %get-tuple-element.27), channel_id=1, source_target_pairs={{0,3},{1,0},{2,1},{3,2},{4,7},{5,4},{6,5},{7,6},{8,11},{9,8},{10,9... | collective-permute-start | bytes 196616 | tf_op jit(solution)/shard_map/ppermute | solution.py:33
  146.0 3.7 %collective-permute-start.12 = (bf16[128,256]{1,0:T(8,128)(2,1)S(1)}, bf16[128,256]{1,0:T(8,128)(2,1)S(1)}, u32[]{:S(2)}, u32[]{:S(2)}) collective-permute-start(bf16[128,256]{1,0:T(8,128)(2,1)S(1)} %get-tuple-element.26), channel_id=1, source_target_pairs={{0,2},{1,3},{2,0},{3,1},{4,6},{5,7},{6,4},{7,5},{8,10},{9,11},{10,... | collective-permute-start | bytes 196616 | tf_op jit(solution)/shard_map/ppermute | solution.py:33
  146.0 3.7 %collective-permute-start.13 = (bf16[128,256]{1,0:T(8,128)(2,1)S(1)}, bf16[128,256]{1,0:T(8,128)(2,1)S(1)}, u32[]{:S(2)}, u32[]{:S(2)}) collective-permute-start(bf16[128,256]{1,0:T(8,128)(2,1)S(1)} %get-tuple-element.25), channel_id=1, source_target_pairs={{0,1},{1,2},{2,3},{3,0},{4,5},{5,6},{6,7},{7,4},{8,9},{9,10},{10,1... | collective-permute-start | bytes 196616 | tf_op jit(solution)/shard_map/ppermute | solution.py:33
  151.4 7.5 %copy-start.7 = (bf16[512,512]{1,0:T(8,128)(2,1)S(1)}, bf16[512,512]{1,0:T(8,128)(2,1)}, u32[]{:S(2)}) copy-start(bf16[512,512]{1,0:T(8,128)(2,1)} %get-tuple-element.15) | copy-start | bytes 1572868
  152.9 6.0 %copy-start.6 = (bf16[128,1024]{1,0:T(8,128)(2,1)}, bf16[128,1024]{1,0:T(8,128)(2,1)S(1)}, u32[]{:S(2)}) copy-start(bf16[128,1024]{1,0:T(8,128)(2,1)S(1)} %convolution_convert_fusion.up_ref) | copy-start | bytes 786436
  152.9 9.8 %collective-permute-start.14 = (bf16[1,1024]{1,0:T(2,128)(2,1)S(1)}, bf16[1,1024]{1,0:T(2,128)(2,1)S(1)}, u32[]{:S(2)}, u32[]{:S(2)}) collective-permute-start(bf16[1,1024]{1,0:T(2,128)(2,1)S(1)} %slice.43), channel_id=1, source_target_pairs={{0,1},{1,2},{2,3},{3,4},{4,5},{5,6},{6,7},{7,8},{8,9},{9,10},{10,1... | collective-permute-start | bytes 6152 | tf_op jit(solution)/shard_map/ppermute | solution.py:24
  159.0 1.0 copy-start.1

commit v20 on v18

--- a/solution.py
+++ b/solution.py
@@ -306,11 +306,17 @@
         prev0 = passed_along(own_pairs, "seq", 2)
         gate = prev0
         if outs:
-            prev0, _ = lax.optimization_barrier((prev0, projected))
+            prev0, _ = lax.optimization_barrier((prev0, outs[-1]))
+        else:
+            prev0, query_rows, key_row = lax.optimization_barrier(
+                (prev0, query_clip.reshape(tok_count, 1),
+                 key_clip.reshape(1, (FREACH + 1) * tok_count))
+            )
         prev1b = pair_swap(prev0, "seq", True)
+        if projected is not None:
+            prev1b, _ = lax.optimization_barrier((prev1b, projected))
         part_out, part_pool = fine_attention(
-            planes, prev0, prev1a, prev1b, query_clip.reshape(tok_count, 1),
-            key_clip.reshape(1, (FREACH + 1) * tok_count), FHEADS,
+            planes, prev0, prev1a, prev1b, query_rows, key_row, FHEADS,
             part * part_width // head_pair_width,
         )
         outs.append(part_out)

time: 163 us -> 163 us (level)
    ppermute x6, waiting for transfers between devices: 42 us -> 44.5 us  [passed_along(): lax.ppermute(value, axis, [(source, source + steps) for source in range(f...]
  transfers between devices with their start and end apart: 15 -> 15, of which waited for: 9 -> 8; matrix products, arithmetic and copies ran while one was open for 9% -> 9% of each run, Pallas kernels for 11% -> 11%
where the time goes in v20:
time: 163 us
  waiting for transfers between devices  52.6 us (32%)
  starting transfers between devices  45.9 us (28%)
  Pallas kernels  40 us (25%)
  local copies, waits for them, and re-layouts  14.3 us (9%)
  matrix products  7.22 us (4%)
  other arithmetic  2.28 us (1%)
    ppermute x6, waiting for transfers between devices, passed_along(): lax.ppermute(value, axis, [(source, source + steps) for source in range(f...  44.5 us
    pallas_call x2, Pallas kernels, fine_attention(): pl.pallas_call(kernel, grid=(nq, pairs), in_specs=[pl.BlockSpec((tile, 1)...  30.8 us
    ppermute x6, starting transfers between devices, passed_along(): lax.ppermute(value, axis, [(source, source + steps) for source in range(f...  27.5 us
    ppermute x3, starting transfers between devices, pair_swap(): lax.ppermute(value, axis, [(source, source + step) for source in range(st...  10.3 us
    ppermute x6, starting transfers between devices, within_group(): return lax.ppermute(value, axis, pairs)  8.16 us
    ppermute x6, waiting for transfers between devices, within_group(): return lax.ppermute(value, axis, pairs)  8.08 us
    pallas_call x1, Pallas kernels, coarse_attention(): pl.pallas_call(kernel, grid=(heads, rows // tile), in_specs=[pl.BlockSpec...  6.8 us
    dot_general x2, matrix products, body(): jnp.einsum('rd,mdc->mrc', part_pool, part_weight, preferred_element_type=...  6.75 us
  transfers between devices with their start and end apart: 15, of which 8 were waited for; matrix products, arithmetic and copies ran while one was open for 9% of the time, Pallas kernels for 11%

profile of v20, /device:TPU:7, one launch (start us, length us, event | category | flops | bytes accessed | tf_op | source)
XLA Modules:
  0.0 162.6 jit_solution(11039362905665266717)
XLA Ops:
  0.0 1.4 collective-permute-start.1
  1.4 2.7 %fusion.16 = (bf16[2,512,512]{2,1,0:T(8,128)(2,1)}, bf16[2,512,512]{2,1,0:T(8,128)(2,1)S(1)}) fusion(bf16[3,512,1024]{2,1,0:T(8,128)(2,1)} %bitcast.54), kind=kLoop, calls=%fused_computation.46 | loop fusion | bytes 4194304 | tf_op jit(solution)/shard_map/slice | solution.py:303
  4.1 3.1 %collective-permute-start = (bf16[2,512,512]{2,1,0:T(8,128)(2,1)S(1)}, bf16[2,512,512]{2,1,0:T(8,128)(2,1)}, u32[]{:S(2)}, u32[]{:S(2)}) collective-permute-start(bf16[2,512,512]{2,1,0:T(8,128)(2,1)S(1)} %get-tuple-element.28), channel_id=1, source_target_pairs={{0,2},{1,3},{2,4},{3,5},{4,6},{5,7},{6,8},{7,9},{8,10},{9,11},{10,... | collective-permute-start | bytes 3145736 | tf_op jit(solution)/shard_map/ppermute | solution.py:24
  8.5 19.5 %collective-permute-done.k0_ref.v0_ref = bf16[2,512,512]{2,1,0:T(8,128)(2,1)} collective-permute-done((bf16[2,512,512]{2,1,0:T(8,128)(2,1)S(1)}, bf16[2,512,512]{2,1,0:T(8,128)(2,1)}, u32[]{:S(2)}, u32[]{:S(2)}) %collective-permute-start) | collective-permute-done | bytes 1048608 | tf_op jit(solution)/shard_map/ppermute | solution.py:24
  28.0 6.6 %collective-permute-start.2 = (bf16[2,512,512]{2,1,0:T(8,128)(2,1)}, bf16[2,512,512]{2,1,0:T(8,128)(2,1)}, u32[]{:S(2)}, u32[]{:S(2)}) collective-permute-start(bf16[2,512,512]{2,1,0:T(8,128)(2,1)} %collective-permute-done.k0_ref.v0_ref), channel_id=1, source_target_pairs={{1,0},{3,2},{5,4},{7,6},{9,8},{11,10},{13,12},{15,14},{17,16},{19,... | collective-permute-start | bytes 3145736 | tf_op jit(solution)/shard_map/ppermute | solution.py:173
  34.6 4.0 %collective-permute-start.3 = (bf16[2,512,512]{2,1,0:T(8,128)(2,1)}, bf16[2,512,512]{2,1,0:T(8,128)(2,1)S(1)}, u32[]{:S(2)}, u32[]{:S(2)}) collective-permute-start(bf16[2,512,512]{2,1,0:T(8,128)(2,1)} %get-tuple-element.19), channel_id=1, source_target_pairs={{0,2},{1,3},{2,4},{3,5},{4,6},{5,7},{6,8},{7,9},{8,10},{9,11},{10,... | collective-permute-start | bytes 3145736 | tf_op jit(solution)/shard_map/ppermute | solution.py:24
  39.5 15.3 %shard_map.46 = (bf16[512,512]{1,0:T(8,128)(2,1)}, bf16[128,512]{1,0:T(8,128)(2,1)}) custom-call(s32[512,1]{1,0:T(8,128)} %copy.6.qclip_ref, s32[1,1536]{1,0:T(1,128)} %reshape_reshape.7.kclip0_ref.kclip1_ref.kclip2_ref, s32[1,1536]{1,0:T(1,128)} %reshape_reshape.7.kclip0_ref.kclip1_ref.kclip2_ref, ...), custom_call_target="tpu_custom_call" | custom-call | tf_op jit(solution)/shard_map/pallas_call | solution.py:117
  54.8 6.0 %collective-permute-done.3.k0_ref.v0_ref = bf16[2,512,512]{2,1,0:T(8,128)(2,1)S(1)} collective-permute-done((bf16[2,512,512]{2,1,0:T(8,128)(2,1)}, bf16[2,512,512]{2,1,0:T(8,128)(2,1)S(1)}, u32[]{:S(2)}, u32[]{:S(2)}) %collective-permute-start.3) | collective-permute-done | bytes 1048608 | tf_op jit(solution)/shard_map/ppermute | solution.py:24
  60.8 2.3 %collective-permute-start.4 = (bf16[2,512,512]{2,1,0:T(8,128)(2,1)S(1)}, bf16[2,512,512]{2,1,0:T(8,128)(2,1)}, u32[]{:S(2)}, u32[]{:S(2)}) collective-permute-start(bf16[2,512,512]{2,1,0:T(8,128)(2,1)S(1)} %collective-permute-done.3.k0_ref.v0_ref), channel_id=1, source_target_pairs={{1,0},{3,2},{5,4},{7,6},{9,8},{11,10},{13,12},{15,14},{17,16},{19,... | collective-permute-start | bytes 3145736 | tf_op jit(solution)/shard_map/ppermute | solution.py:173
  63.1 3.7 %fusion.5 = f32[3,128,1024]{2,1,0:T(8,128)} fusion(bf16[3,1024,1024]{2,1,0:T(8,128)(2,1)} %bitcast.61, bf16[128,512]{1,0:T(8,128)(2,1)} %get-tuple-element.21), kind=kOutput, calls=%fused_computation.6 | convolution fusion | flops 402653184 | bytes 4849664 | tf_op jit(solution)/shard_map/rd,mdc->mrc/dot_general | solution.py:324
  66.8 15.5 %shard_map.47 = (bf16[512,512]{1,0:T(8,128)(2,1)}, bf16[128,512]{1,0:T(8,128)(2,1)}) custom-call(s32[512,1]{1,0:T(8,128)} %copy.6.qclip_ref, s32[1,1536]{1,0:T(1,128)} %reshape_reshape.7.kclip0_ref.kclip1_ref.kclip2_ref, s32[1,1536]{1,0:T(1,128)} %reshape_reshape.7.kclip0_ref.kclip1_ref.kclip2_ref, ...), custom_call_target="tpu_custom_call" | custom-call | tf_op jit(solution)/shard_map/pallas_call | solution.py:117
  82.3 3.0 %fusion.4 = bf16[3,128,1024]{2,1,0:T(8,128)(2,1)S(1)} fusion(f32[3,128,1024]{2,1,0:T(8,128)} %fusion.5, bf16[3,1024,1024]{2,1,0:T(8,128)(2,1)} %bitcast.62, bf16[128,512]{1,0:T(8,128)(2,1)} %get-tuple-element.24), kind=kOutput, calls=%fused_computation.5 | convolution fusion | flops 403439616 | bytes 5636096 | tf_op jit(solution)/shard_map/rd,mdc->mrc/dot_general | solution.py:324
  86.1 1.8 %collective-permute-start.7 = (bf16[3,128,256]{2,1,0:T(8,128)(2,1)S(1)}, bf16[3,128,256]{2,1,0:T(8,128)(2,1)S(1)}, u32[]{:S(2)}, u32[]{:S(2)}) collective-permute-start(bf16[3,128,256]{2,1,0:T(8,128)(2,1)S(1)} %get-tuple-element.29), channel_id=1, source_target_pairs={{0,1},{1,2},{2,3},{3,0},{4,5},{5,6},{6,7},{7,4},{8,9},{9,10},{10,1... | collective-permute-start | bytes 589832 | tf_op jit(solution)/shard_map/ppermute | solution.py:33
  87.9 5.9 %collective-permute-done.5 = bf16[3,128,256]{2,1,0:T(8,128)(2,1)S(1)} collective-permute-done((bf16[3,128,256]{2,1,0:T(8,128)(2,1)}, bf16[3,128,256]{2,1,0:T(8,128)(2,1)S(1)}, u32[]{:S(2)}, u32[]{:S(2)}) %collective-permute-start.5) | collective-permute-done | bytes 196640 | tf_op jit(solution)/shard_map/ppermute | solution.py:33
  93.8 1.1 collective-permute-done.7
  95.2 4.5 %collective-permute-start.8 = (bf16[2,512,256]{2,1,0:T(8,128)(2,1)S(1)}, bf16[2,512,256]{2,1,0:T(8,128)(2,1)S(1)}, u32[]{:S(2)}, u32[]{:S(2)}) collective-permute-start(bf16[2,512,256]{2,1,0:T(8,128)(2,1)S(1)} %bitcast.63), channel_id=1, source_target_pairs={{0,4},{1,5},{2,6},{3,7},{4,8},{5,9},{6,10},{7,11},{8,12},{9,13},{1... | collective-permute-start | bytes 1572872 | tf_op jit(solution)/shard_map/ppermute | solution.py:24
  99.7 9.3 %collective-permute-done.8.k2_ref.v2_ref = bf16[2,512,256]{2,1,0:T(8,128)(2,1)S(1)} collective-permute-done((bf16[2,512,256]{2,1,0:T(8,128)(2,1)S(1)}, bf16[2,512,256]{2,1,0:T(8,128)(2,1)S(1)}, u32[]{:S(2)}, u32[]{:S(2)}) %collective-permute-start.8) | collective-permute-done | bytes 524320 | tf_op jit(solution)/shard_map/ppermute | solution.py:24
  109.8 4.9 %collective-permute-start.9 = (bf16[2,512,256]{2,1,0:T(8,128)(2,1)S(1)}, bf16[2,512,256]{2,1,0:T(8,128)(2,1)}, u32[]{:S(2)}, u32[]{:S(2)}) collective-permute-start(bf16[2,512,256]{2,1,0:T(8,128)(2,1)S(1)} %collective-permute-done.8.k2_ref.v2_ref), channel_id=1, source_target_pairs={{0,4},{1,5},{2,6},{3,7},{4,8},{5,9},{6,10},{7,11},{8,12},{9,13},{1... | collective-permute-start | bytes 1572872 | tf_op jit(solution)/shard_map/ppermute | solution.py:24
  114.7 7.6 %collective-permute-done.9.k1_ref.v1_ref = bf16[2,512,256]{2,1,0:T(8,128)(2,1)} collective-permute-done((bf16[2,512,256]{2,1,0:T(8,128)(2,1)S(1)}, bf16[2,512,256]{2,1,0:T(8,128)(2,1)}, u32[]{:S(2)}, u32[]{:S(2)}) %collective-permute-start.9) | collective-permute-done | bytes 524320 | tf_op jit(solution)/shard_map/ppermute | solution.py:24
  122.3 5.0 %collective-permute-start.10 = (bf16[2,512,256]{2,1,0:T(8,128)(2,1)}, bf16[2,512,256]{2,1,0:T(8,128)(2,1)}, u32[]{:S(2)}, u32[]{:S(2)}) collective-permute-start(bf16[2,512,256]{2,1,0:T(8,128)(2,1)} %collective-permute-done.9.k1_ref.v1_ref), channel_id=1, source_target_pairs={{0,4},{1,5},{2,6},{3,7},{4,8},{5,9},{6,10},{7,11},{8,12},{9,13},{1... | collective-permute-start | bytes 1572872 | tf_op jit(solution)/shard_map/ppermute | solution.py:24
  127.4 0.9 copy.9.qclip_ref
  128.9 1.1 constant_dynamic-update-slice_fusion.1
  130.0 1.1 constant_dynamic-update-slice_fusion.fine_ref
  132.2 2.1 %collective-permute-done.10.k0_ref.v0_ref = bf16[2,512,256]{2,1,0:T(8,128)(2,1)} collective-permute-done((bf16[2,512,256]{2,1,0:T(8,128)(2,1)}, bf16[2,512,256]{2,1,0:T(8,128)(2,1)}, u32[]{:S(2)}, u32[]{:S(2)}) %collective-permute-start.10) | collective-permute-done | bytes 524320 | tf_op jit(solution)/shard_map/ppermute | solution.py:24
  134.4 6.8 %shard_map.48 = bf16[512,256]{1,0:T(8,128)(2,1)} custom-call(s32[512,1]{1,0:T(8,128)} %copy.9.qclip_ref, s32[1,2048]{1,0:T(1,128)} %bitcast.69, s32[1,2048]{1,0:T(1,128)} %bitcast.70, s32[1,2048]{1,0:T(1,128)} %bitcast.71, s32[1,2048]{1,0:T(1,128)} %bitcast.72, bf16[512,256]{1,0:T(8,128)(2,1)} %bitcast.67, ...), custom_call_target="tpu_custom_call" | custom-call | tf_op jit(solution)/shard_map/pallas_call | solution.py:226
  141.2 0.9 constant_dynamic-slice_fusion
  142.1 4.7 %collective-permute-start.11 = (bf16[128,256]{1,0:T(8,128)(2,1)S(1)}, bf16[128,256]{1,0:T(8,128)(2,1)S(1)}, u32[]{:S(2)}, u32[]{:S(2)}) collective-permute-start(bf16[128,256]{1,0:T(8,128)(2,1)S(1)} %get-tuple-element.34), channel_id=1, source_target_pairs={{0,3},{1,0},{2,1},{3,2},{4,7},{5,4},{6,5},{7,6},{8,11},{9,8},{10,9... | collective-permute-start | bytes 196616 | tf_op jit(solution)/shard_map/ppermute | solution.py:33
  146.8 1.7 %collective-permute-start.13 = (bf16[128,256]{1,0:T(8,128)(2,1)S(1)}, bf16[128,256]{1,0:T(8,128)(2,1)S(1)}, u32[]{:S(2)}, u32[]{:S(2)}) collective-permute-start(bf16[128,256]{1,0:T(8,128)(2,1)S(1)} %get-tuple-element.32), channel_id=1, source_target_pairs={{0,1},{1,2},{2,3},{3,0},{4,5},{5,6},{6,7},{7,4},{8,9},{9,10},{10,1... | collective-permute-start | bytes 196616 | tf_op jit(solution)/shard_map/ppermute | solution.py:33
  149.3 1.1 collective-permute-done.12
  152.1 5.9 %collective-permute-start.14 = (bf16[1,1024]{1,0:T(2,128)(2,1)S(1)}, bf16[1,1024]{1,0:T(2,128)(2,1)S(1)}, u32[]{:S(2)}, u32[]{:S(2)}) collective-permute-start(bf16[1,1024]{1,0:T(2,128)(2,1)S(1)} %slice.53), channel_id=1, source_target_pairs={{0,1},{1,2},{2,3},{3,4},{4,5},{5,6},{6,7},{7,8},{8,9},{9,10},{10,1... | collective-permute-start | bytes 6152 | tf_op jit(solution)/shard_map/ppermute | solution.py:24
  158.8 2.4 %shard_map.49 = bf16[512,1024]{1,0:T(8,128)(2,1)} custom-call(bf16[512,1024]{1,0:T(8,128)(2,1)} %copy-done.3, bf16[128,1024]{1,0:T(8,128)(2,1)} %pad_select_fusion.lift_ref), custom_call_target="tpu_custom_call" | custom-call | tf_op jit(solution)/shard_map/pallas_call | solution.py:157
  161.3 1.3 fusion.12
  (58 shorter events, 9.1 us)
Async XLA Ops:
  0.0 151.6 %copy-start = (bf16[1024,1024]{1,0:T(8,128)(2,1)S(1)}, bf16[1024,1024]{1,0:T(8,128)(2,1)}, u32[]{:S(2)}) copy-start(bf16[1024,1024]{1,0:T(8,128)(2,1)} %param.7) | copy-start | bytes 6291460
  0.0 7.3 %copy-start.5 = (s32[2048]{0:T(1024)S(1)}, s32[2048]{0:T(1024)}, u32[]{:S(2)}) copy-start(s32[2048]{0:T(1024)} %param.5) | copy-start | bytes 24580
  0.0 39.5 %collective-permute-start.1 = (bf16[3,512,1024]{2,1,0:T(8,128)(2,1)}, bf16[3,512,1024]{2,1,0:T(8,128)(2,1)}, u32[]{:S(2)}, u32[]{:S(2)}) collective-permute-start(bf16[3,512,1024]{2,1,0:T(8,128)(2,1)} %bitcast.53), channel_id=1, source_target_pairs={{0,1},{2,3},{4,5},{6,7},{8,9},{10,11},{12,13},{14,15},{16,17},{18,... | collective-permute-start | bytes 9437192 | tf_op jit(solution)/shard_map/ppermute | solution.py:173
  4.1 23.9 %collective-permute-start = (bf16[2,512,512]{2,1,0:T(8,128)(2,1)S(1)}, bf16[2,512,512]{2,1,0:T(8,128)(2,1)}, u32[]{:S(2)}, u32[]{:S(2)}) collective-permute-start(bf16[2,512,512]{2,1,0:T(8,128)(2,1)S(1)} %get-tuple-element.28), channel_id=1, source_target_pairs={{0,2},{1,3},{2,4},{3,5},{4,6},{5,7},{6,8},{7,9},{8,10},{9,11},{10,... | collective-permute-start | bytes 3145736 | tf_op jit(solution)/shard_map/ppermute | solution.py:24
  28.0 11.5 %collective-permute-start.2 = (bf16[2,512,512]{2,1,0:T(8,128)(2,1)}, bf16[2,512,512]{2,1,0:T(8,128)(2,1)}, u32[]{:S(2)}, u32[]{:S(2)}) collective-permute-start(bf16[2,512,512]{2,1,0:T(8,128)(2,1)} %collective-permute-done.k0_ref.v0_ref), channel_id=1, source_target_pairs={{1,0},{3,2},{5,4},{7,6},{9,8},{11,10},{13,12},{15,14},{17,16},{19,... | collective-permute-start | bytes 3145736 | tf_op jit(solution)/shard_map/ppermute | solution.py:173
  34.6 26.2 %collective-permute-start.3 = (bf16[2,512,512]{2,1,0:T(8,128)(2,1)}, bf16[2,512,512]{2,1,0:T(8,128)(2,1)S(1)}, u32[]{:S(2)}, u32[]{:S(2)}) collective-permute-start(bf16[2,512,512]{2,1,0:T(8,128)(2,1)} %get-tuple-element.19), channel_id=1, source_target_pairs={{0,2},{1,3},{2,4},{3,5},{4,6},{5,7},{6,8},{7,9},{8,10},{9,11},{10,... | collective-permute-start | bytes 3145736 | tf_op jit(solution)/shard_map/ppermute | solution.py:24
  60.8 6.0 %copy-start.2 = (bf16[2,512,512]{2,1,0:T(8,128)(2,1)}, bf16[2,512,512]{2,1,0:T(8,128)(2,1)S(1)}, u32[]{:S(2)}) copy-start(bf16[2,512,512]{2,1,0:T(8,128)(2,1)S(1)} %collective-permute-done.3.k0_ref.v0_ref) | copy-start | bytes 3145732
  60.8 6.0 %collective-permute-start.4 = (bf16[2,512,512]{2,1,0:T(8,128)(2,1)S(1)}, bf16[2,512,512]{2,1,0:T(8,128)(2,1)}, u32[]{:S(2)}, u32[]{:S(2)}) collective-permute-start(bf16[2,512,512]{2,1,0:T(8,128)(2,1)S(1)} %collective-permute-done.3.k0_ref.v0_ref), channel_id=1, source_target_pairs={{1,0},{3,2},{5,4},{7,6},{9,8},{11,10},{13,12},{15,14},{17,16},{19,... | collective-permute-start | bytes 3145736 | tf_op jit(solution)/shard_map/ppermute | solution.py:173
  86.1 7.7 %collective-permute-start.5 = (bf16[3,128,256]{2,1,0:T(8,128)(2,1)}, bf16[3,128,256]{2,1,0:T(8,128)(2,1)S(1)}, u32[]{:S(2)}, u32[]{:S(2)}) collective-permute-start(bf16[3,128,256]{2,1,0:T(8,128)(2,1)} %get-tuple-element.31), channel_id=1, source_target_pairs={{0,3},{1,0},{2,1},{3,2},{4,7},{5,4},{6,5},{7,6},{8,11},{9,8},{10,9... | collective-permute-start | bytes 589832 | tf_op jit(solution)/shard_map/ppermute | solution.py:33
  86.1 7.7 %collective-permute-start.6 = (bf16[3,128,256]{2,1,0:T(8,128)(2,1)S(1)}, bf16[3,128,256]{2,1,0:T(8,128)(2,1)S(1)}, u32[]{:S(2)}, u32[]{:S(2)}) collective-permute-start(bf16[3,128,256]{2,1,0:T(8,128)(2,1)S(1)} %get-tuple-element.30), channel_id=1, source_target_pairs={{0,2},{1,3},{2,0},{3,1},{4,6},{5,7},{6,4},{7,5},{8,10},{9,11},{10,... | collective-permute-start | bytes 589832 | tf_op jit(solution)/shard_map/ppermute | solution.py:33
  86.1 8.8 %collective-permute-start.7 = (bf16[3,128,256]{2,1,0:T(8,128)(2,1)S(1)}, bf16[3,128,256]{2,1,0:T(8,128)(2,1)S(1)}, u32[]{:S(2)}, u32[]{:S(2)}) collective-permute-start(bf16[3,128,256]{2,1,0:T(8,128)(2,1)S(1)} %get-tuple-element.29), channel_id=1, source_target_pairs={{0,1},{1,2},{2,3},{3,0},{4,5},{5,6},{6,7},{7,4},{8,9},{9,10},{10,1... | collective-permute-start | bytes 589832 | tf_op jit(solution)/shard_map/ppermute | solution.py:33
  95.2 39.2 %copy-start.1 = (bf16[2,4,128,256]{3,2,1,0:T(8,128)(2,1)}, bf16[2,4,128,256]{3,2,1,0:T(8,128)(2,1)S(1)}, u32[]{:S(2)}) copy-start(bf16[2,4,128,256]{3,2,1,0:T(8,128)(2,1)S(1)} %copy.8) | copy-start | bytes 1572868
  95.2 13.8 %collective-permute-start.8 = (bf16[2,512,256]{2,1,0:T(8,128)(2,1)S(1)}, bf16[2,512,256]{2,1,0:T(8,128)(2,1)S(1)}, u32[]{:S(2)}, u32[]{:S(2)}) collective-permute-start(bf16[2,512,256]{2,1,0:T(8,128)(2,1)S(1)} %bitcast.63), channel_id=1, source_target_pairs={{0,4},{1,5},{2,6},{3,7},{4,8},{5,9},{6,10},{7,11},{8,12},{9,13},{1... | collective-permute-start | bytes 1572872 | tf_op jit(solution)/shard_map/ppermute | solution.py:24
  109.0 0.8 copy-start.4
  109.8 12.5 %collective-permute-start.9 = (bf16[2,512,256]{2,1,0:T(8,128)(2,1)S(1)}, bf16[2,512,256]{2,1,0:T(8,128)(2,1)}, u32[]{:S(2)}, u32[]{:S(2)}) collective-permute-start(bf16[2,512,256]{2,1,0:T(8,128)(2,1)S(1)} %collective-permute-done.8.k2_ref.v2_ref), channel_id=1, source_target_pairs={{0,4},{1,5},{2,6},{3,7},{4,8},{5,9},{6,10},{7,11},{8,12},{9,13},{1... | collective-permute-start | bytes 1572872 | tf_op jit(solution)/shard_map/ppermute | solution.py:24
  122.3 12.0 %collective-permute-start.10 = (bf16[2,512,256]{2,1,0:T(8,128)(2,1)}, bf16[2,512,256]{2,1,0:T(8,128)(2,1)}, u32[]{:S(2)}, u32[]{:S(2)}) collective-permute-start(bf16[2,512,256]{2,1,0:T(8,128)(2,1)} %collective-permute-done.9.k1_ref.v1_ref), channel_id=1, source_target_pairs={{0,4},{1,5},{2,6},{3,7},{4,8},{5,9},{6,10},{7,11},{8,12},{9,13},{1... | collective-permute-start | bytes 1572872 | tf_op jit(solution)/shard_map/ppermute | solution.py:24
  131.1 1.1 copy-start.3
  142.1 7.2 %collective-permute-start.11 = (bf16[128,256]{1,0:T(8,128)(2,1)S(1)}, bf16[128,256]{1,0:T(8,128)(2,1)S(1)}, u32[]{:S(2)}, u32[]{:S(2)}) collective-permute-start(bf16[128,256]{1,0:T(8,128)(2,1)S(1)} %get-tuple-element.34), channel_id=1, source_target_pairs={{0,3},{1,0},{2,1},{3,2},{4,7},{5,4},{6,5},{7,6},{8,11},{9,8},{10,9... | collective-permute-start | bytes 196616 | tf_op jit(solution)/shard_map/ppermute | solution.py:33
  146.8 3.7 %collective-permute-start.12 = (bf16[128,256]{1,0:T(8,128)(2,1)S(1)}, bf16[128,256]{1,0:T(8,128)(2,1)S(1)}, u32[]{:S(2)}, u32[]{:S(2)}) collective-permute-start(bf16[128,256]{1,0:T(8,128)(2,1)S(1)} %get-tuple-element.33), channel_id=1, source_target_pairs={{0,2},{1,3},{2,0},{3,1},{4,6},{5,7},{6,4},{7,5},{8,10},{9,11},{10,... | collective-permute-start | bytes 196616 | tf_op jit(solution)/shard_map/ppermute | solution.py:33
  146.8 3.7 %collective-permute-start.13 = (bf16[128,256]{1,0:T(8,128)(2,1)S(1)}, bf16[128,256]{1,0:T(8,128)(2,1)S(1)}, u32[]{:S(2)}, u32[]{:S(2)}) collective-permute-start(bf16[128,256]{1,0:T(8,128)(2,1)S(1)} %get-tuple-element.32), channel_id=1, source_target_pairs={{0,1},{1,2},{2,3},{3,0},{4,5},{5,6},{6,7},{7,4},{8,9},{9,10},{10,1... | collective-permute-start | bytes 196616 | tf_op jit(solution)/shard_map/ppermute | solution.py:33
  152.1 9.2 %collective-permute-start.14 = (bf16[1,1024]{1,0:T(2,128)(2,1)S(1)}, bf16[1,1024]{1,0:T(2,128)(2,1)S(1)}, u32[]{:S(2)}, u32[]{:S(2)}) collective-permute-start(bf16[1,1024]{1,0:T(2,128)(2,1)S(1)} %slice.53), channel_id=1, source_target_pairs={{0,1},{1,2},{2,3},{3,4},{4,5},{5,6},{6,7},{7,8},{8,9},{9,10},{10,1... | collective-permute-start | bytes 6152 | tf_op jit(solution)/shard_map/ppermute | solution.py:24

commit v21 on v18

--- a/solution.py
+++ b/solution.py
@@ -178,35 +178,43 @@
                   out_ref, *, scale):
     tile = q_ref.shape[0]
     seg = k0_ref.shape[0]
-    q = q_ref[...]
-    qclip = qclip_ref[...]
     keys = (k0_ref, k1_ref, k2_ref, k3_ref)
     values = (v0_ref, v1_ref, v2_ref, v3_ref)
     clips = (kc0_ref, kc1_ref, kc2_ref, kc3_ref)
-    qpos = pl.program_id(1) * tile + lax.broadcasted_iota(jnp.int32, (tile, seg), 0)
-    kpos = lax.broadcasted_iota(jnp.int32, (tile, seg), 1)
     last = len(keys) - 1
-    scores = []
-    masks = []
-    for j in range(len(keys)):
-        allowed = clips[j][...] == qclip
-        if j == last:
-            allowed = allowed & (kpos <= qpos)
-        s = lax.dot_general(q, keys[j][...], (((1,), (1,)), ((), ())),
-                            preferred_element_type=jnp.float32) * scale
-        scores.append(jnp.where(allowed, s, -1e30))
-    top = jnp.max(scores[0], axis=1, keepdims=True)
-    for j in range(1, len(keys)):
-        top = jnp.maximum(top, jnp.max(scores[j], axis=1, keepdims=True))
-    total = None
-    summed = None
-    for j in range(len(keys)):
-        w = jnp.exp(scores[j] - top)
-        part = jnp.sum(w, axis=1, keepdims=True)
-        pv = jnp.dot(w.astype(jnp.bfloat16), values[j][...], preferred_element_type=jnp.float32)
-        total = part if total is None else total + part
-        summed = pv if summed is None else summed + pv
-    out_ref[...] = (summed / total).astype(out_ref.dtype)
+
+    def run(step):
+        q = q_ref[...]
+        qclip = qclip_ref[...]
+        own = (step + 1) * tile
+        scores = []
+        for j in range(len(keys)):
+            length = own if j == last else seg
+            allowed = clips[j][:, 0:length] == qclip
+            if j == last:
+                qpos = step * tile + lax.broadcasted_iota(jnp.int32, (tile, length), 0)
+                kpos = lax.broadcasted_iota(jnp.int32, (tile, length), 1)
+                allowed = allowed & (kpos <= qpos)
+            s = lax.dot_general(q, keys[j][0:length, :], (((1,), (1,)), ((), ())),
+                                preferred_element_type=jnp.float32) * scale
+            scores.append(jnp.where(allowed, s, -1e30))
+        top = jnp.max(scores[0], axis=1, keepdims=True)
+        for j in range(1, len(keys)):
+            top = jnp.maximum(top, jnp.max(scores[j], axis=1, keepdims=True))
+        total = None
+        summed = None
+        for j in range(len(keys)):
+            length = own if j == last else seg
+            w = jnp.exp(scores[j] - top)
+            part = jnp.sum(w, axis=1, keepdims=True)
+            pv = jnp.dot(w.astype(jnp.bfloat16), values[j][0:length, :],
+                         preferred_element_type=jnp.float32)
+            total = part if total is None else total + part
+            summed = pv if summed is None else summed + pv
+        out_ref[...] = (summed / total).astype(out_ref.dtype)
+
+    for step in range(seg // tile):
+        pl.when(pl.program_id(1) == step)(functools.partial(run, step))
 
 
 def coarse_attention(queries, windows, qclip, kclip, heads):

time: 163 us -> 162 us (level)
  no operation moved by 1% of the time
where the time goes in v21:
time: 162 us
  waiting for transfers between devices  51.4 us (32%)
  starting transfers between devices  46.4 us (29%)
  Pallas kernels  39.8 us (25%)
  local copies, waits for them, and re-layouts  14.2 us (9%)
  matrix products  7.22 us (4%)
  other arithmetic  2.28 us (1%)
    ppermute x6, waiting for transfers between devices, passed_along(): lax.ppermute(value, axis, [(source, source + steps) for source in range(f...  42 us
    pallas_call x2, Pallas kernels, fine_attention(): pl.pallas_call(kernel, grid=(nq, pairs), in_specs=[pl.BlockSpec((tile, 1)...  30.8 us
    ppermute x6, starting transfers between devices, passed_along(): lax.ppermute(value, axis, [(source, source + steps) for source in range(f...  28.1 us
    ppermute x3, starting transfers between devices, pair_swap(): lax.ppermute(value, axis, [(source, source + step) for source in range(st...  10.3 us
    ppermute x6, starting transfers between devices, within_group(): return lax.ppermute(value, axis, pairs)  8.04 us
    ppermute x6, waiting for transfers between devices, within_group(): return lax.ppermute(value, axis, pairs)  8.03 us
    dot_general x2, matrix products, body(): jnp.einsum('rd,mdc->mrc', part_pool, part_weight, preferred_element_type=...  6.75 us
    pallas_call x1, Pallas kernels, coarse_attention(): pl.pallas_call(kernel, grid=(heads, rows // tile), in_specs=[pl.BlockSpec...  6.6 us
  transfers between devices with their start and end apart: 15, of which 9 were waited for; matrix products, arithmetic and copies ran while one was open for 9% of the time, Pallas kernels for 11%

profile of v21, /device:TPU:7, one launch (start us, length us, event | category | flops | bytes accessed | tf_op | source)
XLA Modules:
  0.0 161.6 jit_solution(16089236676955089757)
XLA Ops:
  0.0 1.4 collective-permute-start.1
  1.4 2.7 %fusion.16 = (bf16[2,512,512]{2,1,0:T(8,128)(2,1)}, bf16[2,512,512]{2,1,0:T(8,128)(2,1)S(1)}) fusion(bf16[3,512,1024]{2,1,0:T(8,128)(2,1)} %bitcast.54), kind=kLoop, calls=%fused_computation.46 | loop fusion | bytes 4194304 | tf_op jit(solution)/shard_map/slice | solution.py:311
  4.1 3.1 %collective-permute-start = (bf16[2,512,512]{2,1,0:T(8,128)(2,1)S(1)}, bf16[2,512,512]{2,1,0:T(8,128)(2,1)}, u32[]{:S(2)}, u32[]{:S(2)}) collective-permute-start(bf16[2,512,512]{2,1,0:T(8,128)(2,1)S(1)} %get-tuple-element.20), channel_id=1, source_target_pairs={{0,2},{1,3},{2,4},{3,5},{4,6},{5,7},{6,8},{7,9},{8,10},{9,11},{10,... | collective-permute-start | bytes 3145736 | tf_op jit(solution)/shard_map/ppermute | solution.py:24
  7.3 20.7 %collective-permute-done.k0_ref.v0_ref = bf16[2,512,512]{2,1,0:T(8,128)(2,1)} collective-permute-done((bf16[2,512,512]{2,1,0:T(8,128)(2,1)S(1)}, bf16[2,512,512]{2,1,0:T(8,128)(2,1)}, u32[]{:S(2)}, u32[]{:S(2)}) %collective-permute-start) | collective-permute-done | bytes 1048608 | tf_op jit(solution)/shard_map/ppermute | solution.py:24
  28.0 6.6 %collective-permute-start.2 = (bf16[2,512,512]{2,1,0:T(8,128)(2,1)}, bf16[2,512,512]{2,1,0:T(8,128)(2,1)}, u32[]{:S(2)}, u32[]{:S(2)}) collective-permute-start(bf16[2,512,512]{2,1,0:T(8,128)(2,1)} %collective-permute-done.k0_ref.v0_ref), channel_id=1, source_target_pairs={{1,0},{3,2},{5,4},{7,6},{9,8},{11,10},{13,12},{15,14},{17,16},{19,... | collective-permute-start | bytes 3145736 | tf_op jit(solution)/shard_map/ppermute | solution.py:173
  34.6 4.0 %collective-permute-start.3 = (bf16[2,512,512]{2,1,0:T(8,128)(2,1)}, bf16[2,512,512]{2,1,0:T(8,128)(2,1)S(1)}, u32[]{:S(2)}, u32[]{:S(2)}) collective-permute-start(bf16[2,512,512]{2,1,0:T(8,128)(2,1)} %get-tuple-element.12), channel_id=1, source_target_pairs={{0,2},{1,3},{2,4},{3,5},{4,6},{5,7},{6,8},{7,9},{8,10},{9,11},{10,... | collective-permute-start | bytes 3145736 | tf_op jit(solution)/shard_map/ppermute | solution.py:24
  40.6 15.3 %shard_map.46 = (bf16[512,512]{1,0:T(8,128)(2,1)}, bf16[128,512]{1,0:T(8,128)(2,1)}) custom-call(s32[512,1]{1,0:T(8,128)} %reshape_reshape.10.qclip_ref, s32[1,1536]{1,0:T(1,128)} %reshape_reshape.9.kclip0_ref.kclip1_ref.kclip2_ref, s32[1,1536]{1,0:T(1,128)} %reshape_reshape.9.kclip0_ref.kclip1_ref.kclip2_ref, ...), custom_call_target="tpu_custom_call" | custom-call | tf_op jit(solution)/shard_map/pallas_call | solution.py:117
  55.9 3.7 %fusion.5 = f32[3,128,1024]{2,1,0:T(8,128)} fusion(bf16[3,1024,1024]{2,1,0:T(8,128)(2,1)} %bitcast.61, bf16[128,512]{1,0:T(8,128)(2,1)} %get-tuple-element.13), kind=kOutput, calls=%fused_computation.6 | convolution fusion | flops 402653184 | bytes 4849664 | tf_op jit(solution)/shard_map/rd,mdc->mrc/dot_general | solution.py:326
  59.7 1.1 collective-permute-done.3.k0_ref.v0_ref
  60.8 2.3 %collective-permute-start.4 = (bf16[2,512,512]{2,1,0:T(8,128)(2,1)S(1)}, bf16[2,512,512]{2,1,0:T(8,128)(2,1)}, u32[]{:S(2)}, u32[]{:S(2)}) collective-permute-start(bf16[2,512,512]{2,1,0:T(8,128)(2,1)S(1)} %collective-permute-done.3.k0_ref.v0_ref), channel_id=1, source_target_pairs={{1,0},{3,2},{5,4},{7,6},{9,8},{11,10},{13,12},{15,14},{17,16},{19,... | collective-permute-start | bytes 3145736 | tf_op jit(solution)/shard_map/ppermute | solution.py:173
  63.1 1.4 collective-permute-done.4.k1b_ref.v1b_ref
  64.5 15.5 %shard_map.47 = (bf16[512,512]{1,0:T(8,128)(2,1)}, bf16[128,512]{1,0:T(8,128)(2,1)}) custom-call(s32[512,1]{1,0:T(8,128)} %reshape_reshape.10.qclip_ref, s32[1,1536]{1,0:T(1,128)} %reshape_reshape.9.kclip0_ref.kclip1_ref.kclip2_ref, s32[1,1536]{1,0:T(1,128)} %reshape_reshape.9.kclip0_ref.kclip1_ref.kclip2_ref, ...), custom_call_target="tpu_custom_call" | custom-call | tf_op jit(solution)/shard_map/pallas_call | solution.py:117
  79.9 3.0 %fusion.4 = bf16[3,128,1024]{2,1,0:T(8,128)(2,1)S(1)} fusion(f32[3,128,1024]{2,1,0:T(8,128)} %fusion.5, bf16[3,1024,1024]{2,1,0:T(8,128)(2,1)} %bitcast.62, bf16[128,512]{1,0:T(8,128)(2,1)} %get-tuple-element.16), kind=kOutput, calls=%fused_computation.5 | convolution fusion | flops 403439616 | bytes 5636096 | tf_op jit(solution)/shard_map/rd,mdc->mrc/dot_general | solution.py:326
  84.1 1.6 %collective-permute-start.7 = (bf16[3,128,256]{2,1,0:T(8,128)(2,1)S(1)}, bf16[3,128,256]{2,1,0:T(8,128)(2,1)S(1)}, u32[]{:S(2)}, u32[]{:S(2)}) collective-permute-start(bf16[3,128,256]{2,1,0:T(8,128)(2,1)S(1)} %get-tuple-element.21), channel_id=1, source_target_pairs={{0,1},{1,2},{2,3},{3,0},{4,5},{5,6},{6,7},{7,4},{8,9},{9,10},{10,1... | collective-permute-start | bytes 589832 | tf_op jit(solution)/shard_map/ppermute | solution.py:33
  85.8 5.6 %collective-permute-done.5 = bf16[3,128,256]{2,1,0:T(8,128)(2,1)S(1)} collective-permute-done((bf16[3,128,256]{2,1,0:T(8,128)(2,1)}, bf16[3,128,256]{2,1,0:T(8,128)(2,1)S(1)}, u32[]{:S(2)}, u32[]{:S(2)}) %collective-permute-start.5) | collective-permute-done | bytes 196640 | tf_op jit(solution)/shard_map/ppermute | solution.py:33
  91.4 1.4 collective-permute-done.7
  93.0 5.0 %collective-permute-start.8 = (bf16[2,512,256]{2,1,0:T(8,128)(2,1)S(1)}, bf16[2,512,256]{2,1,0:T(8,128)(2,1)S(1)}, u32[]{:S(2)}, u32[]{:S(2)}) collective-permute-start(bf16[2,512,256]{2,1,0:T(8,128)(2,1)S(1)} %bitcast.63), channel_id=1, source_target_pairs={{0,4},{1,5},{2,6},{3,7},{4,8},{5,9},{6,10},{7,11},{8,12},{9,13},{1... | collective-permute-start | bytes 1572872 | tf_op jit(solution)/shard_map/ppermute | solution.py:24
  98.1 9.7 %collective-permute-done.8.k2_ref.v2_ref = bf16[2,512,256]{2,1,0:T(8,128)(2,1)S(1)} collective-permute-done((bf16[2,512,256]{2,1,0:T(8,128)(2,1)S(1)}, bf16[2,512,256]{2,1,0:T(8,128)(2,1)S(1)}, u32[]{:S(2)}, u32[]{:S(2)}) %collective-permute-start.8) | collective-permute-done | bytes 524320 | tf_op jit(solution)/shard_map/ppermute | solution.py:24
  108.6 4.9 %collective-permute-start.9 = (bf16[2,512,256]{2,1,0:T(8,128)(2,1)S(1)}, bf16[2,512,256]{2,1,0:T(8,128)(2,1)}, u32[]{:S(2)}, u32[]{:S(2)}) collective-permute-start(bf16[2,512,256]{2,1,0:T(8,128)(2,1)S(1)} %collective-permute-done.8.k2_ref.v2_ref), channel_id=1, source_target_pairs={{0,4},{1,5},{2,6},{3,7},{4,8},{5,9},{6,10},{7,11},{8,12},{9,13},{1... | collective-permute-start | bytes 1572872 | tf_op jit(solution)/shard_map/ppermute | solution.py:24
  113.5 8.0 %collective-permute-done.9.k1_ref.v1_ref = bf16[2,512,256]{2,1,0:T(8,128)(2,1)} collective-permute-done((bf16[2,512,256]{2,1,0:T(8,128)(2,1)S(1)}, bf16[2,512,256]{2,1,0:T(8,128)(2,1)}, u32[]{:S(2)}, u32[]{:S(2)}) %collective-permute-start.9) | collective-permute-done | bytes 524320 | tf_op jit(solution)/shard_map/ppermute | solution.py:24
  121.5 5.0 %collective-permute-start.10 = (bf16[2,512,256]{2,1,0:T(8,128)(2,1)}, bf16[2,512,256]{2,1,0:T(8,128)(2,1)}, u32[]{:S(2)}, u32[]{:S(2)}) collective-permute-start(bf16[2,512,256]{2,1,0:T(8,128)(2,1)} %collective-permute-done.9.k1_ref.v1_ref), channel_id=1, source_target_pairs={{0,4},{1,5},{2,6},{3,7},{4,8},{5,9},{6,10},{7,11},{8,12},{9,13},{1... | collective-permute-start | bytes 1572872 | tf_op jit(solution)/shard_map/ppermute | solution.py:24
  128.1 1.1 constant_dynamic-update-slice_fusion.1
  129.2 1.1 constant_dynamic-update-slice_fusion.fine_ref
  131.4 2.5 %collective-permute-done.10.k0_ref.v0_ref = bf16[2,512,256]{2,1,0:T(8,128)(2,1)} collective-permute-done((bf16[2,512,256]{2,1,0:T(8,128)(2,1)}, bf16[2,512,256]{2,1,0:T(8,128)(2,1)}, u32[]{:S(2)}, u32[]{:S(2)}) %collective-permute-start.10) | collective-permute-done | bytes 524320 | tf_op jit(solution)/shard_map/ppermute | solution.py:24
  133.9 6.6 %shard_map.48 = bf16[512,256]{1,0:T(8,128)(2,1)} custom-call(s32[512,1]{1,0:T(8,128)} %copy.9.qclip_ref, s32[1,2048]{1,0:T(1,128)} %bitcast.69, s32[1,2048]{1,0:T(1,128)} %bitcast.70, s32[1,2048]{1,0:T(1,128)} %bitcast.71, s32[1,2048]{1,0:T(1,128)} %bitcast.72, bf16[512,256]{1,0:T(8,128)(2,1)} %bitcast.67, ...), custom_call_target="tpu_custom_call" | custom-call | tf_op jit(solution)/shard_map/pallas_call | solution.py:234
  140.5 0.9 constant_dynamic-slice_fusion
  141.4 4.3 %collective-permute-start.11 = (bf16[128,256]{1,0:T(8,128)(2,1)S(1)}, bf16[128,256]{1,0:T(8,128)(2,1)S(1)}, u32[]{:S(2)}, u32[]{:S(2)}) collective-permute-start(bf16[128,256]{1,0:T(8,128)(2,1)S(1)} %get-tuple-element.26), channel_id=1, source_target_pairs={{0,3},{1,0},{2,1},{3,2},{4,7},{5,4},{6,5},{7,6},{8,11},{9,8},{10,9... | collective-permute-start | bytes 196616 | tf_op jit(solution)/shard_map/ppermute | solution.py:33
  145.7 1.7 %collective-permute-start.13 = (bf16[128,256]{1,0:T(8,128)(2,1)S(1)}, bf16[128,256]{1,0:T(8,128)(2,1)S(1)}, u32[]{:S(2)}, u32[]{:S(2)}) collective-permute-start(bf16[128,256]{1,0:T(8,128)(2,1)S(1)} %get-tuple-element.24), channel_id=1, source_target_pairs={{0,1},{1,2},{2,3},{3,0},{4,5},{5,6},{6,7},{7,4},{8,9},{9,10},{10,1... | collective-permute-start | bytes 196616 | tf_op jit(solution)/shard_map/ppermute | solution.py:33
  148.3 1.1 collective-permute-done.12
  151.0 5.9 %collective-permute-start.14 = (bf16[1,1024]{1,0:T(2,128)(2,1)S(1)}, bf16[1,1024]{1,0:T(2,128)(2,1)S(1)}, u32[]{:S(2)}, u32[]{:S(2)}) collective-permute-start(bf16[1,1024]{1,0:T(2,128)(2,1)S(1)} %slice.53), channel_id=1, source_target_pairs={{0,1},{1,2},{2,3},{3,4},{4,5},{5,6},{6,7},{7,8},{8,9},{9,10},{10,1... | collective-permute-start | bytes 6152 | tf_op jit(solution)/shard_map/ppermute | solution.py:24
  157.8 2.4 %shard_map.49 = bf16[512,1024]{1,0:T(8,128)(2,1)} custom-call(bf16[512,1024]{1,0:T(8,128)(2,1)} %copy-done.3, bf16[128,1024]{1,0:T(8,128)(2,1)} %pad_select_fusion.lift_ref), custom_call_target="tpu_custom_call" | custom-call | tf_op jit(solution)/shard_map/pallas_call | solution.py:157
  160.2 1.3 fusion.12
  (57 shorter events, 10.2 us)
Async XLA Ops:
  0.0 150.5 %copy-start = (bf16[1024,1024]{1,0:T(8,128)(2,1)S(1)}, bf16[1024,1024]{1,0:T(8,128)(2,1)}, u32[]{:S(2)}) copy-start(bf16[1024,1024]{1,0:T(8,128)(2,1)} %param.7) | copy-start | bytes 6291460
  0.0 38.7 %copy-start.5 = (s32[2048]{0:T(1024)S(1)}, s32[2048]{0:T(1024)}, u32[]{:S(2)}) copy-start(s32[2048]{0:T(1024)} %param.5) | copy-start | bytes 24580
  0.0 40.6 %collective-permute-start.1 = (bf16[3,512,1024]{2,1,0:T(8,128)(2,1)}, bf16[3,512,1024]{2,1,0:T(8,128)(2,1)}, u32[]{:S(2)}, u32[]{:S(2)}) collective-permute-start(bf16[3,512,1024]{2,1,0:T(8,128)(2,1)} %bitcast.53), channel_id=1, source_target_pairs={{0,1},{2,3},{4,5},{6,7},{8,9},{10,11},{12,13},{14,15},{16,17},{18,... | collective-permute-start | bytes 9437192 | tf_op jit(solution)/shard_map/ppermute | solution.py:173
  4.1 23.9 %collective-permute-start = (bf16[2,512,512]{2,1,0:T(8,128)(2,1)S(1)}, bf16[2,512,512]{2,1,0:T(8,128)(2,1)}, u32[]{:S(2)}, u32[]{:S(2)}) collective-permute-start(bf16[2,512,512]{2,1,0:T(8,128)(2,1)S(1)} %get-tuple-element.20), channel_id=1, source_target_pairs={{0,2},{1,3},{2,4},{3,5},{4,6},{5,7},{6,8},{7,9},{8,10},{9,11},{10,... | collective-permute-start | bytes 3145736 | tf_op jit(solution)/shard_map/ppermute | solution.py:24
  28.0 12.6 %collective-permute-start.2 = (bf16[2,512,512]{2,1,0:T(8,128)(2,1)}, bf16[2,512,512]{2,1,0:T(8,128)(2,1)}, u32[]{:S(2)}, u32[]{:S(2)}) collective-permute-start(bf16[2,512,512]{2,1,0:T(8,128)(2,1)} %collective-permute-done.k0_ref.v0_ref), channel_id=1, source_target_pairs={{1,0},{3,2},{5,4},{7,6},{9,8},{11,10},{13,12},{15,14},{17,16},{19,... | collective-permute-start | bytes 3145736 | tf_op jit(solution)/shard_map/ppermute | solution.py:173
  34.6 26.2 %collective-permute-start.3 = (bf16[2,512,512]{2,1,0:T(8,128)(2,1)}, bf16[2,512,512]{2,1,0:T(8,128)(2,1)S(1)}, u32[]{:S(2)}, u32[]{:S(2)}) collective-permute-start(bf16[2,512,512]{2,1,0:T(8,128)(2,1)} %get-tuple-element.12), channel_id=1, source_target_pairs={{0,2},{1,3},{2,4},{3,5},{4,6},{5,7},{6,8},{7,9},{8,10},{9,11},{10,... | collective-permute-start | bytes 3145736 | tf_op jit(solution)/shard_map/ppermute | solution.py:24
  60.8 3.7 %copy-start.2 = (bf16[2,512,512]{2,1,0:T(8,128)(2,1)}, bf16[2,512,512]{2,1,0:T(8,128)(2,1)S(1)}, u32[]{:S(2)}) copy-start(bf16[2,512,512]{2,1,0:T(8,128)(2,1)S(1)} %collective-permute-done.3.k0_ref.v0_ref) | copy-start | bytes 3145732
  60.8 3.7 %collective-permute-start.4 = (bf16[2,512,512]{2,1,0:T(8,128)(2,1)S(1)}, bf16[2,512,512]{2,1,0:T(8,128)(2,1)}, u32[]{:S(2)}, u32[]{:S(2)}) collective-permute-start(bf16[2,512,512]{2,1,0:T(8,128)(2,1)S(1)} %collective-permute-done.3.k0_ref.v0_ref), channel_id=1, source_target_pairs={{1,0},{3,2},{5,4},{7,6},{9,8},{11,10},{13,12},{15,14},{17,16},{19,... | collective-permute-start | bytes 3145736 | tf_op jit(solution)/shard_map/ppermute | solution.py:173
  83.7 7.6 %collective-permute-start.5 = (bf16[3,128,256]{2,1,0:T(8,128)(2,1)}, bf16[3,128,256]{2,1,0:T(8,128)(2,1)S(1)}, u32[]{:S(2)}, u32[]{:S(2)}) collective-permute-start(bf16[3,128,256]{2,1,0:T(8,128)(2,1)} %get-tuple-element.23), channel_id=1, source_target_pairs={{0,3},{1,0},{2,1},{3,2},{4,7},{5,4},{6,5},{7,6},{8,11},{9,8},{10,9... | collective-permute-start | bytes 589832 | tf_op jit(solution)/shard_map/ppermute | solution.py:33
  84.1 7.2 %collective-permute-start.6 = (bf16[3,128,256]{2,1,0:T(8,128)(2,1)S(1)}, bf16[3,128,256]{2,1,0:T(8,128)(2,1)S(1)}, u32[]{:S(2)}, u32[]{:S(2)}) collective-permute-start(bf16[3,128,256]{2,1,0:T(8,128)(2,1)S(1)} %get-tuple-element.22), channel_id=1, source_target_pairs={{0,2},{1,3},{2,0},{3,1},{4,6},{5,7},{6,4},{7,5},{8,10},{9,11},{10,... | collective-permute-start | bytes 589832 | tf_op jit(solution)/shard_map/ppermute | solution.py:33
  84.1 8.6 %collective-permute-start.7 = (bf16[3,128,256]{2,1,0:T(8,128)(2,1)S(1)}, bf16[3,128,256]{2,1,0:T(8,128)(2,1)S(1)}, u32[]{:S(2)}, u32[]{:S(2)}) collective-permute-start(bf16[3,128,256]{2,1,0:T(8,128)(2,1)S(1)} %get-tuple-element.21), channel_id=1, source_target_pairs={{0,1},{1,2},{2,3},{3,0},{4,5},{5,6},{6,7},{7,4},{8,9},{9,10},{10,1... | collective-permute-start | bytes 589832 | tf_op jit(solution)/shard_map/ppermute | solution.py:33
  93.0 40.8 %copy-start.1 = (bf16[2,4,128,256]{3,2,1,0:T(8,128)(2,1)}, bf16[2,4,128,256]{3,2,1,0:T(8,128)(2,1)S(1)}, u32[]{:S(2)}) copy-start(bf16[2,4,128,256]{3,2,1,0:T(8,128)(2,1)S(1)} %copy.8) | copy-start | bytes 1572868
  93.0 14.7 %collective-permute-start.8 = (bf16[2,512,256]{2,1,0:T(8,128)(2,1)S(1)}, bf16[2,512,256]{2,1,0:T(8,128)(2,1)S(1)}, u32[]{:S(2)}, u32[]{:S(2)}) collective-permute-start(bf16[2,512,256]{2,1,0:T(8,128)(2,1)S(1)} %bitcast.63), channel_id=1, source_target_pairs={{0,4},{1,5},{2,6},{3,7},{4,8},{5,9},{6,10},{7,11},{8,12},{9,13},{1... | collective-permute-start | bytes 1572872 | tf_op jit(solution)/shard_map/ppermute | solution.py:24
  107.8 0.8 copy-start.4
  108.6 12.9 %collective-permute-start.9 = (bf16[2,512,256]{2,1,0:T(8,128)(2,1)S(1)}, bf16[2,512,256]{2,1,0:T(8,128)(2,1)}, u32[]{:S(2)}, u32[]{:S(2)}) collective-permute-start(bf16[2,512,256]{2,1,0:T(8,128)(2,1)S(1)} %collective-permute-done.8.k2_ref.v2_ref), channel_id=1, source_target_pairs={{0,4},{1,5},{2,6},{3,7},{4,8},{5,9},{6,10},{7,11},{8,12},{9,13},{1... | collective-permute-start | bytes 1572872 | tf_op jit(solution)/shard_map/ppermute | solution.py:24
  121.5 12.4 %collective-permute-start.10 = (bf16[2,512,256]{2,1,0:T(8,128)(2,1)}, bf16[2,512,256]{2,1,0:T(8,128)(2,1)}, u32[]{:S(2)}, u32[]{:S(2)}) collective-permute-start(bf16[2,512,256]{2,1,0:T(8,128)(2,1)} %collective-permute-done.9.k1_ref.v1_ref), channel_id=1, source_target_pairs={{0,4},{1,5},{2,6},{3,7},{4,8},{5,9},{6,10},{7,11},{8,12},{9,13},{1... | collective-permute-start | bytes 1572872 | tf_op jit(solution)/shard_map/ppermute | solution.py:24
  130.3 1.1 copy-start.3
  141.4 6.9 %collective-permute-start.11 = (bf16[128,256]{1,0:T(8,128)(2,1)S(1)}, bf16[128,256]{1,0:T(8,128)(2,1)S(1)}, u32[]{:S(2)}, u32[]{:S(2)}) collective-permute-start(bf16[128,256]{1,0:T(8,128)(2,1)S(1)} %get-tuple-element.26), channel_id=1, source_target_pairs={{0,3},{1,0},{2,1},{3,2},{4,7},{5,4},{6,5},{7,6},{8,11},{9,8},{10,9... | collective-permute-start | bytes 196616 | tf_op jit(solution)/shard_map/ppermute | solution.py:33
  145.7 3.7 %collective-permute-start.12 = (bf16[128,256]{1,0:T(8,128)(2,1)S(1)}, bf16[128,256]{1,0:T(8,128)(2,1)S(1)}, u32[]{:S(2)}, u32[]{:S(2)}) collective-permute-start(bf16[128,256]{1,0:T(8,128)(2,1)S(1)} %get-tuple-element.25), channel_id=1, source_target_pairs={{0,2},{1,3},{2,0},{3,1},{4,6},{5,7},{6,4},{7,5},{8,10},{9,11},{10,... | collective-permute-start | bytes 196616 | tf_op jit(solution)/shard_map/ppermute | solution.py:33
  145.7 3.7 %collective-permute-start.13 = (bf16[128,256]{1,0:T(8,128)(2,1)S(1)}, bf16[128,256]{1,0:T(8,128)(2,1)S(1)}, u32[]{:S(2)}, u32[]{:S(2)}) collective-permute-start(bf16[128,256]{1,0:T(8,128)(2,1)S(1)} %get-tuple-element.24), channel_id=1, source_target_pairs={{0,1},{1,2},{2,3},{3,0},{4,5},{5,6},{6,7},{7,4},{8,9},{9,10},{10,1... | collective-permute-start | bytes 196616 | tf_op jit(solution)/shard_map/ppermute | solution.py:33
  151.0 9.2 %collective-permute-start.14 = (bf16[1,1024]{1,0:T(2,128)(2,1)S(1)}, bf16[1,1024]{1,0:T(2,128)(2,1)S(1)}, u32[]{:S(2)}, u32[]{:S(2)}) collective-permute-start(bf16[1,1024]{1,0:T(2,128)(2,1)S(1)} %slice.53), channel_id=1, source_target_pairs={{0,1},{1,2},{2,3},{3,4},{4,5},{5,6},{6,7},{7,8},{8,9},{9,10},{10,1... | collective-permute-start | bytes 6152 | tf_op jit(solution)/shard_map/ppermute | solution.py:24

commit v22 on v21

--- a/solution.py
+++ b/solution.py
@@ -175,8 +175,9 @@
 
 def coarse_kernel(qclip_ref, kc0_ref, kc1_ref, kc2_ref, kc3_ref, q_ref,
                   k0_ref, v0_ref, k1_ref, v1_ref, k2_ref, v2_ref, k3_ref, v3_ref,
-                  out_ref, *, scale):
-    tile = q_ref.shape[0]
+                  out_ref, *, scale, heads):
+    tile, width = q_ref.shape
+    head_dim = width // heads
     seg = k0_ref.shape[0]
     keys = (k0_ref, k1_ref, k2_ref, k3_ref)
     values = (v0_ref, v1_ref, v2_ref, v3_ref)
@@ -185,9 +186,11 @@
 
     def run(step):
         q = q_ref[...]
+        lane_head = lax.broadcasted_iota(jnp.int32, (1, width), 1) // head_dim
+        zero = jnp.zeros_like(q)
         qclip = qclip_ref[...]
         own = (step + 1) * tile
-        scores = []
+        masks = []
         for j in range(len(keys)):
             length = own if j == last else seg
             allowed = clips[j][:, 0:length] == qclip
@@ -195,23 +198,32 @@
                 qpos = step * tile + lax.broadcasted_iota(jnp.int32, (tile, length), 0)
                 kpos = lax.broadcasted_iota(jnp.int32, (tile, length), 1)
                 allowed = allowed & (kpos <= qpos)
-            s = lax.dot_general(q, keys[j][0:length, :], (((1,), (1,)), ((), ())),
-                                preferred_element_type=jnp.float32) * scale
-            scores.append(jnp.where(allowed, s, -1e30))
-        top = jnp.max(scores[0], axis=1, keepdims=True)
-        for j in range(1, len(keys)):
-            top = jnp.maximum(top, jnp.max(scores[j], axis=1, keepdims=True))
-        total = None
-        summed = None
-        for j in range(len(keys)):
-            length = own if j == last else seg
-            w = jnp.exp(scores[j] - top)
-            part = jnp.sum(w, axis=1, keepdims=True)
-            pv = jnp.dot(w.astype(jnp.bfloat16), values[j][0:length, :],
-                         preferred_element_type=jnp.float32)
-            total = part if total is None else total + part
-            summed = pv if summed is None else summed + pv
-        out_ref[...] = (summed / total).astype(out_ref.dtype)
+            masks.append(allowed)
+        out = None
+        for h in range(heads):
+            head_q = jnp.where(lane_head == h, q, zero)
+            scores = []
+            for j in range(len(keys)):
+                length = own if j == last else seg
+                s = lax.dot_general(head_q, keys[j][0:length, :], (((1,), (1,)), ((), ())),
+                                    preferred_element_type=jnp.float32) * scale
+                scores.append(jnp.where(masks[j], s, -1e30))
+            top = jnp.max(scores[0], axis=1, keepdims=True)
+            for j in range(1, len(keys)):
+                top = jnp.maximum(top, jnp.max(scores[j], axis=1, keepdims=True))
+            total = None
+            summed = None
+            for j in range(len(keys)):
+                length = own if j == last else seg
+                w = jnp.exp(scores[j] - top)
+                part = jnp.sum(w, axis=1, keepdims=True)
+                pv = jnp.dot(w.astype(jnp.bfloat16), values[j][0:length, :],
+                             preferred_element_type=jnp.float32)
+                total = part if total is None else total + part
+                summed = pv if summed is None else summed + pv
+            result = summed / total
+            out = result if out is None else jnp.where(lane_head == h, result, out)
+        out_ref[...] = out.astype(out_ref.dtype)
 
     for step in range(seg // tile):
         pl.when(pl.program_id(1) == step)(functools.partial(run, step))
@@ -222,21 +234,21 @@
     head_dim = width // heads
     tile = min(FINE_TILE, rows)
     seg = windows[0].shape[1]
-    kernel = functools.partial(coarse_kernel, scale=1.0 / math.sqrt(head_dim))
+    kernel = functools.partial(coarse_kernel, scale=1.0 / math.sqrt(head_dim), heads=heads)
     clip_specs = [pl.BlockSpec((1, seg), functools.partial(lambda j, h, i: (0, j), j))
                   for j in range(len(windows))]
     kv_specs = []
     kv_args = []
     for window in windows:
-        kv_specs.append(pl.BlockSpec((None, seg, head_dim), lambda h, i: (0, 0, h)))
-        kv_specs.append(pl.BlockSpec((None, seg, head_dim), lambda h, i: (1, 0, h)))
+        kv_specs.append(pl.BlockSpec((None, seg, width), lambda h, i: (0, 0, 0)))
+        kv_specs.append(pl.BlockSpec((None, seg, width), lambda h, i: (1, 0, 0)))
         kv_args += [window, window]
     return pl.pallas_call(
         kernel,
-        grid=(heads, rows // tile),
+        grid=(1, rows // tile),
         in_specs=[pl.BlockSpec((tile, 1), lambda h, i: (i, 0))] + clip_specs
-        + [pl.BlockSpec((tile, head_dim), lambda h, i: (i, h))] + kv_specs,
-        out_specs=pl.BlockSpec((tile, head_dim), lambda h, i: (i, h)),
+        + [pl.BlockSpec((tile, width), lambda h, i: (i, 0))] + kv_specs,
+        out_specs=pl.BlockSpec((tile, width), lambda h, i: (i, 0)),
         out_shape=jax.ShapeDtypeStruct((rows, width), jnp.bfloat16),
     )(qclip, *([kclip] * len(windows)), queries, *kv_args)
 

time: 162 us -> 163 us (level)
  no operation moved by 1% of the time
where the time goes in v22:
time: 163 us; the launch traced here: 162 us
  waiting for transfers between devices  51.4 us (32%)
  starting transfers between devices  46.4 us (28%)
  Pallas kernels  40 us (25%)
  local copies, waits for them, and re-layouts  14.2 us (9%)
  matrix products  7.22 us (4%)
  other arithmetic  2.28 us (1%)
    ppermute x6, waiting for transfers between devices, passed_along(): lax.ppermute(value, axis, [(source, source + steps) for source in range(f...  41.9 us
    pallas_call x2, Pallas kernels, fine_attention(): pl.pallas_call(kernel, grid=(nq, pairs), in_specs=[pl.BlockSpec((tile, 1)...  30.8 us
    ppermute x6, starting transfers between devices, passed_along(): lax.ppermute(value, axis, [(source, source + steps) for source in range(f...  28 us
    ppermute x3, starting transfers between devices, pair_swap(): lax.ppermute(value, axis, [(source, source + step) for source in range(st...  10.3 us
    ppermute x6, starting transfers between devices, within_group(): return lax.ppermute(value, axis, pairs)  8.05 us
    ppermute x6, waiting for transfers between devices, within_group(): return lax.ppermute(value, axis, pairs)  8.03 us
    pallas_call x1, Pallas kernels, coarse_attention(): pl.pallas_call(kernel, grid=(1, rows // tile), in_specs=[pl.BlockSpec((ti...  6.77 us
    dot_general x2, matrix products, body(): jnp.einsum('rd,mdc->mrc', part_pool, part_weight, preferred_element_type=...  6.75 us
  transfers between devices with their start and end apart: 15, of which 9 were waited for; matrix products, arithmetic and copies ran while one was open for 9% of the time, Pallas kernels for 11%

profile of v22, /device:TPU:7, one launch (start us, length us, event | category | flops | bytes accessed | tf_op | source)
XLA Modules:
  0.0 161.7 jit_solution(5612685557923714571)
XLA Ops:
  0.0 1.4 collective-permute-start.1
  1.4 2.7 %fusion.16 = (bf16[2,512,512]{2,1,0:T(8,128)(2,1)}, bf16[2,512,512]{2,1,0:T(8,128)(2,1)S(1)}) fusion(bf16[3,512,1024]{2,1,0:T(8,128)(2,1)} %bitcast.54), kind=kLoop, calls=%fused_computation.46 | loop fusion | bytes 4194304 | tf_op jit(solution)/shard_map/slice | solution.py:323
  4.1 3.1 %collective-permute-start = (bf16[2,512,512]{2,1,0:T(8,128)(2,1)S(1)}, bf16[2,512,512]{2,1,0:T(8,128)(2,1)}, u32[]{:S(2)}, u32[]{:S(2)}) collective-permute-start(bf16[2,512,512]{2,1,0:T(8,128)(2,1)S(1)} %get-tuple-element.20), channel_id=1, source_target_pairs={{0,2},{1,3},{2,4},{3,5},{4,6},{5,7},{6,8},{7,9},{8,10},{9,11},{10,... | collective-permute-start | bytes 3145736 | tf_op jit(solution)/shard_map/ppermute | solution.py:24
  7.3 20.7 %collective-permute-done.k0_ref.v0_ref = bf16[2,512,512]{2,1,0:T(8,128)(2,1)} collective-permute-done((bf16[2,512,512]{2,1,0:T(8,128)(2,1)S(1)}, bf16[2,512,512]{2,1,0:T(8,128)(2,1)}, u32[]{:S(2)}, u32[]{:S(2)}) %collective-permute-start) | collective-permute-done | bytes 1048608 | tf_op jit(solution)/shard_map/ppermute | solution.py:24
  28.0 6.6 %collective-permute-start.2 = (bf16[2,512,512]{2,1,0:T(8,128)(2,1)}, bf16[2,512,512]{2,1,0:T(8,128)(2,1)}, u32[]{:S(2)}, u32[]{:S(2)}) collective-permute-start(bf16[2,512,512]{2,1,0:T(8,128)(2,1)} %collective-permute-done.k0_ref.v0_ref), channel_id=1, source_target_pairs={{1,0},{3,2},{5,4},{7,6},{9,8},{11,10},{13,12},{15,14},{17,16},{19,... | collective-permute-start | bytes 3145736 | tf_op jit(solution)/shard_map/ppermute | solution.py:173
  34.6 4.0 %collective-permute-start.3 = (bf16[2,512,512]{2,1,0:T(8,128)(2,1)}, bf16[2,512,512]{2,1,0:T(8,128)(2,1)S(1)}, u32[]{:S(2)}, u32[]{:S(2)}) collective-permute-start(bf16[2,512,512]{2,1,0:T(8,128)(2,1)} %get-tuple-element.12), channel_id=1, source_target_pairs={{0,2},{1,3},{2,4},{3,5},{4,6},{5,7},{6,8},{7,9},{8,10},{9,11},{10,... | collective-permute-start | bytes 3145736 | tf_op jit(solution)/shard_map/ppermute | solution.py:24
  40.6 15.3 %shard_map.46 = (bf16[512,512]{1,0:T(8,128)(2,1)}, bf16[128,512]{1,0:T(8,128)(2,1)}) custom-call(s32[512,1]{1,0:T(8,128)} %reshape_reshape.10.qclip_ref, s32[1,1536]{1,0:T(1,128)} %reshape_reshape.9.kclip0_ref.kclip1_ref.kclip2_ref, s32[1,1536]{1,0:T(1,128)} %reshape_reshape.9.kclip0_ref.kclip1_ref.kclip2_ref, ...), custom_call_target="tpu_custom_call" | custom-call | tf_op jit(solution)/shard_map/pallas_call | solution.py:117
  55.9 3.7 %fusion.5 = f32[3,128,1024]{2,1,0:T(8,128)} fusion(bf16[3,1024,1024]{2,1,0:T(8,128)(2,1)} %bitcast.61, bf16[128,512]{1,0:T(8,128)(2,1)} %get-tuple-element.13), kind=kOutput, calls=%fused_computation.6 | convolution fusion | flops 402653184 | bytes 4849664 | tf_op jit(solution)/shard_map/rd,mdc->mrc/dot_general | solution.py:338
  59.6 1.1 collective-permute-done.3.k0_ref.v0_ref
  60.8 2.3 %collective-permute-start.4 = (bf16[2,512,512]{2,1,0:T(8,128)(2,1)S(1)}, bf16[2,512,512]{2,1,0:T(8,128)(2,1)}, u32[]{:S(2)}, u32[]{:S(2)}) collective-permute-start(bf16[2,512,512]{2,1,0:T(8,128)(2,1)S(1)} %collective-permute-done.3.k0_ref.v0_ref), channel_id=1, source_target_pairs={{1,0},{3,2},{5,4},{7,6},{9,8},{11,10},{13,12},{15,14},{17,16},{19,... | collective-permute-start | bytes 3145736 | tf_op jit(solution)/shard_map/ppermute | solution.py:173
  63.1 1.4 collective-permute-done.4.k1b_ref.v1b_ref
  64.5 15.5 %shard_map.47 = (bf16[512,512]{1,0:T(8,128)(2,1)}, bf16[128,512]{1,0:T(8,128)(2,1)}) custom-call(s32[512,1]{1,0:T(8,128)} %reshape_reshape.10.qclip_ref, s32[1,1536]{1,0:T(1,128)} %reshape_reshape.9.kclip0_ref.kclip1_ref.kclip2_ref, s32[1,1536]{1,0:T(1,128)} %reshape_reshape.9.kclip0_ref.kclip1_ref.kclip2_ref, ...), custom_call_target="tpu_custom_call" | custom-call | tf_op jit(solution)/shard_map/pallas_call | solution.py:117
  79.9 3.0 %fusion.4 = bf16[3,128,1024]{2,1,0:T(8,128)(2,1)S(1)} fusion(f32[3,128,1024]{2,1,0:T(8,128)} %fusion.5, bf16[3,1024,1024]{2,1,0:T(8,128)(2,1)} %bitcast.62, bf16[128,512]{1,0:T(8,128)(2,1)} %get-tuple-element.16), kind=kOutput, calls=%fused_computation.5 | convolution fusion | flops 403439616 | bytes 5636096 | tf_op jit(solution)/shard_map/rd,mdc->mrc/dot_general | solution.py:338
  84.1 1.6 %collective-permute-start.7 = (bf16[3,128,256]{2,1,0:T(8,128)(2,1)S(1)}, bf16[3,128,256]{2,1,0:T(8,128)(2,1)S(1)}, u32[]{:S(2)}, u32[]{:S(2)}) collective-permute-start(bf16[3,128,256]{2,1,0:T(8,128)(2,1)S(1)} %get-tuple-element.21), channel_id=1, source_target_pairs={{0,1},{1,2},{2,3},{3,0},{4,5},{5,6},{6,7},{7,4},{8,9},{9,10},{10,1... | collective-permute-start | bytes 589832 | tf_op jit(solution)/shard_map/ppermute | solution.py:33
  85.8 5.6 %collective-permute-done.5 = bf16[3,128,256]{2,1,0:T(8,128)(2,1)S(1)} collective-permute-done((bf16[3,128,256]{2,1,0:T(8,128)(2,1)}, bf16[3,128,256]{2,1,0:T(8,128)(2,1)S(1)}, u32[]{:S(2)}, u32[]{:S(2)}) %collective-permute-start.5) | collective-permute-done | bytes 196640 | tf_op jit(solution)/shard_map/ppermute | solution.py:33
  91.4 1.4 collective-permute-done.7
  93.0 5.0 %collective-permute-start.8 = (bf16[2,512,256]{2,1,0:T(8,128)(2,1)S(1)}, bf16[2,512,256]{2,1,0:T(8,128)(2,1)S(1)}, u32[]{:S(2)}, u32[]{:S(2)}) collective-permute-start(bf16[2,512,256]{2,1,0:T(8,128)(2,1)S(1)} %bitcast.63), channel_id=1, source_target_pairs={{0,4},{1,5},{2,6},{3,7},{4,8},{5,9},{6,10},{7,11},{8,12},{9,13},{1... | collective-permute-start | bytes 1572872 | tf_op jit(solution)/shard_map/ppermute | solution.py:24
  98.1 9.7 %collective-permute-done.8.k2_ref.v2_ref = bf16[2,512,256]{2,1,0:T(8,128)(2,1)S(1)} collective-permute-done((bf16[2,512,256]{2,1,0:T(8,128)(2,1)S(1)}, bf16[2,512,256]{2,1,0:T(8,128)(2,1)S(1)}, u32[]{:S(2)}, u32[]{:S(2)}) %collective-permute-start.8) | collective-permute-done | bytes 524320 | tf_op jit(solution)/shard_map/ppermute | solution.py:24
  108.5 4.9 %collective-permute-start.9 = (bf16[2,512,256]{2,1,0:T(8,128)(2,1)S(1)}, bf16[2,512,256]{2,1,0:T(8,128)(2,1)}, u32[]{:S(2)}, u32[]{:S(2)}) collective-permute-start(bf16[2,512,256]{2,1,0:T(8,128)(2,1)S(1)} %collective-permute-done.8.k2_ref.v2_ref), channel_id=1, source_target_pairs={{0,4},{1,5},{2,6},{3,7},{4,8},{5,9},{6,10},{7,11},{8,12},{9,13},{1... | collective-permute-start | bytes 1572872 | tf_op jit(solution)/shard_map/ppermute | solution.py:24
  113.5 8.0 %collective-permute-done.9.k1_ref.v1_ref = bf16[2,512,256]{2,1,0:T(8,128)(2,1)} collective-permute-done((bf16[2,512,256]{2,1,0:T(8,128)(2,1)S(1)}, bf16[2,512,256]{2,1,0:T(8,128)(2,1)}, u32[]{:S(2)}, u32[]{:S(2)}) %collective-permute-start.9) | collective-permute-done | bytes 524320 | tf_op jit(solution)/shard_map/ppermute | solution.py:24
  121.4 5.0 %collective-permute-start.10 = (bf16[2,512,256]{2,1,0:T(8,128)(2,1)}, bf16[2,512,256]{2,1,0:T(8,128)(2,1)}, u32[]{:S(2)}, u32[]{:S(2)}) collective-permute-start(bf16[2,512,256]{2,1,0:T(8,128)(2,1)} %collective-permute-done.9.k1_ref.v1_ref), channel_id=1, source_target_pairs={{0,4},{1,5},{2,6},{3,7},{4,8},{5,9},{6,10},{7,11},{8,12},{9,13},{1... | collective-permute-start | bytes 1572872 | tf_op jit(solution)/shard_map/ppermute | solution.py:24
  128.0 1.1 constant_dynamic-update-slice_fusion.1
  129.1 1.1 constant_dynamic-update-slice_fusion.fine_ref
  131.3 2.4 %collective-permute-done.10.k0_ref.v0_ref = bf16[2,512,256]{2,1,0:T(8,128)(2,1)} collective-permute-done((bf16[2,512,256]{2,1,0:T(8,128)(2,1)}, bf16[2,512,256]{2,1,0:T(8,128)(2,1)}, u32[]{:S(2)}, u32[]{:S(2)}) %collective-permute-start.10) | collective-permute-done | bytes 524320 | tf_op jit(solution)/shard_map/ppermute | solution.py:24
  133.8 6.8 %shard_map.48 = bf16[512,256]{1,0:T(8,128)(2,1)} custom-call(s32[512,1]{1,0:T(8,128)} %copy.9.qclip_ref, s32[1,2048]{1,0:T(1,128)} %bitcast.69, s32[1,2048]{1,0:T(1,128)} %bitcast.70, s32[1,2048]{1,0:T(1,128)} %bitcast.71, s32[1,2048]{1,0:T(1,128)} %bitcast.72, bf16[512,256]{1,0:T(8,128)(2,1)} %bitcast.67, ...), custom_call_target="tpu_custom_call" | custom-call | tf_op jit(solution)/shard_map/pallas_call | solution.py:246
  140.6 0.9 constant_dynamic-slice_fusion
  141.5 4.3 %collective-permute-start.11 = (bf16[128,256]{1,0:T(8,128)(2,1)S(1)}, bf16[128,256]{1,0:T(8,128)(2,1)S(1)}, u32[]{:S(2)}, u32[]{:S(2)}) collective-permute-start(bf16[128,256]{1,0:T(8,128)(2,1)S(1)} %get-tuple-element.26), channel_id=1, source_target_pairs={{0,3},{1,0},{2,1},{3,2},{4,7},{5,4},{6,5},{7,6},{8,11},{9,8},{10,9... | collective-permute-start | bytes 196616 | tf_op jit(solution)/shard_map/ppermute | solution.py:33
  145.8 1.7 %collective-permute-start.13 = (bf16[128,256]{1,0:T(8,128)(2,1)S(1)}, bf16[128,256]{1,0:T(8,128)(2,1)S(1)}, u32[]{:S(2)}, u32[]{:S(2)}) collective-permute-start(bf16[128,256]{1,0:T(8,128)(2,1)S(1)} %get-tuple-element.24), channel_id=1, source_target_pairs={{0,1},{1,2},{2,3},{3,0},{4,5},{5,6},{6,7},{7,4},{8,9},{9,10},{10,1... | collective-permute-start | bytes 196616 | tf_op jit(solution)/shard_map/ppermute | solution.py:33
  148.4 1.1 collective-permute-done.12
  151.1 5.9 %collective-permute-start.14 = (bf16[1,1024]{1,0:T(2,128)(2,1)S(1)}, bf16[1,1024]{1,0:T(2,128)(2,1)S(1)}, u32[]{:S(2)}, u32[]{:S(2)}) collective-permute-start(bf16[1,1024]{1,0:T(2,128)(2,1)S(1)} %slice.53), channel_id=1, source_target_pairs={{0,1},{1,2},{2,3},{3,4},{4,5},{5,6},{6,7},{7,8},{8,9},{9,10},{10,1... | collective-permute-start | bytes 6152 | tf_op jit(solution)/shard_map/ppermute | solution.py:24
  157.9 2.4 %shard_map.49 = bf16[512,1024]{1,0:T(8,128)(2,1)} custom-call(bf16[512,1024]{1,0:T(8,128)(2,1)} %copy-done.3, bf16[128,1024]{1,0:T(8,128)(2,1)} %pad_select_fusion.lift_ref), custom_call_target="tpu_custom_call" | custom-call | tf_op jit(solution)/shard_map/pallas_call | solution.py:157
  160.3 1.3 fusion.12
  (57 shorter events, 10.2 us)
Async XLA Ops:
  0.0 150.6 %copy-start = (bf16[1024,1024]{1,0:T(8,128)(2,1)S(1)}, bf16[1024,1024]{1,0:T(8,128)(2,1)}, u32[]{:S(2)}) copy-start(bf16[1024,1024]{1,0:T(8,128)(2,1)} %param.7) | copy-start | bytes 6291460
  0.0 38.7 %copy-start.5 = (s32[2048]{0:T(1024)S(1)}, s32[2048]{0:T(1024)}, u32[]{:S(2)}) copy-start(s32[2048]{0:T(1024)} %param.5) | copy-start | bytes 24580
  0.0 40.6 %collective-permute-start.1 = (bf16[3,512,1024]{2,1,0:T(8,128)(2,1)}, bf16[3,512,1024]{2,1,0:T(8,128)(2,1)}, u32[]{:S(2)}, u32[]{:S(2)}) collective-permute-start(bf16[3,512,1024]{2,1,0:T(8,128)(2,1)} %bitcast.53), channel_id=1, source_target_pairs={{0,1},{2,3},{4,5},{6,7},{8,9},{10,11},{12,13},{14,15},{16,17},{18,... | collective-permute-start | bytes 9437192 | tf_op jit(solution)/shard_map/ppermute | solution.py:173
  4.1 23.9 %collective-permute-start = (bf16[2,512,512]{2,1,0:T(8,128)(2,1)S(1)}, bf16[2,512,512]{2,1,0:T(8,128)(2,1)}, u32[]{:S(2)}, u32[]{:S(2)}) collective-permute-start(bf16[2,512,512]{2,1,0:T(8,128)(2,1)S(1)} %get-tuple-element.20), channel_id=1, source_target_pairs={{0,2},{1,3},{2,4},{3,5},{4,6},{5,7},{6,8},{7,9},{8,10},{9,11},{10,... | collective-permute-start | bytes 3145736 | tf_op jit(solution)/shard_map/ppermute | solution.py:24
  28.0 12.6 %collective-permute-start.2 = (bf16[2,512,512]{2,1,0:T(8,128)(2,1)}, bf16[2,512,512]{2,1,0:T(8,128)(2,1)}, u32[]{:S(2)}, u32[]{:S(2)}) collective-permute-start(bf16[2,512,512]{2,1,0:T(8,128)(2,1)} %collective-permute-done.k0_ref.v0_ref), channel_id=1, source_target_pairs={{1,0},{3,2},{5,4},{7,6},{9,8},{11,10},{13,12},{15,14},{17,16},{19,... | collective-permute-start | bytes 3145736 | tf_op jit(solution)/shard_map/ppermute | solution.py:173
  34.6 26.2 %collective-permute-start.3 = (bf16[2,512,512]{2,1,0:T(8,128)(2,1)}, bf16[2,512,512]{2,1,0:T(8,128)(2,1)S(1)}, u32[]{:S(2)}, u32[]{:S(2)}) collective-permute-start(bf16[2,512,512]{2,1,0:T(8,128)(2,1)} %get-tuple-element.12), channel_id=1, source_target_pairs={{0,2},{1,3},{2,4},{3,5},{4,6},{5,7},{6,8},{7,9},{8,10},{9,11},{10,... | collective-permute-start | bytes 3145736 | tf_op jit(solution)/shard_map/ppermute | solution.py:24
  60.8 3.7 %copy-start.2 = (bf16[2,512,512]{2,1,0:T(8,128)(2,1)}, bf16[2,512,512]{2,1,0:T(8,128)(2,1)S(1)}, u32[]{:S(2)}) copy-start(bf16[2,512,512]{2,1,0:T(8,128)(2,1)S(1)} %collective-permute-done.3.k0_ref.v0_ref) | copy-start | bytes 3145732
  60.8 3.7 %collective-permute-start.4 = (bf16[2,512,512]{2,1,0:T(8,128)(2,1)S(1)}, bf16[2,512,512]{2,1,0:T(8,128)(2,1)}, u32[]{:S(2)}, u32[]{:S(2)}) collective-permute-start(bf16[2,512,512]{2,1,0:T(8,128)(2,1)S(1)} %collective-permute-done.3.k0_ref.v0_ref), channel_id=1, source_target_pairs={{1,0},{3,2},{5,4},{7,6},{9,8},{11,10},{13,12},{15,14},{17,16},{19,... | collective-permute-start | bytes 3145736 | tf_op jit(solution)/shard_map/ppermute | solution.py:173
  83.7 7.6 %collective-permute-start.5 = (bf16[3,128,256]{2,1,0:T(8,128)(2,1)}, bf16[3,128,256]{2,1,0:T(8,128)(2,1)S(1)}, u32[]{:S(2)}, u32[]{:S(2)}) collective-permute-start(bf16[3,128,256]{2,1,0:T(8,128)(2,1)} %get-tuple-element.23), channel_id=1, source_target_pairs={{0,3},{1,0},{2,1},{3,2},{4,7},{5,4},{6,5},{7,6},{8,11},{9,8},{10,9... | collective-permute-start | bytes 589832 | tf_op jit(solution)/shard_map/ppermute | solution.py:33
  84.1 7.2 %collective-permute-start.6 = (bf16[3,128,256]{2,1,0:T(8,128)(2,1)S(1)}, bf16[3,128,256]{2,1,0:T(8,128)(2,1)S(1)}, u32[]{:S(2)}, u32[]{:S(2)}) collective-permute-start(bf16[3,128,256]{2,1,0:T(8,128)(2,1)S(1)} %get-tuple-element.22), channel_id=1, source_target_pairs={{0,2},{1,3},{2,0},{3,1},{4,6},{5,7},{6,4},{7,5},{8,10},{9,11},{10,... | collective-permute-start | bytes 589832 | tf_op jit(solution)/shard_map/ppermute | solution.py:33
  84.1 8.6 %collective-permute-start.7 = (bf16[3,128,256]{2,1,0:T(8,128)(2,1)S(1)}, bf16[3,128,256]{2,1,0:T(8,128)(2,1)S(1)}, u32[]{:S(2)}, u32[]{:S(2)}) collective-permute-start(bf16[3,128,256]{2,1,0:T(8,128)(2,1)S(1)} %get-tuple-element.21), channel_id=1, source_target_pairs={{0,1},{1,2},{2,3},{3,0},{4,5},{5,6},{6,7},{7,4},{8,9},{9,10},{10,1... | collective-permute-start | bytes 589832 | tf_op jit(solution)/shard_map/ppermute | solution.py:33
  93.0 40.8 %copy-start.1 = (bf16[2,4,128,256]{3,2,1,0:T(8,128)(2,1)}, bf16[2,4,128,256]{3,2,1,0:T(8,128)(2,1)S(1)}, u32[]{:S(2)}) copy-start(bf16[2,4,128,256]{3,2,1,0:T(8,128)(2,1)S(1)} %copy.8) | copy-start | bytes 1572868
  93.0 14.7 %collective-permute-start.8 = (bf16[2,512,256]{2,1,0:T(8,128)(2,1)S(1)}, bf16[2,512,256]{2,1,0:T(8,128)(2,1)S(1)}, u32[]{:S(2)}, u32[]{:S(2)}) collective-permute-start(bf16[2,512,256]{2,1,0:T(8,128)(2,1)S(1)} %bitcast.63), channel_id=1, source_target_pairs={{0,4},{1,5},{2,6},{3,7},{4,8},{5,9},{6,10},{7,11},{8,12},{9,13},{1... | collective-permute-start | bytes 1572872 | tf_op jit(solution)/shard_map/ppermute | solution.py:24
  107.7 0.8 copy-start.4
  108.5 12.9 %collective-permute-start.9 = (bf16[2,512,256]{2,1,0:T(8,128)(2,1)S(1)}, bf16[2,512,256]{2,1,0:T(8,128)(2,1)}, u32[]{:S(2)}, u32[]{:S(2)}) collective-permute-start(bf16[2,512,256]{2,1,0:T(8,128)(2,1)S(1)} %collective-permute-done.8.k2_ref.v2_ref), channel_id=1, source_target_pairs={{0,4},{1,5},{2,6},{3,7},{4,8},{5,9},{6,10},{7,11},{8,12},{9,13},{1... | collective-permute-start | bytes 1572872 | tf_op jit(solution)/shard_map/ppermute | solution.py:24
  121.4 12.4 %collective-permute-start.10 = (bf16[2,512,256]{2,1,0:T(8,128)(2,1)}, bf16[2,512,256]{2,1,0:T(8,128)(2,1)}, u32[]{:S(2)}, u32[]{:S(2)}) collective-permute-start(bf16[2,512,256]{2,1,0:T(8,128)(2,1)} %collective-permute-done.9.k1_ref.v1_ref), channel_id=1, source_target_pairs={{0,4},{1,5},{2,6},{3,7},{4,8},{5,9},{6,10},{7,11},{8,12},{9,13},{1... | collective-permute-start | bytes 1572872 | tf_op jit(solution)/shard_map/ppermute | solution.py:24
  130.2 1.1 copy-start.3
  141.5 6.9 %collective-permute-start.11 = (bf16[128,256]{1,0:T(8,128)(2,1)S(1)}, bf16[128,256]{1,0:T(8,128)(2,1)S(1)}, u32[]{:S(2)}, u32[]{:S(2)}) collective-permute-start(bf16[128,256]{1,0:T(8,128)(2,1)S(1)} %get-tuple-element.26), channel_id=1, source_target_pairs={{0,3},{1,0},{2,1},{3,2},{4,7},{5,4},{6,5},{7,6},{8,11},{9,8},{10,9... | collective-permute-start | bytes 196616 | tf_op jit(solution)/shard_map/ppermute | solution.py:33
  145.8 3.7 %collective-permute-start.12 = (bf16[128,256]{1,0:T(8,128)(2,1)S(1)}, bf16[128,256]{1,0:T(8,128)(2,1)S(1)}, u32[]{:S(2)}, u32[]{:S(2)}) collective-permute-start(bf16[128,256]{1,0:T(8,128)(2,1)S(1)} %get-tuple-element.25), channel_id=1, source_target_pairs={{0,2},{1,3},{2,0},{3,1},{4,6},{5,7},{6,4},{7,5},{8,10},{9,11},{10,... | collective-permute-start | bytes 196616 | tf_op jit(solution)/shard_map/ppermute | solution.py:33
  145.8 3.7 %collective-permute-start.13 = (bf16[128,256]{1,0:T(8,128)(2,1)S(1)}, bf16[128,256]{1,0:T(8,128)(2,1)S(1)}, u32[]{:S(2)}, u32[]{:S(2)}) collective-permute-start(bf16[128,256]{1,0:T(8,128)(2,1)S(1)} %get-tuple-element.24), channel_id=1, source_target_pairs={{0,1},{1,2},{2,3},{3,0},{4,5},{5,6},{6,7},{7,4},{8,9},{9,10},{10,1... | collective-permute-start | bytes 196616 | tf_op jit(solution)/shard_map/ppermute | solution.py:33
  151.1 9.2 %collective-permute-start.14 = (bf16[1,1024]{1,0:T(2,128)(2,1)S(1)}, bf16[1,1024]{1,0:T(2,128)(2,1)S(1)}, u32[]{:S(2)}, u32[]{:S(2)}) collective-permute-start(bf16[1,1024]{1,0:T(2,128)(2,1)S(1)} %slice.53), channel_id=1, source_target_pairs={{0,1},{1,2},{2,3},{3,4},{4,5},{5,6},{6,7},{7,8},{8,9},{9,10},{10,1... | collective-permute-start | bytes 6152 | tf_op jit(solution)/shard_map/ppermute | solution.py:24

commit v23 on v21

--- a/solution.py
+++ b/solution.py
@@ -220,7 +220,7 @@
 def coarse_attention(queries, windows, qclip, kclip, heads):
     rows, width = queries.shape
     head_dim = width // heads
-    tile = min(FINE_TILE, rows)
+    tile = min(FINE_TILE // 2, rows)
     seg = windows[0].shape[1]
     kernel = functools.partial(coarse_kernel, scale=1.0 / math.sqrt(head_dim))
     clip_specs = [pl.BlockSpec((1, seg), functools.partial(lambda j, h, i: (0, j), j))

time: 162 us -> 165 us (1.019)
  Pallas kernels: 39.8 us -> 41.9 us
    pallas_call x1, Pallas kernels: 6.6 us -> 8.69 us  [coarse_attention(): pl.pallas_call(kernel, grid=(heads, rows // tile), in_specs=[pl.BlockSpec...]
where the time goes in v23:
time: 165 us; the launch traced here: 164 us
  waiting for transfers between devices  51.4 us (31%)
  starting transfers between devices  46.4 us (28%)
  Pallas kernels  41.9 us (25%)
  local copies, waits for them, and re-layouts  14.2 us (9%)
  matrix products  7.22 us (4%)
  other arithmetic  2.28 us (1%)
    ppermute x6, waiting for transfers between devices, passed_along(): lax.ppermute(value, axis, [(source, source + steps) for source in range(f...  42 us
    pallas_call x2, Pallas kernels, fine_attention(): pl.pallas_call(kernel, grid=(nq, pairs), in_specs=[pl.BlockSpec((tile, 1)...  30.8 us
    ppermute x6, starting transfers between devices, passed_along(): lax.ppermute(value, axis, [(source, source + steps) for source in range(f...  28.1 us
    ppermute x3, starting transfers between devices, pair_swap(): lax.ppermute(value, axis, [(source, source + step) for source in range(st...  10.3 us
    pallas_call x1, Pallas kernels, coarse_attention(): pl.pallas_call(kernel, grid=(heads, rows // tile), in_specs=[pl.BlockSpec...  8.69 us
    ppermute x6, starting transfers between devices, within_group(): return lax.ppermute(value, axis, pairs)  8.04 us
    ppermute x6, waiting for transfers between devices, within_group(): return lax.ppermute(value, axis, pairs)  8.03 us
    dot_general x2, matrix products, body(): jnp.einsum('rd,mdc->mrc', part_pool, part_weight, preferred_element_type=...  6.75 us
  transfers between devices with their start and end apart: 15, of which 9 were waited for; matrix products, arithmetic and copies ran while one was open for 9% of the time, Pallas kernels for 11%

profile of v23, /device:TPU:7, one launch (start us, length us, event | category | flops | bytes accessed | tf_op | source)
XLA Modules:
  0.0 163.7 jit_solution(3745086959709309594)
XLA Ops:
  0.0 1.4 collective-permute-start.1
  1.4 2.7 %fusion.16 = (bf16[2,512,512]{2,1,0:T(8,128)(2,1)}, bf16[2,512,512]{2,1,0:T(8,128)(2,1)S(1)}) fusion(bf16[3,512,1024]{2,1,0:T(8,128)(2,1)} %bitcast.54), kind=kLoop, calls=%fused_computation.46 | loop fusion | bytes 4194304 | tf_op jit(solution)/shard_map/slice | solution.py:311
  4.1 3.1 %collective-permute-start = (bf16[2,512,512]{2,1,0:T(8,128)(2,1)S(1)}, bf16[2,512,512]{2,1,0:T(8,128)(2,1)}, u32[]{:S(2)}, u32[]{:S(2)}) collective-permute-start(bf16[2,512,512]{2,1,0:T(8,128)(2,1)S(1)} %get-tuple-element.20), channel_id=1, source_target_pairs={{0,2},{1,3},{2,4},{3,5},{4,6},{5,7},{6,8},{7,9},{8,10},{9,11},{10,... | collective-permute-start | bytes 3145736 | tf_op jit(solution)/shard_map/ppermute | solution.py:24
  7.3 20.7 %collective-permute-done.k0_ref.v0_ref = bf16[2,512,512]{2,1,0:T(8,128)(2,1)} collective-permute-done((bf16[2,512,512]{2,1,0:T(8,128)(2,1)S(1)}, bf16[2,512,512]{2,1,0:T(8,128)(2,1)}, u32[]{:S(2)}, u32[]{:S(2)}) %collective-permute-start) | collective-permute-done | bytes 1048608 | tf_op jit(solution)/shard_map/ppermute | solution.py:24
  28.0 6.6 %collective-permute-start.2 = (bf16[2,512,512]{2,1,0:T(8,128)(2,1)}, bf16[2,512,512]{2,1,0:T(8,128)(2,1)}, u32[]{:S(2)}, u32[]{:S(2)}) collective-permute-start(bf16[2,512,512]{2,1,0:T(8,128)(2,1)} %collective-permute-done.k0_ref.v0_ref), channel_id=1, source_target_pairs={{1,0},{3,2},{5,4},{7,6},{9,8},{11,10},{13,12},{15,14},{17,16},{19,... | collective-permute-start | bytes 3145736 | tf_op jit(solution)/shard_map/ppermute | solution.py:173
  34.6 4.0 %collective-permute-start.3 = (bf16[2,512,512]{2,1,0:T(8,128)(2,1)}, bf16[2,512,512]{2,1,0:T(8,128)(2,1)S(1)}, u32[]{:S(2)}, u32[]{:S(2)}) collective-permute-start(bf16[2,512,512]{2,1,0:T(8,128)(2,1)} %get-tuple-element.12), channel_id=1, source_target_pairs={{0,2},{1,3},{2,4},{3,5},{4,6},{5,7},{6,8},{7,9},{8,10},{9,11},{10,... | collective-permute-start | bytes 3145736 | tf_op jit(solution)/shard_map/ppermute | solution.py:24
  40.6 15.3 %shard_map.46 = (bf16[512,512]{1,0:T(8,128)(2,1)}, bf16[128,512]{1,0:T(8,128)(2,1)}) custom-call(s32[512,1]{1,0:T(8,128)} %reshape_reshape.10.qclip_ref, s32[1,1536]{1,0:T(1,128)} %reshape_reshape.9.kclip0_ref.kclip1_ref.kclip2_ref, s32[1,1536]{1,0:T(1,128)} %reshape_reshape.9.kclip0_ref.kclip1_ref.kclip2_ref, ...), custom_call_target="tpu_custom_call" | custom-call | tf_op jit(solution)/shard_map/pallas_call | solution.py:117
  55.9 3.7 %fusion.5 = f32[3,128,1024]{2,1,0:T(8,128)} fusion(bf16[3,1024,1024]{2,1,0:T(8,128)(2,1)} %bitcast.61, bf16[128,512]{1,0:T(8,128)(2,1)} %get-tuple-element.13), kind=kOutput, calls=%fused_computation.6 | convolution fusion | flops 402653184 | bytes 4849664 | tf_op jit(solution)/shard_map/rd,mdc->mrc/dot_general | solution.py:326
  59.7 1.1 collective-permute-done.3.k0_ref.v0_ref
  60.8 2.3 %collective-permute-start.4 = (bf16[2,512,512]{2,1,0:T(8,128)(2,1)S(1)}, bf16[2,512,512]{2,1,0:T(8,128)(2,1)}, u32[]{:S(2)}, u32[]{:S(2)}) collective-permute-start(bf16[2,512,512]{2,1,0:T(8,128)(2,1)S(1)} %collective-permute-done.3.k0_ref.v0_ref), channel_id=1, source_target_pairs={{1,0},{3,2},{5,4},{7,6},{9,8},{11,10},{13,12},{15,14},{17,16},{19,... | collective-permute-start | bytes 3145736 | tf_op jit(solution)/shard_map/ppermute | solution.py:173
  63.1 1.4 collective-permute-done.4.k1b_ref.v1b_ref
  64.5 15.5 %shard_map.47 = (bf16[512,512]{1,0:T(8,128)(2,1)}, bf16[128,512]{1,0:T(8,128)(2,1)}) custom-call(s32[512,1]{1,0:T(8,128)} %reshape_reshape.10.qclip_ref, s32[1,1536]{1,0:T(1,128)} %reshape_reshape.9.kclip0_ref.kclip1_ref.kclip2_ref, s32[1,1536]{1,0:T(1,128)} %reshape_reshape.9.kclip0_ref.kclip1_ref.kclip2_ref, ...), custom_call_target="tpu_custom_call" | custom-call | tf_op jit(solution)/shard_map/pallas_call | solution.py:117
  79.9 3.0 %fusion.4 = bf16[3,128,1024]{2,1,0:T(8,128)(2,1)S(1)} fusion(f32[3,128,1024]{2,1,0:T(8,128)} %fusion.5, bf16[3,1024,1024]{2,1,0:T(8,128)(2,1)} %bitcast.62, bf16[128,512]{1,0:T(8,128)(2,1)} %get-tuple-element.16), kind=kOutput, calls=%fused_computation.5 | convolution fusion | flops 403439616 | bytes 5636096 | tf_op jit(solution)/shard_map/rd,mdc->mrc/dot_general | solution.py:326
  84.1 1.6 collective-permute-start.7
  85.8 5.6 %collective-permute-done.5 = bf16[3,128,256]{2,1,0:T(8,128)(2,1)S(1)} collective-permute-done((bf16[3,128,256]{2,1,0:T(8,128)(2,1)}, bf16[3,128,256]{2,1,0:T(8,128)(2,1)S(1)}, u32[]{:S(2)}, u32[]{:S(2)}) %collective-permute-start.5) | collective-permute-done | bytes 196640 | tf_op jit(solution)/shard_map/ppermute | solution.py:33
  91.4 1.4 collective-permute-done.7
  93.0 5.0 %collective-permute-start.8 = (bf16[2,512,256]{2,1,0:T(8,128)(2,1)S(1)}, bf16[2,512,256]{2,1,0:T(8,128)(2,1)S(1)}, u32[]{:S(2)}, u32[]{:S(2)}) collective-permute-start(bf16[2,512,256]{2,1,0:T(8,128)(2,1)S(1)} %bitcast.63), channel_id=1, source_target_pairs={{0,4},{1,5},{2,6},{3,7},{4,8},{5,9},{6,10},{7,11},{8,12},{9,13},{1... | collective-permute-start | bytes 1572872 | tf_op jit(solution)/shard_map/ppermute | solution.py:24
  98.1 9.7 %collective-permute-done.8.k2_ref.v2_ref = bf16[2,512,256]{2,1,0:T(8,128)(2,1)S(1)} collective-permute-done((bf16[2,512,256]{2,1,0:T(8,128)(2,1)S(1)}, bf16[2,512,256]{2,1,0:T(8,128)(2,1)S(1)}, u32[]{:S(2)}, u32[]{:S(2)}) %collective-permute-start.8) | collective-permute-done | bytes 524320 | tf_op jit(solution)/shard_map/ppermute | solution.py:24
  108.6 4.9 %collective-permute-start.9 = (bf16[2,512,256]{2,1,0:T(8,128)(2,1)S(1)}, bf16[2,512,256]{2,1,0:T(8,128)(2,1)}, u32[]{:S(2)}, u32[]{:S(2)}) collective-permute-start(bf16[2,512,256]{2,1,0:T(8,128)(2,1)S(1)} %collective-permute-done.8.k2_ref.v2_ref), channel_id=1, source_target_pairs={{0,4},{1,5},{2,6},{3,7},{4,8},{5,9},{6,10},{7,11},{8,12},{9,13},{1... | collective-permute-start | bytes 1572872 | tf_op jit(solution)/shard_map/ppermute | solution.py:24
  113.5 8.0 %collective-permute-done.9.k1_ref.v1_ref = bf16[2,512,256]{2,1,0:T(8,128)(2,1)} collective-permute-done((bf16[2,512,256]{2,1,0:T(8,128)(2,1)S(1)}, bf16[2,512,256]{2,1,0:T(8,128)(2,1)}, u32[]{:S(2)}, u32[]{:S(2)}) %collective-permute-start.9) | collective-permute-done | bytes 524320 | tf_op jit(solution)/shard_map/ppermute | solution.py:24
  121.5 5.0 %collective-permute-start.10 = (bf16[2,512,256]{2,1,0:T(8,128)(2,1)}, bf16[2,512,256]{2,1,0:T(8,128)(2,1)}, u32[]{:S(2)}, u32[]{:S(2)}) collective-permute-start(bf16[2,512,256]{2,1,0:T(8,128)(2,1)} %collective-permute-done.9.k1_ref.v1_ref), channel_id=1, source_target_pairs={{0,4},{1,5},{2,6},{3,7},{4,8},{5,9},{6,10},{7,11},{8,12},{9,13},{1... | collective-permute-start | bytes 1572872 | tf_op jit(solution)/shard_map/ppermute | solution.py:24
  128.1 1.1 constant_dynamic-update-slice_fusion.1
  129.2 1.1 constant_dynamic-update-slice_fusion.fine_ref
  131.4 2.5 %collective-permute-done.10.k0_ref.v0_ref = bf16[2,512,256]{2,1,0:T(8,128)(2,1)} collective-permute-done((bf16[2,512,256]{2,1,0:T(8,128)(2,1)}, bf16[2,512,256]{2,1,0:T(8,128)(2,1)}, u32[]{:S(2)}, u32[]{:S(2)}) %collective-permute-start.10) | collective-permute-done | bytes 524320 | tf_op jit(solution)/shard_map/ppermute | solution.py:24
  133.9 8.7 %shard_map.48 = bf16[512,256]{1,0:T(8,128)(2,1)} custom-call(s32[512,1]{1,0:T(8,128)} %copy.9.qclip_ref, s32[1,2048]{1,0:T(1,128)} %bitcast.69, s32[1,2048]{1,0:T(1,128)} %bitcast.70, s32[1,2048]{1,0:T(1,128)} %bitcast.71, s32[1,2048]{1,0:T(1,128)} %bitcast.72, bf16[512,256]{1,0:T(8,128)(2,1)} %bitcast.67, ...), custom_call_target="tpu_custom_call" | custom-call | tf_op jit(solution)/shard_map/pallas_call | solution.py:234
  142.6 0.9 constant_dynamic-slice_fusion
  143.5 4.3 %collective-permute-start.11 = (bf16[128,256]{1,0:T(8,128)(2,1)S(1)}, bf16[128,256]{1,0:T(8,128)(2,1)S(1)}, u32[]{:S(2)}, u32[]{:S(2)}) collective-permute-start(bf16[128,256]{1,0:T(8,128)(2,1)S(1)} %get-tuple-element.26), channel_id=1, source_target_pairs={{0,3},{1,0},{2,1},{3,2},{4,7},{5,4},{6,5},{7,6},{8,11},{9,8},{10,9... | collective-permute-start | bytes 196616 | tf_op jit(solution)/shard_map/ppermute | solution.py:33
  147.8 1.7 %collective-permute-start.13 = (bf16[128,256]{1,0:T(8,128)(2,1)S(1)}, bf16[128,256]{1,0:T(8,128)(2,1)S(1)}, u32[]{:S(2)}, u32[]{:S(2)}) collective-permute-start(bf16[128,256]{1,0:T(8,128)(2,1)S(1)} %get-tuple-element.24), channel_id=1, source_target_pairs={{0,1},{1,2},{2,3},{3,0},{4,5},{5,6},{6,7},{7,4},{8,9},{9,10},{10,1... | collective-permute-start | bytes 196616 | tf_op jit(solution)/shard_map/ppermute | solution.py:33
  150.4 1.1 collective-permute-done.12
  153.1 5.9 %collective-permute-start.14 = (bf16[1,1024]{1,0:T(2,128)(2,1)S(1)}, bf16[1,1024]{1,0:T(2,128)(2,1)S(1)}, u32[]{:S(2)}, u32[]{:S(2)}) collective-permute-start(bf16[1,1024]{1,0:T(2,128)(2,1)S(1)} %slice.53), channel_id=1, source_target_pairs={{0,1},{1,2},{2,3},{3,4},{4,5},{5,6},{6,7},{7,8},{8,9},{9,10},{10,1... | collective-permute-start | bytes 6152 | tf_op jit(solution)/shard_map/ppermute | solution.py:24
  159.9 2.4 %shard_map.49 = bf16[512,1024]{1,0:T(8,128)(2,1)} custom-call(bf16[512,1024]{1,0:T(8,128)(2,1)} %copy-done.3, bf16[128,1024]{1,0:T(8,128)(2,1)} %pad_select_fusion.lift_ref), custom_call_target="tpu_custom_call" | custom-call | tf_op jit(solution)/shard_map/pallas_call | solution.py:157
  162.3 1.3 fusion.12
  (57 shorter events, 10.2 us)
Async XLA Ops:
  0.0 152.6 %copy-start = (bf16[1024,1024]{1,0:T(8,128)(2,1)S(1)}, bf16[1024,1024]{1,0:T(8,128)(2,1)}, u32[]{:S(2)}) copy-start(bf16[1024,1024]{1,0:T(8,128)(2,1)} %param.7) | copy-start | bytes 6291460
  0.0 38.7 %copy-start.5 = (s32[2048]{0:T(1024)S(1)}, s32[2048]{0:T(1024)}, u32[]{:S(2)}) copy-start(s32[2048]{0:T(1024)} %param.5) | copy-start | bytes 24580
  0.0 40.6 %collective-permute-start.1 = (bf16[3,512,1024]{2,1,0:T(8,128)(2,1)}, bf16[3,512,1024]{2,1,0:T(8,128)(2,1)}, u32[]{:S(2)}, u32[]{:S(2)}) collective-permute-start(bf16[3,512,1024]{2,1,0:T(8,128)(2,1)} %bitcast.53), channel_id=1, source_target_pairs={{0,1},{2,3},{4,5},{6,7},{8,9},{10,11},{12,13},{14,15},{16,17},{18,... | collective-permute-start | bytes 9437192 | tf_op jit(solution)/shard_map/ppermute | solution.py:173
  4.1 23.9 %collective-permute-start = (bf16[2,512,512]{2,1,0:T(8,128)(2,1)S(1)}, bf16[2,512,512]{2,1,0:T(8,128)(2,1)}, u32[]{:S(2)}, u32[]{:S(2)}) collective-permute-start(bf16[2,512,512]{2,1,0:T(8,128)(2,1)S(1)} %get-tuple-element.20), channel_id=1, source_target_pairs={{0,2},{1,3},{2,4},{3,5},{4,6},{5,7},{6,8},{7,9},{8,10},{9,11},{10,... | collective-permute-start | bytes 3145736 | tf_op jit(solution)/shard_map/ppermute | solution.py:24
  28.0 12.6 %collective-permute-start.2 = (bf16[2,512,512]{2,1,0:T(8,128)(2,1)}, bf16[2,512,512]{2,1,0:T(8,128)(2,1)}, u32[]{:S(2)}, u32[]{:S(2)}) collective-permute-start(bf16[2,512,512]{2,1,0:T(8,128)(2,1)} %collective-permute-done.k0_ref.v0_ref), channel_id=1, source_target_pairs={{1,0},{3,2},{5,4},{7,6},{9,8},{11,10},{13,12},{15,14},{17,16},{19,... | collective-permute-start | bytes 3145736 | tf_op jit(solution)/shard_map/ppermute | solution.py:173
  34.6 26.2 %collective-permute-start.3 = (bf16[2,512,512]{2,1,0:T(8,128)(2,1)}, bf16[2,512,512]{2,1,0:T(8,128)(2,1)S(1)}, u32[]{:S(2)}, u32[]{:S(2)}) collective-permute-start(bf16[2,512,512]{2,1,0:T(8,128)(2,1)} %get-tuple-element.12), channel_id=1, source_target_pairs={{0,2},{1,3},{2,4},{3,5},{4,6},{5,7},{6,8},{7,9},{8,10},{9,11},{10,... | collective-permute-start | bytes 3145736 | tf_op jit(solution)/shard_map/ppermute | solution.py:24
  60.8 3.7 %copy-start.2 = (bf16[2,512,512]{2,1,0:T(8,128)(2,1)}, bf16[2,512,512]{2,1,0:T(8,128)(2,1)S(1)}, u32[]{:S(2)}) copy-start(bf16[2,512,512]{2,1,0:T(8,128)(2,1)S(1)} %collective-permute-done.3.k0_ref.v0_ref) | copy-start | bytes 3145732
  60.8 3.7 %collective-permute-start.4 = (bf16[2,512,512]{2,1,0:T(8,128)(2,1)S(1)}, bf16[2,512,512]{2,1,0:T(8,128)(2,1)}, u32[]{:S(2)}, u32[]{:S(2)}) collective-permute-start(bf16[2,512,512]{2,1,0:T(8,128)(2,1)S(1)} %collective-permute-done.3.k0_ref.v0_ref), channel_id=1, source_target_pairs={{1,0},{3,2},{5,4},{7,6},{9,8},{11,10},{13,12},{15,14},{17,16},{19,... | collective-permute-start | bytes 3145736 | tf_op jit(solution)/shard_map/ppermute | solution.py:173
  83.7 7.6 %collective-permute-start.5 = (bf16[3,128,256]{2,1,0:T(8,128)(2,1)}, bf16[3,128,256]{2,1,0:T(8,128)(2,1)S(1)}, u32[]{:S(2)}, u32[]{:S(2)}) collective-permute-start(bf16[3,128,256]{2,1,0:T(8,128)(2,1)} %get-tuple-element.23), channel_id=1, source_target_pairs={{0,3},{1,0},{2,1},{3,2},{4,7},{5,4},{6,5},{7,6},{8,11},{9,8},{10,9... | collective-permute-start | bytes 589832 | tf_op jit(solution)/shard_map/ppermute | solution.py:33
  84.1 7.2 %collective-permute-start.6 = (bf16[3,128,256]{2,1,0:T(8,128)(2,1)S(1)}, bf16[3,128,256]{2,1,0:T(8,128)(2,1)S(1)}, u32[]{:S(2)}, u32[]{:S(2)}) collective-permute-start(bf16[3,128,256]{2,1,0:T(8,128)(2,1)S(1)} %get-tuple-element.22), channel_id=1, source_target_pairs={{0,2},{1,3},{2,0},{3,1},{4,6},{5,7},{6,4},{7,5},{8,10},{9,11},{10,... | collective-permute-start | bytes 589832 | tf_op jit(solution)/shard_map/ppermute | solution.py:33
  84.1 8.6 %collective-permute-start.7 = (bf16[3,128,256]{2,1,0:T(8,128)(2,1)S(1)}, bf16[3,128,256]{2,1,0:T(8,128)(2,1)S(1)}, u32[]{:S(2)}, u32[]{:S(2)}) collective-permute-start(bf16[3,128,256]{2,1,0:T(8,128)(2,1)S(1)} %get-tuple-element.21), channel_id=1, source_target_pairs={{0,1},{1,2},{2,3},{3,0},{4,5},{5,6},{6,7},{7,4},{8,9},{9,10},{10,1... | collective-permute-start | bytes 589832 | tf_op jit(solution)/shard_map/ppermute | solution.py:33
  93.0 40.8 %copy-start.1 = (bf16[2,4,128,256]{3,2,1,0:T(8,128)(2,1)}, bf16[2,4,128,256]{3,2,1,0:T(8,128)(2,1)S(1)}, u32[]{:S(2)}) copy-start(bf16[2,4,128,256]{3,2,1,0:T(8,128)(2,1)S(1)} %copy.8) | copy-start | bytes 1572868
  93.0 14.7 %collective-permute-start.8 = (bf16[2,512,256]{2,1,0:T(8,128)(2,1)S(1)}, bf16[2,512,256]{2,1,0:T(8,128)(2,1)S(1)}, u32[]{:S(2)}, u32[]{:S(2)}) collective-permute-start(bf16[2,512,256]{2,1,0:T(8,128)(2,1)S(1)} %bitcast.63), channel_id=1, source_target_pairs={{0,4},{1,5},{2,6},{3,7},{4,8},{5,9},{6,10},{7,11},{8,12},{9,13},{1... | collective-permute-start | bytes 1572872 | tf_op jit(solution)/shard_map/ppermute | solution.py:24
  107.8 0.8 copy-start.4
  108.6 12.9 %collective-permute-start.9 = (bf16[2,512,256]{2,1,0:T(8,128)(2,1)S(1)}, bf16[2,512,256]{2,1,0:T(8,128)(2,1)}, u32[]{:S(2)}, u32[]{:S(2)}) collective-permute-start(bf16[2,512,256]{2,1,0:T(8,128)(2,1)S(1)} %collective-permute-done.8.k2_ref.v2_ref), channel_id=1, source_target_pairs={{0,4},{1,5},{2,6},{3,7},{4,8},{5,9},{6,10},{7,11},{8,12},{9,13},{1... | collective-permute-start | bytes 1572872 | tf_op jit(solution)/shard_map/ppermute | solution.py:24
  121.5 12.4 %collective-permute-start.10 = (bf16[2,512,256]{2,1,0:T(8,128)(2,1)}, bf16[2,512,256]{2,1,0:T(8,128)(2,1)}, u32[]{:S(2)}, u32[]{:S(2)}) collective-permute-start(bf16[2,512,256]{2,1,0:T(8,128)(2,1)} %collective-permute-done.9.k1_ref.v1_ref), channel_id=1, source_target_pairs={{0,4},{1,5},{2,6},{3,7},{4,8},{5,9},{6,10},{7,11},{8,12},{9,13},{1... | collective-permute-start | bytes 1572872 | tf_op jit(solution)/shard_map/ppermute | solution.py:24
  130.3 1.1 copy-start.3
  143.5 6.9 %collective-permute-start.11 = (bf16[128,256]{1,0:T(8,128)(2,1)S(1)}, bf16[128,256]{1,0:T(8,128)(2,1)S(1)}, u32[]{:S(2)}, u32[]{:S(2)}) collective-permute-start(bf16[128,256]{1,0:T(8,128)(2,1)S(1)} %get-tuple-element.26), channel_id=1, source_target_pairs={{0,3},{1,0},{2,1},{3,2},{4,7},{5,4},{6,5},{7,6},{8,11},{9,8},{10,9... | collective-permute-start | bytes 196616 | tf_op jit(solution)/shard_map/ppermute | solution.py:33
  147.8 3.7 %collective-permute-start.12 = (bf16[128,256]{1,0:T(8,128)(2,1)S(1)}, bf16[128,256]{1,0:T(8,128)(2,1)S(1)}, u32[]{:S(2)}, u32[]{:S(2)}) collective-permute-start(bf16[128,256]{1,0:T(8,128)(2,1)S(1)} %get-tuple-element.25), channel_id=1, source_target_pairs={{0,2},{1,3},{2,0},{3,1},{4,6},{5,7},{6,4},{7,5},{8,10},{9,11},{10,... | collective-permute-start | bytes 196616 | tf_op jit(solution)/shard_map/ppermute | solution.py:33
  147.8 3.7 %collective-permute-start.13 = (bf16[128,256]{1,0:T(8,128)(2,1)S(1)}, bf16[128,256]{1,0:T(8,128)(2,1)S(1)}, u32[]{:S(2)}, u32[]{:S(2)}) collective-permute-start(bf16[128,256]{1,0:T(8,128)(2,1)S(1)} %get-tuple-element.24), channel_id=1, source_target_pairs={{0,1},{1,2},{2,3},{3,0},{4,5},{5,6},{6,7},{7,4},{8,9},{9,10},{10,1... | collective-permute-start | bytes 196616 | tf_op jit(solution)/shard_map/ppermute | solution.py:33
  153.1 9.2 %collective-permute-start.14 = (bf16[1,1024]{1,0:T(2,128)(2,1)S(1)}, bf16[1,1024]{1,0:T(2,128)(2,1)S(1)}, u32[]{:S(2)}, u32[]{:S(2)}) collective-permute-start(bf16[1,1024]{1,0:T(2,128)(2,1)S(1)} %slice.53), channel_id=1, source_target_pairs={{0,1},{1,2},{2,3},{3,4},{4,5},{5,6},{6,7},{7,8},{8,9},{9,10},{10,1... | collective-permute-start | bytes 6152 | tf_op jit(solution)/shard_map/ppermute | solution.py:24

commit v24 on v21

--- a/solution.py
+++ b/solution.py
@@ -153,7 +153,7 @@
 
 def mix(fine_out, lifted):
     tok, width = fine_out.shape
-    tile = min(FINE_TILE, tok)
+    tile = min(FINE_TILE // 2, tok)
     return pl.pallas_call(
         mix_kernel,
         grid=(tok // tile,),

time: 162 us -> 164 us (1.012)
  transfers between devices with their start and end apart: 15 -> 15, of which waited for: 9 -> 9; matrix products, arithmetic and copies ran while one was open for 9% -> 9% of each run, Pallas kernels for 11% -> 12%
where the time goes in v24:
time: 164 us; the launch traced here: 163 us
  waiting for transfers between devices  51.4 us (31%)
  starting transfers between devices  46.4 us (28%)
  Pallas kernels  41.1 us (25%)
  local copies, waits for them, and re-layouts  14.2 us (9%)
  matrix products  7.22 us (4%)
  other arithmetic  2.28 us (1%)
    ppermute x6, waiting for transfers between devices, passed_along(): lax.ppermute(value, axis, [(source, source + steps) for source in range(f...  42 us
    pallas_call x2, Pallas kernels, fine_attention(): pl.pallas_call(kernel, grid=(nq, pairs), in_specs=[pl.BlockSpec((tile, 1)...  30.8 us
    ppermute x6, starting transfers between devices, passed_along(): lax.ppermute(value, axis, [(source, source + steps) for source in range(f...  28.1 us
    ppermute x3, starting transfers between devices, pair_swap(): lax.ppermute(value, axis, [(source, source + step) for source in range(st...  10.3 us
    ppermute x6, starting transfers between devices, within_group(): return lax.ppermute(value, axis, pairs)  8.04 us
    ppermute x6, waiting for transfers between devices, within_group(): return lax.ppermute(value, axis, pairs)  8.03 us
    dot_general x2, matrix products, body(): jnp.einsum('rd,mdc->mrc', part_pool, part_weight, preferred_element_type=...  6.75 us
    pallas_call x1, Pallas kernels, coarse_attention(): pl.pallas_call(kernel, grid=(heads, rows // tile), in_specs=[pl.BlockSpec...  6.6 us
  transfers between devices with their start and end apart: 15, of which 9 were waited for; matrix products, arithmetic and copies ran while one was open for 9% of the time, Pallas kernels for 12%

profile of v24, /device:TPU:7, one launch (start us, length us, event | category | flops | bytes accessed | tf_op | source)
XLA Modules:
  0.0 162.9 jit_solution(6169382032033769196)
XLA Ops:
  0.0 1.4 collective-permute-start.1
  1.4 2.7 %fusion.16 = (bf16[2,512,512]{2,1,0:T(8,128)(2,1)}, bf16[2,512,512]{2,1,0:T(8,128)(2,1)S(1)}) fusion(bf16[3,512,1024]{2,1,0:T(8,128)(2,1)} %bitcast.54), kind=kLoop, calls=%fused_computation.46 | loop fusion | bytes 4194304 | tf_op jit(solution)/shard_map/slice | solution.py:311
  4.1 3.1 %collective-permute-start = (bf16[2,512,512]{2,1,0:T(8,128)(2,1)S(1)}, bf16[2,512,512]{2,1,0:T(8,128)(2,1)}, u32[]{:S(2)}, u32[]{:S(2)}) collective-permute-start(bf16[2,512,512]{2,1,0:T(8,128)(2,1)S(1)} %get-tuple-element.20), channel_id=1, source_target_pairs={{0,2},{1,3},{2,4},{3,5},{4,6},{5,7},{6,8},{7,9},{8,10},{9,11},{10,... | collective-permute-start | bytes 3145736 | tf_op jit(solution)/shard_map/ppermute | solution.py:24
  7.3 20.7 %collective-permute-done.k0_ref.v0_ref = bf16[2,512,512]{2,1,0:T(8,128)(2,1)} collective-permute-done((bf16[2,512,512]{2,1,0:T(8,128)(2,1)S(1)}, bf16[2,512,512]{2,1,0:T(8,128)(2,1)}, u32[]{:S(2)}, u32[]{:S(2)}) %collective-permute-start) | collective-permute-done | bytes 1048608 | tf_op jit(solution)/shard_map/ppermute | solution.py:24
  28.0 6.6 %collective-permute-start.2 = (bf16[2,512,512]{2,1,0:T(8,128)(2,1)}, bf16[2,512,512]{2,1,0:T(8,128)(2,1)}, u32[]{:S(2)}, u32[]{:S(2)}) collective-permute-start(bf16[2,512,512]{2,1,0:T(8,128)(2,1)} %collective-permute-done.k0_ref.v0_ref), channel_id=1, source_target_pairs={{1,0},{3,2},{5,4},{7,6},{9,8},{11,10},{13,12},{15,14},{17,16},{19,... | collective-permute-start | bytes 3145736 | tf_op jit(solution)/shard_map/ppermute | solution.py:173
  34.6 4.0 %collective-permute-start.3 = (bf16[2,512,512]{2,1,0:T(8,128)(2,1)}, bf16[2,512,512]{2,1,0:T(8,128)(2,1)S(1)}, u32[]{:S(2)}, u32[]{:S(2)}) collective-permute-start(bf16[2,512,512]{2,1,0:T(8,128)(2,1)} %get-tuple-element.12), channel_id=1, source_target_pairs={{0,2},{1,3},{2,4},{3,5},{4,6},{5,7},{6,8},{7,9},{8,10},{9,11},{10,... | collective-permute-start | bytes 3145736 | tf_op jit(solution)/shard_map/ppermute | solution.py:24
  40.6 15.3 %shard_map.46 = (bf16[512,512]{1,0:T(8,128)(2,1)}, bf16[128,512]{1,0:T(8,128)(2,1)}) custom-call(s32[512,1]{1,0:T(8,128)} %reshape_reshape.10.qclip_ref, s32[1,1536]{1,0:T(1,128)} %reshape_reshape.9.kclip0_ref.kclip1_ref.kclip2_ref, s32[1,1536]{1,0:T(1,128)} %reshape_reshape.9.kclip0_ref.kclip1_ref.kclip2_ref, ...), custom_call_target="tpu_custom_call" | custom-call | tf_op jit(solution)/shard_map/pallas_call | solution.py:117
  55.9 3.7 %fusion.5 = f32[3,128,1024]{2,1,0:T(8,128)} fusion(bf16[3,1024,1024]{2,1,0:T(8,128)(2,1)} %bitcast.61, bf16[128,512]{1,0:T(8,128)(2,1)} %get-tuple-element.13), kind=kOutput, calls=%fused_computation.6 | convolution fusion | flops 402653184 | bytes 4849664 | tf_op jit(solution)/shard_map/rd,mdc->mrc/dot_general | solution.py:326
  59.7 1.1 collective-permute-done.3.k0_ref.v0_ref
  60.8 2.3 %collective-permute-start.4 = (bf16[2,512,512]{2,1,0:T(8,128)(2,1)S(1)}, bf16[2,512,512]{2,1,0:T(8,128)(2,1)}, u32[]{:S(2)}, u32[]{:S(2)}) collective-permute-start(bf16[2,512,512]{2,1,0:T(8,128)(2,1)S(1)} %collective-permute-done.3.k0_ref.v0_ref), channel_id=1, source_target_pairs={{1,0},{3,2},{5,4},{7,6},{9,8},{11,10},{13,12},{15,14},{17,16},{19,... | collective-permute-start | bytes 3145736 | tf_op jit(solution)/shard_map/ppermute | solution.py:173
  63.1 1.4 collective-permute-done.4.k1b_ref.v1b_ref
  64.5 15.5 %shard_map.47 = (bf16[512,512]{1,0:T(8,128)(2,1)}, bf16[128,512]{1,0:T(8,128)(2,1)}) custom-call(s32[512,1]{1,0:T(8,128)} %reshape_reshape.10.qclip_ref, s32[1,1536]{1,0:T(1,128)} %reshape_reshape.9.kclip0_ref.kclip1_ref.kclip2_ref, s32[1,1536]{1,0:T(1,128)} %reshape_reshape.9.kclip0_ref.kclip1_ref.kclip2_ref, ...), custom_call_target="tpu_custom_call" | custom-call | tf_op jit(solution)/shard_map/pallas_call | solution.py:117
  79.9 3.0 %fusion.4 = bf16[3,128,1024]{2,1,0:T(8,128)(2,1)S(1)} fusion(f32[3,128,1024]{2,1,0:T(8,128)} %fusion.5, bf16[3,1024,1024]{2,1,0:T(8,128)(2,1)} %bitcast.62, bf16[128,512]{1,0:T(8,128)(2,1)} %get-tuple-element.16), kind=kOutput, calls=%fused_computation.5 | convolution fusion | flops 403439616 | bytes 5636096 | tf_op jit(solution)/shard_map/rd,mdc->mrc/dot_general | solution.py:326
  84.1 1.6 %collective-permute-start.7 = (bf16[3,128,256]{2,1,0:T(8,128)(2,1)S(1)}, bf16[3,128,256]{2,1,0:T(8,128)(2,1)S(1)}, u32[]{:S(2)}, u32[]{:S(2)}) collective-permute-start(bf16[3,128,256]{2,1,0:T(8,128)(2,1)S(1)} %get-tuple-element.21), channel_id=1, source_target_pairs={{0,1},{1,2},{2,3},{3,0},{4,5},{5,6},{6,7},{7,4},{8,9},{9,10},{10,1... | collective-permute-start | bytes 589832 | tf_op jit(solution)/shard_map/ppermute | solution.py:33
  85.8 5.6 %collective-permute-done.5 = bf16[3,128,256]{2,1,0:T(8,128)(2,1)S(1)} collective-permute-done((bf16[3,128,256]{2,1,0:T(8,128)(2,1)}, bf16[3,128,256]{2,1,0:T(8,128)(2,1)S(1)}, u32[]{:S(2)}, u32[]{:S(2)}) %collective-permute-start.5) | collective-permute-done | bytes 196640 | tf_op jit(solution)/shard_map/ppermute | solution.py:33
  91.4 1.4 collective-permute-done.7
  93.0 5.0 %collective-permute-start.8 = (bf16[2,512,256]{2,1,0:T(8,128)(2,1)S(1)}, bf16[2,512,256]{2,1,0:T(8,128)(2,1)S(1)}, u32[]{:S(2)}, u32[]{:S(2)}) collective-permute-start(bf16[2,512,256]{2,1,0:T(8,128)(2,1)S(1)} %bitcast.63), channel_id=1, source_target_pairs={{0,4},{1,5},{2,6},{3,7},{4,8},{5,9},{6,10},{7,11},{8,12},{9,13},{1... | collective-permute-start | bytes 1572872 | tf_op jit(solution)/shard_map/ppermute | solution.py:24
  98.1 9.7 %collective-permute-done.8.k2_ref.v2_ref = bf16[2,512,256]{2,1,0:T(8,128)(2,1)S(1)} collective-permute-done((bf16[2,512,256]{2,1,0:T(8,128)(2,1)S(1)}, bf16[2,512,256]{2,1,0:T(8,128)(2,1)S(1)}, u32[]{:S(2)}, u32[]{:S(2)}) %collective-permute-start.8) | collective-permute-done | bytes 524320 | tf_op jit(solution)/shard_map/ppermute | solution.py:24
  108.6 4.9 %collective-permute-start.9 = (bf16[2,512,256]{2,1,0:T(8,128)(2,1)S(1)}, bf16[2,512,256]{2,1,0:T(8,128)(2,1)}, u32[]{:S(2)}, u32[]{:S(2)}) collective-permute-start(bf16[2,512,256]{2,1,0:T(8,128)(2,1)S(1)} %collective-permute-done.8.k2_ref.v2_ref), channel_id=1, source_target_pairs={{0,4},{1,5},{2,6},{3,7},{4,8},{5,9},{6,10},{7,11},{8,12},{9,13},{1... | collective-permute-start | bytes 1572872 | tf_op jit(solution)/shard_map/ppermute | solution.py:24
  113.5 8.0 %collective-permute-done.9.k1_ref.v1_ref = bf16[2,512,256]{2,1,0:T(8,128)(2,1)} collective-permute-done((bf16[2,512,256]{2,1,0:T(8,128)(2,1)S(1)}, bf16[2,512,256]{2,1,0:T(8,128)(2,1)}, u32[]{:S(2)}, u32[]{:S(2)}) %collective-permute-start.9) | collective-permute-done | bytes 524320 | tf_op jit(solution)/shard_map/ppermute | solution.py:24
  121.5 5.0 %collective-permute-start.10 = (bf16[2,512,256]{2,1,0:T(8,128)(2,1)}, bf16[2,512,256]{2,1,0:T(8,128)(2,1)}, u32[]{:S(2)}, u32[]{:S(2)}) collective-permute-start(bf16[2,512,256]{2,1,0:T(8,128)(2,1)} %collective-permute-done.9.k1_ref.v1_ref), channel_id=1, source_target_pairs={{0,4},{1,5},{2,6},{3,7},{4,8},{5,9},{6,10},{7,11},{8,12},{9,13},{1... | collective-permute-start | bytes 1572872 | tf_op jit(solution)/shard_map/ppermute | solution.py:24
  128.1 1.1 constant_dynamic-update-slice_fusion.1
  129.2 1.1 constant_dynamic-update-slice_fusion.fine_ref
  131.4 2.5 %collective-permute-done.10.k0_ref.v0_ref = bf16[2,512,256]{2,1,0:T(8,128)(2,1)} collective-permute-done((bf16[2,512,256]{2,1,0:T(8,128)(2,1)}, bf16[2,512,256]{2,1,0:T(8,128)(2,1)}, u32[]{:S(2)}, u32[]{:S(2)}) %collective-permute-start.10) | collective-permute-done | bytes 524320 | tf_op jit(solution)/shard_map/ppermute | solution.py:24
  133.9 6.6 %shard_map.48 = bf16[512,256]{1,0:T(8,128)(2,1)} custom-call(s32[512,1]{1,0:T(8,128)} %copy.9.qclip_ref, s32[1,2048]{1,0:T(1,128)} %bitcast.69, s32[1,2048]{1,0:T(1,128)} %bitcast.70, s32[1,2048]{1,0:T(1,128)} %bitcast.71, s32[1,2048]{1,0:T(1,128)} %bitcast.72, bf16[512,256]{1,0:T(8,128)(2,1)} %bitcast.67, ...), custom_call_target="tpu_custom_call" | custom-call | tf_op jit(solution)/shard_map/pallas_call | solution.py:234
  140.5 0.9 constant_dynamic-slice_fusion
  141.4 4.3 %collective-permute-start.11 = (bf16[128,256]{1,0:T(8,128)(2,1)S(1)}, bf16[128,256]{1,0:T(8,128)(2,1)S(1)}, u32[]{:S(2)}, u32[]{:S(2)}) collective-permute-start(bf16[128,256]{1,0:T(8,128)(2,1)S(1)} %get-tuple-element.26), channel_id=1, source_target_pairs={{0,3},{1,0},{2,1},{3,2},{4,7},{5,4},{6,5},{7,6},{8,11},{9,8},{10,9... | collective-permute-start | bytes 196616 | tf_op jit(solution)/shard_map/ppermute | solution.py:33
  145.7 1.7 %collective-permute-start.13 = (bf16[128,256]{1,0:T(8,128)(2,1)S(1)}, bf16[128,256]{1,0:T(8,128)(2,1)S(1)}, u32[]{:S(2)}, u32[]{:S(2)}) collective-permute-start(bf16[128,256]{1,0:T(8,128)(2,1)S(1)} %get-tuple-element.24), channel_id=1, source_target_pairs={{0,1},{1,2},{2,3},{3,0},{4,5},{5,6},{6,7},{7,4},{8,9},{9,10},{10,1... | collective-permute-start | bytes 196616 | tf_op jit(solution)/shard_map/ppermute | solution.py:33
  148.3 1.1 collective-permute-done.12
  151.0 5.9 %collective-permute-start.14 = (bf16[1,1024]{1,0:T(2,128)(2,1)S(1)}, bf16[1,1024]{1,0:T(2,128)(2,1)S(1)}, u32[]{:S(2)}, u32[]{:S(2)}) collective-permute-start(bf16[1,1024]{1,0:T(2,128)(2,1)S(1)} %slice.53), channel_id=1, source_target_pairs={{0,1},{1,2},{2,3},{3,4},{4,5},{5,6},{6,7},{7,8},{8,9},{9,10},{10,1... | collective-permute-start | bytes 6152 | tf_op jit(solution)/shard_map/ppermute | solution.py:24
  157.8 3.7 %shard_map.49 = bf16[512,1024]{1,0:T(8,128)(2,1)} custom-call(bf16[512,1024]{1,0:T(8,128)(2,1)} %copy-done.3, bf16[128,1024]{1,0:T(8,128)(2,1)} %pad_select_fusion.lift_ref), custom_call_target="tpu_custom_call" | custom-call | tf_op jit(solution)/shard_map/pallas_call | solution.py:157
  161.6 1.3 fusion.12
  (57 shorter events, 10.2 us)
Async XLA Ops:
  0.0 150.5 %copy-start = (bf16[1024,1024]{1,0:T(8,128)(2,1)S(1)}, bf16[1024,1024]{1,0:T(8,128)(2,1)}, u32[]{:S(2)}) copy-start(bf16[1024,1024]{1,0:T(8,128)(2,1)} %param.7) | copy-start | bytes 6291460
  0.0 38.7 %copy-start.5 = (s32[2048]{0:T(1024)S(1)}, s32[2048]{0:T(1024)}, u32[]{:S(2)}) copy-start(s32[2048]{0:T(1024)} %param.5) | copy-start | bytes 24580
  0.0 40.6 %collective-permute-start.1 = (bf16[3,512,1024]{2,1,0:T(8,128)(2,1)}, bf16[3,512,1024]{2,1,0:T(8,128)(2,1)}, u32[]{:S(2)}, u32[]{:S(2)}) collective-permute-start(bf16[3,512,1024]{2,1,0:T(8,128)(2,1)} %bitcast.53), channel_id=1, source_target_pairs={{0,1},{2,3},{4,5},{6,7},{8,9},{10,11},{12,13},{14,15},{16,17},{18,... | collective-permute-start | bytes 9437192 | tf_op jit(solution)/shard_map/ppermute | solution.py:173
  4.1 23.9 %collective-permute-start = (bf16[2,512,512]{2,1,0:T(8,128)(2,1)S(1)}, bf16[2,512,512]{2,1,0:T(8,128)(2,1)}, u32[]{:S(2)}, u32[]{:S(2)}) collective-permute-start(bf16[2,512,512]{2,1,0:T(8,128)(2,1)S(1)} %get-tuple-element.20), channel_id=1, source_target_pairs={{0,2},{1,3},{2,4},{3,5},{4,6},{5,7},{6,8},{7,9},{8,10},{9,11},{10,... | collective-permute-start | bytes 3145736 | tf_op jit(solution)/shard_map/ppermute | solution.py:24
  28.0 12.6 %collective-permute-start.2 = (bf16[2,512,512]{2,1,0:T(8,128)(2,1)}, bf16[2,512,512]{2,1,0:T(8,128)(2,1)}, u32[]{:S(2)}, u32[]{:S(2)}) collective-permute-start(bf16[2,512,512]{2,1,0:T(8,128)(2,1)} %collective-permute-done.k0_ref.v0_ref), channel_id=1, source_target_pairs={{1,0},{3,2},{5,4},{7,6},{9,8},{11,10},{13,12},{15,14},{17,16},{19,... | collective-permute-start | bytes 3145736 | tf_op jit(solution)/shard_map/ppermute | solution.py:173
  34.6 26.2 %collective-permute-start.3 = (bf16[2,512,512]{2,1,0:T(8,128)(2,1)}, bf16[2,512,512]{2,1,0:T(8,128)(2,1)S(1)}, u32[]{:S(2)}, u32[]{:S(2)}) collective-permute-start(bf16[2,512,512]{2,1,0:T(8,128)(2,1)} %get-tuple-element.12), channel_id=1, source_target_pairs={{0,2},{1,3},{2,4},{3,5},{4,6},{5,7},{6,8},{7,9},{8,10},{9,11},{10,... | collective-permute-start | bytes 3145736 | tf_op jit(solution)/shard_map/ppermute | solution.py:24
  60.8 3.7 %copy-start.2 = (bf16[2,512,512]{2,1,0:T(8,128)(2,1)}, bf16[2,512,512]{2,1,0:T(8,128)(2,1)S(1)}, u32[]{:S(2)}) copy-start(bf16[2,512,512]{2,1,0:T(8,128)(2,1)S(1)} %collective-permute-done.3.k0_ref.v0_ref) | copy-start | bytes 3145732
  60.8 3.7 %collective-permute-start.4 = (bf16[2,512,512]{2,1,0:T(8,128)(2,1)S(1)}, bf16[2,512,512]{2,1,0:T(8,128)(2,1)}, u32[]{:S(2)}, u32[]{:S(2)}) collective-permute-start(bf16[2,512,512]{2,1,0:T(8,128)(2,1)S(1)} %collective-permute-done.3.k0_ref.v0_ref), channel_id=1, source_target_pairs={{1,0},{3,2},{5,4},{7,6},{9,8},{11,10},{13,12},{15,14},{17,16},{19,... | collective-permute-start | bytes 3145736 | tf_op jit(solution)/shard_map/ppermute | solution.py:173
  83.7 7.6 %collective-permute-start.5 = (bf16[3,128,256]{2,1,0:T(8,128)(2,1)}, bf16[3,128,256]{2,1,0:T(8,128)(2,1)S(1)}, u32[]{:S(2)}, u32[]{:S(2)}) collective-permute-start(bf16[3,128,256]{2,1,0:T(8,128)(2,1)} %get-tuple-element.23), channel_id=1, source_target_pairs={{0,3},{1,0},{2,1},{3,2},{4,7},{5,4},{6,5},{7,6},{8,11},{9,8},{10,9... | collective-permute-start | bytes 589832 | tf_op jit(solution)/shard_map/ppermute | solution.py:33
  84.1 7.2 %collective-permute-start.6 = (bf16[3,128,256]{2,1,0:T(8,128)(2,1)S(1)}, bf16[3,128,256]{2,1,0:T(8,128)(2,1)S(1)}, u32[]{:S(2)}, u32[]{:S(2)}) collective-permute-start(bf16[3,128,256]{2,1,0:T(8,128)(2,1)S(1)} %get-tuple-element.22), channel_id=1, source_target_pairs={{0,2},{1,3},{2,0},{3,1},{4,6},{5,7},{6,4},{7,5},{8,10},{9,11},{10,... | collective-permute-start | bytes 589832 | tf_op jit(solution)/shard_map/ppermute | solution.py:33
  84.1 8.6 %collective-permute-start.7 = (bf16[3,128,256]{2,1,0:T(8,128)(2,1)S(1)}, bf16[3,128,256]{2,1,0:T(8,128)(2,1)S(1)}, u32[]{:S(2)}, u32[]{:S(2)}) collective-permute-start(bf16[3,128,256]{2,1,0:T(8,128)(2,1)S(1)} %get-tuple-element.21), channel_id=1, source_target_pairs={{0,1},{1,2},{2,3},{3,0},{4,5},{5,6},{6,7},{7,4},{8,9},{9,10},{10,1... | collective-permute-start | bytes 589832 | tf_op jit(solution)/shard_map/ppermute | solution.py:33
  93.0 40.8 %copy-start.1 = (bf16[2,4,128,256]{3,2,1,0:T(8,128)(2,1)}, bf16[2,4,128,256]{3,2,1,0:T(8,128)(2,1)S(1)}, u32[]{:S(2)}) copy-start(bf16[2,4,128,256]{3,2,1,0:T(8,128)(2,1)S(1)} %copy.8) | copy-start | bytes 1572868
  93.0 14.7 %collective-permute-start.8 = (bf16[2,512,256]{2,1,0:T(8,128)(2,1)S(1)}, bf16[2,512,256]{2,1,0:T(8,128)(2,1)S(1)}, u32[]{:S(2)}, u32[]{:S(2)}) collective-permute-start(bf16[2,512,256]{2,1,0:T(8,128)(2,1)S(1)} %bitcast.63), channel_id=1, source_target_pairs={{0,4},{1,5},{2,6},{3,7},{4,8},{5,9},{6,10},{7,11},{8,12},{9,13},{1... | collective-permute-start | bytes 1572872 | tf_op jit(solution)/shard_map/ppermute | solution.py:24
  107.8 0.8 copy-start.4
  108.6 12.9 %collective-permute-start.9 = (bf16[2,512,256]{2,1,0:T(8,128)(2,1)S(1)}, bf16[2,512,256]{2,1,0:T(8,128)(2,1)}, u32[]{:S(2)}, u32[]{:S(2)}) collective-permute-start(bf16[2,512,256]{2,1,0:T(8,128)(2,1)S(1)} %collective-permute-done.8.k2_ref.v2_ref), channel_id=1, source_target_pairs={{0,4},{1,5},{2,6},{3,7},{4,8},{5,9},{6,10},{7,11},{8,12},{9,13},{1... | collective-permute-start | bytes 1572872 | tf_op jit(solution)/shard_map/ppermute | solution.py:24
  121.5 12.4 %collective-permute-start.10 = (bf16[2,512,256]{2,1,0:T(8,128)(2,1)}, bf16[2,512,256]{2,1,0:T(8,128)(2,1)}, u32[]{:S(2)}, u32[]{:S(2)}) collective-permute-start(bf16[2,512,256]{2,1,0:T(8,128)(2,1)} %collective-permute-done.9.k1_ref.v1_ref), channel_id=1, source_target_pairs={{0,4},{1,5},{2,6},{3,7},{4,8},{5,9},{6,10},{7,11},{8,12},{9,13},{1... | collective-permute-start | bytes 1572872 | tf_op jit(solution)/shard_map/ppermute | solution.py:24
  130.3 1.1 copy-start.3
  141.4 6.9 %collective-permute-start.11 = (bf16[128,256]{1,0:T(8,128)(2,1)S(1)}, bf16[128,256]{1,0:T(8,128)(2,1)S(1)}, u32[]{:S(2)}, u32[]{:S(2)}) collective-permute-start(bf16[128,256]{1,0:T(8,128)(2,1)S(1)} %get-tuple-element.26), channel_id=1, source_target_pairs={{0,3},{1,0},{2,1},{3,2},{4,7},{5,4},{6,5},{7,6},{8,11},{9,8},{10,9... | collective-permute-start | bytes 196616 | tf_op jit(solution)/shard_map/ppermute | solution.py:33
  145.7 3.7 %collective-permute-start.12 = (bf16[128,256]{1,0:T(8,128)(2,1)S(1)}, bf16[128,256]{1,0:T(8,128)(2,1)S(1)}, u32[]{:S(2)}, u32[]{:S(2)}) collective-permute-start(bf16[128,256]{1,0:T(8,128)(2,1)S(1)} %get-tuple-element.25), channel_id=1, source_target_pairs={{0,2},{1,3},{2,0},{3,1},{4,6},{5,7},{6,4},{7,5},{8,10},{9,11},{10,... | collective-permute-start | bytes 196616 | tf_op jit(solution)/shard_map/ppermute | solution.py:33
  145.7 3.7 %collective-permute-start.13 = (bf16[128,256]{1,0:T(8,128)(2,1)S(1)}, bf16[128,256]{1,0:T(8,128)(2,1)S(1)}, u32[]{:S(2)}, u32[]{:S(2)}) collective-permute-start(bf16[128,256]{1,0:T(8,128)(2,1)S(1)} %get-tuple-element.24), channel_id=1, source_target_pairs={{0,1},{1,2},{2,3},{3,0},{4,5},{5,6},{6,7},{7,4},{8,9},{9,10},{10,1... | collective-permute-start | bytes 196616 | tf_op jit(solution)/shard_map/ppermute | solution.py:33
  151.0 10.5 %collective-permute-start.14 = (bf16[1,1024]{1,0:T(2,128)(2,1)S(1)}, bf16[1,1024]{1,0:T(2,128)(2,1)S(1)}, u32[]{:S(2)}, u32[]{:S(2)}) collective-permute-start(bf16[1,1024]{1,0:T(2,128)(2,1)S(1)} %slice.53), channel_id=1, source_target_pairs={{0,1},{1,2},{2,3},{3,4},{4,5},{5,6},{6,7},{7,8},{8,9},{9,10},{10,1... | collective-permute-start | bytes 6152 | tf_op jit(solution)/shard_map/ppermute | solution.py:24

commit v25 on v24

--- a/solution.py
+++ b/solution.py
@@ -153,7 +153,7 @@
 
 def mix(fine_out, lifted):
     tok, width = fine_out.shape
-    tile = min(FINE_TILE // 2, tok)
+    tile = min(2 * FINE_TILE, tok)
     return pl.pallas_call(
         mix_kernel,
         grid=(tok // tile,),

time: 164 us -> 163 us (level)
  transfers between devices with their start and end apart: 15 -> 15, of which waited for: 9 -> 9; matrix products, arithmetic and copies ran while one was open for 9% -> 9% of each run, Pallas kernels for 12% -> 11%
where the time goes in v25:
time: 163 us; the launch traced here: 162 us
  waiting for transfers between devices  51.4 us (32%)
  starting transfers between devices  46.4 us (28%)
  Pallas kernels  40 us (25%)
  local copies, waits for them, and re-layouts  14.2 us (9%)
  matrix products  7.22 us (4%)
  other arithmetic  2.28 us (1%)
    ppermute x6, waiting for transfers between devices, passed_along(): lax.ppermute(value, axis, [(source, source + steps) for source in range(f...  42 us
    pallas_call x2, Pallas kernels, fine_attention(): pl.pallas_call(kernel, grid=(nq, pairs), in_specs=[pl.BlockSpec((tile, 1)...  30.8 us
    ppermute x6, starting transfers between devices, passed_along(): lax.ppermute(value, axis, [(source, source + steps) for source in range(f...  28.1 us
    ppermute x3, starting transfers between devices, pair_swap(): lax.ppermute(value, axis, [(source, source + step) for source in range(st...  10.3 us
    ppermute x6, starting transfers between devices, within_group(): return lax.ppermute(value, axis, pairs)  8.04 us
    ppermute x6, waiting for transfers between devices, within_group(): return lax.ppermute(value, axis, pairs)  8.03 us
    dot_general x2, matrix products, body(): jnp.einsum('rd,mdc->mrc', part_pool, part_weight, preferred_element_type=...  6.75 us
    pallas_call x1, Pallas kernels, coarse_attention(): pl.pallas_call(kernel, grid=(heads, rows // tile), in_specs=[pl.BlockSpec...  6.6 us
  transfers between devices with their start and end apart: 15, of which 9 were waited for; matrix products, arithmetic and copies ran while one was open for 9% of the time, Pallas kernels for 11%

profile of v25, /device:TPU:7, one launch (start us, length us, event | category | flops | bytes accessed | tf_op | source)
XLA Modules:
  0.0 161.8 jit_solution(6650050274568724257)
XLA Ops:
  0.0 1.4 collective-permute-start.1
  1.4 2.7 %fusion.16 = (bf16[2,512,512]{2,1,0:T(8,128)(2,1)}, bf16[2,512,512]{2,1,0:T(8,128)(2,1)S(1)}) fusion(bf16[3,512,1024]{2,1,0:T(8,128)(2,1)} %bitcast.54), kind=kLoop, calls=%fused_computation.46 | loop fusion | bytes 4194304 | tf_op jit(solution)/shard_map/slice | solution.py:311
  4.1 3.1 %collective-permute-start = (bf16[2,512,512]{2,1,0:T(8,128)(2,1)S(1)}, bf16[2,512,512]{2,1,0:T(8,128)(2,1)}, u32[]{:S(2)}, u32[]{:S(2)}) collective-permute-start(bf16[2,512,512]{2,1,0:T(8,128)(2,1)S(1)} %get-tuple-element.20), channel_id=1, source_target_pairs={{0,2},{1,3},{2,4},{3,5},{4,6},{5,7},{6,8},{7,9},{8,10},{9,11},{10,... | collective-permute-start | bytes 3145736 | tf_op jit(solution)/shard_map/ppermute | solution.py:24
  7.3 20.7 %collective-permute-done.k0_ref.v0_ref = bf16[2,512,512]{2,1,0:T(8,128)(2,1)} collective-permute-done((bf16[2,512,512]{2,1,0:T(8,128)(2,1)S(1)}, bf16[2,512,512]{2,1,0:T(8,128)(2,1)}, u32[]{:S(2)}, u32[]{:S(2)}) %collective-permute-start) | collective-permute-done | bytes 1048608 | tf_op jit(solution)/shard_map/ppermute | solution.py:24
  28.0 6.6 %collective-permute-start.2 = (bf16[2,512,512]{2,1,0:T(8,128)(2,1)}, bf16[2,512,512]{2,1,0:T(8,128)(2,1)}, u32[]{:S(2)}, u32[]{:S(2)}) collective-permute-start(bf16[2,512,512]{2,1,0:T(8,128)(2,1)} %collective-permute-done.k0_ref.v0_ref), channel_id=1, source_target_pairs={{1,0},{3,2},{5,4},{7,6},{9,8},{11,10},{13,12},{15,14},{17,16},{19,... | collective-permute-start | bytes 3145736 | tf_op jit(solution)/shard_map/ppermute | solution.py:173
  34.6 4.0 %collective-permute-start.3 = (bf16[2,512,512]{2,1,0:T(8,128)(2,1)}, bf16[2,512,512]{2,1,0:T(8,128)(2,1)S(1)}, u32[]{:S(2)}, u32[]{:S(2)}) collective-permute-start(bf16[2,512,512]{2,1,0:T(8,128)(2,1)} %get-tuple-element.12), channel_id=1, source_target_pairs={{0,2},{1,3},{2,4},{3,5},{4,6},{5,7},{6,8},{7,9},{8,10},{9,11},{10,... | collective-permute-start | bytes 3145736 | tf_op jit(solution)/shard_map/ppermute | solution.py:24
  40.6 15.3 %shard_map.46 = (bf16[512,512]{1,0:T(8,128)(2,1)}, bf16[128,512]{1,0:T(8,128)(2,1)}) custom-call(s32[512,1]{1,0:T(8,128)} %reshape_reshape.10.qclip_ref, s32[1,1536]{1,0:T(1,128)} %reshape_reshape.9.kclip0_ref.kclip1_ref.kclip2_ref, s32[1,1536]{1,0:T(1,128)} %reshape_reshape.9.kclip0_ref.kclip1_ref.kclip2_ref, ...), custom_call_target="tpu_custom_call" | custom-call | tf_op jit(solution)/shard_map/pallas_call | solution.py:117
  55.9 3.7 %fusion.5 = f32[3,128,1024]{2,1,0:T(8,128)} fusion(bf16[3,1024,1024]{2,1,0:T(8,128)(2,1)} %bitcast.61, bf16[128,512]{1,0:T(8,128)(2,1)} %get-tuple-element.13), kind=kOutput, calls=%fused_computation.6 | convolution fusion | flops 402653184 | bytes 4849664 | tf_op jit(solution)/shard_map/rd,mdc->mrc/dot_general | solution.py:326
  59.7 1.1 collective-permute-done.3.k0_ref.v0_ref
  60.8 2.3 %collective-permute-start.4 = (bf16[2,512,512]{2,1,0:T(8,128)(2,1)S(1)}, bf16[2,512,512]{2,1,0:T(8,128)(2,1)}, u32[]{:S(2)}, u32[]{:S(2)}) collective-permute-start(bf16[2,512,512]{2,1,0:T(8,128)(2,1)S(1)} %collective-permute-done.3.k0_ref.v0_ref), channel_id=1, source_target_pairs={{1,0},{3,2},{5,4},{7,6},{9,8},{11,10},{13,12},{15,14},{17,16},{19,... | collective-permute-start | bytes 3145736 | tf_op jit(solution)/shard_map/ppermute | solution.py:173
  63.1 1.4 collective-permute-done.4.k1b_ref.v1b_ref
  64.5 15.5 %shard_map.47 = (bf16[512,512]{1,0:T(8,128)(2,1)}, bf16[128,512]{1,0:T(8,128)(2,1)}) custom-call(s32[512,1]{1,0:T(8,128)} %reshape_reshape.10.qclip_ref, s32[1,1536]{1,0:T(1,128)} %reshape_reshape.9.kclip0_ref.kclip1_ref.kclip2_ref, s32[1,1536]{1,0:T(1,128)} %reshape_reshape.9.kclip0_ref.kclip1_ref.kclip2_ref, ...), custom_call_target="tpu_custom_call" | custom-call | tf_op jit(solution)/shard_map/pallas_call | solution.py:117
  79.9 3.0 %fusion.4 = bf16[3,128,1024]{2,1,0:T(8,128)(2,1)S(1)} fusion(f32[3,128,1024]{2,1,0:T(8,128)} %fusion.5, bf16[3,1024,1024]{2,1,0:T(8,128)(2,1)} %bitcast.62, bf16[128,512]{1,0:T(8,128)(2,1)} %get-tuple-element.16), kind=kOutput, calls=%fused_computation.5 | convolution fusion | flops 403439616 | bytes 5636096 | tf_op jit(solution)/shard_map/rd,mdc->mrc/dot_general | solution.py:326
  84.1 1.6 %collective-permute-start.7 = (bf16[3,128,256]{2,1,0:T(8,128)(2,1)S(1)}, bf16[3,128,256]{2,1,0:T(8,128)(2,1)S(1)}, u32[]{:S(2)}, u32[]{:S(2)}) collective-permute-start(bf16[3,128,256]{2,1,0:T(8,128)(2,1)S(1)} %get-tuple-element.21), channel_id=1, source_target_pairs={{0,1},{1,2},{2,3},{3,0},{4,5},{5,6},{6,7},{7,4},{8,9},{9,10},{10,1... | collective-permute-start | bytes 589832 | tf_op jit(solution)/shard_map/ppermute | solution.py:33
  85.8 5.6 %collective-permute-done.5 = bf16[3,128,256]{2,1,0:T(8,128)(2,1)S(1)} collective-permute-done((bf16[3,128,256]{2,1,0:T(8,128)(2,1)}, bf16[3,128,256]{2,1,0:T(8,128)(2,1)S(1)}, u32[]{:S(2)}, u32[]{:S(2)}) %collective-permute-start.5) | collective-permute-done | bytes 196640 | tf_op jit(solution)/shard_map/ppermute | solution.py:33
  91.4 1.4 collective-permute-done.7
  93.0 5.0 %collective-permute-start.8 = (bf16[2,512,256]{2,1,0:T(8,128)(2,1)S(1)}, bf16[2,512,256]{2,1,0:T(8,128)(2,1)S(1)}, u32[]{:S(2)}, u32[]{:S(2)}) collective-permute-start(bf16[2,512,256]{2,1,0:T(8,128)(2,1)S(1)} %bitcast.63), channel_id=1, source_target_pairs={{0,4},{1,5},{2,6},{3,7},{4,8},{5,9},{6,10},{7,11},{8,12},{9,13},{1... | collective-permute-start | bytes 1572872 | tf_op jit(solution)/shard_map/ppermute | solution.py:24
  98.1 9.7 %collective-permute-done.8.k2_ref.v2_ref = bf16[2,512,256]{2,1,0:T(8,128)(2,1)S(1)} collective-permute-done((bf16[2,512,256]{2,1,0:T(8,128)(2,1)S(1)}, bf16[2,512,256]{2,1,0:T(8,128)(2,1)S(1)}, u32[]{:S(2)}, u32[]{:S(2)}) %collective-permute-start.8) | collective-permute-done | bytes 524320 | tf_op jit(solution)/shard_map/ppermute | solution.py:24
  108.6 4.9 %collective-permute-start.9 = (bf16[2,512,256]{2,1,0:T(8,128)(2,1)S(1)}, bf16[2,512,256]{2,1,0:T(8,128)(2,1)}, u32[]{:S(2)}, u32[]{:S(2)}) collective-permute-start(bf16[2,512,256]{2,1,0:T(8,128)(2,1)S(1)} %collective-permute-done.8.k2_ref.v2_ref), channel_id=1, source_target_pairs={{0,4},{1,5},{2,6},{3,7},{4,8},{5,9},{6,10},{7,11},{8,12},{9,13},{1... | collective-permute-start | bytes 1572872 | tf_op jit(solution)/shard_map/ppermute | solution.py:24
  113.5 8.0 %collective-permute-done.9.k1_ref.v1_ref = bf16[2,512,256]{2,1,0:T(8,128)(2,1)} collective-permute-done((bf16[2,512,256]{2,1,0:T(8,128)(2,1)S(1)}, bf16[2,512,256]{2,1,0:T(8,128)(2,1)}, u32[]{:S(2)}, u32[]{:S(2)}) %collective-permute-start.9) | collective-permute-done | bytes 524320 | tf_op jit(solution)/shard_map/ppermute | solution.py:24
  121.5 5.0 %collective-permute-start.10 = (bf16[2,512,256]{2,1,0:T(8,128)(2,1)}, bf16[2,512,256]{2,1,0:T(8,128)(2,1)}, u32[]{:S(2)}, u32[]{:S(2)}) collective-permute-start(bf16[2,512,256]{2,1,0:T(8,128)(2,1)} %collective-permute-done.9.k1_ref.v1_ref), channel_id=1, source_target_pairs={{0,4},{1,5},{2,6},{3,7},{4,8},{5,9},{6,10},{7,11},{8,12},{9,13},{1... | collective-permute-start | bytes 1572872 | tf_op jit(solution)/shard_map/ppermute | solution.py:24
  128.1 1.1 constant_dynamic-update-slice_fusion.1
  129.2 1.1 constant_dynamic-update-slice_fusion.fine_ref
  131.4 2.5 %collective-permute-done.10.k0_ref.v0_ref = bf16[2,512,256]{2,1,0:T(8,128)(2,1)} collective-permute-done((bf16[2,512,256]{2,1,0:T(8,128)(2,1)}, bf16[2,512,256]{2,1,0:T(8,128)(2,1)}, u32[]{:S(2)}, u32[]{:S(2)}) %collective-permute-start.10) | collective-permute-done | bytes 524320 | tf_op jit(solution)/shard_map/ppermute | solution.py:24
  133.9 6.6 %shard_map.48 = bf16[512,256]{1,0:T(8,128)(2,1)} custom-call(s32[512,1]{1,0:T(8,128)} %copy.9.qclip_ref, s32[1,2048]{1,0:T(1,128)} %bitcast.69, s32[1,2048]{1,0:T(1,128)} %bitcast.70, s32[1,2048]{1,0:T(1,128)} %bitcast.71, s32[1,2048]{1,0:T(1,128)} %bitcast.72, bf16[512,256]{1,0:T(8,128)(2,1)} %bitcast.67, ...), custom_call_target="tpu_custom_call" | custom-call | tf_op jit(solution)/shard_map/pallas_call | solution.py:234
  140.5 0.9 constant_dynamic-slice_fusion
  141.4 4.3 %collective-permute-start.11 = (bf16[128,256]{1,0:T(8,128)(2,1)S(1)}, bf16[128,256]{1,0:T(8,128)(2,1)S(1)}, u32[]{:S(2)}, u32[]{:S(2)}) collective-permute-start(bf16[128,256]{1,0:T(8,128)(2,1)S(1)} %get-tuple-element.26), channel_id=1, source_target_pairs={{0,3},{1,0},{2,1},{3,2},{4,7},{5,4},{6,5},{7,6},{8,11},{9,8},{10,9... | collective-permute-start | bytes 196616 | tf_op jit(solution)/shard_map/ppermute | solution.py:33
  145.7 1.7 %collective-permute-start.13 = (bf16[128,256]{1,0:T(8,128)(2,1)S(1)}, bf16[128,256]{1,0:T(8,128)(2,1)S(1)}, u32[]{:S(2)}, u32[]{:S(2)}) collective-permute-start(bf16[128,256]{1,0:T(8,128)(2,1)S(1)} %get-tuple-element.24), channel_id=1, source_target_pairs={{0,1},{1,2},{2,3},{3,0},{4,5},{5,6},{6,7},{7,4},{8,9},{9,10},{10,1... | collective-permute-start | bytes 196616 | tf_op jit(solution)/shard_map/ppermute | solution.py:33
  148.3 1.1 collective-permute-done.12
  151.0 5.9 %collective-permute-start.14 = (bf16[1,1024]{1,0:T(2,128)(2,1)S(1)}, bf16[1,1024]{1,0:T(2,128)(2,1)S(1)}, u32[]{:S(2)}, u32[]{:S(2)}) collective-permute-start(bf16[1,1024]{1,0:T(2,128)(2,1)S(1)} %slice.53), channel_id=1, source_target_pairs={{0,1},{1,2},{2,3},{3,4},{4,5},{5,6},{6,7},{7,8},{8,9},{9,10},{10,1... | collective-permute-start | bytes 6152 | tf_op jit(solution)/shard_map/ppermute | solution.py:24
  157.8 2.7 %shard_map.49 = bf16[512,1024]{1,0:T(8,128)(2,1)} custom-call(bf16[512,1024]{1,0:T(8,128)(2,1)} %copy-done.3, bf16[128,1024]{1,0:T(8,128)(2,1)} %pad_select_fusion.lift_ref), custom_call_target="tpu_custom_call" | custom-call | tf_op jit(solution)/shard_map/pallas_call | solution.py:157
  160.5 1.3 fusion.12
  (57 shorter events, 10.2 us)
Async XLA Ops:
  0.0 150.5 %copy-start = (bf16[1024,1024]{1,0:T(8,128)(2,1)S(1)}, bf16[1024,1024]{1,0:T(8,128)(2,1)}, u32[]{:S(2)}) copy-start(bf16[1024,1024]{1,0:T(8,128)(2,1)} %param.7) | copy-start | bytes 6291460
  0.0 38.7 %copy-start.5 = (s32[2048]{0:T(1024)S(1)}, s32[2048]{0:T(1024)}, u32[]{:S(2)}) copy-start(s32[2048]{0:T(1024)} %param.5) | copy-start | bytes 24580
  0.0 40.6 %collective-permute-start.1 = (bf16[3,512,1024]{2,1,0:T(8,128)(2,1)}, bf16[3,512,1024]{2,1,0:T(8,128)(2,1)}, u32[]{:S(2)}, u32[]{:S(2)}) collective-permute-start(bf16[3,512,1024]{2,1,0:T(8,128)(2,1)} %bitcast.53), channel_id=1, source_target_pairs={{0,1},{2,3},{4,5},{6,7},{8,9},{10,11},{12,13},{14,15},{16,17},{18,... | collective-permute-start | bytes 9437192 | tf_op jit(solution)/shard_map/ppermute | solution.py:173
  4.1 23.9 %collective-permute-start = (bf16[2,512,512]{2,1,0:T(8,128)(2,1)S(1)}, bf16[2,512,512]{2,1,0:T(8,128)(2,1)}, u32[]{:S(2)}, u32[]{:S(2)}) collective-permute-start(bf16[2,512,512]{2,1,0:T(8,128)(2,1)S(1)} %get-tuple-element.20), channel_id=1, source_target_pairs={{0,2},{1,3},{2,4},{3,5},{4,6},{5,7},{6,8},{7,9},{8,10},{9,11},{10,... | collective-permute-start | bytes 3145736 | tf_op jit(solution)/shard_map/ppermute | solution.py:24
  28.0 12.6 %collective-permute-start.2 = (bf16[2,512,512]{2,1,0:T(8,128)(2,1)}, bf16[2,512,512]{2,1,0:T(8,128)(2,1)}, u32[]{:S(2)}, u32[]{:S(2)}) collective-permute-start(bf16[2,512,512]{2,1,0:T(8,128)(2,1)} %collective-permute-done.k0_ref.v0_ref), channel_id=1, source_target_pairs={{1,0},{3,2},{5,4},{7,6},{9,8},{11,10},{13,12},{15,14},{17,16},{19,... | collective-permute-start | bytes 3145736 | tf_op jit(solution)/shard_map/ppermute | solution.py:173
  34.6 26.2 %collective-permute-start.3 = (bf16[2,512,512]{2,1,0:T(8,128)(2,1)}, bf16[2,512,512]{2,1,0:T(8,128)(2,1)S(1)}, u32[]{:S(2)}, u32[]{:S(2)}) collective-permute-start(bf16[2,512,512]{2,1,0:T(8,128)(2,1)} %get-tuple-element.12), channel_id=1, source_target_pairs={{0,2},{1,3},{2,4},{3,5},{4,6},{5,7},{6,8},{7,9},{8,10},{9,11},{10,... | collective-permute-start | bytes 3145736 | tf_op jit(solution)/shard_map/ppermute | solution.py:24
  60.8 3.7 %copy-start.2 = (bf16[2,512,512]{2,1,0:T(8,128)(2,1)}, bf16[2,512,512]{2,1,0:T(8,128)(2,1)S(1)}, u32[]{:S(2)}) copy-start(bf16[2,512,512]{2,1,0:T(8,128)(2,1)S(1)} %collective-permute-done.3.k0_ref.v0_ref) | copy-start | bytes 3145732
  60.8 3.7 %collective-permute-start.4 = (bf16[2,512,512]{2,1,0:T(8,128)(2,1)S(1)}, bf16[2,512,512]{2,1,0:T(8,128)(2,1)}, u32[]{:S(2)}, u32[]{:S(2)}) collective-permute-start(bf16[2,512,512]{2,1,0:T(8,128)(2,1)S(1)} %collective-permute-done.3.k0_ref.v0_ref), channel_id=1, source_target_pairs={{1,0},{3,2},{5,4},{7,6},{9,8},{11,10},{13,12},{15,14},{17,16},{19,... | collective-permute-start | bytes 3145736 | tf_op jit(solution)/shard_map/ppermute | solution.py:173
  83.7 7.6 %collective-permute-start.5 = (bf16[3,128,256]{2,1,0:T(8,128)(2,1)}, bf16[3,128,256]{2,1,0:T(8,128)(2,1)S(1)}, u32[]{:S(2)}, u32[]{:S(2)}) collective-permute-start(bf16[3,128,256]{2,1,0:T(8,128)(2,1)} %get-tuple-element.23), channel_id=1, source_target_pairs={{0,3},{1,0},{2,1},{3,2},{4,7},{5,4},{6,5},{7,6},{8,11},{9,8},{10,9... | collective-permute-start | bytes 589832 | tf_op jit(solution)/shard_map/ppermute | solution.py:33
  84.1 7.2 %collective-permute-start.6 = (bf16[3,128,256]{2,1,0:T(8,128)(2,1)S(1)}, bf16[3,128,256]{2,1,0:T(8,128)(2,1)S(1)}, u32[]{:S(2)}, u32[]{:S(2)}) collective-permute-start(bf16[3,128,256]{2,1,0:T(8,128)(2,1)S(1)} %get-tuple-element.22), channel_id=1, source_target_pairs={{0,2},{1,3},{2,0},{3,1},{4,6},{5,7},{6,4},{7,5},{8,10},{9,11},{10,... | collective-permute-start | bytes 589832 | tf_op jit(solution)/shard_map/ppermute | solution.py:33
  84.1 8.6 %collective-permute-start.7 = (bf16[3,128,256]{2,1,0:T(8,128)(2,1)S(1)}, bf16[3,128,256]{2,1,0:T(8,128)(2,1)S(1)}, u32[]{:S(2)}, u32[]{:S(2)}) collective-permute-start(bf16[3,128,256]{2,1,0:T(8,128)(2,1)S(1)} %get-tuple-element.21), channel_id=1, source_target_pairs={{0,1},{1,2},{2,3},{3,0},{4,5},{5,6},{6,7},{7,4},{8,9},{9,10},{10,1... | collective-permute-start | bytes 589832 | tf_op jit(solution)/shard_map/ppermute | solution.py:33
  93.0 40.8 %copy-start.1 = (bf16[2,4,128,256]{3,2,1,0:T(8,128)(2,1)}, bf16[2,4,128,256]{3,2,1,0:T(8,128)(2,1)S(1)}, u32[]{:S(2)}) copy-start(bf16[2,4,128,256]{3,2,1,0:T(8,128)(2,1)S(1)} %copy.8) | copy-start | bytes 1572868
  93.0 14.7 %collective-permute-start.8 = (bf16[2,512,256]{2,1,0:T(8,128)(2,1)S(1)}, bf16[2,512,256]{2,1,0:T(8,128)(2,1)S(1)}, u32[]{:S(2)}, u32[]{:S(2)}) collective-permute-start(bf16[2,512,256]{2,1,0:T(8,128)(2,1)S(1)} %bitcast.63), channel_id=1, source_target_pairs={{0,4},{1,5},{2,6},{3,7},{4,8},{5,9},{6,10},{7,11},{8,12},{9,13},{1... | collective-permute-start | bytes 1572872 | tf_op jit(solution)/shard_map/ppermute | solution.py:24
  107.8 0.8 copy-start.4
  108.6 12.9 %collective-permute-start.9 = (bf16[2,512,256]{2,1,0:T(8,128)(2,1)S(1)}, bf16[2,512,256]{2,1,0:T(8,128)(2,1)}, u32[]{:S(2)}, u32[]{:S(2)}) collective-permute-start(bf16[2,512,256]{2,1,0:T(8,128)(2,1)S(1)} %collective-permute-done.8.k2_ref.v2_ref), channel_id=1, source_target_pairs={{0,4},{1,5},{2,6},{3,7},{4,8},{5,9},{6,10},{7,11},{8,12},{9,13},{1... | collective-permute-start | bytes 1572872 | tf_op jit(solution)/shard_map/ppermute | solution.py:24
  121.5 12.4 %collective-permute-start.10 = (bf16[2,512,256]{2,1,0:T(8,128)(2,1)}, bf16[2,512,256]{2,1,0:T(8,128)(2,1)}, u32[]{:S(2)}, u32[]{:S(2)}) collective-permute-start(bf16[2,512,256]{2,1,0:T(8,128)(2,1)} %collective-permute-done.9.k1_ref.v1_ref), channel_id=1, source_target_pairs={{0,4},{1,5},{2,6},{3,7},{4,8},{5,9},{6,10},{7,11},{8,12},{9,13},{1... | collective-permute-start | bytes 1572872 | tf_op jit(solution)/shard_map/ppermute | solution.py:24
  130.3 1.1 copy-start.3
  141.4 6.9 %collective-permute-start.11 = (bf16[128,256]{1,0:T(8,128)(2,1)S(1)}, bf16[128,256]{1,0:T(8,128)(2,1)S(1)}, u32[]{:S(2)}, u32[]{:S(2)}) collective-permute-start(bf16[128,256]{1,0:T(8,128)(2,1)S(1)} %get-tuple-element.26), channel_id=1, source_target_pairs={{0,3},{1,0},{2,1},{3,2},{4,7},{5,4},{6,5},{7,6},{8,11},{9,8},{10,9... | collective-permute-start | bytes 196616 | tf_op jit(solution)/shard_map/ppermute | solution.py:33
  145.7 3.7 %collective-permute-start.12 = (bf16[128,256]{1,0:T(8,128)(2,1)S(1)}, bf16[128,256]{1,0:T(8,128)(2,1)S(1)}, u32[]{:S(2)}, u32[]{:S(2)}) collective-permute-start(bf16[128,256]{1,0:T(8,128)(2,1)S(1)} %get-tuple-element.25), channel_id=1, source_target_pairs={{0,2},{1,3},{2,0},{3,1},{4,6},{5,7},{6,4},{7,5},{8,10},{9,11},{10,... | collective-permute-start | bytes 196616 | tf_op jit(solution)/shard_map/ppermute | solution.py:33
  145.7 3.7 %collective-permute-start.13 = (bf16[128,256]{1,0:T(8,128)(2,1)S(1)}, bf16[128,256]{1,0:T(8,128)(2,1)S(1)}, u32[]{:S(2)}, u32[]{:S(2)}) collective-permute-start(bf16[128,256]{1,0:T(8,128)(2,1)S(1)} %get-tuple-element.24), channel_id=1, source_target_pairs={{0,1},{1,2},{2,3},{3,0},{4,5},{5,6},{6,7},{7,4},{8,9},{9,10},{10,1... | collective-permute-start | bytes 196616 | tf_op jit(solution)/shard_map/ppermute | solution.py:33
  151.0 9.4 %collective-permute-start.14 = (bf16[1,1024]{1,0:T(2,128)(2,1)S(1)}, bf16[1,1024]{1,0:T(2,128)(2,1)S(1)}, u32[]{:S(2)}, u32[]{:S(2)}) collective-permute-start(bf16[1,1024]{1,0:T(2,128)(2,1)S(1)} %slice.53), channel_id=1, source_target_pairs={{0,1},{1,2},{2,3},{3,4},{4,5},{5,6},{6,7},{7,8},{8,9},{9,10},{10,1... | collective-permute-start | bytes 6152 | tf_op jit(solution)/shard_map/ppermute | solution.py:24
